TPU v7x, 32 devices: a whole 2x2x4 slice. The times are simulated.
32 devices in a mesh: scene: 2 (over y), step: 4 (over x, core), seq: 4 (over z).
Axes of the slice: x: 2, y: 2, z: 4, core: 2. Of those that a mesh axis runs over, the one named last changes fastest.
Arguments:
- queries: bfloat16 [32, 2, 24, 32, 128], P(('scene', 'step'), None, None, 'seq'), parts along dimension 0, may hold values from -256 to 256
- keys: bfloat16 [32, 2, 24, 32, 128], P(('scene', 'step'), None, None, 'seq'), parts along dimension 0, may hold values from -8 to 8
- values: bfloat16 [32, 2, 24, 32, 128], P(('scene', 'step'), None, None, 'seq'), parts along dimension 0, may hold values from -6 to 6
- start_latent: float32 [128, 32], P('scene', 'seq'), parts along dimension 0, may hold values from -6 to 6
- out_weight: bfloat16 [64, 3072], replicated, may hold values from -0.109375 to 0.109375
- cfg_table: float32 [8], replicated, may hold values from 3 to 8
- cfg_index: int32 [2], P('scene'), parts along dimension 0, may hold values from 0 to 7
- step_table: float32 [1000], replicated, may hold values from 0.03 to 0.12
- time_index: int32 [32], P(('scene', 'step')), parts along dimension 0, may hold values from 0 to 999
Outputs:
- new_iterates: float32 [32, 64, 32], P(('scene', 'step'), None, 'seq'), parts along dimension 0
There are 2 independent parts, one for each index of `scene`. A program takes and returns all parts, laid end to end along the dimension named above; an argument that names none is the same for every part. Nothing has to cross between parts.
All inputs are finite; a program needn't handle non-finite values.
Results may differ from a plain program's by a relative error of at most 0.0034.
Values may be sent and summed in bfloat16 or wider, within the bound.
No kernel may reach another device: no remote copies, remote signals or barrier semaphores. Data moves between devices by JAX's collectives and lax.ppermute only.
A program may use at most 64 MiB of HBM per device.

v0:
```python
import jax
import jax.numpy as jnp
from jax import lax
from jax.sharding import PartitionSpec as P

HD = 128
H = 24


def lookup(table, index):
    count = table.shape[0]
    hits = index[..., None] == jnp.arange(count, dtype=jnp.int32)
    return jnp.sum(jnp.where(hits, table, jnp.zeros((), table.dtype)), axis=-1)


def attend(query_rows, key_rows, value_rows):
    length = query_rows.shape[0]
    block_rows = min(512, length)
    scale = HD ** (-0.5)

    def one_block(query_block):
        scores = jnp.dot(query_block, key_rows.T, preferred_element_type=jnp.float32) * scale
        expo = jnp.exp(scores - jnp.max(scores, axis=-1, keepdims=True))
        total = jnp.sum(expo, axis=-1, keepdims=True)
        weights = expo.astype(jnp.bfloat16)
        return (jnp.dot(weights, value_rows, preferred_element_type=jnp.float32) / total).astype(
            jnp.bfloat16
        )

    blocks = query_rows.reshape(length // block_rows, block_rows, query_rows.shape[1])
    return lax.map(one_block, blocks).reshape(query_rows.shape)


def attend_items(pieces):
    query_all, key_all, value_all = pieces
    outputs = lax.map(
        lambda trio: attend(trio[0], trio[1], trio[2]), (query_all[0], key_all[0], value_all[0])
    )
    return outputs[None]


def on_device(
    queries, keys, values, start_latent, out_weight, cfg_table, cfg_index, step_table, time_index
):
    step_dev, branches, heads, tok_dev, head_size = queries.shape
    groups = lax.axis_size("seq")
    items = step_dev * branches * heads

    def to_items(array):
        return array.reshape(groups, items // groups, tok_dev, head_size)

    gathered = attend_items(
        (
            lax.all_to_all(to_items(queries), "seq", split_axis=0, concat_axis=2, tiled=True),
            lax.all_to_all(to_items(keys), "seq", split_axis=0, concat_axis=2, tiled=True),
            lax.all_to_all(to_items(values), "seq", split_axis=0, concat_axis=2, tiled=True),
        )
    )
    returned = lax.all_to_all(gathered, "seq", split_axis=2, concat_axis=0, tiled=True)
    heads_out = returned.reshape(step_dev, branches, heads, tok_dev, head_size)
    wide_out = heads_out.astype(jnp.float32)
    square_sum = jnp.sum(wide_out * wide_out, axis=(2, 4))
    root_mean = jnp.sqrt(square_sum / (H * HD) + 1e-06)
    weight_heads = out_weight.reshape(out_weight.shape[0], heads, head_size)
    drift = (
        jnp.einsum("chd,sbhld->sbcl", weight_heads, heads_out, preferred_element_type=jnp.float32)
        / root_mean[:, :, None, :]
    )
    guide_scale = lookup(cfg_table, cfg_index)[0]
    guided = drift[:, 1] + guide_scale * (drift[:, 0] - drift[:, 1])
    step_len = lookup(step_table, time_index)
    local_cum = jnp.cumsum(step_len[:, None, None] * guided, axis=0)
    group_total = local_cum[-1]
    every_total = lax.all_gather(group_total[None], "step", axis=0, tiled=True)
    position = lax.axis_index("step")
    order = jnp.arange(every_total.shape[0], dtype=jnp.int32)
    earlier = jnp.sum(
        jnp.where((order < position)[:, None, None], every_total, jnp.zeros((), jnp.float32)),
        axis=0,
    )
    return start_latent[None] + earlier[None] + local_cum


def solution(mesh):
    return jax.shard_map(
        on_device,
        mesh=mesh,
        in_specs=(
            P(("scene", "step"), None, None, "seq", None),
            P(("scene", "step"), None, None, "seq", None),
            P(("scene", "step"), None, None, "seq", None),
            P("scene", "seq"),
            P(),
            P(),
            P("scene"),
            P(),
            P(("scene", "step")),
        ),
        out_specs=P(("scene", "step"), None, "seq"),
        check_vma=False,
    )
```

profile of v0, /device:TPU:0, one launch (start us, length us, event | category | flops | bytes accessed | tf_op | source)
XLA Modules:
  0.0 86.2 jit_solution(12332049900195506394)
XLA Ops:
  0.0 18.1 %all_to_all.60 = bf16[4,48,8,128]{3,2,1,0:T(8,128)(2,1)S(1)} all-to-all(bf16[4,48,8,128]{3,2,1,0:T(8,128)(2,1)} %bitcast.96), channel_id=1, replica_groups=mesh['scene'=2,'step'=4,'seq'=4] {'seq'}, dimensions={0} | all-to-all | bytes 786432 | tf_op jit(solution)/shard_map/all_to_all | solution.py:56
  18.1 13.7 %all_to_all.61 = bf16[4,48,8,128]{3,2,1,0:T(8,128)(2,1)S(1)} all-to-all(bf16[4,48,8,128]{3,2,1,0:T(8,128)(2,1)S(1)} %bitcast.97), channel_id=1, replica_groups=mesh['scene'=2,'step'=4,'seq'=4] {'seq'}, dimensions={0} | all-to-all | bytes 786432 | tf_op jit(solution)/shard_map/all_to_all | solution.py:55
  31.9 3.5 %all-to-all-start = ((bf16[4,48,8,128]{3,2,1,0:T(8,128)(2,1)}), bf16[4,48,8,128]{3,2,1,0:T(8,128)(2,1)S(1)}, u32[]{:S(2)}, u32[]{:S(2)}) async-start(bf16[4,48,8,128]{3,2,1,0:T(8,128)(2,1)} %bitcast.4), calls=%async_computation | async-start | bytes 786432 | tf_op jit(solution)/shard_map/all_to_all | solution.py:54
  35.5 10.3 %all-to-all-done = bf16[4,48,8,128]{3,2,1,0:T(8,128)(2,1)S(1)} async-done(((bf16[4,48,8,128]{3,2,1,0:T(8,128)(2,1)}), bf16[4,48,8,128]{3,2,1,0:T(8,128)(2,1)S(1)}, u32[]{:S(2)}, u32[]{:S(2)}) %all-to-all-start) | async-done | bytes 393248 | tf_op jit(solution)/shard_map/all_to_all | solution.py:54
  45.9 18.0 %while.10 = (s32[]{:T(128)}, bf16[48,32,128]{2,1,0:T(8,128)(2,1)S(1)}, bf16[48,32,128]{2,1,0:T(8,128)(2,1)S(1)}, bf16[48,32,128]{2,1,0:T(8,128)(2,1)S(1)}, bf16[48,32,128]{2,1,0:T(8,128)(2,1)S(1)}, /*index=5*/s32[]{:T(128)}) while((s32[]{:T(128)}, bf16[48,32,128]{2,1,0:T(8,128)(2,1)S(1)}, bf16[48,32,128]{2,1,0:T(8,128)(2,1)S(1)}, ...), condition=%wide.region_4.5_spmd, body=%wide.region_1.4_spmd.sunk | while | flops 538562 | bytes 60869 | solution.py:36
  46.5 0.2 fusion.38
  47.2 0.2 fusion.38
  48.0 0.2 fusion.38
  48.7 0.2 fusion.38
  49.5 0.2 fusion.38
  49.8 0.2 fusion.38
  50.2 0.2 fusion.38
  63.9 0.9 %copy.67 = bf16[48,32,128]{2,0,1:T(8,128)(2,1)} copy(bf16[48,32,128]{2,1,0:T(8,128)(2,1)S(1)} %get-tuple-element.47) | data formatting | bytes 786432 | tf_op jit(solution)/shard_map/while | solution.py:36
  64.8 3.6 %all-to-all-start.3 = ((bf16[1,48,32,128]{3,1,0,2:T(8,128)(2,1)}), bf16[1,48,32,128]{3,1,0,2:T(8,128)(2,1)S(1)}, u32[]{:S(2)}, u32[]{:S(2)}) async-start(bf16[1,48,32,128]{3,1,0,2:T(8,128)(2,1)} %bitcast.79), calls=%async_computation.3 | async-start | bytes 786432 | tf_op jit(solution)/shard_map/all_to_all | solution.py:59
  69.2 0.6 copy-done.5
  69.9 0.7 fusion.26
  70.5 0.2 select_reduce_fusion.1
  70.7 7.6 %all-to-all-done.3 = bf16[1,48,32,128]{3,1,0,2:T(8,128)(2,1)S(1)} async-done(((bf16[1,48,32,128]{3,1,0,2:T(8,128)(2,1)}), bf16[1,48,32,128]{3,1,0,2:T(8,128)(2,1)S(1)}, u32[]{:S(2)}, u32[]{:S(2)}) %all-to-all-start.3) | async-done | bytes 393248 | tf_op jit(solution)/shard_map/all_to_all | solution.py:59
  78.4 0.3 multiply_reduce_fusion
  78.7 0.3 fusion.16
  79.0 0.7 fusion.22
  79.7 5.2 %all_gather.3 = f32[4,64,8]{1,2,0:T(8,128)S(1)} all-gather(f32[1,64,8]{1,2,0:T(8,128)S(1)} %slice.15), channel_id=1, replica_groups=mesh['scene'=2,'step'=4,'seq'=4] {'step'}, dimensions={0}, use_global_device_ids=true | all-gather | bytes 10240 | tf_op jit(solution)/shard_map/all_gather | solution.py:74
  84.9 0.6 copy-done.2
  85.5 0.6 broadcast_add_fusion
  (159 shorter events, 16.8 us)
Async XLA Ops:
  0.0 18.1 %copy-start = (bf16[4,2,24,8,128]{4,3,2,1,0:T(8,128)(2,1)S(1)}, bf16[4,2,24,8,128]{4,3,2,1,0:T(8,128)(2,1)}, u32[]{:S(2)}) copy-start(bf16[4,2,24,8,128]{4,3,2,1,0:T(8,128)(2,1)} %param.12) | copy-start | bytes 1179652
  31.9 14.0 %all-to-all-start = ((bf16[4,48,8,128]{3,2,1,0:T(8,128)(2,1)}), bf16[4,48,8,128]{3,2,1,0:T(8,128)(2,1)S(1)}, u32[]{:S(2)}, u32[]{:S(2)}) async-start(bf16[4,48,8,128]{3,2,1,0:T(8,128)(2,1)} %bitcast.4), calls=%async_computation | async-start | bytes 786432 | tf_op jit(solution)/shard_map/all_to_all | solution.py:54
  64.8 3.6 %copy-start.1 = (bf16[64,3072]{1,0:T(8,128)(2,1)S(1)}, bf16[64,3072]{1,0:T(8,128)(2,1)}, u32[]{:S(2)}) copy-start(bf16[64,3072]{1,0:T(8,128)(2,1)} %param.15) | copy-start | bytes 1179652
  64.8 13.4 %all-to-all-start.3 = ((bf16[1,48,32,128]{3,1,0,2:T(8,128)(2,1)}), bf16[1,48,32,128]{3,1,0,2:T(8,128)(2,1)S(1)}, u32[]{:S(2)}, u32[]{:S(2)}) async-start(bf16[1,48,32,128]{3,1,0,2:T(8,128)(2,1)} %bitcast.79), calls=%async_computation.3 | async-start | bytes 786432 | tf_op jit(solution)/shard_map/all_to_all | solution.py:59
  69.2 1.4 %copy-start.3 = (f32[1000]{0:T(1024)S(1)}, f32[1000]{0:T(1024)}, u32[]{:S(2)}) copy-start(f32[1000]{0:T(1024)} %param.18) | copy-start | bytes 12004
  69.2 0.7 copy-start.5
  69.8 0.7 copy-start.4
  84.9 0.7 copy-start.2
where the time goes:
time: 86.6 us; the launch traced here: 86.2 us
  blocking collectives  37 us (43%)
  waiting for transfers between devices  17.9 us (21%)
  matrix products  16.4 us (19%)
  starting transfers between devices  7.05 us (8%)
  other arithmetic  3.93 us (5%)
  local copies, waits for them, and re-layouts  2.56 us (3%)
    all_to_all x1, blocking collectives, on_device(): lax.all_to_all(to_items(values), 'seq', split_axis=0, concat_axis=2, tile...  18.1 us
    all_to_all x1, blocking collectives, on_device(): lax.all_to_all(to_items(keys), 'seq', split_axis=0, concat_axis=2, tiled=...  13.7 us
    all_to_all x1, waiting for transfers between devices, on_device(): lax.all_to_all(to_items(queries), 'seq', split_axis=0, concat_axis=2, til...  10.3 us
    dot_general x48, matrix products, one_block(): jnp.dot(weights, value_rows, preferred_element_type=jnp.float32) / total  8.69 us
    all_to_all x1, waiting for transfers between devices, on_device(): lax.all_to_all(gathered, 'seq', split_axis=2, concat_axis=0, tiled=True)  7.56 us
    dot_general x48, matrix products, one_block(): jnp.dot(query_block, key_rows.T, preferred_element_type=jnp.float32) * scale  7.47 us
    all_gather x1, blocking collectives, on_device(): every_total = lax.all_gather(group_total[None], 'step', axis=0, tiled=True)  5.17 us
    all_to_all x1, starting transfers between devices, on_device(): lax.all_to_all(gathered, 'seq', split_axis=2, concat_axis=0, tiled=True)  3.59 us
  transfers between devices with their start and end apart: 2, of which 2 were waited for; matrix products, arithmetic and copies ran while one was open for 1% of the time, Pallas kernels for 0%

commit v1 on v0

v1 whole, which is shorter than its diff:
```python
import jax
import jax.numpy as jnp
from jax import lax
from jax.sharding import PartitionSpec as P

HD = 128
H = 24


def lookup(table, index):
    count = table.shape[0]
    hits = index[..., None] == jnp.arange(count, dtype=jnp.int32)
    return jnp.sum(jnp.where(hits, table, jnp.zeros((), table.dtype)), axis=-1)


def attend(query_rows, key_rows, value_rows):
    scale = HD ** (-0.5)
    scores = (
        jnp.einsum("iqd,ikd->iqk", query_rows, key_rows, preferred_element_type=jnp.float32) * scale
    )
    expo = jnp.exp(scores - jnp.max(scores, axis=-1, keepdims=True))
    total = jnp.sum(expo, axis=-1, keepdims=True)
    weights = expo.astype(jnp.bfloat16)
    out = jnp.einsum("iqk,ikd->iqd", weights, value_rows, preferred_element_type=jnp.float32)
    return (out / total).astype(jnp.bfloat16)


def on_device(
    queries, keys, values, start_latent, out_weight, cfg_table, cfg_index, step_table, time_index
):
    step_dev, branches, heads, tok_dev, head_size = queries.shape
    groups = lax.axis_size("seq")
    steps_axis = lax.axis_size("step")
    items = step_dev * branches * heads
    per_dev = items // groups
    length = tok_dev * groups
    channels = out_weight.shape[0]
    me = lax.axis_index("seq")

    stacked = jnp.stack([queries, keys, values]).reshape(3, groups, per_dev, tok_dev, head_size)
    gathered = lax.all_to_all(stacked, "seq", split_axis=1, concat_axis=3, tiled=True)
    gathered = gathered.reshape(3, per_dev, length, head_size)
    heads_out = attend(gathered[0], gathered[1], gathered[2])

    weight_heads = out_weight.reshape(channels, heads, head_size)
    guide_scale = lookup(cfg_table, cfg_index)[0]
    step_len = lookup(step_table, time_index)

    if per_dev % (branches * heads) == 0:
        local_steps = per_dev // (branches * heads)
        ho = heads_out.reshape(local_steps, branches, heads, length, head_size)
        wide = ho.astype(jnp.float32)
        square_sum = jnp.sum(wide * wide, axis=(2, 4))
        root_mean = jnp.sqrt(square_sum / (H * HD) + 1e-06)
        drift = (
            jnp.einsum("chd,sbhld->sbcl", weight_heads, ho, preferred_element_type=jnp.float32)
            / root_mean[:, :, None, :]
        )
        guided = drift[:, 1] + guide_scale * (drift[:, 0] - drift[:, 1])
        my_len = lax.dynamic_slice_in_dim(step_len, me * local_steps, local_steps)
        update = my_len[:, None, None] * guided
        every = lax.all_gather(update, ("step", "seq"), axis=0, tiled=True)
        prefix = jnp.cumsum(every, axis=0)
        position = lax.axis_index("step")
        mine = lax.dynamic_slice_in_dim(prefix, position * step_dev, step_dev, axis=0)
        mine = lax.dynamic_slice_in_dim(mine, me * tok_dev, tok_dev, axis=2)
        return start_latent[None] + mine

    assert heads % per_dev == 0
    share = heads // per_dev
    first = me * per_dev
    head_ids = (first + jnp.arange(per_dev, dtype=jnp.int32)) % heads
    chosen = jnp.take(weight_heads, head_ids, axis=1)
    numer = jnp.einsum("cid,ild->cl", chosen, heads_out, preferred_element_type=jnp.float32)
    wide = heads_out.astype(jnp.float32)
    square = jnp.sum(wide * wide, axis=(0, 2))
    partial = jnp.concatenate([numer, square[None]], axis=0)
    partial = partial.reshape(channels + 1, groups, tok_dev)
    returned = lax.all_to_all(partial, "seq", split_axis=1, concat_axis=1, tiled=True)
    returned = returned.reshape(channels + 1, step_dev * branches, share, tok_dev)
    summed = jnp.sum(returned, axis=2).reshape(channels + 1, step_dev, branches, tok_dev)
    numer = jnp.transpose(summed[:channels], (1, 2, 0, 3))
    square_sum = summed[channels]
    root_mean = jnp.sqrt(square_sum / (H * HD) + 1e-06)
    drift = numer / root_mean[:, :, None, :]
    guided = drift[:, 1] + guide_scale * (drift[:, 0] - drift[:, 1])
    local_cum = jnp.cumsum(step_len[:, None, None] * guided, axis=0)
    group_total = local_cum[-1]
    every_total = lax.all_gather(group_total[None], "step", axis=0, tiled=True)
    position = lax.axis_index("step")
    order = jnp.arange(steps_axis, dtype=jnp.int32)
    earlier = jnp.sum(
        jnp.where((order < position)[:, None, None], every_total, jnp.zeros((), jnp.float32)),
        axis=0,
    )
    return start_latent[None] + earlier[None] + local_cum


def solution(mesh):
    return jax.shard_map(
        on_device,
        mesh=mesh,
        in_specs=(
            P(("scene", "step"), None, None, "seq", None),
            P(("scene", "step"), None, None, "seq", None),
            P(("scene", "step"), None, None, "seq", None),
            P("scene", "seq"),
            P(),
            P(),
            P("scene"),
            P(),
            P(("scene", "step")),
        ),
        out_specs=P(("scene", "step"), None, "seq"),
        check_vma=False,
    )
```

time: 86.6 us -> 73.9 us (0.85)
  matrix products: 16.4 us -> 1.24 us
  waiting for transfers between devices: 17.9 us -> 26.3 us
  blocking collectives: 37 us -> 31.3 us
  other arithmetic: 3.93 us -> 5.9 us
  local copies, waits for them, and re-layouts: 2.56 us -> 1.69 us
    all_to_all x2 -> x0, blocking collectives: 31.9 us -> none  [the longest x1 18.1 us: on_device(): lax.all_to_all(to_items(values), 'seq', split_axis=0, concat_axis=2, tile...]
    all_gather x1, blocking collectives: 5.17 us -> 31.3 us  [on_device(): every = lax.all_gather(update, ('step', 'seq'), axis=0, tiled=True)]
    dot_general x97 -> x3, matrix products: 16.4 us -> 1.24 us  [the longest x1 0.65 us: attend(): jnp.einsum('iqk,ikd->iqd', weights, value_rows, preferred_element_type=jn...]
    all_to_all x2 -> x1, waiting for transfers between devices: 17.9 us -> 26.3 us  [on_device(): lax.all_to_all(stacked, 'seq', split_axis=1, concat_axis=3, tiled=True)]
    another operation x1 -> x2, other arithmetic: 0.7 us -> 3.48 us  [the longest x1 2.42 us: on_device(): jnp.stack([queries, keys, values])]
    reduce_sum x51 -> x2, other arithmetic: 1.75 us -> 0.21 us  [the longest x1 0.19 us: attend(): total = jnp.sum(expo, axis=-1, keepdims=True)]
    mul x0 -> x1, other arithmetic: none -> 1.24 us  [on_device(): update = my_len[:, None, None] * guided]
    unnamed x13 -> x11, local copies, waits for them, and re-layouts: 1.33 us -> 0.1 us
  transfers between devices with their start and end apart: 2 -> 1, of which waited for: 2 -> 1; matrix products, arithmetic and copies ran while one was open for 1% -> 2% of each run, Pallas kernels for 0% -> 0%
where the time goes in v1:
time: 73.9 us; the launch traced here: 73.7 us
  blocking collectives  31.3 us (42%)
  waiting for transfers between devices  26.3 us (36%)
  starting transfers between devices  6.46 us (9%)
  other arithmetic  5.9 us (8%)
  local copies, waits for them, and re-layouts  1.69 us (2%)
  matrix products  1.24 us (2%)
  between operations  0.76 us (1%)
    all_gather x1, blocking collectives, on_device(): every = lax.all_gather(update, ('step', 'seq'), axis=0, tiled=True)  31.3 us
    all_to_all x1, waiting for transfers between devices, on_device(): lax.all_to_all(stacked, 'seq', split_axis=1, concat_axis=3, tiled=True)  26.3 us
    all_to_all x1, starting transfers between devices, on_device(): lax.all_to_all(stacked, 'seq', split_axis=1, concat_axis=3, tiled=True)  6.46 us
    another operation x1, other arithmetic, on_device(): jnp.stack([queries, keys, values])  2.42 us
  transfers between devices with their start and end apart: 1, of which 1 were waited for; matrix products, arithmetic and copies ran while one was open for 2% of the time, Pallas kernels for 0%

profile of v1, /device:TPU:0, one launch (start us, length us, event | category | flops | bytes accessed | tf_op | source)
XLA Modules:
  0.0 73.7 jit_solution(12643342871418828922)
XLA Ops:
  0.0 0.0 copy-start
  0.0 2.4 %pad_maximum_fusion = bf16[3,4,48,8,128]{4,3,2,0,1:T(8,128)(2,1)} fusion(bf16[1,4,48,8,128]{4,3,2,0,1:T(8,128)(2,1)} %bitcast.63, bf16[1,4,48,8,128]{4,3,2,0,1:T(8,128)(2,1)} %bitcast.64, bf16[1,4,48,8,128]{4,3,2,0,1:T(8,128)(2,1)} %bitcast.65), kind=kLoop, calls=%fused_computation.3 | loop fusion | flops 1179648 | bytes 2359296 | tf_op jit(solution)/shard_map/stack | solution.py:40
  2.4 6.5 %all-to-all-start = ((bf16[3,4,48,8,128]{4,3,2,0,1:T(8,128)(2,1)}), bf16[3,4,48,8,128]{4,3,2,0,1:T(8,128)(2,1)S(1)}, u32[]{:S(2)}, u32[]{:S(2)}) async-start(bf16[3,4,48,8,128]{4,3,2,0,1:T(8,128)(2,1)} %pad_maximum_fusion), calls=%async_computation | async-start | bytes 2359296 | tf_op jit(solution)/shard_map/all_to_all | solution.py:41
  9.6 0.0 copy-done.1
  9.6 0.1 copy.26
  9.7 0.0 copy-done.2
  9.7 0.0 copy-done.3
  9.7 0.2 select_reduce_fusion
  9.8 0.6 dynamic_slice.8
  10.5 0.0 copy-done.4
  10.5 0.7 fusion.18
  11.1 26.3 %all-to-all-done = bf16[3,4,48,8,128]{4,3,2,0,1:T(8,128)(2,1)S(1)} async-done(((bf16[3,4,48,8,128]{4,3,2,0,1:T(8,128)(2,1)}), bf16[3,4,48,8,128]{4,3,2,0,1:T(8,128)(2,1)S(1)}, u32[]{:S(2)}, u32[]{:S(2)}) %all-to-all-start) | async-done | bytes 1179680 | tf_op jit(solution)/shard_map/all_to_all | solution.py:41
  37.4 0.1 fusion.19
  37.5 0.3 fusion.20
  37.9 0.2 fusion.3
  38.1 0.7 multiply_reduce_fusion
  38.7 0.0 copy-done
  38.8 0.2 fusion.2
  39.0 1.2 %fusion.17 = f32[1,64,32]{1,2,0:T(8,128)S(1)} fusion(f32[1,2,64,32]{2,3,1,0:T(8,128)S(1)} %fusion.2, f32[]{:T(128)} %fusion.18, f32[]{:T(128)} %bitcast), kind=kLoop, calls=%fused_computation.25 | loop fusion | flops 8192 | bytes 24584 | tf_op jit(solution)/shard_map/mul | solution.py:61
  40.3 31.3 %all_gather.3 = f32[16,64,32]{1,2,0:T(8,128)S(1)} all-gather(f32[1,64,32]{1,2,0:T(8,128)S(1)} %fusion.17), channel_id=1, replica_groups=mesh['scene'=2,'step'=4,'seq'=4] {'step','seq'}, dimensions={0}, use_global_device_ids=true | all-gather | bytes 139264 | tf_op jit(solution)/shard_map/all_gather | solution.py:62
  71.6 0.2 copy.32
  71.8 1.1 %fusion.21 = f32[16,64,32]{2,1,0:T(8,128)S(1)} fusion(f32[16,64,32]{2,1,0:T(8,128)S(1)} %copy.32), kind=kOutput, calls=%fused_computation.34 | output fusion | flops 491520 | bytes 262144 | tf_op jit(solution)/shard_map/jit(cumsum)/reduce_window_sum | solution.py:63
  72.9 0.1 dynamic-slice_add_fusion
  73.0 0.7 copy.33
  (6 shorter events, 0.0 us)
Async XLA Ops:
  0.0 38.7 %copy-start = (bf16[64,3072]{1,0:T(8,128)(2,1)S(1)}, bf16[64,3072]{1,0:T(8,128)(2,1)}, u32[]{:S(2)}) copy-start(bf16[64,3072]{1,0:T(8,128)(2,1)} %param.13) | copy-start | bytes 1179652
  2.4 7.1 %copy-start.1 = (f32[64,8]{0,1:T(8,128)S(1)}, f32[64,8]{0,1:T(8,128)}, u32[]{:S(2)}) copy-start(f32[64,8]{0,1:T(8,128)} %param.12) | copy-start | bytes 6148
  2.4 7.2 %copy-start.2 = (f32[1000]{0:T(1024)S(1)}, f32[1000]{0:T(1024)}, u32[]{:S(2)}) copy-start(f32[1000]{0:T(1024)} %param.16) | copy-start | bytes 12004
  2.4 7.2 %copy-start.3 = (s32[4]{0:T(128)S(1)}, s32[4]{0:T(128)}, u32[]{:S(2)}) copy-start(s32[4]{0:T(128)} %param.17) | copy-start | bytes 52
  2.4 8.0 %copy-start.4 = (f32[8]{0:T(128)S(1)}, f32[8]{0:T(128)}, u32[]{:S(2)}) copy-start(f32[8]{0:T(128)} %param.14) | copy-start | bytes 100
  2.4 35.0 %all-to-all-start = ((bf16[3,4,48,8,128]{4,3,2,0,1:T(8,128)(2,1)}), bf16[3,4,48,8,128]{4,3,2,0,1:T(8,128)(2,1)S(1)}, u32[]{:S(2)}, u32[]{:S(2)}) async-start(bf16[3,4,48,8,128]{4,3,2,0,1:T(8,128)(2,1)} %pad_maximum_fusion), calls=%async_computation | async-start | bytes 2359296 | tf_op jit(solution)/shard_map/all_to_all | solution.py:41

commit v2 on v1

--- a/solution.py
+++ b/solution.py
@@ -23,6 +23,17 @@
     weights = expo.astype(jnp.bfloat16)
     out = jnp.einsum("iqk,ikd->iqd", weights, value_rows, preferred_element_type=jnp.float32)
     return (out / total).astype(jnp.bfloat16)
+
+
+def earlier_groups(local_cum, steps_axis):
+    every_total = lax.all_gather(local_cum[-1][None], "step", axis=0, tiled=True)
+    position = lax.axis_index("step")
+    order = jnp.arange(steps_axis, dtype=jnp.int32)
+    earlier = jnp.sum(
+        jnp.where((order < position)[:, None, None], every_total, jnp.zeros((), jnp.float32)),
+        axis=0,
+    )
+    return earlier[None]
 
 
 def on_device(
@@ -59,12 +70,10 @@
         guided = drift[:, 1] + guide_scale * (drift[:, 0] - drift[:, 1])
         my_len = lax.dynamic_slice_in_dim(step_len, me * local_steps, local_steps)
         update = my_len[:, None, None] * guided
-        every = lax.all_gather(update, ("step", "seq"), axis=0, tiled=True)
-        prefix = jnp.cumsum(every, axis=0)
-        position = lax.axis_index("step")
-        mine = lax.dynamic_slice_in_dim(prefix, position * step_dev, step_dev, axis=0)
-        mine = lax.dynamic_slice_in_dim(mine, me * tok_dev, tok_dev, axis=2)
-        return start_latent[None] + mine
+        update = update.reshape(local_steps, channels, groups, tok_dev)
+        local = lax.all_to_all(update, "seq", split_axis=2, concat_axis=0, tiled=True)
+        local_cum = jnp.cumsum(local.reshape(step_dev, channels, tok_dev), axis=0)
+        return start_latent[None] + earlier_groups(local_cum, steps_axis) + local_cum
 
     assert heads % per_dev == 0
     share = heads // per_dev
@@ -85,15 +94,7 @@
     drift = numer / root_mean[:, :, None, :]
     guided = drift[:, 1] + guide_scale * (drift[:, 0] - drift[:, 1])
     local_cum = jnp.cumsum(step_len[:, None, None] * guided, axis=0)
-    group_total = local_cum[-1]
-    every_total = lax.all_gather(group_total[None], "step", axis=0, tiled=True)
-    position = lax.axis_index("step")
-    order = jnp.arange(steps_axis, dtype=jnp.int32)
-    earlier = jnp.sum(
-        jnp.where((order < position)[:, None, None], every_total, jnp.zeros((), jnp.float32)),
-        axis=0,
-    )
-    return start_latent[None] + earlier[None] + local_cum
+    return start_latent[None] + earlier_groups(local_cum, steps_axis) + local_cum
 
 
 def solution(mesh):

time: 73.9 us -> 57.3 us (0.78)
  blocking collectives: 31.3 us -> 5.19 us
  waiting for transfers between devices: 26.3 us -> 31.9 us
  starting transfers between devices: 6.46 us -> 9.7 us
    all_gather x1, blocking collectives: 31.3 us -> 5.19 us  [earlier_groups(): lax.all_gather(local_cum[-1][None], 'step', axis=0, tiled=True)]
    all_to_all x0 -> x1, waiting for transfers between devices: none -> 5.54 us  [on_device(): lax.all_to_all(update, 'seq', split_axis=2, concat_axis=0, tiled=True)]
    all_to_all x0 -> x1, starting transfers between devices: none -> 3.25 us  [on_device(): lax.all_to_all(update, 'seq', split_axis=2, concat_axis=0, tiled=True)]
    mul x1 -> x0, other arithmetic: 1.24 us -> none  [on_device(): update = my_len[:, None, None] * guided]
    unnamed x0 -> x1, other arithmetic: none -> 1.24 us
    another operation x1, other arithmetic: 1.06 us -> 0.04 us  [on_device(): local_cum = jnp.cumsum(local.reshape(step_dev, channels, tok_dev), axis=0)]
  transfers between devices with their start and end apart: 1 -> 2, of which waited for: 1 -> 2; matrix products, arithmetic and copies ran while one was open for 2% -> 3% of each run, Pallas kernels for 0% -> 0%
where the time goes in v2:
time: 57.3 us; the launch traced here: 57 us
  waiting for transfers between devices  31.9 us (56%)
  starting transfers between devices  9.7 us (17%)
  other arithmetic  6.15 us (11%)
  blocking collectives  5.19 us (9%)
  local copies, waits for them, and re-layouts  1.97 us (3%)
  matrix products  1.24 us (2%)
  between operations  0.77 us (1%)
    all_to_all x1, waiting for transfers between devices, on_device(): lax.all_to_all(stacked, 'seq', split_axis=1, concat_axis=3, tiled=True)  26.4 us
    all_to_all x1, starting transfers between devices, on_device(): lax.all_to_all(stacked, 'seq', split_axis=1, concat_axis=3, tiled=True)  6.45 us
    all_to_all x1, waiting for transfers between devices, on_device(): lax.all_to_all(update, 'seq', split_axis=2, concat_axis=0, tiled=True)  5.54 us
    all_gather x1, blocking collectives, earlier_groups(): lax.all_gather(local_cum[-1][None], 'step', axis=0, tiled=True)  5.19 us
    all_to_all x1, starting transfers between devices, on_device(): lax.all_to_all(update, 'seq', split_axis=2, concat_axis=0, tiled=True)  3.25 us
    another operation x1, other arithmetic, on_device(): jnp.stack([queries, keys, values])  2.42 us
    unnamed x1, other arithmetic  1.24 us
  transfers between devices with their start and end apart: 2, of which 2 were waited for; matrix products, arithmetic and copies ran while one was open for 3% of the time, Pallas kernels for 0%

profile of v2, /device:TPU:0, one launch (start us, length us, event | category | flops | bytes accessed | tf_op | source)
XLA Modules:
  0.0 57.0 jit_solution(14321092894772791145)
XLA Ops:
  0.0 0.0 copy-start
  0.0 2.4 %pad_maximum_fusion = bf16[3,4,48,8,128]{4,3,2,0,1:T(8,128)(2,1)} fusion(bf16[1,4,48,8,128]{4,3,2,0,1:T(8,128)(2,1)} %bitcast.85, bf16[1,4,48,8,128]{4,3,2,0,1:T(8,128)(2,1)} %bitcast.86, bf16[1,4,48,8,128]{4,3,2,0,1:T(8,128)(2,1)} %bitcast.87), kind=kLoop, calls=%fused_computation.3 | loop fusion | flops 1179648 | bytes 2359296 | tf_op jit(solution)/shard_map/stack | solution.py:51
  2.4 6.4 %all-to-all-start = ((bf16[3,4,48,8,128]{4,3,2,0,1:T(8,128)(2,1)}), bf16[3,4,48,8,128]{4,3,2,0,1:T(8,128)(2,1)S(1)}, u32[]{:S(2)}, u32[]{:S(2)}) async-start(bf16[3,4,48,8,128]{4,3,2,0,1:T(8,128)(2,1)} %pad_maximum_fusion), calls=%async_computation | async-start | bytes 2359296 | tf_op jit(solution)/shard_map/all_to_all | solution.py:52
  9.6 0.2 select_reduce_fusion.1
  9.7 0.6 %dynamic_slice.3 = f32[1]{0:T(128)} dynamic-slice(f32[4]{0:T(128)S(1)} %select_reduce_fusion.1, s32[]{:T(128)S(6)} %select_n.17), dynamic_slice_sizes={1} | dynamic-slice | bytes 12 | tf_op jit(solution)/shard_map/dynamic_slice | solution.py:71
  10.3 0.0 copy-done.4
  10.4 0.7 %fusion.20 = f32[]{:T(128)} fusion(f32[8]{0:T(128)S(1)} %copy-done.4, s32[]{:T(128)} %bitcast.83), kind=kLoop, calls=%fused_computation.34 | loop fusion | flops 23 | bytes 40 | tf_op jit(solution)/shard_map/reduce_sum | solution.py:13
  11.0 26.4 %all-to-all-done = bf16[3,4,48,8,128]{4,3,2,0,1:T(8,128)(2,1)S(1)} async-done(((bf16[3,4,48,8,128]{4,3,2,0,1:T(8,128)(2,1)}), bf16[3,4,48,8,128]{4,3,2,0,1:T(8,128)(2,1)S(1)}, u32[]{:S(2)}, u32[]{:S(2)}) %all-to-all-start) | async-done | bytes 1179680 | tf_op jit(solution)/shard_map/all_to_all | solution.py:52
  37.4 0.1 fusion.21
  37.5 0.3 fusion.22
  37.8 0.2 fusion.3
  38.0 0.7 %multiply_reduce_fusion = (f32[48,32]{1,0:T(8,128)S(1)}, bf16[48,32,128]{2,1,0:T(8,128)(2,1)S(1)}) fusion(f32[48,32]{1,0:T(8,128)S(1)} %fusion.3, bf16[1,1,48,4,8,128]{5,4,2,0,3,1:T(8,128)(2,1)S(1)} %get-tuple-element.5, f32[48,32,32]{1,2,0:T(8,128)S(1)} %get-tuple-element.9, f32[48,32]{1,0:T(8,128)S(1)} %get-tuple-element.8), kind=kOutput, calls=%fused_computation.7 | convolution fusion | flops 13662720 | bytes 1001472 | tf_op jit(solution)/shard_map/iqk,ikd->iqd/dot_general | solution.py:24
  38.7 0.0 copy-start.1
  38.7 0.3 fusion.2
  39.0 1.2 %fusion.24 = f32[4,1,8,64]{3,2,1,0:T(8,128)S(1)} fusion(f32[1,2,64,32]{2,3,1,0:T(8,128)S(1)} %fusion.2, f32[]{:T(128)} %fusion.20, f32[]{:T(128)} %bitcast), kind=kLoop, calls=%fused_computation.39 | loop fusion | flops 8192 | bytes 24584
  40.3 0.7 %reshape.115 = f32[4,1,512]{2,1,0:T(1,128)} reshape(f32[4,1,8,64]{3,2,1,0:T(8,128)S(1)} %fusion.24) | data formatting | bytes 16384
  40.9 3.2 %all-to-all-start.1 = ((f32[4,1,512]{2,1,0:T(1,128)}), f32[4,1,512]{2,1,0:T(1,128)S(1)}, u32[]{:S(2)}, u32[]{:S(2)}) async-start(f32[4,1,512]{2,1,0:T(1,128)} %reshape.115), calls=%async_computation.1 | async-start | bytes 16384 | tf_op jit(solution)/shard_map/all_to_all | solution.py:74
  44.2 5.5 %all-to-all-done.1 = f32[4,1,512]{2,1,0:T(1,128)S(1)} async-done(((f32[4,1,512]{2,1,0:T(1,128)}), f32[4,1,512]{2,1,0:T(1,128)S(1)}, u32[]{:S(2)}, u32[]{:S(2)}) %all-to-all-start.1) | async-done | bytes 8224 | tf_op jit(solution)/shard_map/all_to_all | solution.py:74
  49.8 0.5 broadcast.46
  50.3 0.7 %reduce.5 = f32[4,512]{1,0:T(4,128)S(1)} reduce(f32[4,1,512]{2,1,0:T(1,128)S(1)} %all-to-all-done.1, f32[]{:T(128)} %broadcast.46), dimensions={1}, to_apply=%all_to_all.25.reduce_sub_computation | reduce | bytes 16388 | tf_op jit(solution)/shard_map/all_to_all | solution.py:74
  50.9 0.1 reshape.116
  51.1 5.2 %all_gather.3 = f32[4,64,8]{1,2,0:T(8,128)S(1)} all-gather(f32[1,64,8]{1,2,0:T(8,128)S(1)} %slice.33), channel_id=1, replica_groups=mesh['scene'=2,'step'=4,'seq'=4] {'step'}, dimensions={0}, use_global_device_ids=true | all-gather | bytes 10240 | tf_op jit(solution)/shard_map/all_gather | solution.py:29
  56.3 0.1 select_reduce_fusion
  56.4 0.6 %broadcast_add_fusion = f32[4,64,8]{1,2,0:T(8,128)} fusion(f32[4,64,8]{1,2,0:T(8,128)S(1)} %fusion.18, f32[64,8]{0,1:T(8,128)S(1)} %add.43), kind=kLoop, calls=%fused_computation.31 | loop fusion | flops 2048 | bytes 18432 | tf_op jit(solution)/shard_map/add | solution.py:76
  (13 shorter events, 0.1 us)
Async XLA Ops:
  0.0 38.7 %copy-start = (bf16[64,3072]{1,0:T(8,128)(2,1)S(1)}, bf16[64,3072]{1,0:T(8,128)(2,1)}, u32[]{:S(2)}) copy-start(bf16[64,3072]{1,0:T(8,128)(2,1)} %param.13) | copy-start | bytes 1179652
  2.4 7.1 %copy-start.2 = (f32[1000]{0:T(1024)S(1)}, f32[1000]{0:T(1024)}, u32[]{:S(2)}) copy-start(f32[1000]{0:T(1024)} %param.16) | copy-start | bytes 12004
  2.4 7.1 %copy-start.3 = (s32[4]{0:T(128)S(1)}, s32[4]{0:T(128)}, u32[]{:S(2)}) copy-start(s32[4]{0:T(128)} %param.17) | copy-start | bytes 52
  2.4 7.9 %copy-start.4 = (f32[8]{0:T(128)S(1)}, f32[8]{0:T(128)}, u32[]{:S(2)}) copy-start(f32[8]{0:T(128)} %param.14) | copy-start | bytes 100
  2.4 35.0 %all-to-all-start = ((bf16[3,4,48,8,128]{4,3,2,0,1:T(8,128)(2,1)}), bf16[3,4,48,8,128]{4,3,2,0,1:T(8,128)(2,1)S(1)}, u32[]{:S(2)}, u32[]{:S(2)}) async-start(bf16[3,4,48,8,128]{4,3,2,0,1:T(8,128)(2,1)} %pad_maximum_fusion), calls=%async_computation | async-start | bytes 2359296 | tf_op jit(solution)/shard_map/all_to_all | solution.py:52
  38.7 17.7 %copy-start.1 = (f32[64,8]{0,1:T(8,128)S(1)}, f32[64,8]{0,1:T(8,128)}, u32[]{:S(2)}) copy-start(f32[64,8]{0,1:T(8,128)} %param.12) | copy-start | bytes 6148
  40.9 8.8 %all-to-all-start.1 = ((f32[4,1,512]{2,1,0:T(1,128)}), f32[4,1,512]{2,1,0:T(1,128)S(1)}, u32[]{:S(2)}, u32[]{:S(2)}) async-start(f32[4,1,512]{2,1,0:T(1,128)} %reshape.115), calls=%async_computation.1 | async-start | bytes 16384 | tf_op jit(solution)/shard_map/all_to_all | solution.py:74

commit v3 on v2

--- a/solution.py
+++ b/solution.py
@@ -23,6 +23,38 @@
     weights = expo.astype(jnp.bfloat16)
     out = jnp.einsum("iqk,ikd->iqd", weights, value_rows, preferred_element_type=jnp.float32)
     return (out / total).astype(jnp.bfloat16)
+
+
+def xor_pairs(size, k):
+    return [(i, i ^ k) for i in range(size)]
+
+
+def gather_prefix(update, me, groups, step_dev, steps_axis):
+    local_steps = update.shape[0]
+    partners = me ^ jnp.arange(groups, dtype=jnp.int32)
+    ordered = jnp.take(update, partners, axis=2)
+    pieces = [ordered[:, :, 0]]
+    sources = [me]
+    for k in range(1, groups):
+        pieces.append(lax.ppermute(ordered[:, :, k], "seq", xor_pairs(groups, k)))
+        sources.append(me ^ k)
+    zero = jnp.zeros((), jnp.float32)
+    outs = []
+    for s in range(step_dev):
+        acc = None
+        for piece, source in zip(pieces, sources):
+            for t in range(local_steps):
+                term = jnp.where(source * local_steps + t <= s, piece[t], zero)
+                acc = term if acc is None else acc + term
+        outs.append(acc)
+    local_cum = jnp.stack(outs)
+    total = outs[-1]
+    position = lax.axis_index("step")
+    earlier = jnp.zeros_like(total)
+    for k in range(1, steps_axis):
+        other = lax.ppermute(total, "step", xor_pairs(steps_axis, k))
+        earlier = earlier + jnp.where((position ^ k) < position, other, zero)
+    return earlier[None] + local_cum
 
 
 def earlier_groups(local_cum, steps_axis):
@@ -71,9 +103,7 @@
         my_len = lax.dynamic_slice_in_dim(step_len, me * local_steps, local_steps)
         update = my_len[:, None, None] * guided
         update = update.reshape(local_steps, channels, groups, tok_dev)
-        local = lax.all_to_all(update, "seq", split_axis=2, concat_axis=0, tiled=True)
-        local_cum = jnp.cumsum(local.reshape(step_dev, channels, tok_dev), axis=0)
-        return start_latent[None] + earlier_groups(local_cum, steps_axis) + local_cum
+        return start_latent[None] + gather_prefix(update, me, groups, step_dev, steps_axis)
 
     assert heads % per_dev == 0
     share = heads // per_dev

time: 57.3 us -> 53.8 us (0.939)
  blocking collectives: 5.19 us -> 0 us
  starting transfers between devices: 9.7 us -> 12.7 us
  other arithmetic: 6.15 us -> 5.42 us
  local copies, waits for them, and re-layouts: 1.97 us -> 1.27 us
    ppermute x0 -> x6, starting transfers between devices: none -> 6.25 us  [the longest x3 4.39 us: gather_prefix(): pieces.append(lax.ppermute(ordered[:, :, k], 'seq', xor_pairs(groups, k)))]
    ppermute x0 -> x6, waiting for transfers between devices: none -> 5.74 us  [the longest x3 3.04 us: gather_prefix(): pieces.append(lax.ppermute(ordered[:, :, k], 'seq', xor_pairs(groups, k)))]
    all_to_all x1 -> x0, waiting for transfers between devices: 5.54 us -> none  [on_device(): lax.all_to_all(update, 'seq', split_axis=2, concat_axis=0, tiled=True)]
    all_gather x1 -> x0, blocking collectives: 5.19 us -> none  [earlier_groups(): lax.all_gather(local_cum[-1][None], 'step', axis=0, tiled=True)]
    all_to_all x1 -> x0, starting transfers between devices: 3.25 us -> none  [on_device(): lax.all_to_all(update, 'seq', split_axis=2, concat_axis=0, tiled=True)]
    unnamed x1 -> x0, other arithmetic: 1.24 us -> none
    mul x0 -> x1, other arithmetic: none -> 1.23 us  [on_device(): update = my_len[:, None, None] * guided]
    unnamed x12 -> x10, local copies, waits for them, and re-layouts: 0.78 us -> 0.02 us
  transfers between devices with their start and end apart: 2 -> 7, of which waited for: 2 -> 5; matrix products, arithmetic and copies ran while one was open for 3% -> 3% of each run, Pallas kernels for 0% -> 0%
where the time goes in v3:
time: 53.8 us; the launch traced here: 53.6 us
  waiting for transfers between devices  32.1 us (60%)
  starting transfers between devices  12.7 us (24%)
  other arithmetic  5.42 us (10%)
  local copies, waits for them, and re-layouts  1.27 us (2%)
  matrix products  1.25 us (2%)
  between operations  0.79 us (1%)
    all_to_all x1, waiting for transfers between devices, on_device(): lax.all_to_all(stacked, 'seq', split_axis=1, concat_axis=3, tiled=True)  26.4 us
    all_to_all x1, starting transfers between devices, on_device(): lax.all_to_all(stacked, 'seq', split_axis=1, concat_axis=3, tiled=True)  6.45 us
    ppermute x3, starting transfers between devices, gather_prefix(): pieces.append(lax.ppermute(ordered[:, :, k], 'seq', xor_pairs(groups, k)))  4.39 us
    ppermute x3, waiting for transfers between devices, gather_prefix(): pieces.append(lax.ppermute(ordered[:, :, k], 'seq', xor_pairs(groups, k)))  3.04 us
    ppermute x3, waiting for transfers between devices, gather_prefix(): other = lax.ppermute(total, 'step', xor_pairs(steps_axis, k))  2.7 us
    another operation x1, other arithmetic, on_device(): jnp.stack([queries, keys, values])  2.42 us
    ppermute x3, starting transfers between devices, gather_prefix(): other = lax.ppermute(total, 'step', xor_pairs(steps_axis, k))  1.86 us
    mul x1, other arithmetic, on_device(): update = my_len[:, None, None] * guided  1.23 us
  transfers between devices with their start and end apart: 7, of which 5 were waited for; matrix products, arithmetic and copies ran while one was open for 3% of the time, Pallas kernels for 0%

profile of v3, /device:TPU:0, one launch (start us, length us, event | category | flops | bytes accessed | tf_op | source)
XLA Modules:
  0.0 53.6 jit_solution(7301235506979418719)
XLA Ops:
  0.0 2.4 %pad_maximum_fusion = bf16[3,4,48,8,128]{4,3,2,0,1:T(8,128)(2,1)} fusion(bf16[1,4,48,8,128]{4,3,2,0,1:T(8,128)(2,1)} %bitcast.114, bf16[1,4,48,8,128]{4,3,2,0,1:T(8,128)(2,1)} %bitcast.115, bf16[1,4,48,8,128]{4,3,2,0,1:T(8,128)(2,1)} %bitcast.116), kind=kLoop, calls=%fused_computation.4 | loop fusion | flops 1179648 | bytes 2359296 | tf_op jit(solution)/shard_map/stack | solution.py:83
  2.4 6.4 %all-to-all-start = ((bf16[3,4,48,8,128]{4,3,2,0,1:T(8,128)(2,1)}), bf16[3,4,48,8,128]{4,3,2,0,1:T(8,128)(2,1)S(1)}, u32[]{:S(2)}, u32[]{:S(2)}) async-start(bf16[3,4,48,8,128]{4,3,2,0,1:T(8,128)(2,1)} %pad_maximum_fusion), calls=%async_computation | async-start | bytes 2359296 | tf_op jit(solution)/shard_map/all_to_all | solution.py:84
  9.6 0.2 select_reduce_fusion
  9.7 0.6 %dynamic_slice.3 = f32[1]{0:T(128)} dynamic-slice(f32[4]{0:T(128)S(1)} %select_reduce_fusion, s32[]{:T(128)S(6)} %select_n.224), dynamic_slice_sizes={1} | dynamic-slice | bytes 12 | tf_op jit(solution)/shard_map/dynamic_slice | solution.py:103
  10.4 0.6 %fusion.28 = f32[]{:T(128)} fusion(f32[8]{0:T(128)S(1)} %copy-done.4, s32[]{:T(128)} %bitcast.112), kind=kLoop, calls=%fused_computation.58 | loop fusion | flops 23 | bytes 40 | tf_op jit(solution)/shard_map/reduce_sum | solution.py:13
  11.0 26.4 %all-to-all-done = bf16[3,4,48,8,128]{4,3,2,0,1:T(8,128)(2,1)S(1)} async-done(((bf16[3,4,48,8,128]{4,3,2,0,1:T(8,128)(2,1)}), bf16[3,4,48,8,128]{4,3,2,0,1:T(8,128)(2,1)S(1)}, u32[]{:S(2)}, u32[]{:S(2)}) %all-to-all-start) | async-done | bytes 1179680 | tf_op jit(solution)/shard_map/all_to_all | solution.py:84
  37.4 0.1 fusion.30
  37.5 0.3 fusion.31
  37.8 0.2 fusion.3
  38.0 0.7 %multiply_reduce_fusion = (f32[48,32]{1,0:T(8,128)S(1)}, bf16[48,32,128]{2,1,0:T(8,128)(2,1)S(1)}) fusion(f32[48,32]{1,0:T(8,128)S(1)} %fusion.3, bf16[1,1,48,4,8,128]{5,4,2,0,3,1:T(8,128)(2,1)S(1)} %get-tuple-element.5, f32[48,32,32]{1,2,0:T(8,128)S(1)} %get-tuple-element.15, f32[48,32]{1,0:T(8,128)S(1)} %get-tuple-element.14), kind=kOutput, calls=%fused_computation.8 | convolution fusion | flops 13662720 | bytes 1001472 | tf_op jit(solution)/shard_map/iqk,ikd->iqd/dot_general | solution.py:24
  38.8 0.3 fusion.2
  39.0 1.2 %fusion.18 = f32[64,4,8]{0,2,1:T(8,128)S(1)} fusion(f32[1,2,64,32]{2,3,1,0:T(8,128)S(1)} %fusion.2, f32[]{:T(128)} %fusion.28, f32[]{:T(128)} %bitcast), kind=kLoop, calls=%fused_computation.26 | loop fusion | flops 8192 | bytes 24584 | tf_op jit(solution)/shard_map/mul | solution.py:104
  40.3 0.6 %gather_fusion = f32[4,64,8]{1,2,0:T(8,128)S(1)} fusion(f32[64,4,8]{0,2,1:T(8,128)S(1)} %fusion.18, s32[1024]{0:T(1024)S(1)} %pad_clamp_fusion), kind=kCustom, calls=%fused_computation | custom fusion | bytes 16400 | tf_op jit(solution)/shard_map/jit(_take)/gather | solution.py:35
  40.8 0.1 bitcast_select_fusion
  40.9 0.0 collective-permute-start
  40.9 2.0 %collective-permute-start.1 = (f32[1,64,8]{1,2,0:T(8,128)S(1)}, f32[1,64,8]{1,2,0:T(8,128)S(1)}, u32[]{:S(2)}, u32[]{:S(2)}) collective-permute-start(f32[1,64,8]{1,2,0:T(8,128)S(1)} %get-tuple-element.13), channel_id=1, source_target_pairs={{0,2},{1,3},{2,0},{3,1},{4,6},{5,7},{6,4},{7,5},{8,10},{9,11},{10,... | collective-permute-start | bytes 6152 | tf_op jit(solution)/shard_map/ppermute | solution.py:39
  42.9 2.4 %collective-permute-start.2 = (f32[1,64,8]{1,2,0:T(8,128)S(1)}, f32[1,64,8]{1,2,0:T(8,128)S(1)}, u32[]{:S(2)}, u32[]{:S(2)}) collective-permute-start(f32[1,64,8]{1,2,0:T(8,128)S(1)} %get-tuple-element.12), channel_id=1, source_target_pairs={{0,3},{1,2},{2,1},{3,0},{4,7},{5,6},{6,5},{7,4},{8,11},{9,10},{10,... | collective-permute-start | bytes 6152 | tf_op jit(solution)/shard_map/ppermute | solution.py:39
  45.3 0.2 collective-permute-done.1
  45.5 2.8 %collective-permute-done.2 = f32[1,64,8]{1,2,0:T(8,128)S(1)} collective-permute-done((f32[1,64,8]{1,2,0:T(8,128)S(1)}, f32[1,64,8]{1,2,0:T(8,128)S(1)}, u32[]{:S(2)}, u32[]{:S(2)}) %collective-permute-start.2) | collective-permute-done | bytes 2080 | tf_op jit(solution)/shard_map/ppermute | solution.py:39
  48.4 1.6 %collective-permute-start.4 = (f32[64,8]{0,1:T(8,128)S(1)}, f32[64,8]{0,1:T(8,128)S(1)}, u32[]{:S(2)}, u32[]{:S(2)}) collective-permute-start(f32[64,8]{0,1:T(8,128)S(1)} %bitcast_add_fusion.4), channel_id=1, source_target_pairs={{0,8},{4,12},{8,0},{12,4},{1,9},{5,13},{9,1},{13,5},{2,10},{6,14},... | collective-permute-start | bytes 6152 | tf_op jit(solution)/shard_map/ppermute | solution.py:55
  49.9 0.3 collective-permute-start.5
  50.2 1.8 %collective-permute-done.4 = f32[64,8]{0,1:T(8,128)S(1)} collective-permute-done((f32[64,8]{0,1:T(8,128)S(1)}, f32[64,8]{0,1:T(8,128)S(1)}, u32[]{:S(2)}, u32[]{:S(2)}) %collective-permute-start.4) | collective-permute-done | bytes 2080 | tf_op jit(solution)/shard_map/ppermute | solution.py:55
  52.0 0.9 %collective-permute-done.5 = f32[64,8]{0,1:T(8,128)S(1)} collective-permute-done((f32[64,8]{0,1:T(8,128)S(1)}, f32[64,8]{0,1:T(8,128)S(1)}, u32[]{:S(2)}, u32[]{:S(2)}) %collective-permute-start.5) | collective-permute-done | bytes 2080 | tf_op jit(solution)/shard_map/ppermute | solution.py:55
  53.0 0.6 %fusion.19 = f32[4,64,8]{1,2,0:T(8,128)} fusion(f32[1,64,8]{1,2,0:T(8,128)S(1)} %get-tuple-element.9, f32[1,64,8]{1,2,0:T(8,128)S(1)} %get-tuple-element.10, f32[1,64,8]{1,2,0:T(8,128)S(1)} %fusion.25, f32[1,64,8]{1,2,0:T(8,128)S(1)} %get-tuple-element.8, f32[64,8]{0,1:T(8,128)S(1)} %select_add_fusion, f32[64,8]{0,1:T(8,128)S(1)} %copy-done.1), kind=kLoop, calls=%fused_computation.29 | loop fusion | flops 10240 | bytes 20480 | tf_op jit(solution)/shard_map/add | solution.py:106
  (23 shorter events, 0.1 us)
Async XLA Ops:
  0.0 38.7 %copy-start = (bf16[64,3072]{1,0:T(8,128)(2,1)S(1)}, bf16[64,3072]{1,0:T(8,128)(2,1)}, u32[]{:S(2)}) copy-start(bf16[64,3072]{1,0:T(8,128)(2,1)} %param.13) | copy-start | bytes 1179652
  2.4 7.1 %copy-start.2 = (f32[1000]{0:T(1024)S(1)}, f32[1000]{0:T(1024)}, u32[]{:S(2)}) copy-start(f32[1000]{0:T(1024)} %param.16) | copy-start | bytes 12004
  2.4 7.1 %copy-start.3 = (s32[4]{0:T(128)S(1)}, s32[4]{0:T(128)}, u32[]{:S(2)}) copy-start(s32[4]{0:T(128)} %param.17) | copy-start | bytes 52
  2.4 8.0 %copy-start.4 = (f32[8]{0:T(128)S(1)}, f32[8]{0:T(128)}, u32[]{:S(2)}) copy-start(f32[8]{0:T(128)} %param.14) | copy-start | bytes 100
  2.4 35.0 %all-to-all-start = ((bf16[3,4,48,8,128]{4,3,2,0,1:T(8,128)(2,1)}), bf16[3,4,48,8,128]{4,3,2,0,1:T(8,128)(2,1)S(1)}, u32[]{:S(2)}, u32[]{:S(2)}) async-start(bf16[3,4,48,8,128]{4,3,2,0,1:T(8,128)(2,1)} %pad_maximum_fusion), calls=%async_computation | async-start | bytes 2359296 | tf_op jit(solution)/shard_map/all_to_all | solution.py:84
  38.7 14.3 %copy-start.1 = (f32[64,8]{0,1:T(8,128)S(1)}, f32[64,8]{0,1:T(8,128)}, u32[]{:S(2)}) copy-start(f32[64,8]{0,1:T(8,128)} %param.12) | copy-start | bytes 6148
  40.9 4.4 %collective-permute-start = (f32[1,64,8]{1,2,0:T(8,128)S(1)}, f32[1,64,8]{1,2,0:T(8,128)S(1)}, u32[]{:S(2)}, u32[]{:S(2)}) collective-permute-start(f32[1,64,8]{1,2,0:T(8,128)S(1)} %get-tuple-element.11), channel_id=1, source_target_pairs={{0,1},{1,0},{2,3},{3,2},{4,5},{5,4},{6,7},{7,6},{8,9},{9,8},{10,11... | collective-permute-start | bytes 6152 | tf_op jit(solution)/shard_map/ppermute | solution.py:39
  40.9 4.6 %collective-permute-start.1 = (f32[1,64,8]{1,2,0:T(8,128)S(1)}, f32[1,64,8]{1,2,0:T(8,128)S(1)}, u32[]{:S(2)}, u32[]{:S(2)}) collective-permute-start(f32[1,64,8]{1,2,0:T(8,128)S(1)} %get-tuple-element.13), channel_id=1, source_target_pairs={{0,2},{1,3},{2,0},{3,1},{4,6},{5,7},{6,4},{7,5},{8,10},{9,11},{10,... | collective-permute-start | bytes 6152 | tf_op jit(solution)/shard_map/ppermute | solution.py:39
  42.9 5.4 %collective-permute-start.2 = (f32[1,64,8]{1,2,0:T(8,128)S(1)}, f32[1,64,8]{1,2,0:T(8,128)S(1)}, u32[]{:S(2)}, u32[]{:S(2)}) collective-permute-start(f32[1,64,8]{1,2,0:T(8,128)S(1)} %get-tuple-element.12), channel_id=1, source_target_pairs={{0,3},{1,2},{2,1},{3,0},{4,7},{5,6},{6,5},{7,4},{8,11},{9,10},{10,... | collective-permute-start | bytes 6152 | tf_op jit(solution)/shard_map/ppermute | solution.py:39
  48.3 1.9 %collective-permute-start.3 = (f32[64,8]{0,1:T(8,128)S(1)}, f32[64,8]{0,1:T(8,128)S(1)}, u32[]{:S(2)}, u32[]{:S(2)}) collective-permute-start(f32[64,8]{0,1:T(8,128)S(1)} %bitcast_add_fusion.4), channel_id=1, source_target_pairs={{0,4},{4,0},{8,12},{12,8},{1,5},{5,1},{9,13},{13,9},{2,6},{6,2},{1... | collective-permute-start | bytes 6152 | tf_op jit(solution)/shard_map/ppermute | solution.py:55
  48.4 3.7 %collective-permute-start.4 = (f32[64,8]{0,1:T(8,128)S(1)}, f32[64,8]{0,1:T(8,128)S(1)}, u32[]{:S(2)}, u32[]{:S(2)}) collective-permute-start(f32[64,8]{0,1:T(8,128)S(1)} %bitcast_add_fusion.4), channel_id=1, source_target_pairs={{0,8},{4,12},{8,0},{12,4},{1,9},{5,13},{9,1},{13,5},{2,10},{6,14},... | collective-permute-start | bytes 6152 | tf_op jit(solution)/shard_map/ppermute | solution.py:55
  49.9 3.0 %collective-permute-start.5 = (f32[64,8]{0,1:T(8,128)S(1)}, f32[64,8]{0,1:T(8,128)S(1)}, u32[]{:S(2)}, u32[]{:S(2)}) collective-permute-start(f32[64,8]{0,1:T(8,128)S(1)} %bitcast_add_fusion.4), channel_id=1, source_target_pairs={{0,12},{4,8},{8,4},{12,0},{1,13},{5,9},{9,5},{13,1},{2,14},{6,10},... | collective-permute-start | bytes 6152 | tf_op jit(solution)/shard_map/ppermute | solution.py:55

commit v4 on v3

--- a/solution.py
+++ b/solution.py
@@ -80,8 +80,9 @@
     channels = out_weight.shape[0]
     me = lax.axis_index("seq")
 
-    stacked = jnp.stack([queries, keys, values]).reshape(3, groups, per_dev, tok_dev, head_size)
-    gathered = lax.all_to_all(stacked, "seq", split_axis=1, concat_axis=3, tiled=True)
+    chunks = [a.reshape(groups, per_dev, tok_dev, head_size) for a in (queries, keys, values)]
+    stacked = jnp.stack(chunks, axis=1)
+    gathered = lax.all_to_all(stacked, "seq", split_axis=0, concat_axis=3, tiled=True)
     gathered = gathered.reshape(3, per_dev, length, head_size)
     heads_out = attend(gathered[0], gathered[1], gathered[2])
 

time: 53.8 us -> 53.8 us (level)
  no operation moved by 1% of the time
where the time goes in v4:
time: 53.8 us; the launch traced here: 53.6 us
  waiting for transfers between devices  32.1 us (60%)
  starting transfers between devices  12.7 us (24%)
  other arithmetic  5.42 us (10%)
  local copies, waits for them, and re-layouts  1.27 us (2%)
  matrix products  1.25 us (2%)
  between operations  0.79 us (1%)
    all_to_all x1, waiting for transfers between devices, on_device(): lax.all_to_all(stacked, 'seq', split_axis=0, concat_axis=3, tiled=True)  26.4 us
    all_to_all x1, starting transfers between devices, on_device(): lax.all_to_all(stacked, 'seq', split_axis=0, concat_axis=3, tiled=True)  6.45 us
    ppermute x3, starting transfers between devices, gather_prefix(): pieces.append(lax.ppermute(ordered[:, :, k], 'seq', xor_pairs(groups, k)))  4.39 us
    ppermute x3, waiting for transfers between devices, gather_prefix(): pieces.append(lax.ppermute(ordered[:, :, k], 'seq', xor_pairs(groups, k)))  3.04 us
    ppermute x3, waiting for transfers between devices, gather_prefix(): other = lax.ppermute(total, 'step', xor_pairs(steps_axis, k))  2.7 us
    another operation x1, other arithmetic, on_device(): stacked = jnp.stack(chunks, axis=1)  2.42 us
    ppermute x3, starting transfers between devices, gather_prefix(): other = lax.ppermute(total, 'step', xor_pairs(steps_axis, k))  1.86 us
    mul x1, other arithmetic, on_device(): update = my_len[:, None, None] * guided  1.23 us
  transfers between devices with their start and end apart: 7, of which 5 were waited for; matrix products, arithmetic and copies ran while one was open for 3% of the time, Pallas kernels for 0%

profile of v4, /device:TPU:0, one launch (start us, length us, event | category | flops | bytes accessed | tf_op | source)
XLA Modules:
  0.0 53.6 jit_solution(7301235506979418719)
XLA Ops:
  0.0 2.4 %pad_maximum_fusion = bf16[4,3,48,8,128]{4,3,2,1,0:T(8,128)(2,1)} fusion(bf16[4,1,48,8,128]{4,3,2,1,0:T(8,128)(2,1)} %bitcast.114, bf16[4,1,48,8,128]{4,3,2,1,0:T(8,128)(2,1)} %bitcast.115, bf16[4,1,48,8,128]{4,3,2,1,0:T(8,128)(2,1)} %bitcast.116), kind=kLoop, calls=%fused_computation.4 | loop fusion | flops 1179648 | bytes 2359296 | tf_op jit(solution)/shard_map/stack | solution.py:84
  2.4 6.4 %all-to-all-start = ((bf16[4,3,48,8,128]{4,3,2,1,0:T(8,128)(2,1)}), bf16[4,3,48,8,128]{4,3,2,1,0:T(8,128)(2,1)S(1)}, u32[]{:S(2)}, u32[]{:S(2)}) async-start(bf16[4,3,48,8,128]{4,3,2,1,0:T(8,128)(2,1)} %pad_maximum_fusion), calls=%async_computation | async-start | bytes 2359296 | tf_op jit(solution)/shard_map/all_to_all | solution.py:85
  9.6 0.2 select_reduce_fusion
  9.7 0.6 %dynamic_slice.3 = f32[1]{0:T(128)} dynamic-slice(f32[4]{0:T(128)S(1)} %select_reduce_fusion, s32[]{:T(128)S(6)} %select_n.224), dynamic_slice_sizes={1} | dynamic-slice | bytes 12 | tf_op jit(solution)/shard_map/dynamic_slice | solution.py:104
  10.4 0.6 %fusion.28 = f32[]{:T(128)} fusion(f32[8]{0:T(128)S(1)} %copy-done.4, s32[]{:T(128)} %bitcast.112), kind=kLoop, calls=%fused_computation.58 | loop fusion | flops 23 | bytes 40 | tf_op jit(solution)/shard_map/reduce_sum | solution.py:13
  11.0 26.4 %all-to-all-done = bf16[4,3,48,8,128]{4,3,2,1,0:T(8,128)(2,1)S(1)} async-done(((bf16[4,3,48,8,128]{4,3,2,1,0:T(8,128)(2,1)}), bf16[4,3,48,8,128]{4,3,2,1,0:T(8,128)(2,1)S(1)}, u32[]{:S(2)}, u32[]{:S(2)}) %all-to-all-start) | async-done | bytes 1179680 | tf_op jit(solution)/shard_map/all_to_all | solution.py:85
  37.4 0.1 fusion.30
  37.5 0.3 fusion.31
  37.8 0.2 fusion.3
  38.0 0.7 %multiply_reduce_fusion = (f32[48,32]{1,0:T(8,128)S(1)}, bf16[48,32,128]{2,1,0:T(8,128)(2,1)S(1)}) fusion(f32[48,32]{1,0:T(8,128)S(1)} %fusion.3, bf16[1,1,48,4,8,128]{5,4,2,1,3,0:T(8,128)(2,1)S(1)} %get-tuple-element.5, f32[48,32,32]{1,2,0:T(8,128)S(1)} %get-tuple-element.15, f32[48,32]{1,0:T(8,128)S(1)} %get-tuple-element.14), kind=kOutput, calls=%fused_computation.8 | convolution fusion | flops 13662720 | bytes 1001472 | tf_op jit(solution)/shard_map/iqk,ikd->iqd/dot_general | solution.py:24
  38.8 0.3 fusion.2
  39.0 1.2 %fusion.18 = f32[64,4,8]{0,2,1:T(8,128)S(1)} fusion(f32[1,2,64,32]{2,3,1,0:T(8,128)S(1)} %fusion.2, f32[]{:T(128)} %fusion.28, f32[]{:T(128)} %bitcast), kind=kLoop, calls=%fused_computation.26 | loop fusion | flops 8192 | bytes 24584 | tf_op jit(solution)/shard_map/mul | solution.py:105
  40.3 0.6 %gather_fusion = f32[4,64,8]{1,2,0:T(8,128)S(1)} fusion(f32[64,4,8]{0,2,1:T(8,128)S(1)} %fusion.18, s32[1024]{0:T(1024)S(1)} %pad_clamp_fusion), kind=kCustom, calls=%fused_computation | custom fusion | bytes 16400 | tf_op jit(solution)/shard_map/jit(_take)/gather | solution.py:35
  40.8 0.1 bitcast_select_fusion
  40.9 0.0 collective-permute-start
  40.9 2.0 %collective-permute-start.1 = (f32[1,64,8]{1,2,0:T(8,128)S(1)}, f32[1,64,8]{1,2,0:T(8,128)S(1)}, u32[]{:S(2)}, u32[]{:S(2)}) collective-permute-start(f32[1,64,8]{1,2,0:T(8,128)S(1)} %get-tuple-element.13), channel_id=1, source_target_pairs={{0,2},{1,3},{2,0},{3,1},{4,6},{5,7},{6,4},{7,5},{8,10},{9,11},{10,... | collective-permute-start | bytes 6152 | tf_op jit(solution)/shard_map/ppermute | solution.py:39
  42.9 2.4 %collective-permute-start.2 = (f32[1,64,8]{1,2,0:T(8,128)S(1)}, f32[1,64,8]{1,2,0:T(8,128)S(1)}, u32[]{:S(2)}, u32[]{:S(2)}) collective-permute-start(f32[1,64,8]{1,2,0:T(8,128)S(1)} %get-tuple-element.12), channel_id=1, source_target_pairs={{0,3},{1,2},{2,1},{3,0},{4,7},{5,6},{6,5},{7,4},{8,11},{9,10},{10,... | collective-permute-start | bytes 6152 | tf_op jit(solution)/shard_map/ppermute | solution.py:39
  45.3 0.2 collective-permute-done.1
  45.5 2.8 %collective-permute-done.2 = f32[1,64,8]{1,2,0:T(8,128)S(1)} collective-permute-done((f32[1,64,8]{1,2,0:T(8,128)S(1)}, f32[1,64,8]{1,2,0:T(8,128)S(1)}, u32[]{:S(2)}, u32[]{:S(2)}) %collective-permute-start.2) | collective-permute-done | bytes 2080 | tf_op jit(solution)/shard_map/ppermute | solution.py:39
  48.4 1.6 %collective-permute-start.4 = (f32[64,8]{0,1:T(8,128)S(1)}, f32[64,8]{0,1:T(8,128)S(1)}, u32[]{:S(2)}, u32[]{:S(2)}) collective-permute-start(f32[64,8]{0,1:T(8,128)S(1)} %bitcast_add_fusion.4), channel_id=1, source_target_pairs={{0,8},{4,12},{8,0},{12,4},{1,9},{5,13},{9,1},{13,5},{2,10},{6,14},... | collective-permute-start | bytes 6152 | tf_op jit(solution)/shard_map/ppermute | solution.py:55
  49.9 0.3 collective-permute-start.5
  50.2 1.8 %collective-permute-done.4 = f32[64,8]{0,1:T(8,128)S(1)} collective-permute-done((f32[64,8]{0,1:T(8,128)S(1)}, f32[64,8]{0,1:T(8,128)S(1)}, u32[]{:S(2)}, u32[]{:S(2)}) %collective-permute-start.4) | collective-permute-done | bytes 2080 | tf_op jit(solution)/shard_map/ppermute | solution.py:55
  52.0 0.9 %collective-permute-done.5 = f32[64,8]{0,1:T(8,128)S(1)} collective-permute-done((f32[64,8]{0,1:T(8,128)S(1)}, f32[64,8]{0,1:T(8,128)S(1)}, u32[]{:S(2)}, u32[]{:S(2)}) %collective-permute-start.5) | collective-permute-done | bytes 2080 | tf_op jit(solution)/shard_map/ppermute | solution.py:55
  53.0 0.6 %fusion.19 = f32[4,64,8]{1,2,0:T(8,128)} fusion(f32[1,64,8]{1,2,0:T(8,128)S(1)} %get-tuple-element.9, f32[1,64,8]{1,2,0:T(8,128)S(1)} %get-tuple-element.10, f32[1,64,8]{1,2,0:T(8,128)S(1)} %fusion.25, f32[1,64,8]{1,2,0:T(8,128)S(1)} %get-tuple-element.8, f32[64,8]{0,1:T(8,128)S(1)} %select_add_fusion, f32[64,8]{0,1:T(8,128)S(1)} %copy-done.1), kind=kLoop, calls=%fused_computation.29 | loop fusion | flops 10240 | bytes 20480 | tf_op jit(solution)/shard_map/add | solution.py:107
  (23 shorter events, 0.1 us)
Async XLA Ops:
  0.0 38.7 %copy-start = (bf16[64,3072]{1,0:T(8,128)(2,1)S(1)}, bf16[64,3072]{1,0:T(8,128)(2,1)}, u32[]{:S(2)}) copy-start(bf16[64,3072]{1,0:T(8,128)(2,1)} %param.13) | copy-start | bytes 1179652
  2.4 7.1 %copy-start.2 = (f32[1000]{0:T(1024)S(1)}, f32[1000]{0:T(1024)}, u32[]{:S(2)}) copy-start(f32[1000]{0:T(1024)} %param.16) | copy-start | bytes 12004
  2.4 7.1 %copy-start.3 = (s32[4]{0:T(128)S(1)}, s32[4]{0:T(128)}, u32[]{:S(2)}) copy-start(s32[4]{0:T(128)} %param.17) | copy-start | bytes 52
  2.4 8.0 %copy-start.4 = (f32[8]{0:T(128)S(1)}, f32[8]{0:T(128)}, u32[]{:S(2)}) copy-start(f32[8]{0:T(128)} %param.14) | copy-start | bytes 100
  2.4 35.0 %all-to-all-start = ((bf16[4,3,48,8,128]{4,3,2,1,0:T(8,128)(2,1)}), bf16[4,3,48,8,128]{4,3,2,1,0:T(8,128)(2,1)S(1)}, u32[]{:S(2)}, u32[]{:S(2)}) async-start(bf16[4,3,48,8,128]{4,3,2,1,0:T(8,128)(2,1)} %pad_maximum_fusion), calls=%async_computation | async-start | bytes 2359296 | tf_op jit(solution)/shard_map/all_to_all | solution.py:85
  38.7 14.3 %copy-start.1 = (f32[64,8]{0,1:T(8,128)S(1)}, f32[64,8]{0,1:T(8,128)}, u32[]{:S(2)}) copy-start(f32[64,8]{0,1:T(8,128)} %param.12) | copy-start | bytes 6148
  40.9 4.4 %collective-permute-start = (f32[1,64,8]{1,2,0:T(8,128)S(1)}, f32[1,64,8]{1,2,0:T(8,128)S(1)}, u32[]{:S(2)}, u32[]{:S(2)}) collective-permute-start(f32[1,64,8]{1,2,0:T(8,128)S(1)} %get-tuple-element.11), channel_id=1, source_target_pairs={{0,1},{1,0},{2,3},{3,2},{4,5},{5,4},{6,7},{7,6},{8,9},{9,8},{10,11... | collective-permute-start | bytes 6152 | tf_op jit(solution)/shard_map/ppermute | solution.py:39
  40.9 4.6 %collective-permute-start.1 = (f32[1,64,8]{1,2,0:T(8,128)S(1)}, f32[1,64,8]{1,2,0:T(8,128)S(1)}, u32[]{:S(2)}, u32[]{:S(2)}) collective-permute-start(f32[1,64,8]{1,2,0:T(8,128)S(1)} %get-tuple-element.13), channel_id=1, source_target_pairs={{0,2},{1,3},{2,0},{3,1},{4,6},{5,7},{6,4},{7,5},{8,10},{9,11},{10,... | collective-permute-start | bytes 6152 | tf_op jit(solution)/shard_map/ppermute | solution.py:39
  42.9 5.4 %collective-permute-start.2 = (f32[1,64,8]{1,2,0:T(8,128)S(1)}, f32[1,64,8]{1,2,0:T(8,128)S(1)}, u32[]{:S(2)}, u32[]{:S(2)}) collective-permute-start(f32[1,64,8]{1,2,0:T(8,128)S(1)} %get-tuple-element.12), channel_id=1, source_target_pairs={{0,3},{1,2},{2,1},{3,0},{4,7},{5,6},{6,5},{7,4},{8,11},{9,10},{10,... | collective-permute-start | bytes 6152 | tf_op jit(solution)/shard_map/ppermute | solution.py:39
  48.3 1.9 %collective-permute-start.3 = (f32[64,8]{0,1:T(8,128)S(1)}, f32[64,8]{0,1:T(8,128)S(1)}, u32[]{:S(2)}, u32[]{:S(2)}) collective-permute-start(f32[64,8]{0,1:T(8,128)S(1)} %bitcast_add_fusion.4), channel_id=1, source_target_pairs={{0,4},{4,0},{8,12},{12,8},{1,5},{5,1},{9,13},{13,9},{2,6},{6,2},{1... | collective-permute-start | bytes 6152 | tf_op jit(solution)/shard_map/ppermute | solution.py:55
  48.4 3.7 %collective-permute-start.4 = (f32[64,8]{0,1:T(8,128)S(1)}, f32[64,8]{0,1:T(8,128)S(1)}, u32[]{:S(2)}, u32[]{:S(2)}) collective-permute-start(f32[64,8]{0,1:T(8,128)S(1)} %bitcast_add_fusion.4), channel_id=1, source_target_pairs={{0,8},{4,12},{8,0},{12,4},{1,9},{5,13},{9,1},{13,5},{2,10},{6,14},... | collective-permute-start | bytes 6152 | tf_op jit(solution)/shard_map/ppermute | solution.py:55
  49.9 3.0 %collective-permute-start.5 = (f32[64,8]{0,1:T(8,128)S(1)}, f32[64,8]{0,1:T(8,128)S(1)}, u32[]{:S(2)}, u32[]{:S(2)}) collective-permute-start(f32[64,8]{0,1:T(8,128)S(1)} %bitcast_add_fusion.4), channel_id=1, source_target_pairs={{0,12},{4,8},{8,4},{12,0},{1,13},{5,9},{9,5},{13,1},{2,14},{6,10},... | collective-permute-start | bytes 6152 | tf_op jit(solution)/shard_map/ppermute | solution.py:55

commit v5 on v4

--- a/solution.py
+++ b/solution.py
@@ -29,10 +29,13 @@
     return [(i, i ^ k) for i in range(size)]
 
 
-def gather_prefix(update, me, groups, step_dev, steps_axis):
+def gather_prefix(update, me, groups, step_dev, steps_axis, partner_order):
     local_steps = update.shape[0]
-    partners = me ^ jnp.arange(groups, dtype=jnp.int32)
-    ordered = jnp.take(update, partners, axis=2)
+    if partner_order:
+        ordered = update
+    else:
+        partners = me ^ jnp.arange(groups, dtype=jnp.int32)
+        ordered = jnp.take(update, partners, axis=2)
     pieces = [ordered[:, :, 0]]
     sources = [me]
     for k in range(1, groups):
@@ -81,16 +84,30 @@
     me = lax.axis_index("seq")
 
     chunks = [a.reshape(groups, per_dev, tok_dev, head_size) for a in (queries, keys, values)]
-    stacked = jnp.stack(chunks, axis=1)
-    gathered = lax.all_to_all(stacked, "seq", split_axis=0, concat_axis=3, tiled=True)
-    gathered = gathered.reshape(3, per_dev, length, head_size)
+    whole_steps = per_dev % (branches * heads) == 0
+    if whole_steps and groups & (groups - 1) == 0:
+        arrived = []
+        for k in range(groups):
+            piece = jnp.stack(
+                [lax.dynamic_index_in_dim(c, me ^ k, 0, keepdims=False) for c in chunks]
+            )
+            if k:
+                piece = lax.ppermute(piece, "seq", xor_pairs(groups, k))
+            arrived.append(piece)
+        gathered = jnp.concatenate(arrived, axis=2)
+        partner_order = True
+    else:
+        stacked = jnp.stack(chunks, axis=1)
+        gathered = lax.all_to_all(stacked, "seq", split_axis=0, concat_axis=3, tiled=True)
+        gathered = gathered.reshape(3, per_dev, length, head_size)
+        partner_order = False
     heads_out = attend(gathered[0], gathered[1], gathered[2])
 
     weight_heads = out_weight.reshape(channels, heads, head_size)
     guide_scale = lookup(cfg_table, cfg_index)[0]
     step_len = lookup(step_table, time_index)
 
-    if per_dev % (branches * heads) == 0:
+    if whole_steps:
         local_steps = per_dev // (branches * heads)
         ho = heads_out.reshape(local_steps, branches, heads, length, head_size)
         wide = ho.astype(jnp.float32)
@@ -104,7 +121,9 @@
         my_len = lax.dynamic_slice_in_dim(step_len, me * local_steps, local_steps)
         update = my_len[:, None, None] * guided
         update = update.reshape(local_steps, channels, groups, tok_dev)
-        return start_latent[None] + gather_prefix(update, me, groups, step_dev, steps_axis)
+        return start_latent[None] + gather_prefix(
+            update, me, groups, step_dev, steps_axis, partner_order
+        )
 
     assert heads % per_dev == 0
     share = heads // per_dev

time: 53.8 us -> 49.6 us (0.922)
  waiting for transfers between devices: 32.1 us -> 25.3 us
  starting transfers between devices: 12.7 us -> 15.7 us
  other arithmetic: 5.42 us -> 3.28 us
  local copies, waits for them, and re-layouts: 1.27 us -> 3.04 us
    all_to_all x1 -> x0, waiting for transfers between devices: 26.4 us -> none  [on_device(): lax.all_to_all(stacked, 'seq', split_axis=0, concat_axis=3, tiled=True)]
    ppermute x0 -> x3, waiting for transfers between devices: none -> 18.6 us  [on_device(): piece = lax.ppermute(piece, 'seq', xor_pairs(groups, k))]
    all_to_all x1 -> x0, starting transfers between devices: 6.45 us -> none  [on_device(): lax.all_to_all(stacked, 'seq', split_axis=0, concat_axis=3, tiled=True)]
    ppermute x0 -> x3, starting transfers between devices: none -> 5.81 us  [on_device(): piece = lax.ppermute(piece, 'seq', xor_pairs(groups, k))]
    ppermute x3, starting transfers between devices: 4.39 us -> 8 us  [gather_prefix(): pieces.append(lax.ppermute(ordered[:, :, k], 'seq', xor_pairs(groups, k)))]
    dynamic_slice x0 -> x2, local copies, waits for them, and re-layouts: none -> 2.39 us  [on_device(): lax.dynamic_index_in_dim(c, me ^ k, 0, keepdims=False)]
    another operation x1 -> x3, other arithmetic: 2.42 us -> 0.11 us  [on_device(): jnp.stack([lax.dynamic_index_in_dim(c, me ^ k, 0, keepdims=False) for c i...]
    ppermute x3, waiting for transfers between devices: 3.04 us -> 4.02 us  [gather_prefix(): pieces.append(lax.ppermute(ordered[:, :, k], 'seq', xor_pairs(groups, k)))]
  transfers between devices with their start and end apart: 7 -> 9, of which waited for: 5 -> 6; matrix products, arithmetic and copies ran while one was open for 3% -> 3% of each run, Pallas kernels for 0% -> 0%
where the time goes in v5:
time: 49.6 us; the launch traced here: 49.4 us
  waiting for transfers between devices  25.3 us (51%)
  starting transfers between devices  15.7 us (32%)
  other arithmetic  3.28 us (7%)
  local copies, waits for them, and re-layouts  3.04 us (6%)
  matrix products  1.24 us (2%)
  between operations  0.82 us (2%)
    ppermute x3, waiting for transfers between devices, on_device(): piece = lax.ppermute(piece, 'seq', xor_pairs(groups, k))  18.6 us
    ppermute x3, starting transfers between devices, gather_prefix(): pieces.append(lax.ppermute(ordered[:, :, k], 'seq', xor_pairs(groups, k)))  8 us
    ppermute x3, starting transfers between devices, on_device(): piece = lax.ppermute(piece, 'seq', xor_pairs(groups, k))  5.81 us
    ppermute x3, waiting for transfers between devices, gather_prefix(): pieces.append(lax.ppermute(ordered[:, :, k], 'seq', xor_pairs(groups, k)))  4.02 us
    ppermute x3, waiting for transfers between devices, gather_prefix(): other = lax.ppermute(total, 'step', xor_pairs(steps_axis, k))  2.7 us
    dynamic_slice x2, local copies, waits for them, and re-layouts, on_device(): lax.dynamic_index_in_dim(c, me ^ k, 0, keepdims=False)  2.39 us
    ppermute x3, starting transfers between devices, gather_prefix(): other = lax.ppermute(total, 'step', xor_pairs(steps_axis, k))  1.86 us
    mul x1, other arithmetic, on_device(): update = my_len[:, None, None] * guided  1.24 us
  transfers between devices with their start and end apart: 9, of which 6 were waited for; matrix products, arithmetic and copies ran while one was open for 3% of the time, Pallas kernels for 0%

profile of v5, /device:TPU:0, one launch (start us, length us, event | category | flops | bytes accessed | tf_op | source)
XLA Modules:
  0.0 49.4 jit_solution(3807442102453589817)
XLA Ops:
  0.0 1.1 %constant_dynamic-slice_fusion.11 = (bf16[1,48,8,128]{3,2,1,0:T(8,128)(2,1)S(1)}, bf16[1,48,8,128]{3,2,1,0:T(8,128)(2,1)S(1)}, bf16[1,48,8,128]{3,2,1,0:T(8,128)(2,1)S(1)}, bf16[1,48,8,128]{3,2,1,0:T(8,128)(2,1)S(1)}) fusion(bf16[4,48,8,128]{3,2,1,0:T(8,128)(2,1)} %bitcast.100, s32[]{:T(128)S(6)} %select_n.214, s32[]{:T(128)S(6)} %select_n.217, ...), kind=kLoop, calls=%fused_computation.60 | loop fusion | bytes 786448 | tf_op jit(solution)/shard_map/jit(dynamic_index_in_dim)/dynamic_slice | solution.py:92
  1.1 1.3 %constant_dynamic-slice_fusion.9 = (bf16[1,48,8,128]{3,2,1,0:T(8,128)(2,1)S(1)}, bf16[1,48,8,128]{3,2,1,0:T(8,128)(2,1)S(1)}, bf16[1,48,8,128]{3,2,1,0:T(8,128)(...) fusion(bf16[4,48,8,128]{3,2,1,0:T(8,128)(2,1)} %bitcast.101, ...), kind=kLoop, calls=%fused_computation.58 | loop fusion | bytes 1572880 | tf_op jit(solution)/shard_map/jit(dynamic_index_in_dim)/dynamic_slice | solution.py:92
  2.5 3.1 %collective-permute-start = (bf16[3,48,8,128]{3,2,1,0:T(8,128)(2,1)S(1)}, bf16[3,48,8,128]{3,2,1,0:T(8,128)(2,1)S(1)}, u32[]{:S(2)}, u32[]{:S(2)}) collective-permute-start(bf16[3,48,8,128]{3,2,1,0:T(8,128)(2,1)S(1)} %pad_maximum_fusion.1), channel_id=1, source_target_pairs={{0,1},{1,0},{2,3},{3,2},{4,5},{5,4},{6,7},{7,6},{8,9},{9,8},{10,11... | collective-permute-start | bytes 884744 | tf_op jit(solution)/shard_map/ppermute | solution.py:95
  5.6 2.7 %collective-permute-start.1 = (bf16[3,48,8,128]{3,2,1,0:T(8,128)(2,1)S(1)}, bf16[3,48,8,128]{3,2,1,0:T(8,128)(2,1)S(1)}, u32[]{:S(2)}, u32[]{:S(2)}) collective-permute-start(bf16[3,48,8,128]{3,2,1,0:T(8,128)(2,1)S(1)} %pad_maximum_fusion.2), channel_id=1, source_target_pairs={{0,2},{1,3},{2,0},{3,1},{4,6},{5,7},{6,4},{7,5},{8,10},{9,11},{10,... | collective-permute-start | bytes 884744 | tf_op jit(solution)/shard_map/ppermute | solution.py:95
  8.4 0.2 select_reduce_fusion
  8.6 0.6 %dynamic_slice.40 = f32[1]{0:T(128)} dynamic-slice(f32[4]{0:T(128)S(1)} %select_reduce_fusion, s32[]{:T(128)S(6)} %select_n.214), dynamic_slice_sizes={1} | dynamic-slice | bytes 12 | tf_op jit(solution)/shard_map/dynamic_slice | solution.py:121
  9.9 0.7 %fusion.21 = f32[]{:T(128)} fusion(f32[8]{0:T(128)S(1)} %copy-done.4, s32[]{:T(128)} %bitcast.99), kind=kLoop, calls=%fused_computation.63 | loop fusion | flops 23 | bytes 40 | tf_op jit(solution)/shard_map/reduce_sum | solution.py:13
  10.5 7.5 %collective-permute-done = bf16[3,48,8,128]{3,2,1,0:T(8,128)(2,1)S(1)} collective-permute-done((bf16[3,48,8,128]{3,2,1,0:T(8,128)(2,1)S(1)}, bf16[3,48,8,128]{3,2,1,0:T(8,128)(2,1)S(1)}, u32[]{:S(2)}, u32[]{:S(2)}) %collective-permute-start) | collective-permute-done | bytes 294944 | tf_op jit(solution)/shard_map/ppermute | solution.py:95
  18.1 11.1 %collective-permute-done.1 = bf16[3,48,8,128]{3,2,1,0:T(8,128)(2,1)S(1)} collective-permute-done((bf16[3,48,8,128]{3,2,1,0:T(8,128)(2,1)S(1)}, bf16[3,48,8,128]{3,2,1,0:T(8,128)(2,1)S(1)}, u32[]{:S(2)}, u32[]{:S(2)}) %collective-permute-start.1) | collective-permute-done | bytes 294944 | tf_op jit(solution)/shard_map/ppermute | solution.py:95
  29.2 0.2 pad_maximum_fusion
  29.4 0.3 fusion.22
  29.9 0.7 %multiply_reduce_fusion = (f32[48,32]{1,0:T(8,128)S(1)}, bf16[48,32,128]{2,1,0:T(8,128)(2,1)S(1)}) fusion(f32[48,32]{1,0:T(8,128)S(1)} %fusion.3, bf16[3,48,32,128]{3,2,1,0:T(8,128)(2,1)S(1)} %pad_maximum_fusion, f32[48,32,32]{1,2,0:T(8,128)S(1)} %get-tuple-element.24, f32[48,32]{1,0:T(8,128)S(1)} %get-tuple-element.23), kind=kOutput, calls=%fused_computation.7 | convolution fusion | flops 13662720 | bytes 1628160 | tf_op jit(solution)/shard_map/iqk,ikd->iqd/dot_general | solution.py:24
  30.6 0.2 fusion.2
  30.9 1.2 %fusion.11 = f32[1,64,4,8]{1,3,2,0:T(8,128)S(1)} fusion(f32[1,2,64,32]{2,3,1,0:T(8,128)S(1)} %fusion.2, f32[]{:T(128)} %fusion.21, f32[]{:T(128)} %bitcast), kind=kLoop, calls=%fused_computation.24 | loop fusion | flops 8192 | bytes 24584 | tf_op jit(solution)/shard_map/mul | solution.py:122
  32.1 5.5 %collective-permute-start.3 = (f32[1,64,8]{1,2,0:T(8,128)S(1)}, f32[1,64,8]{1,2,0:T(8,128)S(1)}, u32[]{:S(2)}, u32[]{:S(2)}) collective-permute-start(f32[1,64,8]{1,2,0:T(8,128)S(1)} %get-tuple-element.20), channel_id=1, source_target_pairs={{0,1},{1,0},{2,3},{3,2},{4,5},{5,4},{6,7},{7,6},{8,9},{9,8},{10,11... | collective-permute-start | bytes 6152 | tf_op jit(solution)/shard_map/ppermute | solution.py:42
  37.7 1.1 %collective-permute-start.4 = (f32[1,64,8]{1,2,0:T(8,128)S(1)}, f32[1,64,8]{1,2,0:T(8,128)S(1)}, u32[]{:S(2)}, u32[]{:S(2)}) collective-permute-start(f32[1,64,8]{1,2,0:T(8,128)S(1)} %get-tuple-element.22), channel_id=1, source_target_pairs={{0,2},{1,3},{2,0},{3,1},{4,6},{5,7},{6,4},{7,5},{8,10},{9,11},{10,... | collective-permute-start | bytes 6152 | tf_op jit(solution)/shard_map/ppermute | solution.py:42
  38.7 1.4 %collective-permute-start.5 = (f32[1,64,8]{1,2,0:T(8,128)S(1)}, f32[1,64,8]{1,2,0:T(8,128)S(1)}, u32[]{:S(2)}, u32[]{:S(2)}) collective-permute-start(f32[1,64,8]{1,2,0:T(8,128)S(1)} %get-tuple-element.21), channel_id=1, source_target_pairs={{0,3},{1,2},{2,1},{3,0},{4,7},{5,6},{6,5},{7,4},{8,11},{9,10},{10,... | collective-permute-start | bytes 6152 | tf_op jit(solution)/shard_map/ppermute | solution.py:42
  40.1 2.0 %collective-permute-done.4 = f32[1,64,8]{1,2,0:T(8,128)S(1)} collective-permute-done((f32[1,64,8]{1,2,0:T(8,128)S(1)}, f32[1,64,8]{1,2,0:T(8,128)S(1)}, u32[]{:S(2)}, u32[]{:S(2)}) %collective-permute-start.4) | collective-permute-done | bytes 2080 | tf_op jit(solution)/shard_map/ppermute | solution.py:42
  42.2 2.0 %collective-permute-done.5 = f32[1,64,8]{1,2,0:T(8,128)S(1)} collective-permute-done((f32[1,64,8]{1,2,0:T(8,128)S(1)}, f32[1,64,8]{1,2,0:T(8,128)S(1)}, u32[]{:S(2)}, u32[]{:S(2)}) %collective-permute-start.5) | collective-permute-done | bytes 2080 | tf_op jit(solution)/shard_map/ppermute | solution.py:42
  44.2 1.6 %collective-permute-start.7 = (f32[64,8]{0,1:T(8,128)S(1)}, f32[64,8]{0,1:T(8,128)S(1)}, u32[]{:S(2)}, u32[]{:S(2)}) collective-permute-start(f32[64,8]{0,1:T(8,128)S(1)} %bitcast_add_fusion.4), channel_id=1, source_target_pairs={{0,8},{4,12},{8,0},{12,4},{1,9},{5,13},{9,1},{13,5},{2,10},{6,14},... | collective-permute-start | bytes 6152 | tf_op jit(solution)/shard_map/ppermute | solution.py:58
  45.7 0.3 collective-permute-start.8
  46.1 1.8 %collective-permute-done.7 = f32[64,8]{0,1:T(8,128)S(1)} collective-permute-done((f32[64,8]{0,1:T(8,128)S(1)}, f32[64,8]{0,1:T(8,128)S(1)}, u32[]{:S(2)}, u32[]{:S(2)}) %collective-permute-start.7) | collective-permute-done | bytes 2080 | tf_op jit(solution)/shard_map/ppermute | solution.py:58
  47.8 0.9 %collective-permute-done.8 = f32[64,8]{0,1:T(8,128)S(1)} collective-permute-done((f32[64,8]{0,1:T(8,128)S(1)}, f32[64,8]{0,1:T(8,128)S(1)}, u32[]{:S(2)}, u32[]{:S(2)}) %collective-permute-start.8) | collective-permute-done | bytes 2080 | tf_op jit(solution)/shard_map/ppermute | solution.py:58
  48.8 0.6 %fusion.12 = f32[4,64,8]{1,2,0:T(8,128)} fusion(f32[1,64,8]{1,2,0:T(8,128)S(1)} %get-tuple-element.18, f32[1,64,8]{1,2,0:T(8,128)S(1)} %get-tuple-element.19, f32[1,64,8]{1,2,0:T(8,128)S(1)} %fusion.18, f32[1,64,8]{1,2,0:T(8,128)S(1)} %get-tuple-element.17, f32[64,8]{0,1:T(8,128)S(1)} %select_add_fusion, f32[64,8]{0,1:T(8,128)S(1)} %copy-done.1), kind=kLoop, calls=%fused_computation.27 | loop fusion | flops 10240 | bytes 20480 | tf_op jit(solution)/shard_map/add | solution.py:124
  (26 shorter events, 0.5 us)
Async XLA Ops:
  0.0 30.6 %copy-start = (bf16[64,3072]{1,0:T(8,128)(2,1)S(1)}, bf16[64,3072]{1,0:T(8,128)(2,1)}, u32[]{:S(2)}) copy-start(bf16[64,3072]{1,0:T(8,128)(2,1)} %param.13) | copy-start | bytes 1179652
  2.4 6.0 %copy-start.2 = (f32[1000]{0:T(1024)S(1)}, f32[1000]{0:T(1024)}, u32[]{:S(2)}) copy-start(f32[1000]{0:T(1024)} %param.16) | copy-start | bytes 12004
  2.4 6.0 %copy-start.3 = (s32[4]{0:T(128)S(1)}, s32[4]{0:T(128)}, u32[]{:S(2)}) copy-start(s32[4]{0:T(128)} %param.17) | copy-start | bytes 52
  2.4 7.4 %copy-start.4 = (f32[8]{0:T(128)S(1)}, f32[8]{0:T(128)}, u32[]{:S(2)}) copy-start(f32[8]{0:T(128)} %param.14) | copy-start | bytes 100
  2.5 15.6 %collective-permute-start = (bf16[3,48,8,128]{3,2,1,0:T(8,128)(2,1)S(1)}, bf16[3,48,8,128]{3,2,1,0:T(8,128)(2,1)S(1)}, u32[]{:S(2)}, u32[]{:S(2)}) collective-permute-start(bf16[3,48,8,128]{3,2,1,0:T(8,128)(2,1)S(1)} %pad_maximum_fusion.1), channel_id=1, source_target_pairs={{0,1},{1,0},{2,3},{3,2},{4,5},{5,4},{6,7},{7,6},{8,9},{9,8},{10,11... | collective-permute-start | bytes 884744 | tf_op jit(solution)/shard_map/ppermute | solution.py:95
  5.6 23.5 %collective-permute-start.1 = (bf16[3,48,8,128]{3,2,1,0:T(8,128)(2,1)S(1)}, bf16[3,48,8,128]{3,2,1,0:T(8,128)(2,1)S(1)}, u32[]{:S(2)}, u32[]{:S(2)}) collective-permute-start(bf16[3,48,8,128]{3,2,1,0:T(8,128)(2,1)S(1)} %pad_maximum_fusion.2), channel_id=1, source_target_pairs={{0,2},{1,3},{2,0},{3,1},{4,6},{5,7},{6,4},{7,5},{8,10},{9,11},{10,... | collective-permute-start | bytes 884744 | tf_op jit(solution)/shard_map/ppermute | solution.py:95
  8.3 20.9 %collective-permute-start.2 = (bf16[3,48,8,128]{3,2,1,0:T(8,128)(2,1)S(1)}, bf16[3,48,8,128]{3,2,1,0:T(8,128)(2,1)S(1)}, u32[]{:S(2)}, u32[]{:S(2)}) collective-permute-start(bf16[3,48,8,128]{3,2,1,0:T(8,128)(2,1)S(1)} %pad_maximum_fusion.3), channel_id=1, source_target_pairs={{0,3},{1,2},{2,1},{3,0},{4,7},{5,6},{6,5},{7,4},{8,11},{9,10},{10,... | collective-permute-start | bytes 884744 | tf_op jit(solution)/shard_map/ppermute | solution.py:95
  30.6 18.2 %copy-start.1 = (f32[64,8]{0,1:T(8,128)S(1)}, f32[64,8]{0,1:T(8,128)}, u32[]{:S(2)}) copy-start(f32[64,8]{0,1:T(8,128)} %param.12) | copy-start | bytes 6148
  32.1 8.0 %collective-permute-start.3 = (f32[1,64,8]{1,2,0:T(8,128)S(1)}, f32[1,64,8]{1,2,0:T(8,128)S(1)}, u32[]{:S(2)}, u32[]{:S(2)}) collective-permute-start(f32[1,64,8]{1,2,0:T(8,128)S(1)} %get-tuple-element.20), channel_id=1, source_target_pairs={{0,1},{1,0},{2,3},{3,2},{4,5},{5,4},{6,7},{7,6},{8,9},{9,8},{10,11... | collective-permute-start | bytes 6152 | tf_op jit(solution)/shard_map/ppermute | solution.py:42
  37.7 4.5 %collective-permute-start.4 = (f32[1,64,8]{1,2,0:T(8,128)S(1)}, f32[1,64,8]{1,2,0:T(8,128)S(1)}, u32[]{:S(2)}, u32[]{:S(2)}) collective-permute-start(f32[1,64,8]{1,2,0:T(8,128)S(1)} %get-tuple-element.22), channel_id=1, source_target_pairs={{0,2},{1,3},{2,0},{3,1},{4,6},{5,7},{6,4},{7,5},{8,10},{9,11},{10,... | collective-permute-start | bytes 6152 | tf_op jit(solution)/shard_map/ppermute | solution.py:42
  38.7 5.4 %collective-permute-start.5 = (f32[1,64,8]{1,2,0:T(8,128)S(1)}, f32[1,64,8]{1,2,0:T(8,128)S(1)}, u32[]{:S(2)}, u32[]{:S(2)}) collective-permute-start(f32[1,64,8]{1,2,0:T(8,128)S(1)} %get-tuple-element.21), channel_id=1, source_target_pairs={{0,3},{1,2},{2,1},{3,0},{4,7},{5,6},{6,5},{7,4},{8,11},{9,10},{10,... | collective-permute-start | bytes 6152 | tf_op jit(solution)/shard_map/ppermute | solution.py:42
  44.2 1.9 %collective-permute-start.6 = (f32[64,8]{0,1:T(8,128)S(1)}, f32[64,8]{0,1:T(8,128)S(1)}, u32[]{:S(2)}, u32[]{:S(2)}) collective-permute-start(f32[64,8]{0,1:T(8,128)S(1)} %bitcast_add_fusion.4), channel_id=1, source_target_pairs={{0,4},{4,0},{8,12},{12,8},{1,5},{5,1},{9,13},{13,9},{2,6},{6,2},{1... | collective-permute-start | bytes 6152 | tf_op jit(solution)/shard_map/ppermute | solution.py:58
  44.2 3.7 %collective-permute-start.7 = (f32[64,8]{0,1:T(8,128)S(1)}, f32[64,8]{0,1:T(8,128)S(1)}, u32[]{:S(2)}, u32[]{:S(2)}) collective-permute-start(f32[64,8]{0,1:T(8,128)S(1)} %bitcast_add_fusion.4), channel_id=1, source_target_pairs={{0,8},{4,12},{8,0},{12,4},{1,9},{5,13},{9,1},{13,5},{2,10},{6,14},... | collective-permute-start | bytes 6152 | tf_op jit(solution)/shard_map/ppermute | solution.py:58
  45.7 3.0 %collective-permute-start.8 = (f32[64,8]{0,1:T(8,128)S(1)}, f32[64,8]{0,1:T(8,128)S(1)}, u32[]{:S(2)}, u32[]{:S(2)}) collective-permute-start(f32[64,8]{0,1:T(8,128)S(1)} %bitcast_add_fusion.4), channel_id=1, source_target_pairs={{0,12},{4,8},{8,4},{12,0},{1,13},{5,9},{9,5},{13,1},{2,14},{6,10},... | collective-permute-start | bytes 6152 | tf_op jit(solution)/shard_map/ppermute | solution.py:58

commit v6 on v5

--- a/solution.py
+++ b/solution.py
@@ -86,15 +86,15 @@
     chunks = [a.reshape(groups, per_dev, tok_dev, head_size) for a in (queries, keys, values)]
     whole_steps = per_dev % (branches * heads) == 0
     if whole_steps and groups & (groups - 1) == 0:
-        arrived = []
-        for k in range(groups):
-            piece = jnp.stack(
-                [lax.dynamic_index_in_dim(c, me ^ k, 0, keepdims=False) for c in chunks]
-            )
+        arrived = {}
+        for k in reversed(range(groups)):
+            pieces = [lax.dynamic_index_in_dim(c, me ^ k, 0, keepdims=False) for c in chunks]
             if k:
-                piece = lax.ppermute(piece, "seq", xor_pairs(groups, k))
-            arrived.append(piece)
-        gathered = jnp.concatenate(arrived, axis=2)
+                pieces = [lax.ppermute(p, "seq", xor_pairs(groups, k)) for p in pieces]
+            arrived[k] = pieces
+        gathered = [
+            jnp.concatenate([arrived[k][i] for k in range(groups)], axis=1) for i in range(3)
+        ]
         partner_order = True
     else:
         stacked = jnp.stack(chunks, axis=1)

time: 49.6 us -> 48 us (0.968)
  waiting for transfers between devices: 25.3 us -> 13.2 us
  starting transfers between devices: 15.7 us -> 26.5 us
    ppermute x3 -> x9, starting transfers between devices: 5.81 us -> 20.5 us  [on_device(): pieces = [lax.ppermute(p, 'seq', xor_pairs(groups, k)) for p in pieces]]
    ppermute x3 -> x9, waiting for transfers between devices: 18.6 us -> 6.48 us  [on_device(): pieces = [lax.ppermute(p, 'seq', xor_pairs(groups, k)) for p in pieces]]
    ppermute x3, starting transfers between devices: 8 us -> 4.04 us  [gather_prefix(): pieces.append(lax.ppermute(ordered[:, :, k], 'seq', xor_pairs(groups, k)))]
    dynamic_slice x2 -> x0, local copies, waits for them, and re-layouts: 2.39 us -> none  [on_device(): lax.dynamic_index_in_dim(c, me ^ k, 0, keepdims=False)]
    squeeze x0 -> x3, local copies, waits for them, and re-layouts: none -> 1.21 us  [on_device(): lax.dynamic_index_in_dim(c, me ^ k, 0, keepdims=False)]
    unnamed x10 -> x14, local copies, waits for them, and re-layouts: 0.03 us -> 1.24 us
  transfers between devices with their start and end apart: 9 -> 15, of which waited for: 6 -> 7; matrix products, arithmetic and copies ran while one was open for 3% -> 4% of each run, Pallas kernels for 0% -> 0%
where the time goes in v6:
time: 48 us; the launch traced here: 47.8 us
  starting transfers between devices  26.5 us (55%)
  waiting for transfers between devices  13.2 us (28%)
  local copies, waits for them, and re-layouts  3.06 us (6%)
  other arithmetic  2.98 us (6%)
  matrix products  1.25 us (3%)
  between operations  0.81 us (2%)
    ppermute x9, starting transfers between devices, on_device(): pieces = [lax.ppermute(p, 'seq', xor_pairs(groups, k)) for p in pieces]  20.5 us
    ppermute x9, waiting for transfers between devices, on_device(): pieces = [lax.ppermute(p, 'seq', xor_pairs(groups, k)) for p in pieces]  6.48 us
    ppermute x3, waiting for transfers between devices, gather_prefix(): pieces.append(lax.ppermute(ordered[:, :, k], 'seq', xor_pairs(groups, k)))  4.05 us
    ppermute x3, starting transfers between devices, gather_prefix(): pieces.append(lax.ppermute(ordered[:, :, k], 'seq', xor_pairs(groups, k)))  4.04 us
    ppermute x3, waiting for transfers between devices, gather_prefix(): other = lax.ppermute(total, 'step', xor_pairs(steps_axis, k))  2.69 us
    ppermute x3, starting transfers between devices, gather_prefix(): other = lax.ppermute(total, 'step', xor_pairs(steps_axis, k))  1.93 us
    mul x1, other arithmetic, on_device(): update = my_len[:, None, None] * guided  1.26 us
    unnamed x14, local copies, waits for them, and re-layouts  1.24 us
  transfers between devices with their start and end apart: 15, of which 7 were waited for; matrix products, arithmetic and copies ran while one was open for 4% of the time, Pallas kernels for 0%

profile of v6, /device:TPU:0, one launch (start us, length us, event | category | flops | bytes accessed | tf_op | source)
XLA Modules:
  0.0 47.8 jit_solution(1920984318285825151)
XLA Ops:
  0.0 1.1 %dynamic-slice_bitcast_fusion.11 = (bf16[48,8,128]{2,1,0:T(8,128)(2,1)S(1)}, bf16[48,8,128]{2,1,0:T(8,128)(2,1)S(1)}, bf16[48,8,128]{2,1,0:T(8,128)(2,1)S(1)}, bf16[48,8,128]{2,1,0:T(8,128)(2,1)S(1)}) fusion(bf16[4,48,8,128]{3,2,1,0:T(8,128)(2,1)} %bitcast.109, s32[]{:T(128)S(6)} %select_n.214, s32[]{:T(128)S(6)} %select_n.217, s32[]{:T(128)S(6)} %select_n.216, ...), kind=kLoop, calls=%fused_computation.45 | loop fusion | bytes 786448 | tf_op jit(solution)/shard_map/jit(dynamic_index_in_dim)/squeeze | solution.py:91
  1.1 3.1 %collective-permute-start = (bf16[48,8,128]{2,1,0:T(8,128)(2,1)S(1)}, bf16[48,8,128]{2,1,0:T(8,128)(2,1)S(1)}, u32[]{:S(2)}, u32[]{:S(2)}) collective-permute-start(bf16[48,8,128]{2,1,0:T(8,128)(2,1)S(1)} %get-tuple-element.16), channel_id=1, source_target_pairs={{0,1},{1,0},{2,3},{3,2},{4,5},{5,4},{6,7},{7,6},{8,9},{9,8},{10,11... | collective-permute-start | bytes 294920 | tf_op jit(solution)/shard_map/ppermute | solution.py:93
  4.2 2.6 %collective-permute-start.1 = (bf16[48,8,128]{2,1,0:T(8,128)(2,1)S(1)}, bf16[48,8,128]{2,1,0:T(8,128)(2,1)S(1)}, u32[]{:S(2)}, u32[]{:S(2)}) collective-permute-start(bf16[48,8,128]{2,1,0:T(8,128)(2,1)S(1)} %get-tuple-element.15), channel_id=1, source_target_pairs={{0,2},{1,3},{2,0},{3,1},{4,6},{5,7},{6,4},{7,5},{8,10},{9,11},{10,... | collective-permute-start | bytes 294920 | tf_op jit(solution)/shard_map/ppermute | solution.py:93
  6.9 0.9 %collective-permute-start.3 = (bf16[48,8,128]{2,1,0:T(8,128)(2,1)S(1)}, bf16[48,8,128]{2,1,0:T(8,128)(2,1)S(1)}, u32[]{:S(2)}, u32[]{:S(2)}) collective-permute-start(bf16[48,8,128]{2,1,0:T(8,128)(2,1)S(1)} %get-tuple-element.12), channel_id=1, source_target_pairs={{0,1},{1,0},{2,3},{3,2},{4,5},{5,4},{6,7},{7,6},{8,9},{9,8},{10,11... | collective-permute-start | bytes 294920 | tf_op jit(solution)/shard_map/ppermute | solution.py:93
  7.8 3.5 %collective-permute-start.4 = (bf16[48,8,128]{2,1,0:T(8,128)(2,1)S(1)}, bf16[48,8,128]{2,1,0:T(8,128)(2,1)S(1)}, u32[]{:S(2)}, u32[]{:S(2)}) collective-permute-start(bf16[48,8,128]{2,1,0:T(8,128)(2,1)S(1)} %get-tuple-element.11), channel_id=1, source_target_pairs={{0,2},{1,3},{2,0},{3,1},{4,6},{5,7},{6,4},{7,5},{8,10},{9,11},{10,... | collective-permute-start | bytes 294920 | tf_op jit(solution)/shard_map/ppermute | solution.py:93
  11.5 0.6 %dynamic_slice.40 = f32[1]{0:T(128)} dynamic-slice(f32[4]{0:T(128)S(1)} %select_reduce_fusion, s32[]{:T(128)S(6)} %select_n.214), dynamic_slice_sizes={1} | dynamic-slice | bytes 12 | tf_op jit(solution)/shard_map/dynamic_slice | solution.py:121
  13.0 0.5 %copy-done.6 = f32[8]{0:T(128)S(1)} copy-done((f32[8]{0:T(128)S(1)}, f32[8]{0:T(128)}, u32[]{:S(2)}) %copy-start.6) | copy-done | bytes 56
  13.5 0.7 %fusion.42 = f32[]{:T(128)} fusion(f32[8]{0:T(128)S(1)} %copy-done.6, s32[]{:T(128)} %bitcast.108), kind=kLoop, calls=%fused_computation.77 | loop fusion | flops 23 | bytes 40 | tf_op jit(solution)/shard_map/reduce_sum | solution.py:13
  14.2 0.7 %collective-permute-done.1 = bf16[48,8,128]{2,1,0:T(8,128)(2,1)S(1)} collective-permute-done((bf16[48,8,128]{2,1,0:T(8,128)(2,1)S(1)}, bf16[48,8,128]{2,1,0:T(8,128)(2,1)S(1)}, u32[]{:S(2)}, u32[]{:S(2)}) %collective-permute-start.1) | collective-permute-done | bytes 98336 | tf_op jit(solution)/shard_map/ppermute | solution.py:93
  14.9 0.7 %collective-permute-start.6 = (bf16[48,8,128]{2,1,0:T(8,128)(2,1)S(1)}, bf16[48,8,128]{2,1,0:T(8,128)(2,1)S(1)}, u32[]{:S(2)}, u32[]{:S(2)}) collective-permute-start(bf16[48,8,128]{2,1,0:T(8,128)(2,1)S(1)} %get-tuple-element.8), channel_id=1, source_target_pairs={{0,1},{1,0},{2,3},{3,2},{4,5},{5,4},{6,7},{7,6},{8,9},{9,8},{10,11... | collective-permute-start | bytes 294920 | tf_op jit(solution)/shard_map/ppermute | solution.py:93
  15.6 9.2 %collective-permute-start.7 = (bf16[48,8,128]{2,1,0:T(8,128)(2,1)S(1)}, bf16[48,8,128]{2,1,0:T(8,128)(2,1)S(1)}, u32[]{:S(2)}, u32[]{:S(2)}) collective-permute-start(bf16[48,8,128]{2,1,0:T(8,128)(2,1)S(1)} %get-tuple-element.7), channel_id=1, source_target_pairs={{0,2},{1,3},{2,0},{3,1},{4,6},{5,7},{6,4},{7,5},{8,10},{9,11},{10,... | collective-permute-start | bytes 294920 | tf_op jit(solution)/shard_map/ppermute | solution.py:93
  24.8 0.4 collective-permute-start.8
  25.8 5.7 %collective-permute-done.7 = bf16[48,8,128]{2,1,0:T(8,128)(2,1)S(1)} collective-permute-done((bf16[48,8,128]{2,1,0:T(8,128)(2,1)S(1)}, bf16[48,8,128]{2,1,0:T(8,128)(2,1)S(1)}, u32[]{:S(2)}, u32[]{:S(2)}) %collective-permute-start.7) | collective-permute-done | bytes 98336 | tf_op jit(solution)/shard_map/ppermute | solution.py:93
  31.5 0.6 %multiply_reduce_fusion = (f32[48,32]{1,0:T(8,128)S(1)}, bf16[48,32,128]{2,1,0:T(8,128)(2,1)S(1)}) fusion(f32[48,32]{1,0:T(8,128)S(1)} %fusion.3, bf16[48,8,128]{2,1,0:T(8,128)(2,1)S(1)} %collective-permute-done.8, bf16[48,8,128]{2,1,0:T(8,128)(2,1)S(1)} %collective-permute-done.7, bf16[48,8,128]{2,1,0:T(8,128)(2,1)S(1)} %collective-permute-done.6, ...), kind=kOutput, calls=%fused_computation.6 | convolution fusion | flops 15235584 | bytes 1001472 | tf_op jit(solution)/shard_map/iqk,ikd->iqd/dot_general | solution.py:24
  32.5 1.3 %fusion.32 = f32[1,64,4,8]{1,3,2,0:T(8,128)S(1)} fusion(f32[1,2,64,32]{2,3,1,0:T(8,128)S(1)} %fusion.2, f32[]{:T(128)} %fusion.42, f32[]{:T(128)} %bitcast), kind=kLoop, calls=%fused_computation.50 | loop fusion | flops 8192 | bytes 24584 | tf_op jit(solution)/shard_map/mul | solution.py:122
  33.8 2.7 %collective-permute-start.10 = (f32[1,64,8]{1,2,0:T(8,128)S(1)}, f32[1,64,8]{1,2,0:T(8,128)S(1)}, u32[]{:S(2)}, u32[]{:S(2)}) collective-permute-start(f32[1,64,8]{1,2,0:T(8,128)S(1)} %get-tuple-element.22), channel_id=1, source_target_pairs={{0,2},{1,3},{2,0},{3,1},{4,6},{5,7},{6,4},{7,5},{8,10},{9,11},{10,... | collective-permute-start | bytes 6152 | tf_op jit(solution)/shard_map/ppermute | solution.py:42
  36.4 1.3 %collective-permute-start.11 = (f32[1,64,8]{1,2,0:T(8,128)S(1)}, f32[1,64,8]{1,2,0:T(8,128)S(1)}, u32[]{:S(2)}, u32[]{:S(2)}) collective-permute-start(f32[1,64,8]{1,2,0:T(8,128)S(1)} %get-tuple-element.21), channel_id=1, source_target_pairs={{0,3},{1,2},{2,1},{3,0},{4,7},{5,6},{6,5},{7,4},{8,11},{9,10},{10,... | collective-permute-start | bytes 6152 | tf_op jit(solution)/shard_map/ppermute | solution.py:42
  37.8 0.5 %collective-permute-done.10 = f32[1,64,8]{1,2,0:T(8,128)S(1)} collective-permute-done((f32[1,64,8]{1,2,0:T(8,128)S(1)}, f32[1,64,8]{1,2,0:T(8,128)S(1)}, u32[]{:S(2)}, u32[]{:S(2)}) %collective-permute-start.10) | collective-permute-done | bytes 2080 | tf_op jit(solution)/shard_map/ppermute | solution.py:42
  38.3 3.5 %collective-permute-done.11 = f32[1,64,8]{1,2,0:T(8,128)S(1)} collective-permute-done((f32[1,64,8]{1,2,0:T(8,128)S(1)}, f32[1,64,8]{1,2,0:T(8,128)S(1)}, u32[]{:S(2)}, u32[]{:S(2)}) %collective-permute-start.11) | collective-permute-done | bytes 2080 | tf_op jit(solution)/shard_map/ppermute | solution.py:42
  41.9 1.6 %collective-permute-start.13 = (f32[64,8]{0,1:T(8,128)S(1)}, f32[64,8]{0,1:T(8,128)S(1)}, u32[]{:S(2)}, u32[]{:S(2)}) collective-permute-start(f32[64,8]{0,1:T(8,128)S(1)} %bitcast_add_fusion.4), channel_id=1, source_target_pairs={{0,8},{4,12},{8,0},{12,4},{1,9},{5,13},{9,1},{13,5},{2,10},{6,14},... | collective-permute-start | bytes 6152 | tf_op jit(solution)/shard_map/ppermute | solution.py:58
  43.8 1.8 %collective-permute-done.13 = f32[64,8]{0,1:T(8,128)S(1)} collective-permute-done((f32[64,8]{0,1:T(8,128)S(1)}, f32[64,8]{0,1:T(8,128)S(1)}, u32[]{:S(2)}, u32[]{:S(2)}) %collective-permute-start.13) | collective-permute-done | bytes 2080 | tf_op jit(solution)/shard_map/ppermute | solution.py:58
  45.6 0.9 %collective-permute-done.14 = f32[64,8]{0,1:T(8,128)S(1)} collective-permute-done((f32[64,8]{0,1:T(8,128)S(1)}, f32[64,8]{0,1:T(8,128)S(1)}, u32[]{:S(2)}, u32[]{:S(2)}) %collective-permute-start.14) | collective-permute-done | bytes 2080 | tf_op jit(solution)/shard_map/ppermute | solution.py:58
  46.5 0.7 %copy-done.3 = f32[64,8]{0,1:T(8,128)S(1)} copy-done((f32[64,8]{0,1:T(8,128)S(1)}, f32[64,8]{0,1:T(8,128)}, u32[]{:S(2)}) %copy-start.3) | copy-done | bytes 2072
  47.2 0.6 %fusion.33 = f32[4,64,8]{1,2,0:T(8,128)} fusion(f32[1,64,8]{1,2,0:T(8,128)S(1)} %get-tuple-element.18, f32[1,64,8]{1,2,0:T(8,128)S(1)} %get-tuple-element.19, f32[1,64,8]{1,2,0:T(8,128)S(1)} %fusion.39, f32[1,64,8]{1,2,0:T(8,128)S(1)} %get-tuple-element.17, f32[64,8]{0,1:T(8,128)S(1)} %select_add_fusion, f32[64,8]{0,1:T(8,128)S(1)} %copy-done.3), kind=kLoop, calls=%fused_computation.53 | loop fusion | flops 10240 | bytes 20480 | tf_op jit(solution)/shard_map/add | solution.py:124
  (39 shorter events, 1.8 us)
Async XLA Ops:
  0.0 32.2 %copy-start = (bf16[64,3072]{1,0:T(8,128)(2,1)S(1)}, bf16[64,3072]{1,0:T(8,128)(2,1)}, u32[]{:S(2)}) copy-start(bf16[64,3072]{1,0:T(8,128)(2,1)} %param.13) | copy-start | bytes 1179652
  0.0 6.8 %copy-start.1 = (bf16[4,2,24,8,128]{4,3,2,1,0:T(8,128)(2,1)S(1)}, bf16[4,2,24,8,128]{4,3,2,1,0:T(8,128)(2,1)}, u32[]{:S(2)}) copy-start(bf16[4,2,24,8,128]{4,3,2,1,0:T(8,128)(2,1)} %param.10) | copy-start | bytes 1179652
  1.1 11.7 %collective-permute-start = (bf16[48,8,128]{2,1,0:T(8,128)(2,1)S(1)}, bf16[48,8,128]{2,1,0:T(8,128)(2,1)S(1)}, u32[]{:S(2)}, u32[]{:S(2)}) collective-permute-start(bf16[48,8,128]{2,1,0:T(8,128)(2,1)S(1)} %get-tuple-element.16), channel_id=1, source_target_pairs={{0,1},{1,0},{2,3},{3,2},{4,5},{5,4},{6,7},{7,6},{8,9},{9,8},{10,11... | collective-permute-start | bytes 294920 | tf_op jit(solution)/shard_map/ppermute | solution.py:93
  4.2 10.7 %collective-permute-start.1 = (bf16[48,8,128]{2,1,0:T(8,128)(2,1)S(1)}, bf16[48,8,128]{2,1,0:T(8,128)(2,1)S(1)}, u32[]{:S(2)}, u32[]{:S(2)}) collective-permute-start(bf16[48,8,128]{2,1,0:T(8,128)(2,1)S(1)} %get-tuple-element.15), channel_id=1, source_target_pairs={{0,2},{1,3},{2,0},{3,1},{4,6},{5,7},{6,4},{7,5},{8,10},{9,11},{10,... | collective-permute-start | bytes 294920 | tf_op jit(solution)/shard_map/ppermute | solution.py:93
  6.8 8.8 %collective-permute-start.2 = (bf16[48,8,128]{2,1,0:T(8,128)(2,1)S(1)}, bf16[48,8,128]{2,1,0:T(8,128)(2,1)S(1)}, u32[]{:S(2)}, u32[]{:S(2)}) collective-permute-start(bf16[48,8,128]{2,1,0:T(8,128)(2,1)S(1)} %get-tuple-element.14), channel_id=1, source_target_pairs={{0,3},{1,2},{2,1},{3,0},{4,7},{5,6},{6,5},{7,4},{8,11},{9,10},{10,... | collective-permute-start | bytes 294920 | tf_op jit(solution)/shard_map/ppermute | solution.py:93
  6.8 4.5 %copy-start.4 = (f32[1000]{0:T(1024)S(1)}, f32[1000]{0:T(1024)}, u32[]{:S(2)}) copy-start(f32[1000]{0:T(1024)} %param.16) | copy-start | bytes 12004
  6.8 6.0 %copy-start.2 = (bf16[4,2,24,8,128]{4,3,2,1,0:T(8,128)(2,1)S(1)}, bf16[4,2,24,8,128]{4,3,2,1,0:T(8,128)(2,1)}, u32[]{:S(2)}) copy-start(bf16[4,2,24,8,128]{4,3,2,1,0:T(8,128)(2,1)} %param.11) | copy-start | bytes 1179652
  6.9 4.4 %copy-start.5 = (s32[4]{0:T(128)S(1)}, s32[4]{0:T(128)}, u32[]{:S(2)}) copy-start(s32[4]{0:T(128)} %param.17) | copy-start | bytes 52
  6.9 17.9 %collective-permute-start.3 = (bf16[48,8,128]{2,1,0:T(8,128)(2,1)S(1)}, bf16[48,8,128]{2,1,0:T(8,128)(2,1)S(1)}, u32[]{:S(2)}, u32[]{:S(2)}) collective-permute-start(bf16[48,8,128]{2,1,0:T(8,128)(2,1)S(1)} %get-tuple-element.12), channel_id=1, source_target_pairs={{0,1},{1,0},{2,3},{3,2},{4,5},{5,4},{6,7},{7,6},{8,9},{9,8},{10,11... | collective-permute-start | bytes 294920 | tf_op jit(solution)/shard_map/ppermute | solution.py:93
  7.8 17.4 %collective-permute-start.4 = (bf16[48,8,128]{2,1,0:T(8,128)(2,1)S(1)}, bf16[48,8,128]{2,1,0:T(8,128)(2,1)S(1)}, u32[]{:S(2)}, u32[]{:S(2)}) collective-permute-start(bf16[48,8,128]{2,1,0:T(8,128)(2,1)S(1)} %get-tuple-element.11), channel_id=1, source_target_pairs={{0,2},{1,3},{2,0},{3,1},{4,6},{5,7},{6,4},{7,5},{8,10},{9,11},{10,... | collective-permute-start | bytes 294920 | tf_op jit(solution)/shard_map/ppermute | solution.py:93
  12.9 0.7 %copy-start.6 = (f32[8]{0:T(128)S(1)}, f32[8]{0:T(128)}, u32[]{:S(2)}) copy-start(f32[8]{0:T(128)} %param.14) | copy-start | bytes 100
  12.9 12.4 %collective-permute-start.5 = (bf16[48,8,128]{2,1,0:T(8,128)(2,1)S(1)}, bf16[48,8,128]{2,1,0:T(8,128)(2,1)S(1)}, u32[]{:S(2)}, u32[]{:S(2)}) collective-permute-start(bf16[48,8,128]{2,1,0:T(8,128)(2,1)S(1)} %get-tuple-element.10), channel_id=1, source_target_pairs={{0,3},{1,2},{2,1},{3,0},{4,7},{5,6},{6,5},{7,4},{8,11},{9,10},{10,... | collective-permute-start | bytes 294920 | tf_op jit(solution)/shard_map/ppermute | solution.py:93
  14.9 10.9 %collective-permute-start.6 = (bf16[48,8,128]{2,1,0:T(8,128)(2,1)S(1)}, bf16[48,8,128]{2,1,0:T(8,128)(2,1)S(1)}, u32[]{:S(2)}, u32[]{:S(2)}) collective-permute-start(bf16[48,8,128]{2,1,0:T(8,128)(2,1)S(1)} %get-tuple-element.8), channel_id=1, source_target_pairs={{0,1},{1,0},{2,3},{3,2},{4,5},{5,4},{6,7},{7,6},{8,9},{9,8},{10,11... | collective-permute-start | bytes 294920 | tf_op jit(solution)/shard_map/ppermute | solution.py:93
  15.6 15.9 %collective-permute-start.7 = (bf16[48,8,128]{2,1,0:T(8,128)(2,1)S(1)}, bf16[48,8,128]{2,1,0:T(8,128)(2,1)S(1)}, u32[]{:S(2)}, u32[]{:S(2)}) collective-permute-start(bf16[48,8,128]{2,1,0:T(8,128)(2,1)S(1)} %get-tuple-element.7), channel_id=1, source_target_pairs={{0,2},{1,3},{2,0},{3,1},{4,6},{5,7},{6,4},{7,5},{8,10},{9,11},{10,... | collective-permute-start | bytes 294920 | tf_op jit(solution)/shard_map/ppermute | solution.py:93
  24.8 6.7 %collective-permute-start.8 = (bf16[48,8,128]{2,1,0:T(8,128)(2,1)S(1)}, bf16[48,8,128]{2,1,0:T(8,128)(2,1)S(1)}, u32[]{:S(2)}, u32[]{:S(2)}) collective-permute-start(bf16[48,8,128]{2,1,0:T(8,128)(2,1)S(1)} %get-tuple-element.6), channel_id=1, source_target_pairs={{0,3},{1,2},{2,1},{3,0},{4,7},{5,6},{6,5},{7,4},{8,11},{9,10},{10,... | collective-permute-start | bytes 294920 | tf_op jit(solution)/shard_map/ppermute | solution.py:93
  33.8 4.6 %collective-permute-start.10 = (f32[1,64,8]{1,2,0:T(8,128)S(1)}, f32[1,64,8]{1,2,0:T(8,128)S(1)}, u32[]{:S(2)}, u32[]{:S(2)}) collective-permute-start(f32[1,64,8]{1,2,0:T(8,128)S(1)} %get-tuple-element.22), channel_id=1, source_target_pairs={{0,2},{1,3},{2,0},{3,1},{4,6},{5,7},{6,4},{7,5},{8,10},{9,11},{10,... | collective-permute-start | bytes 6152 | tf_op jit(solution)/shard_map/ppermute | solution.py:42
  36.4 5.4 %collective-permute-start.11 = (f32[1,64,8]{1,2,0:T(8,128)S(1)}, f32[1,64,8]{1,2,0:T(8,128)S(1)}, u32[]{:S(2)}, u32[]{:S(2)}) collective-permute-start(f32[1,64,8]{1,2,0:T(8,128)S(1)} %get-tuple-element.21), channel_id=1, source_target_pairs={{0,3},{1,2},{2,1},{3,0},{4,7},{5,6},{6,5},{7,4},{8,11},{9,10},{10,... | collective-permute-start | bytes 6152 | tf_op jit(solution)/shard_map/ppermute | solution.py:42
  37.8 4.1 %collective-permute-start.9 = (f32[1,64,8]{1,2,0:T(8,128)S(1)}, f32[1,64,8]{1,2,0:T(8,128)S(1)}, u32[]{:S(2)}, u32[]{:S(2)}) collective-permute-start(f32[1,64,8]{1,2,0:T(8,128)S(1)} %get-tuple-element.20), channel_id=1, source_target_pairs={{0,1},{1,0},{2,3},{3,2},{4,5},{5,4},{6,7},{7,6},{8,9},{9,8},{10,11... | collective-permute-start | bytes 6152 | tf_op jit(solution)/shard_map/ppermute | solution.py:42
  41.9 2.0 %collective-permute-start.12 = (f32[64,8]{0,1:T(8,128)S(1)}, f32[64,8]{0,1:T(8,128)S(1)}, u32[]{:S(2)}, u32[]{:S(2)}) collective-permute-start(f32[64,8]{0,1:T(8,128)S(1)} %bitcast_add_fusion.4), channel_id=1, source_target_pairs={{0,4},{4,0},{8,12},{12,8},{1,5},{5,1},{9,13},{13,9},{2,6},{6,2},{1... | collective-permute-start | bytes 6152 | tf_op jit(solution)/shard_map/ppermute | solution.py:58
  41.9 3.7 %collective-permute-start.13 = (f32[64,8]{0,1:T(8,128)S(1)}, f32[64,8]{0,1:T(8,128)S(1)}, u32[]{:S(2)}, u32[]{:S(2)}) collective-permute-start(f32[64,8]{0,1:T(8,128)S(1)} %bitcast_add_fusion.4), channel_id=1, source_target_pairs={{0,8},{4,12},{8,0},{12,4},{1,9},{5,13},{9,1},{13,5},{2,10},{6,14},... | collective-permute-start | bytes 6152 | tf_op jit(solution)/shard_map/ppermute | solution.py:58
  43.5 3.0 %collective-permute-start.14 = (f32[64,8]{0,1:T(8,128)S(1)}, f32[64,8]{0,1:T(8,128)S(1)}, u32[]{:S(2)}, u32[]{:S(2)}) collective-permute-start(f32[64,8]{0,1:T(8,128)S(1)} %bitcast_add_fusion.4), channel_id=1, source_target_pairs={{0,12},{4,8},{8,4},{12,0},{1,13},{5,9},{9,5},{13,1},{2,14},{6,10},... | collective-permute-start | bytes 6152 | tf_op jit(solution)/shard_map/ppermute | solution.py:58
  46.5 0.7 %copy-start.3 = (f32[64,8]{0,1:T(8,128)S(1)}, f32[64,8]{0,1:T(8,128)}, u32[]{:S(2)}) copy-start(f32[64,8]{0,1:T(8,128)} %param.12) | copy-start | bytes 6148

commit v7 on v6

--- a/solution.py
+++ b/solution.py
@@ -29,17 +29,17 @@
     return [(i, i ^ k) for i in range(size)]
 
 
-def gather_prefix(update, me, groups, step_dev, steps_axis, partner_order):
+def gather_prefix(update, start, me, groups, step_dev, steps_axis, partner_order):
     local_steps = update.shape[0]
     if partner_order:
         ordered = update
     else:
         partners = me ^ jnp.arange(groups, dtype=jnp.int32)
-        ordered = jnp.take(update, partners, axis=2)
-    pieces = [ordered[:, :, 0]]
+        ordered = jnp.take(update, partners, axis=1)
+    pieces = [ordered[:, 0]]
     sources = [me]
     for k in range(1, groups):
-        pieces.append(lax.ppermute(ordered[:, :, k], "seq", xor_pairs(groups, k)))
+        pieces.append(lax.ppermute(ordered[:, k], "seq", xor_pairs(groups, k)))
         sources.append(me ^ k)
     zero = jnp.zeros((), jnp.float32)
     outs = []
@@ -50,14 +50,14 @@
                 term = jnp.where(source * local_steps + t <= s, piece[t], zero)
                 acc = term if acc is None else acc + term
         outs.append(acc)
-    local_cum = jnp.stack(outs)
     total = outs[-1]
+    local_cum = jnp.stack(outs) + start[None]
     position = lax.axis_index("step")
     earlier = jnp.zeros_like(total)
     for k in range(1, steps_axis):
         other = lax.ppermute(total, "step", xor_pairs(steps_axis, k))
         earlier = earlier + jnp.where((position ^ k) < position, other, zero)
-    return earlier[None] + local_cum
+    return jnp.transpose(local_cum + earlier[None], (0, 2, 1))
 
 
 def earlier_groups(local_cum, steps_axis):
@@ -114,15 +114,15 @@
         square_sum = jnp.sum(wide * wide, axis=(2, 4))
         root_mean = jnp.sqrt(square_sum / (H * HD) + 1e-06)
         drift = (
-            jnp.einsum("chd,sbhld->sbcl", weight_heads, ho, preferred_element_type=jnp.float32)
-            / root_mean[:, :, None, :]
+            jnp.einsum("chd,sbhld->sblc", weight_heads, ho, preferred_element_type=jnp.float32)
+            / root_mean[:, :, :, None]
         )
         guided = drift[:, 1] + guide_scale * (drift[:, 0] - drift[:, 1])
         my_len = lax.dynamic_slice_in_dim(step_len, me * local_steps, local_steps)
         update = my_len[:, None, None] * guided
-        update = update.reshape(local_steps, channels, groups, tok_dev)
-        return start_latent[None] + gather_prefix(
-            update, me, groups, step_dev, steps_axis, partner_order
+        update = update.reshape(local_steps, groups, tok_dev, channels)
+        return gather_prefix(
+            update, start_latent.T, me, groups, step_dev, steps_axis, partner_order
         )
 
     assert heads % per_dev == 0

time: 48 us -> 48 us (level)
    add x1 -> x0, other arithmetic: 0.61 us -> none  [on_device(): start_latent[None]]
    transpose x0 -> x1, other arithmetic: none -> 0.61 us  [gather_prefix(): return jnp.transpose(local_cum + earlier[None], (0, 2, 1))]
where the time goes in v7:
time: 48 us; the launch traced here: 47.8 us
  starting transfers between devices  26.5 us (55%)
  waiting for transfers between devices  13.2 us (28%)
  local copies, waits for them, and re-layouts  3.06 us (6%)
  other arithmetic  2.98 us (6%)
  matrix products  1.25 us (3%)
  between operations  0.81 us (2%)
    ppermute x9, starting transfers between devices, on_device(): pieces = [lax.ppermute(p, 'seq', xor_pairs(groups, k)) for p in pieces]  20.5 us
    ppermute x9, waiting for transfers between devices, on_device(): pieces = [lax.ppermute(p, 'seq', xor_pairs(groups, k)) for p in pieces]  6.48 us
    ppermute x3, waiting for transfers between devices, gather_prefix(): pieces.append(lax.ppermute(ordered[:, k], 'seq', xor_pairs(groups, k)))  4.05 us
    ppermute x3, starting transfers between devices, gather_prefix(): pieces.append(lax.ppermute(ordered[:, k], 'seq', xor_pairs(groups, k)))  4.04 us
    ppermute x3, waiting for transfers between devices, gather_prefix(): other = lax.ppermute(total, 'step', xor_pairs(steps_axis, k))  2.69 us
    ppermute x3, starting transfers between devices, gather_prefix(): other = lax.ppermute(total, 'step', xor_pairs(steps_axis, k))  1.93 us
    mul x1, other arithmetic, on_device(): update = my_len[:, None, None] * guided  1.26 us
    unnamed x14, local copies, waits for them, and re-layouts  1.24 us
  transfers between devices with their start and end apart: 15, of which 7 were waited for; matrix products, arithmetic and copies ran while one was open for 4% of the time, Pallas kernels for 0%

profile of v7, /device:TPU:0, one launch (start us, length us, event | category | flops | bytes accessed | tf_op | source)
XLA Modules:
  0.0 47.8 jit_solution(2298525441134556231)
XLA Ops:
  0.0 1.1 %dynamic-slice_bitcast_fusion.11 = (bf16[48,8,128]{2,1,0:T(8,128)(2,1)S(1)}, bf16[48,8,128]{2,1,0:T(8,128)(2,1)S(1)}, bf16[48,8,128]{2,1,0:T(8,128)(2,1)S(1)}, bf16[48,8,128]{2,1,0:T(8,128)(2,1)S(1)}) fusion(bf16[4,48,8,128]{3,2,1,0:T(8,128)(2,1)} %bitcast.111, s32[]{:T(128)S(6)} %select_n.213, s32[]{:T(128)S(6)} %select_n.216, s32[]{:T(128)S(6)} %select_n.215, ...), kind=kLoop, calls=%fused_computation.45 | loop fusion | bytes 786448 | tf_op jit(solution)/shard_map/jit(dynamic_index_in_dim)/squeeze | solution.py:91
  1.1 3.1 %collective-permute-start = (bf16[48,8,128]{2,1,0:T(8,128)(2,1)S(1)}, bf16[48,8,128]{2,1,0:T(8,128)(2,1)S(1)}, u32[]{:S(2)}, u32[]{:S(2)}) collective-permute-start(bf16[48,8,128]{2,1,0:T(8,128)(2,1)S(1)} %get-tuple-element.16), channel_id=1, source_target_pairs={{0,1},{1,0},{2,3},{3,2},{4,5},{5,4},{6,7},{7,6},{8,9},{9,8},{10,11... | collective-permute-start | bytes 294920 | tf_op jit(solution)/shard_map/ppermute | solution.py:93
  4.2 2.6 %collective-permute-start.1 = (bf16[48,8,128]{2,1,0:T(8,128)(2,1)S(1)}, bf16[48,8,128]{2,1,0:T(8,128)(2,1)S(1)}, u32[]{:S(2)}, u32[]{:S(2)}) collective-permute-start(bf16[48,8,128]{2,1,0:T(8,128)(2,1)S(1)} %get-tuple-element.15), channel_id=1, source_target_pairs={{0,2},{1,3},{2,0},{3,1},{4,6},{5,7},{6,4},{7,5},{8,10},{9,11},{10,... | collective-permute-start | bytes 294920 | tf_op jit(solution)/shard_map/ppermute | solution.py:93
  6.9 0.9 %collective-permute-start.3 = (bf16[48,8,128]{2,1,0:T(8,128)(2,1)S(1)}, bf16[48,8,128]{2,1,0:T(8,128)(2,1)S(1)}, u32[]{:S(2)}, u32[]{:S(2)}) collective-permute-start(bf16[48,8,128]{2,1,0:T(8,128)(2,1)S(1)} %get-tuple-element.12), channel_id=1, source_target_pairs={{0,1},{1,0},{2,3},{3,2},{4,5},{5,4},{6,7},{7,6},{8,9},{9,8},{10,11... | collective-permute-start | bytes 294920 | tf_op jit(solution)/shard_map/ppermute | solution.py:93
  7.8 3.5 %collective-permute-start.4 = (bf16[48,8,128]{2,1,0:T(8,128)(2,1)S(1)}, bf16[48,8,128]{2,1,0:T(8,128)(2,1)S(1)}, u32[]{:S(2)}, u32[]{:S(2)}) collective-permute-start(bf16[48,8,128]{2,1,0:T(8,128)(2,1)S(1)} %get-tuple-element.11), channel_id=1, source_target_pairs={{0,2},{1,3},{2,0},{3,1},{4,6},{5,7},{6,4},{7,5},{8,10},{9,11},{10,... | collective-permute-start | bytes 294920 | tf_op jit(solution)/shard_map/ppermute | solution.py:93
  11.5 0.6 %dynamic_slice.40 = f32[1]{0:T(128)} dynamic-slice(f32[4]{0:T(128)S(1)} %select_reduce_fusion, s32[]{:T(128)S(6)} %select_n.213), dynamic_slice_sizes={1} | dynamic-slice | bytes 12 | tf_op jit(solution)/shard_map/dynamic_slice | solution.py:121
  13.0 0.5 %copy-done.6 = f32[8]{0:T(128)S(1)} copy-done((f32[8]{0:T(128)S(1)}, f32[8]{0:T(128)}, u32[]{:S(2)}) %copy-start.6) | copy-done | bytes 56
  13.5 0.7 %fusion.43 = f32[]{:T(128)} fusion(f32[8]{0:T(128)S(1)} %copy-done.6, s32[]{:T(128)} %bitcast.110), kind=kLoop, calls=%fused_computation.78 | loop fusion | flops 23 | bytes 40 | tf_op jit(solution)/shard_map/reduce_sum | solution.py:13
  14.2 0.7 %collective-permute-done.1 = bf16[48,8,128]{2,1,0:T(8,128)(2,1)S(1)} collective-permute-done((bf16[48,8,128]{2,1,0:T(8,128)(2,1)S(1)}, bf16[48,8,128]{2,1,0:T(8,128)(2,1)S(1)}, u32[]{:S(2)}, u32[]{:S(2)}) %collective-permute-start.1) | collective-permute-done | bytes 98336 | tf_op jit(solution)/shard_map/ppermute | solution.py:93
  14.9 0.7 %collective-permute-start.6 = (bf16[48,8,128]{2,1,0:T(8,128)(2,1)S(1)}, bf16[48,8,128]{2,1,0:T(8,128)(2,1)S(1)}, u32[]{:S(2)}, u32[]{:S(2)}) collective-permute-start(bf16[48,8,128]{2,1,0:T(8,128)(2,1)S(1)} %get-tuple-element.8), channel_id=1, source_target_pairs={{0,1},{1,0},{2,3},{3,2},{4,5},{5,4},{6,7},{7,6},{8,9},{9,8},{10,11... | collective-permute-start | bytes 294920 | tf_op jit(solution)/shard_map/ppermute | solution.py:93
  15.6 9.2 %collective-permute-start.7 = (bf16[48,8,128]{2,1,0:T(8,128)(2,1)S(1)}, bf16[48,8,128]{2,1,0:T(8,128)(2,1)S(1)}, u32[]{:S(2)}, u32[]{:S(2)}) collective-permute-start(bf16[48,8,128]{2,1,0:T(8,128)(2,1)S(1)} %get-tuple-element.7), channel_id=1, source_target_pairs={{0,2},{1,3},{2,0},{3,1},{4,6},{5,7},{6,4},{7,5},{8,10},{9,11},{10,... | collective-permute-start | bytes 294920 | tf_op jit(solution)/shard_map/ppermute | solution.py:93
  24.8 0.4 collective-permute-start.8
  25.8 5.7 %collective-permute-done.7 = bf16[48,8,128]{2,1,0:T(8,128)(2,1)S(1)} collective-permute-done((bf16[48,8,128]{2,1,0:T(8,128)(2,1)S(1)}, bf16[48,8,128]{2,1,0:T(8,128)(2,1)S(1)}, u32[]{:S(2)}, u32[]{:S(2)}) %collective-permute-start.7) | collective-permute-done | bytes 98336 | tf_op jit(solution)/shard_map/ppermute | solution.py:93
  31.5 0.6 %multiply_reduce_fusion = (f32[48,32]{1,0:T(8,128)S(1)}, bf16[48,32,128]{2,1,0:T(8,128)(2,1)S(1)}) fusion(f32[48,32]{1,0:T(8,128)S(1)} %fusion.3, bf16[48,8,128]{2,1,0:T(8,128)(2,1)S(1)} %collective-permute-done.8, bf16[48,8,128]{2,1,0:T(8,128)(2,1)S(1)} %collective-permute-done.7, bf16[48,8,128]{2,1,0:T(8,128)(2,1)S(1)} %collective-permute-done.6, ...), kind=kOutput, calls=%fused_computation.6 | convolution fusion | flops 15235584 | bytes 1001472 | tf_op jit(solution)/shard_map/iqk,ikd->iqd/dot_general | solution.py:24
  32.5 1.3 %fusion.32 = f32[1,4,8,64]{3,2,1,0:T(8,128)S(1)} fusion(f32[1,2,32,64]{3,2,1,0:T(8,128)S(1)} %fusion.2, f32[]{:T(128)} %fusion.43, f32[]{:T(128)} %bitcast), kind=kLoop, calls=%fused_computation.50 | loop fusion | flops 8192 | bytes 24584 | tf_op jit(solution)/shard_map/mul | solution.py:122
  33.8 2.7 %collective-permute-start.10 = (f32[1,8,64]{2,1,0:T(8,128)S(1)}, f32[1,8,64]{2,1,0:T(8,128)S(1)}, u32[]{:S(2)}, u32[]{:S(2)}) collective-permute-start(f32[1,8,64]{2,1,0:T(8,128)S(1)} %get-tuple-element.22), channel_id=1, source_target_pairs={{0,2},{1,3},{2,0},{3,1},{4,6},{5,7},{6,4},{7,5},{8,10},{9,11},{10,... | collective-permute-start | bytes 6152 | tf_op jit(solution)/shard_map/ppermute | solution.py:42
  36.4 1.3 %collective-permute-start.11 = (f32[1,8,64]{2,1,0:T(8,128)S(1)}, f32[1,8,64]{2,1,0:T(8,128)S(1)}, u32[]{:S(2)}, u32[]{:S(2)}) collective-permute-start(f32[1,8,64]{2,1,0:T(8,128)S(1)} %get-tuple-element.21), channel_id=1, source_target_pairs={{0,3},{1,2},{2,1},{3,0},{4,7},{5,6},{6,5},{7,4},{8,11},{9,10},{10,... | collective-permute-start | bytes 6152 | tf_op jit(solution)/shard_map/ppermute | solution.py:42
  37.8 0.5 %collective-permute-done.10 = f32[1,8,64]{2,1,0:T(8,128)S(1)} collective-permute-done((f32[1,8,64]{2,1,0:T(8,128)S(1)}, f32[1,8,64]{2,1,0:T(8,128)S(1)}, u32[]{:S(2)}, u32[]{:S(2)}) %collective-permute-start.10) | collective-permute-done | bytes 2080 | tf_op jit(solution)/shard_map/ppermute | solution.py:42
  38.3 3.5 %collective-permute-done.11 = f32[1,8,64]{2,1,0:T(8,128)S(1)} collective-permute-done((f32[1,8,64]{2,1,0:T(8,128)S(1)}, f32[1,8,64]{2,1,0:T(8,128)S(1)}, u32[]{:S(2)}, u32[]{:S(2)}) %collective-permute-start.11) | collective-permute-done | bytes 2080 | tf_op jit(solution)/shard_map/ppermute | solution.py:42
  41.9 1.6 %collective-permute-start.13 = (f32[8,64]{1,0:T(8,128)S(1)}, f32[8,64]{1,0:T(8,128)S(1)}, u32[]{:S(2)}, u32[]{:S(2)}) collective-permute-start(f32[8,64]{1,0:T(8,128)S(1)} %bitcast_add_fusion), channel_id=1, source_target_pairs={{0,8},{4,12},{8,0},{12,4},{1,9},{5,13},{9,1},{13,5},{2,10},{6,14},... | collective-permute-start | bytes 6152 | tf_op jit(solution)/shard_map/ppermute | solution.py:58
  43.8 1.8 %collective-permute-done.13 = f32[8,64]{1,0:T(8,128)S(1)} collective-permute-done((f32[8,64]{1,0:T(8,128)S(1)}, f32[8,64]{1,0:T(8,128)S(1)}, u32[]{:S(2)}, u32[]{:S(2)}) %collective-permute-start.13) | collective-permute-done | bytes 2080 | tf_op jit(solution)/shard_map/ppermute | solution.py:58
  45.6 0.9 %collective-permute-done.14 = f32[8,64]{1,0:T(8,128)S(1)} collective-permute-done((f32[8,64]{1,0:T(8,128)S(1)}, f32[8,64]{1,0:T(8,128)S(1)}, u32[]{:S(2)}, u32[]{:S(2)}) %collective-permute-start.14) | collective-permute-done | bytes 2080 | tf_op jit(solution)/shard_map/ppermute | solution.py:58
  46.5 0.7 %copy-done.3 = f32[64,8]{0,1:T(8,128)S(1)} copy-done((f32[64,8]{0,1:T(8,128)S(1)}, f32[64,8]{0,1:T(8,128)}, u32[]{:S(2)}) %copy-start.3) | copy-done | bytes 2072
  47.2 0.6 %fusion.34 = f32[4,64,8]{1,2,0:T(8,128)} fusion(f32[1,8,64]{2,1,0:T(8,128)S(1)} %get-tuple-element.18, f32[1,8,64]{2,1,0:T(8,128)S(1)} %get-tuple-element.19, f32[1,8,64]{2,1,0:T(8,128)S(1)} %fusion.40, f32[1,8,64]{2,1,0:T(8,128)S(1)} %get-tuple-element.17, f32[8,64]{1,0:T(8,128)S(1)} %select_add_fusion, f32[8,64]{1,0:T(8,128)S(1)} %bitcast.115), kind=kLoop, calls=%fused_computation.54 | loop fusion | flops 10240 | bytes 20480 | tf_op jit(solution)/shard_map/transpose | solution.py:60
  (39 shorter events, 1.8 us)
Async XLA Ops:
  0.0 32.2 %copy-start = (bf16[64,3072]{1,0:T(8,128)(2,1)S(1)}, bf16[64,3072]{1,0:T(8,128)(2,1)}, u32[]{:S(2)}) copy-start(bf16[64,3072]{1,0:T(8,128)(2,1)} %param.13) | copy-start | bytes 1179652
  0.0 6.8 %copy-start.1 = (bf16[4,2,24,8,128]{4,3,2,1,0:T(8,128)(2,1)S(1)}, bf16[4,2,24,8,128]{4,3,2,1,0:T(8,128)(2,1)}, u32[]{:S(2)}) copy-start(bf16[4,2,24,8,128]{4,3,2,1,0:T(8,128)(2,1)} %param.10) | copy-start | bytes 1179652
  1.1 11.7 %collective-permute-start = (bf16[48,8,128]{2,1,0:T(8,128)(2,1)S(1)}, bf16[48,8,128]{2,1,0:T(8,128)(2,1)S(1)}, u32[]{:S(2)}, u32[]{:S(2)}) collective-permute-start(bf16[48,8,128]{2,1,0:T(8,128)(2,1)S(1)} %get-tuple-element.16), channel_id=1, source_target_pairs={{0,1},{1,0},{2,3},{3,2},{4,5},{5,4},{6,7},{7,6},{8,9},{9,8},{10,11... | collective-permute-start | bytes 294920 | tf_op jit(solution)/shard_map/ppermute | solution.py:93
  4.2 10.7 %collective-permute-start.1 = (bf16[48,8,128]{2,1,0:T(8,128)(2,1)S(1)}, bf16[48,8,128]{2,1,0:T(8,128)(2,1)S(1)}, u32[]{:S(2)}, u32[]{:S(2)}) collective-permute-start(bf16[48,8,128]{2,1,0:T(8,128)(2,1)S(1)} %get-tuple-element.15), channel_id=1, source_target_pairs={{0,2},{1,3},{2,0},{3,1},{4,6},{5,7},{6,4},{7,5},{8,10},{9,11},{10,... | collective-permute-start | bytes 294920 | tf_op jit(solution)/shard_map/ppermute | solution.py:93
  6.8 8.8 %collective-permute-start.2 = (bf16[48,8,128]{2,1,0:T(8,128)(2,1)S(1)}, bf16[48,8,128]{2,1,0:T(8,128)(2,1)S(1)}, u32[]{:S(2)}, u32[]{:S(2)}) collective-permute-start(bf16[48,8,128]{2,1,0:T(8,128)(2,1)S(1)} %get-tuple-element.14), channel_id=1, source_target_pairs={{0,3},{1,2},{2,1},{3,0},{4,7},{5,6},{6,5},{7,4},{8,11},{9,10},{10,... | collective-permute-start | bytes 294920 | tf_op jit(solution)/shard_map/ppermute | solution.py:93
  6.8 4.5 %copy-start.4 = (f32[1000]{0:T(1024)S(1)}, f32[1000]{0:T(1024)}, u32[]{:S(2)}) copy-start(f32[1000]{0:T(1024)} %param.16) | copy-start | bytes 12004
  6.8 6.0 %copy-start.2 = (bf16[4,2,24,8,128]{4,3,2,1,0:T(8,128)(2,1)S(1)}, bf16[4,2,24,8,128]{4,3,2,1,0:T(8,128)(2,1)}, u32[]{:S(2)}) copy-start(bf16[4,2,24,8,128]{4,3,2,1,0:T(8,128)(2,1)} %param.11) | copy-start | bytes 1179652
  6.9 4.4 %copy-start.5 = (s32[4]{0:T(128)S(1)}, s32[4]{0:T(128)}, u32[]{:S(2)}) copy-start(s32[4]{0:T(128)} %param.17) | copy-start | bytes 52
  6.9 17.9 %collective-permute-start.3 = (bf16[48,8,128]{2,1,0:T(8,128)(2,1)S(1)}, bf16[48,8,128]{2,1,0:T(8,128)(2,1)S(1)}, u32[]{:S(2)}, u32[]{:S(2)}) collective-permute-start(bf16[48,8,128]{2,1,0:T(8,128)(2,1)S(1)} %get-tuple-element.12), channel_id=1, source_target_pairs={{0,1},{1,0},{2,3},{3,2},{4,5},{5,4},{6,7},{7,6},{8,9},{9,8},{10,11... | collective-permute-start | bytes 294920 | tf_op jit(solution)/shard_map/ppermute | solution.py:93
  7.8 17.4 %collective-permute-start.4 = (bf16[48,8,128]{2,1,0:T(8,128)(2,1)S(1)}, bf16[48,8,128]{2,1,0:T(8,128)(2,1)S(1)}, u32[]{:S(2)}, u32[]{:S(2)}) collective-permute-start(bf16[48,8,128]{2,1,0:T(8,128)(2,1)S(1)} %get-tuple-element.11), channel_id=1, source_target_pairs={{0,2},{1,3},{2,0},{3,1},{4,6},{5,7},{6,4},{7,5},{8,10},{9,11},{10,... | collective-permute-start | bytes 294920 | tf_op jit(solution)/shard_map/ppermute | solution.py:93
  12.9 0.7 %copy-start.6 = (f32[8]{0:T(128)S(1)}, f32[8]{0:T(128)}, u32[]{:S(2)}) copy-start(f32[8]{0:T(128)} %param.14) | copy-start | bytes 100
  12.9 12.4 %collective-permute-start.5 = (bf16[48,8,128]{2,1,0:T(8,128)(2,1)S(1)}, bf16[48,8,128]{2,1,0:T(8,128)(2,1)S(1)}, u32[]{:S(2)}, u32[]{:S(2)}) collective-permute-start(bf16[48,8,128]{2,1,0:T(8,128)(2,1)S(1)} %get-tuple-element.10), channel_id=1, source_target_pairs={{0,3},{1,2},{2,1},{3,0},{4,7},{5,6},{6,5},{7,4},{8,11},{9,10},{10,... | collective-permute-start | bytes 294920 | tf_op jit(solution)/shard_map/ppermute | solution.py:93
  14.9 10.9 %collective-permute-start.6 = (bf16[48,8,128]{2,1,0:T(8,128)(2,1)S(1)}, bf16[48,8,128]{2,1,0:T(8,128)(2,1)S(1)}, u32[]{:S(2)}, u32[]{:S(2)}) collective-permute-start(bf16[48,8,128]{2,1,0:T(8,128)(2,1)S(1)} %get-tuple-element.8), channel_id=1, source_target_pairs={{0,1},{1,0},{2,3},{3,2},{4,5},{5,4},{6,7},{7,6},{8,9},{9,8},{10,11... | collective-permute-start | bytes 294920 | tf_op jit(solution)/shard_map/ppermute | solution.py:93
  15.6 15.9 %collective-permute-start.7 = (bf16[48,8,128]{2,1,0:T(8,128)(2,1)S(1)}, bf16[48,8,128]{2,1,0:T(8,128)(2,1)S(1)}, u32[]{:S(2)}, u32[]{:S(2)}) collective-permute-start(bf16[48,8,128]{2,1,0:T(8,128)(2,1)S(1)} %get-tuple-element.7), channel_id=1, source_target_pairs={{0,2},{1,3},{2,0},{3,1},{4,6},{5,7},{6,4},{7,5},{8,10},{9,11},{10,... | collective-permute-start | bytes 294920 | tf_op jit(solution)/shard_map/ppermute | solution.py:93
  24.8 6.7 %collective-permute-start.8 = (bf16[48,8,128]{2,1,0:T(8,128)(2,1)S(1)}, bf16[48,8,128]{2,1,0:T(8,128)(2,1)S(1)}, u32[]{:S(2)}, u32[]{:S(2)}) collective-permute-start(bf16[48,8,128]{2,1,0:T(8,128)(2,1)S(1)} %get-tuple-element.6), channel_id=1, source_target_pairs={{0,3},{1,2},{2,1},{3,0},{4,7},{5,6},{6,5},{7,4},{8,11},{9,10},{10,... | collective-permute-start | bytes 294920 | tf_op jit(solution)/shard_map/ppermute | solution.py:93
  33.8 4.6 %collective-permute-start.10 = (f32[1,8,64]{2,1,0:T(8,128)S(1)}, f32[1,8,64]{2,1,0:T(8,128)S(1)}, u32[]{:S(2)}, u32[]{:S(2)}) collective-permute-start(f32[1,8,64]{2,1,0:T(8,128)S(1)} %get-tuple-element.22), channel_id=1, source_target_pairs={{0,2},{1,3},{2,0},{3,1},{4,6},{5,7},{6,4},{7,5},{8,10},{9,11},{10,... | collective-permute-start | bytes 6152 | tf_op jit(solution)/shard_map/ppermute | solution.py:42
  36.4 5.4 %collective-permute-start.11 = (f32[1,8,64]{2,1,0:T(8,128)S(1)}, f32[1,8,64]{2,1,0:T(8,128)S(1)}, u32[]{:S(2)}, u32[]{:S(2)}) collective-permute-start(f32[1,8,64]{2,1,0:T(8,128)S(1)} %get-tuple-element.21), channel_id=1, source_target_pairs={{0,3},{1,2},{2,1},{3,0},{4,7},{5,6},{6,5},{7,4},{8,11},{9,10},{10,... | collective-permute-start | bytes 6152 | tf_op jit(solution)/shard_map/ppermute | solution.py:42
  37.8 4.1 %collective-permute-start.9 = (f32[1,8,64]{2,1,0:T(8,128)S(1)}, f32[1,8,64]{2,1,0:T(8,128)S(1)}, u32[]{:S(2)}, u32[]{:S(2)}) collective-permute-start(f32[1,8,64]{2,1,0:T(8,128)S(1)} %get-tuple-element.20), channel_id=1, source_target_pairs={{0,1},{1,0},{2,3},{3,2},{4,5},{5,4},{6,7},{7,6},{8,9},{9,8},{10,11... | collective-permute-start | bytes 6152 | tf_op jit(solution)/shard_map/ppermute | solution.py:42
  41.9 2.0 %collective-permute-start.12 = (f32[8,64]{1,0:T(8,128)S(1)}, f32[8,64]{1,0:T(8,128)S(1)}, u32[]{:S(2)}, u32[]{:S(2)}) collective-permute-start(f32[8,64]{1,0:T(8,128)S(1)} %bitcast_add_fusion), channel_id=1, source_target_pairs={{0,4},{4,0},{8,12},{12,8},{1,5},{5,1},{9,13},{13,9},{2,6},{6,2},{1... | collective-permute-start | bytes 6152 | tf_op jit(solution)/shard_map/ppermute | solution.py:58
  41.9 3.7 %collective-permute-start.13 = (f32[8,64]{1,0:T(8,128)S(1)}, f32[8,64]{1,0:T(8,128)S(1)}, u32[]{:S(2)}, u32[]{:S(2)}) collective-permute-start(f32[8,64]{1,0:T(8,128)S(1)} %bitcast_add_fusion), channel_id=1, source_target_pairs={{0,8},{4,12},{8,0},{12,4},{1,9},{5,13},{9,1},{13,5},{2,10},{6,14},... | collective-permute-start | bytes 6152 | tf_op jit(solution)/shard_map/ppermute | solution.py:58
  43.5 3.0 %collective-permute-start.14 = (f32[8,64]{1,0:T(8,128)S(1)}, f32[8,64]{1,0:T(8,128)S(1)}, u32[]{:S(2)}, u32[]{:S(2)}) collective-permute-start(f32[8,64]{1,0:T(8,128)S(1)} %bitcast_add_fusion), channel_id=1, source_target_pairs={{0,12},{4,8},{8,4},{12,0},{1,13},{5,9},{9,5},{13,1},{2,14},{6,10},... | collective-permute-start | bytes 6152 | tf_op jit(solution)/shard_map/ppermute | solution.py:58
  46.5 0.7 %copy-start.3 = (f32[64,8]{0,1:T(8,128)S(1)}, f32[64,8]{0,1:T(8,128)}, u32[]{:S(2)}) copy-start(f32[64,8]{0,1:T(8,128)} %param.12) | copy-start | bytes 6148

commit v8 on v7

--- a/solution.py
+++ b/solution.py
@@ -117,9 +117,16 @@
             jnp.einsum("chd,sbhld->sblc", weight_heads, ho, preferred_element_type=jnp.float32)
             / root_mean[:, :, :, None]
         )
-        guided = drift[:, 1] + guide_scale * (drift[:, 0] - drift[:, 1])
         my_len = lax.dynamic_slice_in_dim(step_len, me * local_steps, local_steps)
-        update = my_len[:, None, None] * guided
+        shape = (local_steps, length, channels)
+        scale_full, len_full = lax.optimization_barrier(
+            (
+                jnp.broadcast_to(guide_scale, shape),
+                jnp.broadcast_to(my_len[:, None, None], shape),
+            )
+        )
+        guided = drift[:, 1] + scale_full * (drift[:, 0] - drift[:, 1])
+        update = len_full * guided
         update = update.reshape(local_steps, groups, tok_dev, channels)
         return gather_prefix(
             update, start_latent.T, me, groups, step_dev, steps_axis, partner_order

time: 48 us -> 46.8 us (0.975)
  local copies, waits for them, and re-layouts: 3.06 us -> 4.43 us
  other arithmetic: 2.98 us -> 1.69 us
  starting transfers between devices: 26.5 us -> 25.5 us
    broadcast_in_dim x0 -> x2, local copies, waits for them, and re-layouts: none -> 1.28 us  [the longest x1 0.65 us: on_device(): jnp.broadcast_to(my_len[:, None, None], shape)]
    mul x1 -> x0, other arithmetic: 1.26 us -> none  [on_device(): update = my_len[:, None, None] * guided]
    ppermute x9, starting transfers between devices: 20.5 us -> 19.5 us  [on_device(): pieces = [lax.ppermute(p, 'seq', xor_pairs(groups, k)) for p in pieces]]
  transfers between devices with their start and end apart: 15 -> 15, of which waited for: 7 -> 6; matrix products, arithmetic and copies ran while one was open for 4% -> 7% of each run, Pallas kernels for 0% -> 0%
where the time goes in v8:
time: 46.8 us; the launch traced here: 46.6 us
  starting transfers between devices  25.5 us (54%)
  waiting for transfers between devices  12.9 us (28%)
  local copies, waits for them, and re-layouts  4.43 us (9%)
  other arithmetic  1.69 us (4%)
  matrix products  1.25 us (3%)
  between operations  0.82 us (2%)
    ppermute x9, starting transfers between devices, on_device(): pieces = [lax.ppermute(p, 'seq', xor_pairs(groups, k)) for p in pieces]  19.5 us
    ppermute x9, waiting for transfers between devices, on_device(): pieces = [lax.ppermute(p, 'seq', xor_pairs(groups, k)) for p in pieces]  6.19 us
    ppermute x3, waiting for transfers between devices, gather_prefix(): pieces.append(lax.ppermute(ordered[:, k], 'seq', xor_pairs(groups, k)))  4.06 us
    ppermute x3, starting transfers between devices, gather_prefix(): pieces.append(lax.ppermute(ordered[:, k], 'seq', xor_pairs(groups, k)))  4.04 us
    ppermute x3, waiting for transfers between devices, gather_prefix(): other = lax.ppermute(total, 'step', xor_pairs(steps_axis, k))  2.68 us
    ppermute x3, starting transfers between devices, gather_prefix(): other = lax.ppermute(total, 'step', xor_pairs(steps_axis, k))  1.93 us
    unnamed x14, local copies, waits for them, and re-layouts  1.36 us
    squeeze x3, local copies, waits for them, and re-layouts, on_device(): lax.dynamic_index_in_dim(c, me ^ k, 0, keepdims=False)  1.2 us
  transfers between devices with their start and end apart: 15, of which 6 were waited for; matrix products, arithmetic and copies ran while one was open for 7% of the time, Pallas kernels for 0%

profile of v8, /device:TPU:0, one launch (start us, length us, event | category | flops | bytes accessed | tf_op | source)
XLA Modules:
  0.0 46.6 jit_solution(11251669630050756831)
XLA Ops:
  0.0 1.1 %dynamic-slice_bitcast_fusion.11 = (bf16[48,8,128]{2,1,0:T(8,128)(2,1)S(1)}, bf16[48,8,128]{2,1,0:T(8,128)(2,1)S(1)}, bf16[48,8,128]{2,1,0:T(8,128)(2,1)S(1)}, bf16[48,8,128]{2,1,0:T(8,128)(2,1)S(1)}) fusion(bf16[4,48,8,128]{3,2,1,0:T(8,128)(2,1)} %bitcast.115, s32[]{:T(128)S(6)} %select_n.214, s32[]{:T(128)S(6)} %select_n.217, s32[]{:T(128)S(6)} %select_n.216, ...), kind=kLoop, calls=%fused_computation.45 | loop fusion | bytes 786448 | tf_op jit(solution)/shard_map/jit(dynamic_index_in_dim)/squeeze | solution.py:91
  1.1 3.1 %collective-permute-start = (bf16[48,8,128]{2,1,0:T(8,128)(2,1)S(1)}, bf16[48,8,128]{2,1,0:T(8,128)(2,1)S(1)}, u32[]{:S(2)}, u32[]{:S(2)}) collective-permute-start(bf16[48,8,128]{2,1,0:T(8,128)(2,1)S(1)} %get-tuple-element.20), channel_id=1, source_target_pairs={{0,1},{1,0},{2,3},{3,2},{4,5},{5,4},{6,7},{7,6},{8,9},{9,8},{10,11... | collective-permute-start | bytes 294920 | tf_op jit(solution)/shard_map/ppermute | solution.py:93
  4.2 2.6 %collective-permute-start.1 = (bf16[48,8,128]{2,1,0:T(8,128)(2,1)S(1)}, bf16[48,8,128]{2,1,0:T(8,128)(2,1)S(1)}, u32[]{:S(2)}, u32[]{:S(2)}) collective-permute-start(bf16[48,8,128]{2,1,0:T(8,128)(2,1)S(1)} %get-tuple-element.19), channel_id=1, source_target_pairs={{0,2},{1,3},{2,0},{3,1},{4,6},{5,7},{6,4},{7,5},{8,10},{9,11},{10,... | collective-permute-start | bytes 294920 | tf_op jit(solution)/shard_map/ppermute | solution.py:93
  6.9 0.9 %collective-permute-start.3 = (bf16[48,8,128]{2,1,0:T(8,128)(2,1)S(1)}, bf16[48,8,128]{2,1,0:T(8,128)(2,1)S(1)}, u32[]{:S(2)}, u32[]{:S(2)}) collective-permute-start(bf16[48,8,128]{2,1,0:T(8,128)(2,1)S(1)} %get-tuple-element.16), channel_id=1, source_target_pairs={{0,1},{1,0},{2,3},{3,2},{4,5},{5,4},{6,7},{7,6},{8,9},{9,8},{10,11... | collective-permute-start | bytes 294920 | tf_op jit(solution)/shard_map/ppermute | solution.py:93
  7.8 3.5 %collective-permute-start.4 = (bf16[48,8,128]{2,1,0:T(8,128)(2,1)S(1)}, bf16[48,8,128]{2,1,0:T(8,128)(2,1)S(1)}, u32[]{:S(2)}, u32[]{:S(2)}) collective-permute-start(bf16[48,8,128]{2,1,0:T(8,128)(2,1)S(1)} %get-tuple-element.15), channel_id=1, source_target_pairs={{0,2},{1,3},{2,0},{3,1},{4,6},{5,7},{6,4},{7,5},{8,10},{9,11},{10,... | collective-permute-start | bytes 294920 | tf_op jit(solution)/shard_map/ppermute | solution.py:93
  11.5 0.6 %dynamic_slice.40 = f32[1]{0:T(128)} dynamic-slice(f32[4]{0:T(128)S(1)} %select_reduce_fusion, s32[]{:T(128)S(6)} %select_n.214), dynamic_slice_sizes={1} | dynamic-slice | bytes 12 | tf_op jit(solution)/shard_map/dynamic_slice | solution.py:120
  12.8 0.6 %copy-done.6 = f32[8]{0:T(128)S(1)} copy-done((f32[8]{0:T(128)S(1)}, f32[8]{0:T(128)}, u32[]{:S(2)}) %copy-start.6) | copy-done | bytes 56
  13.4 0.6 %fusion.44 = f32[]{:T(128)} fusion(f32[8]{0:T(128)S(1)} %copy-done.6, s32[]{:T(128)} %bitcast.114), kind=kLoop, calls=%fused_computation.79 | loop fusion | flops 23 | bytes 40 | tf_op jit(solution)/shard_map/reduce_sum | solution.py:13
  14.0 0.6 %broadcast_in_dim.65 = f32[1,32,64]{2,1,0:T(8,128)S(1)} broadcast(f32[]{:T(128)} %bitcast.1), dimensions={} | broadcast | bytes 8196 | tf_op jit(solution)/shard_map/broadcast_in_dim | solution.py:125
  14.7 0.6 %broadcast_in_dim.61 = f32[1,32,64]{2,1,0:T(8,128)S(1)} broadcast(f32[]{:T(128)} %fusion.44), dimensions={} | broadcast | bytes 8196 | tf_op jit(solution)/shard_map/broadcast_in_dim | solution.py:124
  15.5 0.6 %collective-permute-start.6 = (bf16[48,8,128]{2,1,0:T(8,128)(2,1)S(1)}, bf16[48,8,128]{2,1,0:T(8,128)(2,1)S(1)}, u32[]{:S(2)}, u32[]{:S(2)}) collective-permute-start(bf16[48,8,128]{2,1,0:T(8,128)(2,1)S(1)} %get-tuple-element.12), channel_id=1, source_target_pairs={{0,1},{1,0},{2,3},{3,2},{4,5},{5,4},{6,7},{7,6},{8,9},{9,8},{10,11... | collective-permute-start | bytes 294920 | tf_op jit(solution)/shard_map/ppermute | solution.py:93
  16.1 8.7 %collective-permute-start.7 = (bf16[48,8,128]{2,1,0:T(8,128)(2,1)S(1)}, bf16[48,8,128]{2,1,0:T(8,128)(2,1)S(1)}, u32[]{:S(2)}, u32[]{:S(2)}) collective-permute-start(bf16[48,8,128]{2,1,0:T(8,128)(2,1)S(1)} %get-tuple-element.11), channel_id=1, source_target_pairs={{0,2},{1,3},{2,0},{3,1},{4,6},{5,7},{6,4},{7,5},{8,10},{9,11},{10,... | collective-permute-start | bytes 294920 | tf_op jit(solution)/shard_map/ppermute | solution.py:93
  24.8 0.5 %collective-permute-done.4 = bf16[48,8,128]{2,1,0:T(8,128)(2,1)S(1)} collective-permute-done((bf16[48,8,128]{2,1,0:T(8,128)(2,1)S(1)}, bf16[48,8,128]{2,1,0:T(8,128)(2,1)S(1)}, u32[]{:S(2)}, u32[]{:S(2)}) %collective-permute-start.4) | collective-permute-done | bytes 98336 | tf_op jit(solution)/shard_map/ppermute | solution.py:93
  25.8 5.7 %collective-permute-done.7 = bf16[48,8,128]{2,1,0:T(8,128)(2,1)S(1)} collective-permute-done((bf16[48,8,128]{2,1,0:T(8,128)(2,1)S(1)}, bf16[48,8,128]{2,1,0:T(8,128)(2,1)S(1)}, u32[]{:S(2)}, u32[]{:S(2)}) %collective-permute-start.7) | collective-permute-done | bytes 98336 | tf_op jit(solution)/shard_map/ppermute | solution.py:93
  31.5 0.6 %multiply_reduce_fusion = (f32[48,32]{1,0:T(8,128)S(1)}, bf16[48,32,128]{2,1,0:T(8,128)(2,1)S(1)}) fusion(f32[48,32]{1,0:T(8,128)S(1)} %fusion.3, bf16[48,8,128]{2,1,0:T(8,128)(2,1)S(1)} %collective-permute-done.8, bf16[48,8,128]{2,1,0:T(8,128)(2,1)S(1)} %collective-permute-done.7, bf16[48,8,128]{2,1,0:T(8,128)(2,1)S(1)} %collective-permute-done.6, ...), kind=kOutput, calls=%fused_computation.6 | convolution fusion | flops 15235584 | bytes 1001472 | tf_op jit(solution)/shard_map/iqk,ikd->iqd/dot_general | solution.py:24
  32.5 2.7 %collective-permute-start.10 = (f32[1,8,64]{2,1,0:T(8,128)S(1)}, f32[1,8,64]{2,1,0:T(8,128)S(1)}, u32[]{:S(2)}, u32[]{:S(2)}) collective-permute-start(f32[1,8,64]{2,1,0:T(8,128)S(1)} %get-tuple-element.26), channel_id=1, source_target_pairs={{0,2},{1,3},{2,0},{3,1},{4,6},{5,7},{6,4},{7,5},{8,10},{9,11},{10,... | collective-permute-start | bytes 6152 | tf_op jit(solution)/shard_map/ppermute | solution.py:42
  35.2 1.3 %collective-permute-start.11 = (f32[1,8,64]{2,1,0:T(8,128)S(1)}, f32[1,8,64]{2,1,0:T(8,128)S(1)}, u32[]{:S(2)}, u32[]{:S(2)}) collective-permute-start(f32[1,8,64]{2,1,0:T(8,128)S(1)} %get-tuple-element.25), channel_id=1, source_target_pairs={{0,3},{1,2},{2,1},{3,0},{4,7},{5,6},{6,5},{7,4},{8,11},{9,10},{10,... | collective-permute-start | bytes 6152 | tf_op jit(solution)/shard_map/ppermute | solution.py:42
  36.5 0.5 %collective-permute-done.10 = f32[1,8,64]{2,1,0:T(8,128)S(1)} collective-permute-done((f32[1,8,64]{2,1,0:T(8,128)S(1)}, f32[1,8,64]{2,1,0:T(8,128)S(1)}, u32[]{:S(2)}, u32[]{:S(2)}) %collective-permute-start.10) | collective-permute-done | bytes 2080 | tf_op jit(solution)/shard_map/ppermute | solution.py:42
  37.1 3.5 %collective-permute-done.11 = f32[1,8,64]{2,1,0:T(8,128)S(1)} collective-permute-done((f32[1,8,64]{2,1,0:T(8,128)S(1)}, f32[1,8,64]{2,1,0:T(8,128)S(1)}, u32[]{:S(2)}, u32[]{:S(2)}) %collective-permute-start.11) | collective-permute-done | bytes 2080 | tf_op jit(solution)/shard_map/ppermute | solution.py:42
  40.7 1.6 %collective-permute-start.13 = (f32[8,64]{1,0:T(8,128)S(1)}, f32[8,64]{1,0:T(8,128)S(1)}, u32[]{:S(2)}, u32[]{:S(2)}) collective-permute-start(f32[8,64]{1,0:T(8,128)S(1)} %bitcast_add_fusion), channel_id=1, source_target_pairs={{0,8},{4,12},{8,0},{12,4},{1,9},{5,13},{9,1},{13,5},{2,10},{6,14},... | collective-permute-start | bytes 6152 | tf_op jit(solution)/shard_map/ppermute | solution.py:58
  42.6 1.8 %collective-permute-done.13 = f32[8,64]{1,0:T(8,128)S(1)} collective-permute-done((f32[8,64]{1,0:T(8,128)S(1)}, f32[8,64]{1,0:T(8,128)S(1)}, u32[]{:S(2)}, u32[]{:S(2)}) %collective-permute-start.13) | collective-permute-done | bytes 2080 | tf_op jit(solution)/shard_map/ppermute | solution.py:58
  44.4 0.9 %collective-permute-done.14 = f32[8,64]{1,0:T(8,128)S(1)} collective-permute-done((f32[8,64]{1,0:T(8,128)S(1)}, f32[8,64]{1,0:T(8,128)S(1)}, u32[]{:S(2)}, u32[]{:S(2)}) %collective-permute-start.14) | collective-permute-done | bytes 2080 | tf_op jit(solution)/shard_map/ppermute | solution.py:58
  45.3 0.7 %copy-done.3 = f32[64,8]{0,1:T(8,128)S(1)} copy-done((f32[64,8]{0,1:T(8,128)S(1)}, f32[64,8]{0,1:T(8,128)}, u32[]{:S(2)}) %copy-start.3) | copy-done | bytes 2072
  46.0 0.6 %fusion.35 = f32[4,64,8]{1,2,0:T(8,128)} fusion(f32[1,8,64]{2,1,0:T(8,128)S(1)} %get-tuple-element.22, f32[1,8,64]{2,1,0:T(8,128)S(1)} %get-tuple-element.23, f32[1,8,64]{2,1,0:T(8,128)S(1)} %fusion.41, f32[1,8,64]{2,1,0:T(8,128)S(1)} %get-tuple-element.21, f32[8,64]{1,0:T(8,128)S(1)} %select_add_fusion, f32[8,64]{1,0:T(8,128)S(1)} %bitcast.119), kind=kLoop, calls=%fused_computation.55 | loop fusion | flops 10240 | bytes 20480 | tf_op jit(solution)/shard_map/transpose | solution.py:60
  (41 shorter events, 1.7 us)
Async XLA Ops:
  0.0 32.2 %copy-start = (bf16[64,3072]{1,0:T(8,128)(2,1)S(1)}, bf16[64,3072]{1,0:T(8,128)(2,1)}, u32[]{:S(2)}) copy-start(bf16[64,3072]{1,0:T(8,128)(2,1)} %param.13) | copy-start | bytes 1179652
  0.0 6.8 %copy-start.1 = (bf16[4,2,24,8,128]{4,3,2,1,0:T(8,128)(2,1)S(1)}, bf16[4,2,24,8,128]{4,3,2,1,0:T(8,128)(2,1)}, u32[]{:S(2)}) copy-start(bf16[4,2,24,8,128]{4,3,2,1,0:T(8,128)(2,1)} %param.10) | copy-start | bytes 1179652
  1.1 14.2 %collective-permute-start = (bf16[48,8,128]{2,1,0:T(8,128)(2,1)S(1)}, bf16[48,8,128]{2,1,0:T(8,128)(2,1)S(1)}, u32[]{:S(2)}, u32[]{:S(2)}) collective-permute-start(bf16[48,8,128]{2,1,0:T(8,128)(2,1)S(1)} %get-tuple-element.20), channel_id=1, source_target_pairs={{0,1},{1,0},{2,3},{3,2},{4,5},{5,4},{6,7},{7,6},{8,9},{9,8},{10,11... | collective-permute-start | bytes 294920 | tf_op jit(solution)/shard_map/ppermute | solution.py:93
  4.2 11.3 %collective-permute-start.1 = (bf16[48,8,128]{2,1,0:T(8,128)(2,1)S(1)}, bf16[48,8,128]{2,1,0:T(8,128)(2,1)S(1)}, u32[]{:S(2)}, u32[]{:S(2)}) collective-permute-start(bf16[48,8,128]{2,1,0:T(8,128)(2,1)S(1)} %get-tuple-element.19), channel_id=1, source_target_pairs={{0,2},{1,3},{2,0},{3,1},{4,6},{5,7},{6,4},{7,5},{8,10},{9,11},{10,... | collective-permute-start | bytes 294920 | tf_op jit(solution)/shard_map/ppermute | solution.py:93
  6.8 9.3 %collective-permute-start.2 = (bf16[48,8,128]{2,1,0:T(8,128)(2,1)S(1)}, bf16[48,8,128]{2,1,0:T(8,128)(2,1)S(1)}, u32[]{:S(2)}, u32[]{:S(2)}) collective-permute-start(bf16[48,8,128]{2,1,0:T(8,128)(2,1)S(1)} %get-tuple-element.18), channel_id=1, source_target_pairs={{0,3},{1,2},{2,1},{3,0},{4,7},{5,6},{6,5},{7,4},{8,11},{9,10},{10,... | collective-permute-start | bytes 294920 | tf_op jit(solution)/shard_map/ppermute | solution.py:93
  6.8 4.5 %copy-start.4 = (f32[1000]{0:T(1024)S(1)}, f32[1000]{0:T(1024)}, u32[]{:S(2)}) copy-start(f32[1000]{0:T(1024)} %param.16) | copy-start | bytes 12004
  6.8 8.6 %copy-start.2 = (bf16[4,2,24,8,128]{4,3,2,1,0:T(8,128)(2,1)S(1)}, bf16[4,2,24,8,128]{4,3,2,1,0:T(8,128)(2,1)}, u32[]{:S(2)}) copy-start(bf16[4,2,24,8,128]{4,3,2,1,0:T(8,128)(2,1)} %param.11) | copy-start | bytes 1179652
  6.9 4.4 %copy-start.5 = (s32[4]{0:T(128)S(1)}, s32[4]{0:T(128)}, u32[]{:S(2)}) copy-start(s32[4]{0:T(128)} %param.17) | copy-start | bytes 52
  6.9 17.9 %collective-permute-start.3 = (bf16[48,8,128]{2,1,0:T(8,128)(2,1)S(1)}, bf16[48,8,128]{2,1,0:T(8,128)(2,1)S(1)}, u32[]{:S(2)}, u32[]{:S(2)}) collective-permute-start(bf16[48,8,128]{2,1,0:T(8,128)(2,1)S(1)} %get-tuple-element.16), channel_id=1, source_target_pairs={{0,1},{1,0},{2,3},{3,2},{4,5},{5,4},{6,7},{7,6},{8,9},{9,8},{10,11... | collective-permute-start | bytes 294920 | tf_op jit(solution)/shard_map/ppermute | solution.py:93
  7.8 17.4 %collective-permute-start.4 = (bf16[48,8,128]{2,1,0:T(8,128)(2,1)S(1)}, bf16[48,8,128]{2,1,0:T(8,128)(2,1)S(1)}, u32[]{:S(2)}, u32[]{:S(2)}) collective-permute-start(bf16[48,8,128]{2,1,0:T(8,128)(2,1)S(1)} %get-tuple-element.15), channel_id=1, source_target_pairs={{0,2},{1,3},{2,0},{3,1},{4,6},{5,7},{6,4},{7,5},{8,10},{9,11},{10,... | collective-permute-start | bytes 294920 | tf_op jit(solution)/shard_map/ppermute | solution.py:93
  12.8 0.7 %copy-start.6 = (f32[8]{0:T(128)S(1)}, f32[8]{0:T(128)}, u32[]{:S(2)}) copy-start(f32[8]{0:T(128)} %param.14) | copy-start | bytes 100
  15.3 9.9 %collective-permute-start.5 = (bf16[48,8,128]{2,1,0:T(8,128)(2,1)S(1)}, bf16[48,8,128]{2,1,0:T(8,128)(2,1)S(1)}, u32[]{:S(2)}, u32[]{:S(2)}) collective-permute-start(bf16[48,8,128]{2,1,0:T(8,128)(2,1)S(1)} %get-tuple-element.14), channel_id=1, source_target_pairs={{0,3},{1,2},{2,1},{3,0},{4,7},{5,6},{6,5},{7,4},{8,11},{9,10},{10,... | collective-permute-start | bytes 294920 | tf_op jit(solution)/shard_map/ppermute | solution.py:93
  15.5 10.3 %collective-permute-start.6 = (bf16[48,8,128]{2,1,0:T(8,128)(2,1)S(1)}, bf16[48,8,128]{2,1,0:T(8,128)(2,1)S(1)}, u32[]{:S(2)}, u32[]{:S(2)}) collective-permute-start(bf16[48,8,128]{2,1,0:T(8,128)(2,1)S(1)} %get-tuple-element.12), channel_id=1, source_target_pairs={{0,1},{1,0},{2,3},{3,2},{4,5},{5,4},{6,7},{7,6},{8,9},{9,8},{10,11... | collective-permute-start | bytes 294920 | tf_op jit(solution)/shard_map/ppermute | solution.py:93
  16.1 15.4 %collective-permute-start.7 = (bf16[48,8,128]{2,1,0:T(8,128)(2,1)S(1)}, bf16[48,8,128]{2,1,0:T(8,128)(2,1)S(1)}, u32[]{:S(2)}, u32[]{:S(2)}) collective-permute-start(bf16[48,8,128]{2,1,0:T(8,128)(2,1)S(1)} %get-tuple-element.11), channel_id=1, source_target_pairs={{0,2},{1,3},{2,0},{3,1},{4,6},{5,7},{6,4},{7,5},{8,10},{9,11},{10,... | collective-permute-start | bytes 294920 | tf_op jit(solution)/shard_map/ppermute | solution.py:93
  24.8 6.7 %collective-permute-start.8 = (bf16[48,8,128]{2,1,0:T(8,128)(2,1)S(1)}, bf16[48,8,128]{2,1,0:T(8,128)(2,1)S(1)}, u32[]{:S(2)}, u32[]{:S(2)}) collective-permute-start(bf16[48,8,128]{2,1,0:T(8,128)(2,1)S(1)} %get-tuple-element.10), channel_id=1, source_target_pairs={{0,3},{1,2},{2,1},{3,0},{4,7},{5,6},{6,5},{7,4},{8,11},{9,10},{10,... | collective-permute-start | bytes 294920 | tf_op jit(solution)/shard_map/ppermute | solution.py:93
  32.5 4.6 %collective-permute-start.10 = (f32[1,8,64]{2,1,0:T(8,128)S(1)}, f32[1,8,64]{2,1,0:T(8,128)S(1)}, u32[]{:S(2)}, u32[]{:S(2)}) collective-permute-start(f32[1,8,64]{2,1,0:T(8,128)S(1)} %get-tuple-element.26), channel_id=1, source_target_pairs={{0,2},{1,3},{2,0},{3,1},{4,6},{5,7},{6,4},{7,5},{8,10},{9,11},{10,... | collective-permute-start | bytes 6152 | tf_op jit(solution)/shard_map/ppermute | solution.py:42
  35.2 5.4 %collective-permute-start.11 = (f32[1,8,64]{2,1,0:T(8,128)S(1)}, f32[1,8,64]{2,1,0:T(8,128)S(1)}, u32[]{:S(2)}, u32[]{:S(2)}) collective-permute-start(f32[1,8,64]{2,1,0:T(8,128)S(1)} %get-tuple-element.25), channel_id=1, source_target_pairs={{0,3},{1,2},{2,1},{3,0},{4,7},{5,6},{6,5},{7,4},{8,11},{9,10},{10,... | collective-permute-start | bytes 6152 | tf_op jit(solution)/shard_map/ppermute | solution.py:42
  36.5 4.1 %collective-permute-start.9 = (f32[1,8,64]{2,1,0:T(8,128)S(1)}, f32[1,8,64]{2,1,0:T(8,128)S(1)}, u32[]{:S(2)}, u32[]{:S(2)}) collective-permute-start(f32[1,8,64]{2,1,0:T(8,128)S(1)} %get-tuple-element.24), channel_id=1, source_target_pairs={{0,1},{1,0},{2,3},{3,2},{4,5},{5,4},{6,7},{7,6},{8,9},{9,8},{10,11... | collective-permute-start | bytes 6152 | tf_op jit(solution)/shard_map/ppermute | solution.py:42
  40.6 2.0 %collective-permute-start.12 = (f32[8,64]{1,0:T(8,128)S(1)}, f32[8,64]{1,0:T(8,128)S(1)}, u32[]{:S(2)}, u32[]{:S(2)}) collective-permute-start(f32[8,64]{1,0:T(8,128)S(1)} %bitcast_add_fusion), channel_id=1, source_target_pairs={{0,4},{4,0},{8,12},{12,8},{1,5},{5,1},{9,13},{13,9},{2,6},{6,2},{1... | collective-permute-start | bytes 6152 | tf_op jit(solution)/shard_map/ppermute | solution.py:58
  40.7 3.7 %collective-permute-start.13 = (f32[8,64]{1,0:T(8,128)S(1)}, f32[8,64]{1,0:T(8,128)S(1)}, u32[]{:S(2)}, u32[]{:S(2)}) collective-permute-start(f32[8,64]{1,0:T(8,128)S(1)} %bitcast_add_fusion), channel_id=1, source_target_pairs={{0,8},{4,12},{8,0},{12,4},{1,9},{5,13},{9,1},{13,5},{2,10},{6,14},... | collective-permute-start | bytes 6152 | tf_op jit(solution)/shard_map/ppermute | solution.py:58
  42.2 3.0 %collective-permute-start.14 = (f32[8,64]{1,0:T(8,128)S(1)}, f32[8,64]{1,0:T(8,128)S(1)}, u32[]{:S(2)}, u32[]{:S(2)}) collective-permute-start(f32[8,64]{1,0:T(8,128)S(1)} %bitcast_add_fusion), channel_id=1, source_target_pairs={{0,12},{4,8},{8,4},{12,0},{1,13},{5,9},{9,5},{13,1},{2,14},{6,10},... | collective-permute-start | bytes 6152 | tf_op jit(solution)/shard_map/ppermute | solution.py:58
  45.3 0.7 %copy-start.3 = (f32[64,8]{0,1:T(8,128)S(1)}, f32[64,8]{0,1:T(8,128)}, u32[]{:S(2)}) copy-start(f32[64,8]{0,1:T(8,128)} %param.12) | copy-start | bytes 6148

commit v9 on v8

--- a/solution.py
+++ b/solution.py
@@ -51,7 +51,7 @@
                 acc = term if acc is None else acc + term
         outs.append(acc)
     total = outs[-1]
-    local_cum = jnp.stack(outs) + start[None]
+    local_cum = lax.optimization_barrier(jnp.stack(outs) + start[None])
     position = lax.axis_index("step")
     earlier = jnp.zeros_like(total)
     for k in range(1, steps_axis):
@@ -119,17 +119,18 @@
         )
         my_len = lax.dynamic_slice_in_dim(step_len, me * local_steps, local_steps)
         shape = (local_steps, length, channels)
-        scale_full, len_full = lax.optimization_barrier(
+        scale_full, len_full, start_t = lax.optimization_barrier(
             (
                 jnp.broadcast_to(guide_scale, shape),
                 jnp.broadcast_to(my_len[:, None, None], shape),
+                start_latent.T,
             )
         )
         guided = drift[:, 1] + scale_full * (drift[:, 0] - drift[:, 1])
         update = len_full * guided
         update = update.reshape(local_steps, groups, tok_dev, channels)
         return gather_prefix(
-            update, start_latent.T, me, groups, step_dev, steps_axis, partner_order
+            update, start_t, me, groups, step_dev, steps_axis, partner_order
         )
 
     assert heads % per_dev == 0

time: 46.8 us -> 46.1 us (0.985)
  waiting for transfers between devices: 12.9 us -> 12.3 us
    ppermute x3, waiting for transfers between devices: 2.68 us -> 2 us  [gather_prefix(): other = lax.ppermute(total, 'step', xor_pairs(steps_axis, k))]
where the time goes in v9:
time: 46.1 us; the launch traced here: 45.9 us
  starting transfers between devices  25.5 us (55%)
  waiting for transfers between devices  12.3 us (27%)
  local copies, waits for them, and re-layouts  4.43 us (10%)
  other arithmetic  1.69 us (4%)
  matrix products  1.25 us (3%)
  between operations  0.82 us (2%)
    ppermute x9, starting transfers between devices, on_device(): pieces = [lax.ppermute(p, 'seq', xor_pairs(groups, k)) for p in pieces]  19.5 us
    ppermute x9, waiting for transfers between devices, on_device(): pieces = [lax.ppermute(p, 'seq', xor_pairs(groups, k)) for p in pieces]  6.19 us
    ppermute x3, waiting for transfers between devices, gather_prefix(): pieces.append(lax.ppermute(ordered[:, k], 'seq', xor_pairs(groups, k)))  4.06 us
    ppermute x3, starting transfers between devices, gather_prefix(): pieces.append(lax.ppermute(ordered[:, k], 'seq', xor_pairs(groups, k)))  4.04 us
    ppermute x3, waiting for transfers between devices, gather_prefix(): other = lax.ppermute(total, 'step', xor_pairs(steps_axis, k))  2 us
    ppermute x3, starting transfers between devices, gather_prefix(): other = lax.ppermute(total, 'step', xor_pairs(steps_axis, k))  1.93 us
    unnamed x14, local copies, waits for them, and re-layouts  1.35 us
    squeeze x3, local copies, waits for them, and re-layouts, on_device(): lax.dynamic_index_in_dim(c, me ^ k, 0, keepdims=False)  1.2 us
  transfers between devices with their start and end apart: 15, of which 6 were waited for; matrix products, arithmetic and copies ran while one was open for 7% of the time, Pallas kernels for 0%

profile of v9, /device:TPU:0, one launch (start us, length us, event | category | flops | bytes accessed | tf_op | source)
XLA Modules:
  0.0 45.9 jit_solution(7604623663095909563)
XLA Ops:
  0.0 1.1 %dynamic-slice_bitcast_fusion.11 = (bf16[48,8,128]{2,1,0:T(8,128)(2,1)S(1)}, bf16[48,8,128]{2,1,0:T(8,128)(2,1)S(1)}, bf16[48,8,128]{2,1,0:T(8,128)(2,1)S(1)}, bf16[48,8,128]{2,1,0:T(8,128)(2,1)S(1)}) fusion(bf16[4,48,8,128]{3,2,1,0:T(8,128)(2,1)} %bitcast.115, s32[]{:T(128)S(6)} %select_n.214, s32[]{:T(128)S(6)} %select_n.217, s32[]{:T(128)S(6)} %select_n.216, ...), kind=kLoop, calls=%fused_computation.45 | loop fusion | bytes 786448 | tf_op jit(solution)/shard_map/jit(dynamic_index_in_dim)/squeeze | solution.py:91
  1.1 3.1 %collective-permute-start = (bf16[48,8,128]{2,1,0:T(8,128)(2,1)S(1)}, bf16[48,8,128]{2,1,0:T(8,128)(2,1)S(1)}, u32[]{:S(2)}, u32[]{:S(2)}) collective-permute-start(bf16[48,8,128]{2,1,0:T(8,128)(2,1)S(1)} %get-tuple-element.22), channel_id=1, source_target_pairs={{0,1},{1,0},{2,3},{3,2},{4,5},{5,4},{6,7},{7,6},{8,9},{9,8},{10,11... | collective-permute-start | bytes 294920 | tf_op jit(solution)/shard_map/ppermute | solution.py:93
  4.2 2.6 %collective-permute-start.1 = (bf16[48,8,128]{2,1,0:T(8,128)(2,1)S(1)}, bf16[48,8,128]{2,1,0:T(8,128)(2,1)S(1)}, u32[]{:S(2)}, u32[]{:S(2)}) collective-permute-start(bf16[48,8,128]{2,1,0:T(8,128)(2,1)S(1)} %get-tuple-element.21), channel_id=1, source_target_pairs={{0,2},{1,3},{2,0},{3,1},{4,6},{5,7},{6,4},{7,5},{8,10},{9,11},{10,... | collective-permute-start | bytes 294920 | tf_op jit(solution)/shard_map/ppermute | solution.py:93
  6.9 0.9 %collective-permute-start.3 = (bf16[48,8,128]{2,1,0:T(8,128)(2,1)S(1)}, bf16[48,8,128]{2,1,0:T(8,128)(2,1)S(1)}, u32[]{:S(2)}, u32[]{:S(2)}) collective-permute-start(bf16[48,8,128]{2,1,0:T(8,128)(2,1)S(1)} %get-tuple-element.18), channel_id=1, source_target_pairs={{0,1},{1,0},{2,3},{3,2},{4,5},{5,4},{6,7},{7,6},{8,9},{9,8},{10,11... | collective-permute-start | bytes 294920 | tf_op jit(solution)/shard_map/ppermute | solution.py:93
  7.8 3.5 %collective-permute-start.4 = (bf16[48,8,128]{2,1,0:T(8,128)(2,1)S(1)}, bf16[48,8,128]{2,1,0:T(8,128)(2,1)S(1)}, u32[]{:S(2)}, u32[]{:S(2)}) collective-permute-start(bf16[48,8,128]{2,1,0:T(8,128)(2,1)S(1)} %get-tuple-element.17), channel_id=1, source_target_pairs={{0,2},{1,3},{2,0},{3,1},{4,6},{5,7},{6,4},{7,5},{8,10},{9,11},{10,... | collective-permute-start | bytes 294920 | tf_op jit(solution)/shard_map/ppermute | solution.py:93
  11.5 0.6 %dynamic_slice.40 = f32[1]{0:T(128)} dynamic-slice(f32[4]{0:T(128)S(1)} %select_reduce_fusion, s32[]{:T(128)S(6)} %select_n.214), dynamic_slice_sizes={1} | dynamic-slice | bytes 12 | tf_op jit(solution)/shard_map/dynamic_slice | solution.py:120
  12.8 0.6 %copy-done.6 = f32[8]{0:T(128)S(1)} copy-done((f32[8]{0:T(128)S(1)}, f32[8]{0:T(128)}, u32[]{:S(2)}) %copy-start.6) | copy-done | bytes 56
  13.4 0.6 %fusion.42 = f32[]{:T(128)} fusion(f32[8]{0:T(128)S(1)} %copy-done.6, s32[]{:T(128)} %bitcast.114), kind=kLoop, calls=%fused_computation.78 | loop fusion | flops 23 | bytes 40 | tf_op jit(solution)/shard_map/reduce_sum | solution.py:13
  14.0 0.6 %broadcast_in_dim.65 = f32[1,32,64]{2,1,0:T(8,128)S(1)} broadcast(f32[]{:T(128)} %bitcast.1), dimensions={} | broadcast | bytes 8196 | tf_op jit(solution)/shard_map/broadcast_in_dim | solution.py:125
  14.7 0.6 %broadcast_in_dim.61 = f32[1,32,64]{2,1,0:T(8,128)S(1)} broadcast(f32[]{:T(128)} %fusion.42), dimensions={} | broadcast | bytes 8196 | tf_op jit(solution)/shard_map/broadcast_in_dim | solution.py:124
  15.5 0.6 %collective-permute-start.6 = (bf16[48,8,128]{2,1,0:T(8,128)(2,1)S(1)}, bf16[48,8,128]{2,1,0:T(8,128)(2,1)S(1)}, u32[]{:S(2)}, u32[]{:S(2)}) collective-permute-start(bf16[48,8,128]{2,1,0:T(8,128)(2,1)S(1)} %get-tuple-element.14), channel_id=1, source_target_pairs={{0,1},{1,0},{2,3},{3,2},{4,5},{5,4},{6,7},{7,6},{8,9},{9,8},{10,11... | collective-permute-start | bytes 294920 | tf_op jit(solution)/shard_map/ppermute | solution.py:93
  16.1 8.7 %collective-permute-start.7 = (bf16[48,8,128]{2,1,0:T(8,128)(2,1)S(1)}, bf16[48,8,128]{2,1,0:T(8,128)(2,1)S(1)}, u32[]{:S(2)}, u32[]{:S(2)}) collective-permute-start(bf16[48,8,128]{2,1,0:T(8,128)(2,1)S(1)} %get-tuple-element.13), channel_id=1, source_target_pairs={{0,2},{1,3},{2,0},{3,1},{4,6},{5,7},{6,4},{7,5},{8,10},{9,11},{10,... | collective-permute-start | bytes 294920 | tf_op jit(solution)/shard_map/ppermute | solution.py:93
  24.8 0.5 %collective-permute-done.4 = bf16[48,8,128]{2,1,0:T(8,128)(2,1)S(1)} collective-permute-done((bf16[48,8,128]{2,1,0:T(8,128)(2,1)S(1)}, bf16[48,8,128]{2,1,0:T(8,128)(2,1)S(1)}, u32[]{:S(2)}, u32[]{:S(2)}) %collective-permute-start.4) | collective-permute-done | bytes 98336 | tf_op jit(solution)/shard_map/ppermute | solution.py:93
  25.8 5.7 %collective-permute-done.7 = bf16[48,8,128]{2,1,0:T(8,128)(2,1)S(1)} collective-permute-done((bf16[48,8,128]{2,1,0:T(8,128)(2,1)S(1)}, bf16[48,8,128]{2,1,0:T(8,128)(2,1)S(1)}, u32[]{:S(2)}, u32[]{:S(2)}) %collective-permute-start.7) | collective-permute-done | bytes 98336 | tf_op jit(solution)/shard_map/ppermute | solution.py:93
  31.5 0.6 %multiply_reduce_fusion = (f32[48,32]{1,0:T(8,128)S(1)}, bf16[48,32,128]{2,1,0:T(8,128)(2,1)S(1)}) fusion(f32[48,32]{1,0:T(8,128)S(1)} %fusion.3, bf16[48,8,128]{2,1,0:T(8,128)(2,1)S(1)} %collective-permute-done.8, bf16[48,8,128]{2,1,0:T(8,128)(2,1)S(1)} %collective-permute-done.7, bf16[48,8,128]{2,1,0:T(8,128)(2,1)S(1)} %collective-permute-done.6, ...), kind=kOutput, calls=%fused_computation.6 | convolution fusion | flops 15235584 | bytes 1001472 | tf_op jit(solution)/shard_map/iqk,ikd->iqd/dot_general | solution.py:24
  32.5 2.7 %collective-permute-start.10 = (f32[1,8,64]{2,1,0:T(8,128)S(1)}, f32[1,8,64]{2,1,0:T(8,128)S(1)}, u32[]{:S(2)}, u32[]{:S(2)}) collective-permute-start(f32[1,8,64]{2,1,0:T(8,128)S(1)} %get-tuple-element.28), channel_id=1, source_target_pairs={{0,2},{1,3},{2,0},{3,1},{4,6},{5,7},{6,4},{7,5},{8,10},{9,11},{10,... | collective-permute-start | bytes 6152 | tf_op jit(solution)/shard_map/ppermute | solution.py:42
  35.2 1.3 %collective-permute-start.11 = (f32[1,8,64]{2,1,0:T(8,128)S(1)}, f32[1,8,64]{2,1,0:T(8,128)S(1)}, u32[]{:S(2)}, u32[]{:S(2)}) collective-permute-start(f32[1,8,64]{2,1,0:T(8,128)S(1)} %get-tuple-element.27), channel_id=1, source_target_pairs={{0,3},{1,2},{2,1},{3,0},{4,7},{5,6},{6,5},{7,4},{8,11},{9,10},{10,... | collective-permute-start | bytes 6152 | tf_op jit(solution)/shard_map/ppermute | solution.py:42
  36.5 0.5 %collective-permute-done.10 = f32[1,8,64]{2,1,0:T(8,128)S(1)} collective-permute-done((f32[1,8,64]{2,1,0:T(8,128)S(1)}, f32[1,8,64]{2,1,0:T(8,128)S(1)}, u32[]{:S(2)}, u32[]{:S(2)}) %collective-permute-start.10) | collective-permute-done | bytes 2080 | tf_op jit(solution)/shard_map/ppermute | solution.py:42
  37.1 3.5 %collective-permute-done.11 = f32[1,8,64]{2,1,0:T(8,128)S(1)} collective-permute-done((f32[1,8,64]{2,1,0:T(8,128)S(1)}, f32[1,8,64]{2,1,0:T(8,128)S(1)}, u32[]{:S(2)}, u32[]{:S(2)}) %collective-permute-start.11) | collective-permute-done | bytes 2080 | tf_op jit(solution)/shard_map/ppermute | solution.py:42
  40.7 1.6 %collective-permute-start.13 = (f32[8,64]{1,0:T(8,128)S(1)}, f32[8,64]{1,0:T(8,128)S(1)}, u32[]{:S(2)}, u32[]{:S(2)}) collective-permute-start(f32[8,64]{1,0:T(8,128)S(1)} %bitcast_add_fusion), channel_id=1, source_target_pairs={{0,8},{4,12},{8,0},{12,4},{1,9},{5,13},{9,1},{13,5},{2,10},{6,14},... | collective-permute-start | bytes 6152 | tf_op jit(solution)/shard_map/ppermute | solution.py:58
  42.6 0.7 %copy-done.3 = f32[64,8]{0,1:T(8,128)S(1)} copy-done((f32[64,8]{0,1:T(8,128)S(1)}, f32[64,8]{0,1:T(8,128)}, u32[]{:S(2)}) %copy-start.3) | copy-done | bytes 2072
  43.3 1.1 %collective-permute-done.13 = f32[8,64]{1,0:T(8,128)S(1)} collective-permute-done((f32[8,64]{1,0:T(8,128)S(1)}, f32[8,64]{1,0:T(8,128)S(1)}, u32[]{:S(2)}, u32[]{:S(2)}) %collective-permute-start.13) | collective-permute-done | bytes 2080 | tf_op jit(solution)/shard_map/ppermute | solution.py:58
  44.4 0.9 %collective-permute-done.14 = f32[8,64]{1,0:T(8,128)S(1)} collective-permute-done((f32[8,64]{1,0:T(8,128)S(1)}, f32[8,64]{1,0:T(8,128)S(1)}, u32[]{:S(2)}, u32[]{:S(2)}) %collective-permute-start.14) | collective-permute-done | bytes 2080 | tf_op jit(solution)/shard_map/ppermute | solution.py:58
  45.3 0.6 %add_bitcast_fusion = f32[4,64,8]{1,2,0:T(8,128)} fusion(f32[4,8,64]{2,1,0:T(8,128)S(1)} %maximum_add_fusion, f32[8,64]{1,0:T(8,128)S(1)} %select_add_fusion), kind=kLoop, calls=%fused_computation.54 | loop fusion | flops 2048 | bytes 18432 | tf_op jit(solution)/shard_map/transpose | solution.py:60
  (42 shorter events, 1.7 us)
Async XLA Ops:
  0.0 32.2 %copy-start = (bf16[64,3072]{1,0:T(8,128)(2,1)S(1)}, bf16[64,3072]{1,0:T(8,128)(2,1)}, u32[]{:S(2)}) copy-start(bf16[64,3072]{1,0:T(8,128)(2,1)} %param.13) | copy-start | bytes 1179652
  0.0 6.8 %copy-start.1 = (bf16[4,2,24,8,128]{4,3,2,1,0:T(8,128)(2,1)S(1)}, bf16[4,2,24,8,128]{4,3,2,1,0:T(8,128)(2,1)}, u32[]{:S(2)}) copy-start(bf16[4,2,24,8,128]{4,3,2,1,0:T(8,128)(2,1)} %param.10) | copy-start | bytes 1179652
  1.1 14.2 %collective-permute-start = (bf16[48,8,128]{2,1,0:T(8,128)(2,1)S(1)}, bf16[48,8,128]{2,1,0:T(8,128)(2,1)S(1)}, u32[]{:S(2)}, u32[]{:S(2)}) collective-permute-start(bf16[48,8,128]{2,1,0:T(8,128)(2,1)S(1)} %get-tuple-element.22), channel_id=1, source_target_pairs={{0,1},{1,0},{2,3},{3,2},{4,5},{5,4},{6,7},{7,6},{8,9},{9,8},{10,11... | collective-permute-start | bytes 294920 | tf_op jit(solution)/shard_map/ppermute | solution.py:93
  4.2 11.3 %collective-permute-start.1 = (bf16[48,8,128]{2,1,0:T(8,128)(2,1)S(1)}, bf16[48,8,128]{2,1,0:T(8,128)(2,1)S(1)}, u32[]{:S(2)}, u32[]{:S(2)}) collective-permute-start(bf16[48,8,128]{2,1,0:T(8,128)(2,1)S(1)} %get-tuple-element.21), channel_id=1, source_target_pairs={{0,2},{1,3},{2,0},{3,1},{4,6},{5,7},{6,4},{7,5},{8,10},{9,11},{10,... | collective-permute-start | bytes 294920 | tf_op jit(solution)/shard_map/ppermute | solution.py:93
  6.8 9.3 %collective-permute-start.2 = (bf16[48,8,128]{2,1,0:T(8,128)(2,1)S(1)}, bf16[48,8,128]{2,1,0:T(8,128)(2,1)S(1)}, u32[]{:S(2)}, u32[]{:S(2)}) collective-permute-start(bf16[48,8,128]{2,1,0:T(8,128)(2,1)S(1)} %get-tuple-element.20), channel_id=1, source_target_pairs={{0,3},{1,2},{2,1},{3,0},{4,7},{5,6},{6,5},{7,4},{8,11},{9,10},{10,... | collective-permute-start | bytes 294920 | tf_op jit(solution)/shard_map/ppermute | solution.py:93
  6.8 4.5 %copy-start.4 = (f32[1000]{0:T(1024)S(1)}, f32[1000]{0:T(1024)}, u32[]{:S(2)}) copy-start(f32[1000]{0:T(1024)} %param.16) | copy-start | bytes 12004
  6.8 8.6 %copy-start.2 = (bf16[4,2,24,8,128]{4,3,2,1,0:T(8,128)(2,1)S(1)}, bf16[4,2,24,8,128]{4,3,2,1,0:T(8,128)(2,1)}, u32[]{:S(2)}) copy-start(bf16[4,2,24,8,128]{4,3,2,1,0:T(8,128)(2,1)} %param.11) | copy-start | bytes 1179652
  6.9 4.4 %copy-start.5 = (s32[4]{0:T(128)S(1)}, s32[4]{0:T(128)}, u32[]{:S(2)}) copy-start(s32[4]{0:T(128)} %param.17) | copy-start | bytes 52
  6.9 17.9 %collective-permute-start.3 = (bf16[48,8,128]{2,1,0:T(8,128)(2,1)S(1)}, bf16[48,8,128]{2,1,0:T(8,128)(2,1)S(1)}, u32[]{:S(2)}, u32[]{:S(2)}) collective-permute-start(bf16[48,8,128]{2,1,0:T(8,128)(2,1)S(1)} %get-tuple-element.18), channel_id=1, source_target_pairs={{0,1},{1,0},{2,3},{3,2},{4,5},{5,4},{6,7},{7,6},{8,9},{9,8},{10,11... | collective-permute-start | bytes 294920 | tf_op jit(solution)/shard_map/ppermute | solution.py:93
  7.8 17.4 %collective-permute-start.4 = (bf16[48,8,128]{2,1,0:T(8,128)(2,1)S(1)}, bf16[48,8,128]{2,1,0:T(8,128)(2,1)S(1)}, u32[]{:S(2)}, u32[]{:S(2)}) collective-permute-start(bf16[48,8,128]{2,1,0:T(8,128)(2,1)S(1)} %get-tuple-element.17), channel_id=1, source_target_pairs={{0,2},{1,3},{2,0},{3,1},{4,6},{5,7},{6,4},{7,5},{8,10},{9,11},{10,... | collective-permute-start | bytes 294920 | tf_op jit(solution)/shard_map/ppermute | solution.py:93
  12.8 0.7 %copy-start.6 = (f32[8]{0:T(128)S(1)}, f32[8]{0:T(128)}, u32[]{:S(2)}) copy-start(f32[8]{0:T(128)} %param.14) | copy-start | bytes 100
  15.3 9.9 %collective-permute-start.5 = (bf16[48,8,128]{2,1,0:T(8,128)(2,1)S(1)}, bf16[48,8,128]{2,1,0:T(8,128)(2,1)S(1)}, u32[]{:S(2)}, u32[]{:S(2)}) collective-permute-start(bf16[48,8,128]{2,1,0:T(8,128)(2,1)S(1)} %get-tuple-element.16), channel_id=1, source_target_pairs={{0,3},{1,2},{2,1},{3,0},{4,7},{5,6},{6,5},{7,4},{8,11},{9,10},{10,... | collective-permute-start | bytes 294920 | tf_op jit(solution)/shard_map/ppermute | solution.py:93
  15.5 10.3 %collective-permute-start.6 = (bf16[48,8,128]{2,1,0:T(8,128)(2,1)S(1)}, bf16[48,8,128]{2,1,0:T(8,128)(2,1)S(1)}, u32[]{:S(2)}, u32[]{:S(2)}) collective-permute-start(bf16[48,8,128]{2,1,0:T(8,128)(2,1)S(1)} %get-tuple-element.14), channel_id=1, source_target_pairs={{0,1},{1,0},{2,3},{3,2},{4,5},{5,4},{6,7},{7,6},{8,9},{9,8},{10,11... | collective-permute-start | bytes 294920 | tf_op jit(solution)/shard_map/ppermute | solution.py:93
  16.1 15.4 %collective-permute-start.7 = (bf16[48,8,128]{2,1,0:T(8,128)(2,1)S(1)}, bf16[48,8,128]{2,1,0:T(8,128)(2,1)S(1)}, u32[]{:S(2)}, u32[]{:S(2)}) collective-permute-start(bf16[48,8,128]{2,1,0:T(8,128)(2,1)S(1)} %get-tuple-element.13), channel_id=1, source_target_pairs={{0,2},{1,3},{2,0},{3,1},{4,6},{5,7},{6,4},{7,5},{8,10},{9,11},{10,... | collective-permute-start | bytes 294920 | tf_op jit(solution)/shard_map/ppermute | solution.py:93
  24.8 6.7 %collective-permute-start.8 = (bf16[48,8,128]{2,1,0:T(8,128)(2,1)S(1)}, bf16[48,8,128]{2,1,0:T(8,128)(2,1)S(1)}, u32[]{:S(2)}, u32[]{:S(2)}) collective-permute-start(bf16[48,8,128]{2,1,0:T(8,128)(2,1)S(1)} %get-tuple-element.12), channel_id=1, source_target_pairs={{0,3},{1,2},{2,1},{3,0},{4,7},{5,6},{6,5},{7,4},{8,11},{9,10},{10,... | collective-permute-start | bytes 294920 | tf_op jit(solution)/shard_map/ppermute | solution.py:93
  32.5 4.6 %collective-permute-start.10 = (f32[1,8,64]{2,1,0:T(8,128)S(1)}, f32[1,8,64]{2,1,0:T(8,128)S(1)}, u32[]{:S(2)}, u32[]{:S(2)}) collective-permute-start(f32[1,8,64]{2,1,0:T(8,128)S(1)} %get-tuple-element.28), channel_id=1, source_target_pairs={{0,2},{1,3},{2,0},{3,1},{4,6},{5,7},{6,4},{7,5},{8,10},{9,11},{10,... | collective-permute-start | bytes 6152 | tf_op jit(solution)/shard_map/ppermute | solution.py:42
  35.2 5.4 %collective-permute-start.11 = (f32[1,8,64]{2,1,0:T(8,128)S(1)}, f32[1,8,64]{2,1,0:T(8,128)S(1)}, u32[]{:S(2)}, u32[]{:S(2)}) collective-permute-start(f32[1,8,64]{2,1,0:T(8,128)S(1)} %get-tuple-element.27), channel_id=1, source_target_pairs={{0,3},{1,2},{2,1},{3,0},{4,7},{5,6},{6,5},{7,4},{8,11},{9,10},{10,... | collective-permute-start | bytes 6152 | tf_op jit(solution)/shard_map/ppermute | solution.py:42
  36.5 4.1 %collective-permute-start.9 = (f32[1,8,64]{2,1,0:T(8,128)S(1)}, f32[1,8,64]{2,1,0:T(8,128)S(1)}, u32[]{:S(2)}, u32[]{:S(2)}) collective-permute-start(f32[1,8,64]{2,1,0:T(8,128)S(1)} %get-tuple-element.26), channel_id=1, source_target_pairs={{0,1},{1,0},{2,3},{3,2},{4,5},{5,4},{6,7},{7,6},{8,9},{9,8},{10,11... | collective-permute-start | bytes 6152 | tf_op jit(solution)/shard_map/ppermute | solution.py:42
  40.6 2.7 %collective-permute-start.12 = (f32[8,64]{1,0:T(8,128)S(1)}, f32[8,64]{1,0:T(8,128)S(1)}, u32[]{:S(2)}, u32[]{:S(2)}) collective-permute-start(f32[8,64]{1,0:T(8,128)S(1)} %bitcast_add_fusion), channel_id=1, source_target_pairs={{0,4},{4,0},{8,12},{12,8},{1,5},{5,1},{9,13},{13,9},{2,6},{6,2},{1... | collective-permute-start | bytes 6152 | tf_op jit(solution)/shard_map/ppermute | solution.py:58
  40.7 3.7 %collective-permute-start.13 = (f32[8,64]{1,0:T(8,128)S(1)}, f32[8,64]{1,0:T(8,128)S(1)}, u32[]{:S(2)}, u32[]{:S(2)}) collective-permute-start(f32[8,64]{1,0:T(8,128)S(1)} %bitcast_add_fusion), channel_id=1, source_target_pairs={{0,8},{4,12},{8,0},{12,4},{1,9},{5,13},{9,1},{13,5},{2,10},{6,14},... | collective-permute-start | bytes 6152 | tf_op jit(solution)/shard_map/ppermute | solution.py:58
  42.2 3.0 %collective-permute-start.14 = (f32[8,64]{1,0:T(8,128)S(1)}, f32[8,64]{1,0:T(8,128)S(1)}, u32[]{:S(2)}, u32[]{:S(2)}) collective-permute-start(f32[8,64]{1,0:T(8,128)S(1)} %bitcast_add_fusion), channel_id=1, source_target_pairs={{0,12},{4,8},{8,4},{12,0},{1,13},{5,9},{9,5},{13,1},{2,14},{6,10},... | collective-permute-start | bytes 6152 | tf_op jit(solution)/shard_map/ppermute | solution.py:58
  42.6 0.7 %copy-start.3 = (f32[64,8]{0,1:T(8,128)S(1)}, f32[64,8]{0,1:T(8,128)}, u32[]{:S(2)}) copy-start(f32[64,8]{0,1:T(8,128)} %param.12) | copy-start | bytes 6148

commit v10 on v9

--- a/solution.py
+++ b/solution.py
@@ -89,7 +89,10 @@
         arrived = {}
         for k in reversed(range(groups)):
             pieces = [lax.dynamic_index_in_dim(c, me ^ k, 0, keepdims=False) for c in chunks]
-            if k:
+            if k >= 2:
+                sent = lax.ppermute(jnp.stack(pieces), "seq", xor_pairs(groups, k))
+                pieces = [sent[i] for i in range(3)]
+            elif k:
                 pieces = [lax.ppermute(p, "seq", xor_pairs(groups, k)) for p in pieces]
             arrived[k] = pieces
         gathered = [

time: 46.1 us -> 48.3 us (1.048)
  waiting for transfers between devices: 12.3 us -> 19.1 us
  starting transfers between devices: 25.5 us -> 19.6 us
  local copies, waits for them, and re-layouts: 4.43 us -> 5.51 us
    ppermute x9 -> x3, starting transfers between devices: 19.5 us -> 2.33 us  [on_device(): pieces = [lax.ppermute(p, 'seq', xor_pairs(groups, k)) for p in pieces]]
    ppermute x0 -> x2, waiting for transfers between devices: none -> 12.7 us  [on_device(): sent = lax.ppermute(jnp.stack(pieces), 'seq', xor_pairs(groups, k))]
    ppermute x9 -> x3, waiting for transfers between devices: 6.19 us -> 0.01 us  [on_device(): pieces = [lax.ppermute(p, 'seq', xor_pairs(groups, k)) for p in pieces]]
    ppermute x3, starting transfers between devices: 4.04 us -> 9.62 us  [gather_prefix(): pieces.append(lax.ppermute(ordered[:, k], 'seq', xor_pairs(groups, k)))]
    ppermute x0 -> x2, starting transfers between devices: none -> 5.52 us  [on_device(): sent = lax.ppermute(jnp.stack(pieces), 'seq', xor_pairs(groups, k))]
    unnamed x14, local copies, waits for them, and re-layouts: 1.35 us -> 2.41 us
  transfers between devices with their start and end apart: 15 -> 11, of which waited for: 6 -> 5; matrix products, arithmetic and copies ran while one was open for 7% -> 7% of each run, Pallas kernels for 0% -> 0%
where the time goes in v10:
time: 48.3 us; the launch traced here: 48 us
  starting transfers between devices  19.6 us (41%)
  waiting for transfers between devices  19.1 us (40%)
  local copies, waits for them, and re-layouts  5.51 us (11%)
  other arithmetic  1.76 us (4%)
  matrix products  1.26 us (3%)
  between operations  0.83 us (2%)
    ppermute x2, waiting for transfers between devices, on_device(): sent = lax.ppermute(jnp.stack(pieces), 'seq', xor_pairs(groups, k))  12.7 us
    ppermute x3, starting transfers between devices, gather_prefix(): pieces.append(lax.ppermute(ordered[:, k], 'seq', xor_pairs(groups, k)))  9.62 us
    ppermute x2, starting transfers between devices, on_device(): sent = lax.ppermute(jnp.stack(pieces), 'seq', xor_pairs(groups, k))  5.52 us
    ppermute x3, waiting for transfers between devices, gather_prefix(): pieces.append(lax.ppermute(ordered[:, k], 'seq', xor_pairs(groups, k)))  4.02 us
    unnamed x14, local copies, waits for them, and re-layouts  2.41 us
    ppermute x3, waiting for transfers between devices, gather_prefix(): other = lax.ppermute(total, 'step', xor_pairs(steps_axis, k))  2.35 us
    ppermute x3, starting transfers between devices, on_device(): pieces = [lax.ppermute(p, 'seq', xor_pairs(groups, k)) for p in pieces]  2.33 us
    ppermute x3, starting transfers between devices, gather_prefix(): other = lax.ppermute(total, 'step', xor_pairs(steps_axis, k))  2.14 us
  transfers between devices with their start and end apart: 11, of which 5 were waited for; matrix products, arithmetic and copies ran while one was open for 7% of the time, Pallas kernels for 0%

profile of v10, /device:TPU:0, one launch (start us, length us, event | category | flops | bytes accessed | tf_op | source)
XLA Modules:
  0.0 48.0 jit_solution(4169036664508830555)
XLA Ops:
  0.0 1.1 %dynamic-slice_bitcast_fusion.1 = (bf16[48,8,128]{2,1,0:T(8,128)(2,1)S(1)}, bf16[48,8,128]{2,1,0:T(8,128)(2,1)S(1)}, bf16[1,48,8,128]{3,2,1,0:T(8,128)(2,1)S(1)}, bf16[1,48,8,128]{3,2,1,0:T(8,128)(2,1)S(1)}) fusion(bf16[4,48,8,128]{3,2,1,0:T(8,128)(2,1)} %bitcast.115, s32[]{:T(128)S(6)} %select_n.214, s32[]{:T(128)S(6)} %select_n.215, s32[]{:T(128)S(6)} %select_n.217, ...), kind=kLoop, calls=%fused_computation.43 | loop fusion | bytes 786448 | tf_op jit(solution)/shard_map/jit(dynamic_index_in_dim)/squeeze | solution.py:91
  1.3 1.0 %copy-done.2 = bf16[4,2,24,8,128]{4,3,2,1,0:T(8,128)(2,1)S(1)} copy-done((bf16[4,2,24,8,128]{4,3,2,1,0:T(8,128)(2,1)S(1)}, bf16[4,2,24,8,128]{4,3,2,1,0:T(8,128)(2,1)}, u32[]{:S(2)}) %copy-start.2) | copy-done | bytes 393240
  2.3 4.1 %collective-permute-start.1 = (bf16[3,48,8,128]{3,2,1,0:T(8,128)(2,1)S(1)}, bf16[3,48,8,128]{3,2,1,0:T(8,128)(2,1)S(1)}, u32[]{:S(2)}, u32[]{:S(2)}) collective-permute-start(bf16[3,48,8,128]{3,2,1,0:T(8,128)(2,1)S(1)} %pad_maximum_fusion), channel_id=1, source_target_pairs={{0,2},{1,3},{2,0},{3,1},{4,6},{5,7},{6,4},{7,5},{8,10},{9,11},{10,... | collective-permute-start | bytes 884744 | tf_op jit(solution)/shard_map/ppermute | solution.py:93
  6.5 1.4 %collective-permute-start.2 = (bf16[3,48,8,128]{3,2,1,0:T(8,128)(2,1)S(1)}, bf16[3,48,8,128]{3,2,1,0:T(8,128)(2,1)S(1)}, u32[]{:S(2)}, u32[]{:S(2)}) collective-permute-start(bf16[3,48,8,128]{3,2,1,0:T(8,128)(2,1)S(1)} %pad_maximum_fusion.1), channel_id=1, source_target_pairs={{0,3},{1,2},{2,1},{3,0},{4,7},{5,6},{6,5},{7,4},{8,11},{9,10},{10,... | collective-permute-start | bytes 884744 | tf_op jit(solution)/shard_map/ppermute | solution.py:93
  7.9 0.3 collective-permute-start
  8.2 1.7 %collective-permute-start.3 = (bf16[48,8,128]{2,1,0:T(8,128)(2,1)S(1)}, bf16[48,8,128]{2,1,0:T(8,128)(2,1)S(1)}, u32[]{:S(2)}, u32[]{:S(2)}) collective-permute-start(bf16[48,8,128]{2,1,0:T(8,128)(2,1)S(1)} %get-tuple-element.16), channel_id=1, source_target_pairs={{0,1},{1,0},{2,3},{3,2},{4,5},{5,4},{6,7},{7,6},{8,9},{9,8},{10,11... | collective-permute-start | bytes 294920 | tf_op jit(solution)/shard_map/ppermute | solution.py:96
  10.4 0.6 %dynamic_slice.40 = f32[1]{0:T(128)} dynamic-slice(f32[4]{0:T(128)S(1)} %select_reduce_fusion, s32[]{:T(128)S(6)} %select_n.214), dynamic_slice_sizes={1} | dynamic-slice | bytes 12 | tf_op jit(solution)/shard_map/dynamic_slice | solution.py:123
  11.7 0.6 %copy-done.6 = f32[8]{0:T(128)S(1)} copy-done((f32[8]{0:T(128)S(1)}, f32[8]{0:T(128)}, u32[]{:S(2)}) %copy-start.6) | copy-done | bytes 56
  12.3 0.6 %fusion.42 = f32[]{:T(128)} fusion(f32[8]{0:T(128)S(1)} %copy-done.6, s32[]{:T(128)} %bitcast.114), kind=kLoop, calls=%fused_computation.86 | loop fusion | flops 23 | bytes 40 | tf_op jit(solution)/shard_map/reduce_sum | solution.py:13
  12.9 0.6 %broadcast_in_dim.65 = f32[1,32,64]{2,1,0:T(8,128)S(1)} broadcast(f32[]{:T(128)} %bitcast.1), dimensions={} | broadcast | bytes 8196 | tf_op jit(solution)/shard_map/broadcast_in_dim | solution.py:128
  13.6 0.6 %broadcast_in_dim.61 = f32[1,32,64]{2,1,0:T(8,128)S(1)} broadcast(f32[]{:T(128)} %fusion.42), dimensions={} | broadcast | bytes 8196 | tf_op jit(solution)/shard_map/broadcast_in_dim | solution.py:127
  14.2 12.7 %collective-permute-done.1 = bf16[3,48,8,128]{3,2,1,0:T(8,128)(2,1)S(1)} collective-permute-done((bf16[3,48,8,128]{3,2,1,0:T(8,128)(2,1)S(1)}, bf16[3,48,8,128]{3,2,1,0:T(8,128)(2,1)S(1)}, u32[]{:S(2)}, u32[]{:S(2)}) %collective-permute-start.1) | collective-permute-done | bytes 294944 | tf_op jit(solution)/shard_map/ppermute | solution.py:93
  27.0 0.3 fusion.45
  27.6 0.7 %multiply_reduce_fusion = (f32[48,32]{1,0:T(8,128)S(1)}, bf16[48,32,128]{2,1,0:T(8,128)(2,1)S(1)}) fusion(f32[48,32]{1,0:T(8,128)S(1)} %fusion.3, bf16[48,8,128]{2,1,0:T(8,128)(2,1)S(1)} %get-tuple-element.26, bf16[48,8,128]{2,1,0:T(8,128)(2,1)S(1)} %get-tuple-element.23, bf16[48,8,128]{2,1,0:T(8,128)(2,1)S(1)} %collective-permute-done.4, ...), kind=kOutput, calls=%fused_computation.6 | convolution fusion | flops 15235584 | bytes 1001472 | tf_op jit(solution)/shard_map/iqk,ikd->iqd/dot_general | solution.py:24
  28.6 6.2 %collective-permute-start.5 = (f32[1,8,64]{2,1,0:T(8,128)S(1)}, f32[1,8,64]{2,1,0:T(8,128)S(1)}, u32[]{:S(2)}, u32[]{:S(2)}) collective-permute-start(f32[1,8,64]{2,1,0:T(8,128)S(1)} %get-tuple-element.32), channel_id=1, source_target_pairs={{0,1},{1,0},{2,3},{3,2},{4,5},{5,4},{6,7},{7,6},{8,9},{9,8},{10,11... | collective-permute-start | bytes 6152 | tf_op jit(solution)/shard_map/ppermute | solution.py:42
  34.8 2.0 %collective-permute-start.6 = (f32[1,8,64]{2,1,0:T(8,128)S(1)}, f32[1,8,64]{2,1,0:T(8,128)S(1)}, u32[]{:S(2)}, u32[]{:S(2)}) collective-permute-start(f32[1,8,64]{2,1,0:T(8,128)S(1)} %get-tuple-element.34), channel_id=1, source_target_pairs={{0,2},{1,3},{2,0},{3,1},{4,6},{5,7},{6,4},{7,5},{8,10},{9,11},{10,... | collective-permute-start | bytes 6152 | tf_op jit(solution)/shard_map/ppermute | solution.py:42
  36.8 1.4 %collective-permute-start.7 = (f32[1,8,64]{2,1,0:T(8,128)S(1)}, f32[1,8,64]{2,1,0:T(8,128)S(1)}, u32[]{:S(2)}, u32[]{:S(2)}) collective-permute-start(f32[1,8,64]{2,1,0:T(8,128)S(1)} %get-tuple-element.33), channel_id=1, source_target_pairs={{0,3},{1,2},{2,1},{3,0},{4,7},{5,6},{6,5},{7,4},{8,11},{9,10},{10,... | collective-permute-start | bytes 6152 | tf_op jit(solution)/shard_map/ppermute | solution.py:42
  38.2 1.1 %collective-permute-done.6 = f32[1,8,64]{2,1,0:T(8,128)S(1)} collective-permute-done((f32[1,8,64]{2,1,0:T(8,128)S(1)}, f32[1,8,64]{2,1,0:T(8,128)S(1)}, u32[]{:S(2)}, u32[]{:S(2)}) %collective-permute-start.6) | collective-permute-done | bytes 2080 | tf_op jit(solution)/shard_map/ppermute | solution.py:42
  39.3 2.9 %collective-permute-done.7 = f32[1,8,64]{2,1,0:T(8,128)S(1)} collective-permute-done((f32[1,8,64]{2,1,0:T(8,128)S(1)}, f32[1,8,64]{2,1,0:T(8,128)S(1)}, u32[]{:S(2)}, u32[]{:S(2)}) %collective-permute-start.7) | collective-permute-done | bytes 2080 | tf_op jit(solution)/shard_map/ppermute | solution.py:42
  42.2 1.6 %collective-permute-start.8 = (f32[8,64]{1,0:T(8,128)S(1)}, f32[8,64]{1,0:T(8,128)S(1)}, u32[]{:S(2)}, u32[]{:S(2)}) collective-permute-start(f32[8,64]{1,0:T(8,128)S(1)} %bitcast_add_fusion), channel_id=1, source_target_pairs={{0,4},{4,0},{8,12},{12,8},{1,5},{5,1},{9,13},{13,9},{2,6},{6,2},{1... | collective-permute-start | bytes 6152 | tf_op jit(solution)/shard_map/ppermute | solution.py:58
  43.8 0.5 %collective-permute-start.9 = (f32[8,64]{1,0:T(8,128)S(1)}, f32[8,64]{1,0:T(8,128)S(1)}, u32[]{:S(2)}, u32[]{:S(2)}) collective-permute-start(f32[8,64]{1,0:T(8,128)S(1)} %bitcast_add_fusion), channel_id=1, source_target_pairs={{0,8},{4,12},{8,0},{12,4},{1,9},{5,13},{9,1},{13,5},{2,10},{6,14},... | collective-permute-start | bytes 6152 | tf_op jit(solution)/shard_map/ppermute | solution.py:58
  44.4 0.7 %copy-done.3 = f32[64,8]{0,1:T(8,128)S(1)} copy-done((f32[64,8]{0,1:T(8,128)S(1)}, f32[64,8]{0,1:T(8,128)}, u32[]{:S(2)}) %copy-start.3) | copy-done | bytes 2072
  45.3 2.2 %collective-permute-done.9 = f32[8,64]{1,0:T(8,128)S(1)} collective-permute-done((f32[8,64]{1,0:T(8,128)S(1)}, f32[8,64]{1,0:T(8,128)S(1)}, u32[]{:S(2)}, u32[]{:S(2)}) %collective-permute-start.9) | collective-permute-done | bytes 2080 | tf_op jit(solution)/shard_map/ppermute | solution.py:58
  47.4 0.6 %add_bitcast_fusion = f32[4,64,8]{1,2,0:T(8,128)} fusion(f32[4,8,64]{2,1,0:T(8,128)S(1)} %maximum_add_fusion, f32[8,64]{1,0:T(8,128)S(1)} %select_add_fusion), kind=kLoop, calls=%fused_computation.56 | loop fusion | flops 2048 | bytes 18432 | tf_op jit(solution)/shard_map/transpose | solution.py:60
  (38 shorter events, 1.5 us)
Async XLA Ops:
  0.0 28.3 %copy-start = (bf16[64,3072]{1,0:T(8,128)(2,1)S(1)}, bf16[64,3072]{1,0:T(8,128)(2,1)}, u32[]{:S(2)}) copy-start(bf16[64,3072]{1,0:T(8,128)(2,1)} %param.13) | copy-start | bytes 1179652
  0.0 1.2 %copy-start.1 = (bf16[4,2,24,8,128]{4,3,2,1,0:T(8,128)(2,1)S(1)}, bf16[4,2,24,8,128]{4,3,2,1,0:T(8,128)(2,1)}, u32[]{:S(2)}) copy-start(bf16[4,2,24,8,128]{4,3,2,1,0:T(8,128)(2,1)} %param.10) | copy-start | bytes 1179652
  1.2 1.0 %copy-start.2 = (bf16[4,2,24,8,128]{4,3,2,1,0:T(8,128)(2,1)S(1)}, bf16[4,2,24,8,128]{4,3,2,1,0:T(8,128)(2,1)}, u32[]{:S(2)}) copy-start(bf16[4,2,24,8,128]{4,3,2,1,0:T(8,128)(2,1)} %param.9) | copy-start | bytes 1179652
  2.3 24.6 %collective-permute-start.1 = (bf16[3,48,8,128]{3,2,1,0:T(8,128)(2,1)S(1)}, bf16[3,48,8,128]{3,2,1,0:T(8,128)(2,1)S(1)}, u32[]{:S(2)}, u32[]{:S(2)}) collective-permute-start(bf16[3,48,8,128]{3,2,1,0:T(8,128)(2,1)S(1)} %pad_maximum_fusion), channel_id=1, source_target_pairs={{0,2},{1,3},{2,0},{3,1},{4,6},{5,7},{6,4},{7,5},{8,10},{9,11},{10,... | collective-permute-start | bytes 884744 | tf_op jit(solution)/shard_map/ppermute | solution.py:93
  6.4 3.8 %copy-start.4 = (f32[1000]{0:T(1024)S(1)}, f32[1000]{0:T(1024)}, u32[]{:S(2)}) copy-start(f32[1000]{0:T(1024)} %param.16) | copy-start | bytes 12004
  6.5 20.5 %collective-permute-start.2 = (bf16[3,48,8,128]{3,2,1,0:T(8,128)(2,1)S(1)}, bf16[3,48,8,128]{3,2,1,0:T(8,128)(2,1)S(1)}, u32[]{:S(2)}, u32[]{:S(2)}) collective-permute-start(bf16[3,48,8,128]{3,2,1,0:T(8,128)(2,1)S(1)} %pad_maximum_fusion.1), channel_id=1, source_target_pairs={{0,3},{1,2},{2,1},{3,0},{4,7},{5,6},{6,5},{7,4},{8,11},{9,10},{10,... | collective-permute-start | bytes 884744 | tf_op jit(solution)/shard_map/ppermute | solution.py:93
  7.9 19.1 %collective-permute-start = (bf16[48,8,128]{2,1,0:T(8,128)(2,1)S(1)}, bf16[48,8,128]{2,1,0:T(8,128)(2,1)S(1)}, u32[]{:S(2)}, u32[]{:S(2)}) collective-permute-start(bf16[48,8,128]{2,1,0:T(8,128)(2,1)S(1)} %get-tuple-element.22), channel_id=1, source_target_pairs={{0,1},{1,0},{2,3},{3,2},{4,5},{5,4},{6,7},{7,6},{8,9},{9,8},{10,11... | collective-permute-start | bytes 294920 | tf_op jit(solution)/shard_map/ppermute | solution.py:96
  8.2 2.0 %copy-start.5 = (s32[4]{0:T(128)S(1)}, s32[4]{0:T(128)}, u32[]{:S(2)}) copy-start(s32[4]{0:T(128)} %param.17) | copy-start | bytes 52
  8.2 18.8 %collective-permute-start.3 = (bf16[48,8,128]{2,1,0:T(8,128)(2,1)S(1)}, bf16[48,8,128]{2,1,0:T(8,128)(2,1)S(1)}, u32[]{:S(2)}, u32[]{:S(2)}) collective-permute-start(bf16[48,8,128]{2,1,0:T(8,128)(2,1)S(1)} %get-tuple-element.16), channel_id=1, source_target_pairs={{0,1},{1,0},{2,3},{3,2},{4,5},{5,4},{6,7},{7,6},{8,9},{9,8},{10,11... | collective-permute-start | bytes 294920 | tf_op jit(solution)/shard_map/ppermute | solution.py:96
  9.9 17.7 %collective-permute-start.4 = (bf16[48,8,128]{2,1,0:T(8,128)(2,1)S(1)}, bf16[48,8,128]{2,1,0:T(8,128)(2,1)S(1)}, u32[]{:S(2)}, u32[]{:S(2)}) collective-permute-start(bf16[48,8,128]{2,1,0:T(8,128)(2,1)S(1)} %get-tuple-element.12), channel_id=1, source_target_pairs={{0,1},{1,0},{2,3},{3,2},{4,5},{5,4},{6,7},{7,6},{8,9},{9,8},{10,11... | collective-permute-start | bytes 294920 | tf_op jit(solution)/shard_map/ppermute | solution.py:96
  11.6 0.7 %copy-start.6 = (f32[8]{0:T(128)S(1)}, f32[8]{0:T(128)}, u32[]{:S(2)}) copy-start(f32[8]{0:T(128)} %param.14) | copy-start | bytes 100
  28.6 9.6 %collective-permute-start.5 = (f32[1,8,64]{2,1,0:T(8,128)S(1)}, f32[1,8,64]{2,1,0:T(8,128)S(1)}, u32[]{:S(2)}, u32[]{:S(2)}) collective-permute-start(f32[1,8,64]{2,1,0:T(8,128)S(1)} %get-tuple-element.32), channel_id=1, source_target_pairs={{0,1},{1,0},{2,3},{3,2},{4,5},{5,4},{6,7},{7,6},{8,9},{9,8},{10,11... | collective-permute-start | bytes 6152 | tf_op jit(solution)/shard_map/ppermute | solution.py:42
  34.8 4.5 %collective-permute-start.6 = (f32[1,8,64]{2,1,0:T(8,128)S(1)}, f32[1,8,64]{2,1,0:T(8,128)S(1)}, u32[]{:S(2)}, u32[]{:S(2)}) collective-permute-start(f32[1,8,64]{2,1,0:T(8,128)S(1)} %get-tuple-element.34), channel_id=1, source_target_pairs={{0,2},{1,3},{2,0},{3,1},{4,6},{5,7},{6,4},{7,5},{8,10},{9,11},{10,... | collective-permute-start | bytes 6152 | tf_op jit(solution)/shard_map/ppermute | solution.py:42
  36.8 5.4 %collective-permute-start.7 = (f32[1,8,64]{2,1,0:T(8,128)S(1)}, f32[1,8,64]{2,1,0:T(8,128)S(1)}, u32[]{:S(2)}, u32[]{:S(2)}) collective-permute-start(f32[1,8,64]{2,1,0:T(8,128)S(1)} %get-tuple-element.33), channel_id=1, source_target_pairs={{0,3},{1,2},{2,1},{3,0},{4,7},{5,6},{6,5},{7,4},{8,11},{9,10},{10,... | collective-permute-start | bytes 6152 | tf_op jit(solution)/shard_map/ppermute | solution.py:42
  42.2 3.0 %collective-permute-start.10 = (f32[8,64]{1,0:T(8,128)S(1)}, f32[8,64]{1,0:T(8,128)S(1)}, u32[]{:S(2)}, u32[]{:S(2)}) collective-permute-start(f32[8,64]{1,0:T(8,128)S(1)} %bitcast_add_fusion), channel_id=1, source_target_pairs={{0,12},{4,8},{8,4},{12,0},{1,13},{5,9},{9,5},{13,1},{2,14},{6,10},... | collective-permute-start | bytes 6152 | tf_op jit(solution)/shard_map/ppermute | solution.py:58
  42.2 3.0 %collective-permute-start.8 = (f32[8,64]{1,0:T(8,128)S(1)}, f32[8,64]{1,0:T(8,128)S(1)}, u32[]{:S(2)}, u32[]{:S(2)}) collective-permute-start(f32[8,64]{1,0:T(8,128)S(1)} %bitcast_add_fusion), channel_id=1, source_target_pairs={{0,4},{4,0},{8,12},{12,8},{1,5},{5,1},{9,13},{13,9},{2,6},{6,2},{1... | collective-permute-start | bytes 6152 | tf_op jit(solution)/shard_map/ppermute | solution.py:58
  43.8 3.6 %collective-permute-start.9 = (f32[8,64]{1,0:T(8,128)S(1)}, f32[8,64]{1,0:T(8,128)S(1)}, u32[]{:S(2)}, u32[]{:S(2)}) collective-permute-start(f32[8,64]{1,0:T(8,128)S(1)} %bitcast_add_fusion), channel_id=1, source_target_pairs={{0,8},{4,12},{8,0},{12,4},{1,9},{5,13},{9,1},{13,5},{2,10},{6,14},... | collective-permute-start | bytes 6152 | tf_op jit(solution)/shard_map/ppermute | solution.py:58
  44.4 0.7 %copy-start.3 = (f32[64,8]{0,1:T(8,128)S(1)}, f32[64,8]{0,1:T(8,128)}, u32[]{:S(2)}) copy-start(f32[64,8]{0,1:T(8,128)} %param.12) | copy-start | bytes 6148

commit v11 on v9

--- a/solution.py
+++ b/solution.py
@@ -117,15 +117,18 @@
             jnp.einsum("chd,sbhld->sblc", weight_heads, ho, preferred_element_type=jnp.float32)
             / root_mean[:, :, :, None]
         )
-        my_len = lax.dynamic_slice_in_dim(step_len, me * local_steps, local_steps)
+        owner = jnp.arange(step_dev, dtype=jnp.int32) // local_steps == me
+        slot = jnp.arange(step_dev, dtype=jnp.int32) % local_steps
+        mine = (owner[:, None] & (slot[:, None] == jnp.arange(local_steps)))[:, :, None, None]
+        len_full = jnp.sum(
+            jnp.where(mine, step_len[:, None, None, None], jnp.zeros((), jnp.float32)), axis=0
+        )
         shape = (local_steps, length, channels)
-        scale_full, len_full, start_t = lax.optimization_barrier(
-            (
-                jnp.broadcast_to(guide_scale, shape),
-                jnp.broadcast_to(my_len[:, None, None], shape),
-                start_latent.T,
-            )
+        coef = lax.optimization_barrier(
+            jnp.stack([jnp.broadcast_to(guide_scale, shape), jnp.broadcast_to(len_full, shape)])
         )
+        scale_full, len_full = coef[0], coef[1]
+        start_t = start_latent.T
         guided = drift[:, 1] + scale_full * (drift[:, 0] - drift[:, 1])
         update = len_full * guided
         update = update.reshape(local_steps, groups, tok_dev, channels)

time: 46.1 us -> 46.1 us (level)
  other arithmetic: 1.69 us -> 2.39 us
  local copies, waits for them, and re-layouts: 4.43 us -> 3.94 us
    another operation x0 -> x2, local copies, waits for them, and re-layouts: none -> 1.38 us  [on_device(): jnp.stack([jnp.broadcast_to(guide_scale, shape), jnp.broadcast_to(len_ful...]
    broadcast_in_dim x2 -> x0, local copies, waits for them, and re-layouts: 1.28 us -> none  [the longest x1 0.65 us: on_device(): jnp.broadcast_to(my_len[:, None, None], shape)]
    reduce_sum x0 -> x1, other arithmetic: none -> 0.66 us  [on_device(): jnp.sum(jnp.where(mine, step_len[:, None, None, None], jnp.zeros((), jnp....]
    dynamic_slice x1 -> x0, local copies, waits for them, and re-layouts: 0.59 us -> none  [on_device(): my_len = lax.dynamic_slice_in_dim(step_len, me * local_steps, local_steps)]
  transfers between devices with their start and end apart: 15 -> 15, of which waited for: 6 -> 6; matrix products, arithmetic and copies ran while one was open for 7% -> 8% of each run, Pallas kernels for 0% -> 0%
where the time goes in v11:
time: 46.1 us; the launch traced here: 45.9 us
  starting transfers between devices  25.3 us (55%)
  waiting for transfers between devices  12.3 us (27%)
  local copies, waits for them, and re-layouts  3.94 us (9%)
  other arithmetic  2.39 us (5%)
  matrix products  1.25 us (3%)
  between operations  0.81 us (2%)
    ppermute x9, starting transfers between devices, on_device(): pieces = [lax.ppermute(p, 'seq', xor_pairs(groups, k)) for p in pieces]  19.3 us
    ppermute x9, waiting for transfers between devices, on_device(): pieces = [lax.ppermute(p, 'seq', xor_pairs(groups, k)) for p in pieces]  6.19 us
    ppermute x3, waiting for transfers between devices, gather_prefix(): pieces.append(lax.ppermute(ordered[:, k], 'seq', xor_pairs(groups, k)))  4.05 us
    ppermute x3, starting transfers between devices, gather_prefix(): pieces.append(lax.ppermute(ordered[:, k], 'seq', xor_pairs(groups, k)))  4.04 us
    ppermute x3, waiting for transfers between devices, gather_prefix(): other = lax.ppermute(total, 'step', xor_pairs(steps_axis, k))  2.01 us
    ppermute x3, starting transfers between devices, gather_prefix(): other = lax.ppermute(total, 'step', xor_pairs(steps_axis, k))  1.93 us
    another operation x2, local copies, waits for them, and re-layouts, on_device(): jnp.stack([jnp.broadcast_to(guide_scale, shape), jnp.broadcast_to(len_ful...  1.38 us
    unnamed x14, local copies, waits for them, and re-layouts  1.35 us
  transfers between devices with their start and end apart: 15, of which 6 were waited for; matrix products, arithmetic and copies ran while one was open for 8% of the time, Pallas kernels for 0%

profile of v11, /device:TPU:0, one launch (start us, length us, event | category | flops | bytes accessed | tf_op | source)
XLA Modules:
  0.0 45.9 jit_solution(2730477965594077054)
XLA Ops:
  0.0 1.1 %dynamic-slice_bitcast_fusion.11 = (bf16[48,8,128]{2,1,0:T(8,128)(2,1)S(1)}, bf16[48,8,128]{2,1,0:T(8,128)(2,1)S(1)}, bf16[48,8,128]{2,1,0:T(8,128)(2,1)S(1)}, bf16[48,8,128]{2,1,0:T(8,128)(2,1)S(1)}) fusion(bf16[4,48,8,128]{3,2,1,0:T(8,128)(2,1)} %bitcast.119, s32[]{:T(128)S(6)} %select_n.238, s32[]{:T(128)S(6)} %select_n.241, s32[]{:T(128)S(6)} %select_n.240, ...), kind=kLoop, calls=%fused_computation.45 | loop fusion | bytes 786448 | tf_op jit(solution)/shard_map/jit(dynamic_index_in_dim)/squeeze | solution.py:91
  1.1 3.1 %collective-permute-start = (bf16[48,8,128]{2,1,0:T(8,128)(2,1)S(1)}, bf16[48,8,128]{2,1,0:T(8,128)(2,1)S(1)}, u32[]{:S(2)}, u32[]{:S(2)}) collective-permute-start(bf16[48,8,128]{2,1,0:T(8,128)(2,1)S(1)} %get-tuple-element.16), channel_id=1, source_target_pairs={{0,1},{1,0},{2,3},{3,2},{4,5},{5,4},{6,7},{7,6},{8,9},{9,8},{10,11... | collective-permute-start | bytes 294920 | tf_op jit(solution)/shard_map/ppermute | solution.py:93
  4.2 2.6 %collective-permute-start.1 = (bf16[48,8,128]{2,1,0:T(8,128)(2,1)S(1)}, bf16[48,8,128]{2,1,0:T(8,128)(2,1)S(1)}, u32[]{:S(2)}, u32[]{:S(2)}) collective-permute-start(bf16[48,8,128]{2,1,0:T(8,128)(2,1)S(1)} %get-tuple-element.15), channel_id=1, source_target_pairs={{0,2},{1,3},{2,0},{3,1},{4,6},{5,7},{6,4},{7,5},{8,10},{9,11},{10,... | collective-permute-start | bytes 294920 | tf_op jit(solution)/shard_map/ppermute | solution.py:93
  6.9 0.9 %collective-permute-start.3 = (bf16[48,8,128]{2,1,0:T(8,128)(2,1)S(1)}, bf16[48,8,128]{2,1,0:T(8,128)(2,1)S(1)}, u32[]{:S(2)}, u32[]{:S(2)}) collective-permute-start(bf16[48,8,128]{2,1,0:T(8,128)(2,1)S(1)} %get-tuple-element.12), channel_id=1, source_target_pairs={{0,1},{1,0},{2,3},{3,2},{4,5},{5,4},{6,7},{7,6},{8,9},{9,8},{10,11... | collective-permute-start | bytes 294920 | tf_op jit(solution)/shard_map/ppermute | solution.py:93
  7.8 3.5 %collective-permute-start.4 = (bf16[48,8,128]{2,1,0:T(8,128)(2,1)S(1)}, bf16[48,8,128]{2,1,0:T(8,128)(2,1)S(1)}, u32[]{:S(2)}, u32[]{:S(2)}) collective-permute-start(bf16[48,8,128]{2,1,0:T(8,128)(2,1)S(1)} %get-tuple-element.11), channel_id=1, source_target_pairs={{0,2},{1,3},{2,0},{3,1},{4,6},{5,7},{6,4},{7,5},{8,10},{9,11},{10,... | collective-permute-start | bytes 294920 | tf_op jit(solution)/shard_map/ppermute | solution.py:93
  11.5 0.7 %fusion.42 = f32[]{:T(128)} fusion(f32[4]{0:T(128)S(1)} %select_reduce_fusion, s32[]{:T(128)S(6)} %axis_index.22), kind=kLoop, calls=%fused_computation.81 | loop fusion | flops 11 | bytes 24 | tf_op jit(solution)/shard_map/reduce_sum | solution.py:123
  12.8 0.6 %copy-done.6 = f32[8]{0:T(128)S(1)} copy-done((f32[8]{0:T(128)S(1)}, f32[8]{0:T(128)}, u32[]{:S(2)}) %copy-start.6) | copy-done | bytes 56
  13.5 0.7 %fusion.41 = f32[]{:T(128)} fusion(f32[8]{0:T(128)S(1)} %copy-done.6, s32[]{:T(128)} %bitcast.118), kind=kLoop, calls=%fused_computation.80 | loop fusion | flops 23 | bytes 40 | tf_op jit(solution)/shard_map/reduce_sum | solution.py:13
  14.2 1.3 %stack.12 = f32[2]{0:T(128)S(1)} pad(f32[1]{0:T(128)} %bitcast.1, f32[]{:T(128)} %fusion.42), padding=0_1 | pad | bytes 16 | tf_op jit(solution)/shard_map/stack | solution.py:128
  15.7 0.6 %collective-permute-start.6 = (bf16[48,8,128]{2,1,0:T(8,128)(2,1)S(1)}, bf16[48,8,128]{2,1,0:T(8,128)(2,1)S(1)}, u32[]{:S(2)}, u32[]{:S(2)}) collective-permute-start(bf16[48,8,128]{2,1,0:T(8,128)(2,1)S(1)} %get-tuple-element.8), channel_id=1, source_target_pairs={{0,1},{1,0},{2,3},{3,2},{4,5},{5,4},{6,7},{7,6},{8,9},{9,8},{10,11... | collective-permute-start | bytes 294920 | tf_op jit(solution)/shard_map/ppermute | solution.py:93
  16.2 8.5 %collective-permute-start.7 = (bf16[48,8,128]{2,1,0:T(8,128)(2,1)S(1)}, bf16[48,8,128]{2,1,0:T(8,128)(2,1)S(1)}, u32[]{:S(2)}, u32[]{:S(2)}) collective-permute-start(bf16[48,8,128]{2,1,0:T(8,128)(2,1)S(1)} %get-tuple-element.7), channel_id=1, source_target_pairs={{0,2},{1,3},{2,0},{3,1},{4,6},{5,7},{6,4},{7,5},{8,10},{9,11},{10,... | collective-permute-start | bytes 294920 | tf_op jit(solution)/shard_map/ppermute | solution.py:93
  24.8 0.5 %collective-permute-done.4 = bf16[48,8,128]{2,1,0:T(8,128)(2,1)S(1)} collective-permute-done((bf16[48,8,128]{2,1,0:T(8,128)(2,1)S(1)}, bf16[48,8,128]{2,1,0:T(8,128)(2,1)S(1)}, u32[]{:S(2)}, u32[]{:S(2)}) %collective-permute-start.4) | collective-permute-done | bytes 98336 | tf_op jit(solution)/shard_map/ppermute | solution.py:93
  25.3 0.3 fusion.45
  25.8 5.7 %collective-permute-done.7 = bf16[48,8,128]{2,1,0:T(8,128)(2,1)S(1)} collective-permute-done((bf16[48,8,128]{2,1,0:T(8,128)(2,1)S(1)}, bf16[48,8,128]{2,1,0:T(8,128)(2,1)S(1)}, u32[]{:S(2)}, u32[]{:S(2)}) %collective-permute-start.7) | collective-permute-done | bytes 98336 | tf_op jit(solution)/shard_map/ppermute | solution.py:93
  31.5 0.6 %multiply_reduce_fusion = (f32[48,32]{1,0:T(8,128)S(1)}, bf16[48,32,128]{2,1,0:T(8,128)(2,1)S(1)}) fusion(f32[48,32]{1,0:T(8,128)S(1)} %fusion.3, bf16[48,8,128]{2,1,0:T(8,128)(2,1)S(1)} %collective-permute-done.8, bf16[48,8,128]{2,1,0:T(8,128)(2,1)S(1)} %collective-permute-done.7, bf16[48,8,128]{2,1,0:T(8,128)(2,1)S(1)} %collective-permute-done.6, ...), kind=kOutput, calls=%fused_computation.6 | convolution fusion | flops 15235584 | bytes 1001472 | tf_op jit(solution)/shard_map/iqk,ikd->iqd/dot_general | solution.py:24
  32.5 2.7 %collective-permute-start.10 = (f32[1,8,64]{2,1,0:T(8,128)S(1)}, f32[1,8,64]{2,1,0:T(8,128)S(1)}, u32[]{:S(2)}, u32[]{:S(2)}) collective-permute-start(f32[1,8,64]{2,1,0:T(8,128)S(1)} %get-tuple-element.22), channel_id=1, source_target_pairs={{0,2},{1,3},{2,0},{3,1},{4,6},{5,7},{6,4},{7,5},{8,10},{9,11},{10,... | collective-permute-start | bytes 6152 | tf_op jit(solution)/shard_map/ppermute | solution.py:42
  35.2 1.3 %collective-permute-start.11 = (f32[1,8,64]{2,1,0:T(8,128)S(1)}, f32[1,8,64]{2,1,0:T(8,128)S(1)}, u32[]{:S(2)}, u32[]{:S(2)}) collective-permute-start(f32[1,8,64]{2,1,0:T(8,128)S(1)} %get-tuple-element.21), channel_id=1, source_target_pairs={{0,3},{1,2},{2,1},{3,0},{4,7},{5,6},{6,5},{7,4},{8,11},{9,10},{10,... | collective-permute-start | bytes 6152 | tf_op jit(solution)/shard_map/ppermute | solution.py:42
  36.5 0.5 %collective-permute-done.10 = f32[1,8,64]{2,1,0:T(8,128)S(1)} collective-permute-done((f32[1,8,64]{2,1,0:T(8,128)S(1)}, f32[1,8,64]{2,1,0:T(8,128)S(1)}, u32[]{:S(2)}, u32[]{:S(2)}) %collective-permute-start.10) | collective-permute-done | bytes 2080 | tf_op jit(solution)/shard_map/ppermute | solution.py:42
  37.1 3.5 %collective-permute-done.11 = f32[1,8,64]{2,1,0:T(8,128)S(1)} collective-permute-done((f32[1,8,64]{2,1,0:T(8,128)S(1)}, f32[1,8,64]{2,1,0:T(8,128)S(1)}, u32[]{:S(2)}, u32[]{:S(2)}) %collective-permute-start.11) | collective-permute-done | bytes 2080 | tf_op jit(solution)/shard_map/ppermute | solution.py:42
  40.7 1.6 %collective-permute-start.13 = (f32[8,64]{1,0:T(8,128)S(1)}, f32[8,64]{1,0:T(8,128)S(1)}, u32[]{:S(2)}, u32[]{:S(2)}) collective-permute-start(f32[8,64]{1,0:T(8,128)S(1)} %bitcast_add_fusion), channel_id=1, source_target_pairs={{0,8},{4,12},{8,0},{12,4},{1,9},{5,13},{9,1},{13,5},{2,10},{6,14},... | collective-permute-start | bytes 6152 | tf_op jit(solution)/shard_map/ppermute | solution.py:58
  42.6 0.7 %copy-done.3 = f32[64,8]{0,1:T(8,128)S(1)} copy-done((f32[64,8]{0,1:T(8,128)S(1)}, f32[64,8]{0,1:T(8,128)}, u32[]{:S(2)}) %copy-start.3) | copy-done | bytes 2072
  43.3 1.1 %collective-permute-done.13 = f32[8,64]{1,0:T(8,128)S(1)} collective-permute-done((f32[8,64]{1,0:T(8,128)S(1)}, f32[8,64]{1,0:T(8,128)S(1)}, u32[]{:S(2)}, u32[]{:S(2)}) %collective-permute-start.13) | collective-permute-done | bytes 2080 | tf_op jit(solution)/shard_map/ppermute | solution.py:58
  44.4 0.9 %collective-permute-done.14 = f32[8,64]{1,0:T(8,128)S(1)} collective-permute-done((f32[8,64]{1,0:T(8,128)S(1)}, f32[8,64]{1,0:T(8,128)S(1)}, u32[]{:S(2)}, u32[]{:S(2)}) %collective-permute-start.14) | collective-permute-done | bytes 2080 | tf_op jit(solution)/shard_map/ppermute | solution.py:58
  45.3 0.6 %add_bitcast_fusion = f32[4,64,8]{1,2,0:T(8,128)} fusion(f32[4,8,64]{2,1,0:T(8,128)S(1)} %maximum_add_fusion, f32[8,64]{1,0:T(8,128)S(1)} %select_add_fusion), kind=kLoop, calls=%fused_computation.55 | loop fusion | flops 2048 | bytes 18432 | tf_op jit(solution)/shard_map/transpose | solution.py:60
  (42 shorter events, 1.4 us)
Async XLA Ops:
  0.0 32.2 %copy-start = (bf16[64,3072]{1,0:T(8,128)(2,1)S(1)}, bf16[64,3072]{1,0:T(8,128)(2,1)}, u32[]{:S(2)}) copy-start(bf16[64,3072]{1,0:T(8,128)(2,1)} %param.13) | copy-start | bytes 1179652
  0.0 6.8 %copy-start.1 = (bf16[4,2,24,8,128]{4,3,2,1,0:T(8,128)(2,1)S(1)}, bf16[4,2,24,8,128]{4,3,2,1,0:T(8,128)(2,1)}, u32[]{:S(2)}) copy-start(bf16[4,2,24,8,128]{4,3,2,1,0:T(8,128)(2,1)} %param.10) | copy-start | bytes 1179652
  1.1 14.4 %collective-permute-start = (bf16[48,8,128]{2,1,0:T(8,128)(2,1)S(1)}, bf16[48,8,128]{2,1,0:T(8,128)(2,1)S(1)}, u32[]{:S(2)}, u32[]{:S(2)}) collective-permute-start(bf16[48,8,128]{2,1,0:T(8,128)(2,1)S(1)} %get-tuple-element.16), channel_id=1, source_target_pairs={{0,1},{1,0},{2,3},{3,2},{4,5},{5,4},{6,7},{7,6},{8,9},{9,8},{10,11... | collective-permute-start | bytes 294920 | tf_op jit(solution)/shard_map/ppermute | solution.py:93
  4.2 11.4 %collective-permute-start.1 = (bf16[48,8,128]{2,1,0:T(8,128)(2,1)S(1)}, bf16[48,8,128]{2,1,0:T(8,128)(2,1)S(1)}, u32[]{:S(2)}, u32[]{:S(2)}) collective-permute-start(bf16[48,8,128]{2,1,0:T(8,128)(2,1)S(1)} %get-tuple-element.15), channel_id=1, source_target_pairs={{0,2},{1,3},{2,0},{3,1},{4,6},{5,7},{6,4},{7,5},{8,10},{9,11},{10,... | collective-permute-start | bytes 294920 | tf_op jit(solution)/shard_map/ppermute | solution.py:93
  6.8 9.4 %collective-permute-start.2 = (bf16[48,8,128]{2,1,0:T(8,128)(2,1)S(1)}, bf16[48,8,128]{2,1,0:T(8,128)(2,1)S(1)}, u32[]{:S(2)}, u32[]{:S(2)}) collective-permute-start(bf16[48,8,128]{2,1,0:T(8,128)(2,1)S(1)} %get-tuple-element.14), channel_id=1, source_target_pairs={{0,3},{1,2},{2,1},{3,0},{4,7},{5,6},{6,5},{7,4},{8,11},{9,10},{10,... | collective-permute-start | bytes 294920 | tf_op jit(solution)/shard_map/ppermute | solution.py:93
  6.8 4.5 %copy-start.4 = (f32[1000]{0:T(1024)S(1)}, f32[1000]{0:T(1024)}, u32[]{:S(2)}) copy-start(f32[1000]{0:T(1024)} %param.16) | copy-start | bytes 12004
  6.8 8.8 %copy-start.2 = (bf16[4,2,24,8,128]{4,3,2,1,0:T(8,128)(2,1)S(1)}, bf16[4,2,24,8,128]{4,3,2,1,0:T(8,128)(2,1)}, u32[]{:S(2)}) copy-start(bf16[4,2,24,8,128]{4,3,2,1,0:T(8,128)(2,1)} %param.11) | copy-start | bytes 1179652
  6.9 4.4 %copy-start.5 = (s32[4]{0:T(128)S(1)}, s32[4]{0:T(128)}, u32[]{:S(2)}) copy-start(s32[4]{0:T(128)} %param.17) | copy-start | bytes 52
  6.9 17.9 %collective-permute-start.3 = (bf16[48,8,128]{2,1,0:T(8,128)(2,1)S(1)}, bf16[48,8,128]{2,1,0:T(8,128)(2,1)S(1)}, u32[]{:S(2)}, u32[]{:S(2)}) collective-permute-start(bf16[48,8,128]{2,1,0:T(8,128)(2,1)S(1)} %get-tuple-element.12), channel_id=1, source_target_pairs={{0,1},{1,0},{2,3},{3,2},{4,5},{5,4},{6,7},{7,6},{8,9},{9,8},{10,11... | collective-permute-start | bytes 294920 | tf_op jit(solution)/shard_map/ppermute | solution.py:93
  7.8 17.4 %collective-permute-start.4 = (bf16[48,8,128]{2,1,0:T(8,128)(2,1)S(1)}, bf16[48,8,128]{2,1,0:T(8,128)(2,1)S(1)}, u32[]{:S(2)}, u32[]{:S(2)}) collective-permute-start(bf16[48,8,128]{2,1,0:T(8,128)(2,1)S(1)} %get-tuple-element.11), channel_id=1, source_target_pairs={{0,2},{1,3},{2,0},{3,1},{4,6},{5,7},{6,4},{7,5},{8,10},{9,11},{10,... | collective-permute-start | bytes 294920 | tf_op jit(solution)/shard_map/ppermute | solution.py:93
  12.8 0.7 %copy-start.6 = (f32[8]{0:T(128)S(1)}, f32[8]{0:T(128)}, u32[]{:S(2)}) copy-start(f32[8]{0:T(128)} %param.14) | copy-start | bytes 100
  15.5 9.7 %collective-permute-start.5 = (bf16[48,8,128]{2,1,0:T(8,128)(2,1)S(1)}, bf16[48,8,128]{2,1,0:T(8,128)(2,1)S(1)}, u32[]{:S(2)}, u32[]{:S(2)}) collective-permute-start(bf16[48,8,128]{2,1,0:T(8,128)(2,1)S(1)} %get-tuple-element.10), channel_id=1, source_target_pairs={{0,3},{1,2},{2,1},{3,0},{4,7},{5,6},{6,5},{7,4},{8,11},{9,10},{10,... | collective-permute-start | bytes 294920 | tf_op jit(solution)/shard_map/ppermute | solution.py:93
  15.7 10.2 %collective-permute-start.6 = (bf16[48,8,128]{2,1,0:T(8,128)(2,1)S(1)}, bf16[48,8,128]{2,1,0:T(8,128)(2,1)S(1)}, u32[]{:S(2)}, u32[]{:S(2)}) collective-permute-start(bf16[48,8,128]{2,1,0:T(8,128)(2,1)S(1)} %get-tuple-element.8), channel_id=1, source_target_pairs={{0,1},{1,0},{2,3},{3,2},{4,5},{5,4},{6,7},{7,6},{8,9},{9,8},{10,11... | collective-permute-start | bytes 294920 | tf_op jit(solution)/shard_map/ppermute | solution.py:93
  16.2 15.3 %collective-permute-start.7 = (bf16[48,8,128]{2,1,0:T(8,128)(2,1)S(1)}, bf16[48,8,128]{2,1,0:T(8,128)(2,1)S(1)}, u32[]{:S(2)}, u32[]{:S(2)}) collective-permute-start(bf16[48,8,128]{2,1,0:T(8,128)(2,1)S(1)} %get-tuple-element.7), channel_id=1, source_target_pairs={{0,2},{1,3},{2,0},{3,1},{4,6},{5,7},{6,4},{7,5},{8,10},{9,11},{10,... | collective-permute-start | bytes 294920 | tf_op jit(solution)/shard_map/ppermute | solution.py:93
  24.8 6.7 %collective-permute-start.8 = (bf16[48,8,128]{2,1,0:T(8,128)(2,1)S(1)}, bf16[48,8,128]{2,1,0:T(8,128)(2,1)S(1)}, u32[]{:S(2)}, u32[]{:S(2)}) collective-permute-start(bf16[48,8,128]{2,1,0:T(8,128)(2,1)S(1)} %get-tuple-element.6), channel_id=1, source_target_pairs={{0,3},{1,2},{2,1},{3,0},{4,7},{5,6},{6,5},{7,4},{8,11},{9,10},{10,... | collective-permute-start | bytes 294920 | tf_op jit(solution)/shard_map/ppermute | solution.py:93
  32.5 4.6 %collective-permute-start.10 = (f32[1,8,64]{2,1,0:T(8,128)S(1)}, f32[1,8,64]{2,1,0:T(8,128)S(1)}, u32[]{:S(2)}, u32[]{:S(2)}) collective-permute-start(f32[1,8,64]{2,1,0:T(8,128)S(1)} %get-tuple-element.22), channel_id=1, source_target_pairs={{0,2},{1,3},{2,0},{3,1},{4,6},{5,7},{6,4},{7,5},{8,10},{9,11},{10,... | collective-permute-start | bytes 6152 | tf_op jit(solution)/shard_map/ppermute | solution.py:42
  35.2 5.4 %collective-permute-start.11 = (f32[1,8,64]{2,1,0:T(8,128)S(1)}, f32[1,8,64]{2,1,0:T(8,128)S(1)}, u32[]{:S(2)}, u32[]{:S(2)}) collective-permute-start(f32[1,8,64]{2,1,0:T(8,128)S(1)} %get-tuple-element.21), channel_id=1, source_target_pairs={{0,3},{1,2},{2,1},{3,0},{4,7},{5,6},{6,5},{7,4},{8,11},{9,10},{10,... | collective-permute-start | bytes 6152 | tf_op jit(solution)/shard_map/ppermute | solution.py:42
  36.5 4.1 %collective-permute-start.9 = (f32[1,8,64]{2,1,0:T(8,128)S(1)}, f32[1,8,64]{2,1,0:T(8,128)S(1)}, u32[]{:S(2)}, u32[]{:S(2)}) collective-permute-start(f32[1,8,64]{2,1,0:T(8,128)S(1)} %get-tuple-element.20), channel_id=1, source_target_pairs={{0,1},{1,0},{2,3},{3,2},{4,5},{5,4},{6,7},{7,6},{8,9},{9,8},{10,11... | collective-permute-start | bytes 6152 | tf_op jit(solution)/shard_map/ppermute | solution.py:42
  40.6 2.7 %collective-permute-start.12 = (f32[8,64]{1,0:T(8,128)S(1)}, f32[8,64]{1,0:T(8,128)S(1)}, u32[]{:S(2)}, u32[]{:S(2)}) collective-permute-start(f32[8,64]{1,0:T(8,128)S(1)} %bitcast_add_fusion), channel_id=1, source_target_pairs={{0,4},{4,0},{8,12},{12,8},{1,5},{5,1},{9,13},{13,9},{2,6},{6,2},{1... | collective-permute-start | bytes 6152 | tf_op jit(solution)/shard_map/ppermute | solution.py:58
  40.7 3.7 %collective-permute-start.13 = (f32[8,64]{1,0:T(8,128)S(1)}, f32[8,64]{1,0:T(8,128)S(1)}, u32[]{:S(2)}, u32[]{:S(2)}) collective-permute-start(f32[8,64]{1,0:T(8,128)S(1)} %bitcast_add_fusion), channel_id=1, source_target_pairs={{0,8},{4,12},{8,0},{12,4},{1,9},{5,13},{9,1},{13,5},{2,10},{6,14},... | collective-permute-start | bytes 6152 | tf_op jit(solution)/shard_map/ppermute | solution.py:58
  42.2 3.0 %collective-permute-start.14 = (f32[8,64]{1,0:T(8,128)S(1)}, f32[8,64]{1,0:T(8,128)S(1)}, u32[]{:S(2)}, u32[]{:S(2)}) collective-permute-start(f32[8,64]{1,0:T(8,128)S(1)} %bitcast_add_fusion), channel_id=1, source_target_pairs={{0,12},{4,8},{8,4},{12,0},{1,13},{5,9},{9,5},{13,1},{2,14},{6,10},... | collective-permute-start | bytes 6152 | tf_op jit(solution)/shard_map/ppermute | solution.py:58
  42.6 0.7 %copy-start.3 = (f32[64,8]{0,1:T(8,128)S(1)}, f32[64,8]{0,1:T(8,128)}, u32[]{:S(2)}) copy-start(f32[64,8]{0,1:T(8,128)} %param.12) | copy-start | bytes 6148

commit v12 on v11

--- a/solution.py
+++ b/solution.py
@@ -27,6 +27,31 @@
 
 def xor_pairs(size, k):
     return [(i, i ^ k) for i in range(size)]
+
+
+def gather_all_prefix(update, start, me, groups, step_dev, steps_axis, partner_order):
+    local_steps = update.shape[0]
+    if partner_order:
+        natural = jnp.take(update, me ^ jnp.arange(groups, dtype=jnp.int32), axis=1)
+    else:
+        natural = update
+    blocks = jnp.transpose(natural, (1, 0, 2, 3))
+    sent = jnp.broadcast_to(blocks[None], (steps_axis,) + blocks.shape)
+    sent = sent.reshape((steps_axis * groups,) + blocks.shape[1:])
+    got = lax.all_to_all(sent, ("step", "seq"), split_axis=0, concat_axis=0, tiled=True)
+    position = lax.axis_index("step")
+    zero = jnp.zeros((), jnp.float32)
+    outs = []
+    for s in range(step_dev):
+        acc = None
+        for src in range(steps_axis * groups):
+            for t in range(local_steps):
+                step_of = (src // groups) * step_dev + (src % groups) * local_steps + t
+                term = jnp.where(step_of <= position * step_dev + s, got[src, t], zero)
+                acc = term if acc is None else acc + term
+        outs.append(acc)
+    local = jnp.stack(outs) + start[None]
+    return jnp.transpose(local, (0, 2, 1))
 
 
 def gather_prefix(update, start, me, groups, step_dev, steps_axis, partner_order):
@@ -132,7 +157,7 @@
         guided = drift[:, 1] + scale_full * (drift[:, 0] - drift[:, 1])
         update = len_full * guided
         update = update.reshape(local_steps, groups, tok_dev, channels)
-        return gather_prefix(
+        return gather_all_prefix(
             update, start_t, me, groups, step_dev, steps_axis, partner_order
         )
 

time: 46.1 us -> 48.2 us (1.046)
  starting transfers between devices: 25.3 us -> 22.1 us
  local copies, waits for them, and re-layouts: 3.94 us -> 6.29 us
  waiting for transfers between devices: 12.3 us -> 14.1 us
  other arithmetic: 2.39 us -> 3.22 us
    all_to_all x0 -> x1, waiting for transfers between devices: none -> 6.39 us  [gather_all_prefix(): lax.all_to_all(sent, ('step', 'seq'), split_axis=0, concat_axis=0, tiled=...]
    ppermute x6 -> x0, waiting for transfers between devices: 6.06 us -> none  [the longest x3 4.05 us: gather_prefix(): pieces.append(lax.ppermute(ordered[:, k], 'seq', xor_pairs(groups, k)))]
    ppermute x6 -> x0, starting transfers between devices: 5.98 us -> none  [the longest x3 4.04 us: gather_prefix(): pieces.append(lax.ppermute(ordered[:, k], 'seq', xor_pairs(groups, k)))]
    all_to_all x0 -> x1, starting transfers between devices: none -> 4.94 us  [gather_all_prefix(): lax.all_to_all(sent, ('step', 'seq'), split_axis=0, concat_axis=0, tiled=...]
    ppermute x9, starting transfers between devices: 19.3 us -> 17.2 us  [on_device(): pieces = [lax.ppermute(p, 'seq', xor_pairs(groups, k)) for p in pieces]]
    ppermute x9, waiting for transfers between devices: 6.19 us -> 7.73 us  [on_device(): pieces = [lax.ppermute(p, 'seq', xor_pairs(groups, k)) for p in pieces]]
    unnamed x14 -> x16, local copies, waits for them, and re-layouts: 1.35 us -> 2.7 us
    all_to_all x0 -> x1, other arithmetic: none -> 0.72 us  [gather_all_prefix(): lax.all_to_all(sent, ('step', 'seq'), split_axis=0, concat_axis=0, tiled=...]
  transfers between devices with their start and end apart: 15 -> 10, of which waited for: 6 -> 3; matrix products, arithmetic and copies ran while one was open for 8% -> 7% of each run, Pallas kernels for 0% -> 0%
where the time goes in v12:
time: 48.2 us; the launch traced here: 47.9 us
  starting transfers between devices  22.1 us (46%)
  waiting for transfers between devices  14.1 us (29%)
  local copies, waits for them, and re-layouts  6.29 us (13%)
  other arithmetic  3.22 us (7%)
  matrix products  1.25 us (3%)
  between operations  0.92 us (2%)
    ppermute x9, starting transfers between devices, on_device(): pieces = [lax.ppermute(p, 'seq', xor_pairs(groups, k)) for p in pieces]  17.2 us
    ppermute x9, waiting for transfers between devices, on_device(): pieces = [lax.ppermute(p, 'seq', xor_pairs(groups, k)) for p in pieces]  7.73 us
    all_to_all x1, waiting for transfers between devices, gather_all_prefix(): lax.all_to_all(sent, ('step', 'seq'), split_axis=0, concat_axis=0, tiled=...  6.39 us
    all_to_all x1, starting transfers between devices, gather_all_prefix(): lax.all_to_all(sent, ('step', 'seq'), split_axis=0, concat_axis=0, tiled=...  4.94 us
    unnamed x16, local copies, waits for them, and re-layouts  2.7 us
    another operation x2, local copies, waits for them, and re-layouts, on_device(): jnp.stack([jnp.broadcast_to(guide_scale, shape), jnp.broadcast_to(len_ful...  1.32 us
    squeeze x3, local copies, waits for them, and re-layouts, on_device(): lax.dynamic_index_in_dim(c, me ^ k, 0, keepdims=False)  1.21 us
  transfers between devices with their start and end apart: 10, of which 3 were waited for; matrix products, arithmetic and copies ran while one was open for 7% of the time, Pallas kernels for 0%

profile of v12, /device:TPU:0, one launch (start us, length us, event | category | flops | bytes accessed | tf_op | source)
XLA Modules:
  0.0 47.9 jit_solution(6852017554675319061)
XLA Ops:
  0.0 1.1 %dynamic-slice_bitcast_fusion.11 = (bf16[48,8,128]{2,1,0:T(8,128)(2,1)S(1)}, bf16[48,8,128]{2,1,0:T(8,128)(2,1)S(1)}, bf16[48,8,128]{2,1,0:T(8,128)(2,1)S(1)}, bf16[48,8,128]{2,1,0:T(8,128)(2,1)S(1)}) fusion(bf16[4,48,8,128]{3,2,1,0:T(8,128)(2,1)} %bitcast.92, s32[]{:T(128)S(6)} %select_n.1078, s32[]{:T(128)S(6)} %select_n.1081, s32[]{:T(128)S(6)} %select_n.1080, ...), kind=kLoop, calls=%fused_computation.46 | loop fusion | bytes 786448 | tf_op jit(solution)/shard_map/jit(dynamic_index_in_dim)/squeeze | solution.py:116
  1.1 3.1 %collective-permute-start = (bf16[48,8,128]{2,1,0:T(8,128)(2,1)S(1)}, bf16[48,8,128]{2,1,0:T(8,128)(2,1)S(1)}, u32[]{:S(2)}, u32[]{:S(2)}) collective-permute-start(bf16[48,8,128]{2,1,0:T(8,128)(2,1)S(1)} %get-tuple-element.16), channel_id=1, source_target_pairs={{0,1},{1,0},{2,3},{3,2},{4,5},{5,4},{6,7},{7,6},{8,9},{9,8},{10,11... | collective-permute-start | bytes 294920 | tf_op jit(solution)/shard_map/ppermute | solution.py:118
  4.2 2.6 %collective-permute-start.1 = (bf16[48,8,128]{2,1,0:T(8,128)(2,1)S(1)}, bf16[48,8,128]{2,1,0:T(8,128)(2,1)S(1)}, u32[]{:S(2)}, u32[]{:S(2)}) collective-permute-start(bf16[48,8,128]{2,1,0:T(8,128)(2,1)S(1)} %get-tuple-element.15), channel_id=1, source_target_pairs={{0,2},{1,3},{2,0},{3,1},{4,6},{5,7},{6,4},{7,5},{8,10},{9,11},{10,... | collective-permute-start | bytes 294920 | tf_op jit(solution)/shard_map/ppermute | solution.py:118
  6.9 1.0 %collective-permute-start.3 = (bf16[48,8,128]{2,1,0:T(8,128)(2,1)S(1)}, bf16[48,8,128]{2,1,0:T(8,128)(2,1)S(1)}, u32[]{:S(2)}, u32[]{:S(2)}) collective-permute-start(bf16[48,8,128]{2,1,0:T(8,128)(2,1)S(1)} %get-tuple-element.12), channel_id=1, source_target_pairs={{0,1},{1,0},{2,3},{3,2},{4,5},{5,4},{6,7},{7,6},{8,9},{9,8},{10,11... | collective-permute-start | bytes 294920 | tf_op jit(solution)/shard_map/ppermute | solution.py:118
  7.8 3.5 %collective-permute-start.4 = (bf16[48,8,128]{2,1,0:T(8,128)(2,1)S(1)}, bf16[48,8,128]{2,1,0:T(8,128)(2,1)S(1)}, u32[]{:S(2)}, u32[]{:S(2)}) collective-permute-start(bf16[48,8,128]{2,1,0:T(8,128)(2,1)S(1)} %get-tuple-element.11), channel_id=1, source_target_pairs={{0,2},{1,3},{2,0},{3,1},{4,6},{5,7},{6,4},{7,5},{8,10},{9,11},{10,... | collective-permute-start | bytes 294920 | tf_op jit(solution)/shard_map/ppermute | solution.py:118
  11.4 0.6 %copy-done.4 = f32[1000]{0:T(1024)S(1)} copy-done((f32[1000]{0:T(1024)S(1)}, f32[1000]{0:T(1024)}, u32[]{:S(2)}) %copy-start.4) | copy-done | bytes 4024
  12.2 0.6 %fusion.36 = f32[]{:T(128)} fusion(f32[4]{0:T(128)S(1)} %select_reduce_fusion, s32[]{:T(128)S(6)} %axis_index.25), kind=kLoop, calls=%fused_computation.73 | loop fusion | flops 11 | bytes 24 | tf_op jit(solution)/shard_map/reduce_sum | solution.py:148
  13.5 0.6 %copy-done.6 = f32[8]{0:T(128)S(1)} copy-done((f32[8]{0:T(128)S(1)}, f32[8]{0:T(128)}, u32[]{:S(2)}) %copy-start.6) | copy-done | bytes 56
  14.1 0.7 %fusion.35 = f32[]{:T(128)} fusion(f32[8]{0:T(128)S(1)} %copy-done.6, s32[]{:T(128)} %bitcast.91), kind=kLoop, calls=%fused_computation.72 | loop fusion | flops 23 | bytes 40 | tf_op jit(solution)/shard_map/reduce_sum | solution.py:13
  14.8 1.2 %stack.12 = f32[2]{0:T(128)S(1)} pad(f32[1]{0:T(128)} %bitcast.1, f32[]{:T(128)} %fusion.36), padding=0_1 | pad | bytes 16 | tf_op jit(solution)/shard_map/stack | solution.py:153
  16.1 0.4 collective-permute-start.5
  16.8 6.4 %collective-permute-start.7 = (bf16[48,8,128]{2,1,0:T(8,128)(2,1)S(1)}, bf16[48,8,128]{2,1,0:T(8,128)(2,1)S(1)}, u32[]{:S(2)}, u32[]{:S(2)}) collective-permute-start(bf16[48,8,128]{2,1,0:T(8,128)(2,1)S(1)} %get-tuple-element.7), channel_id=1, source_target_pairs={{0,2},{1,3},{2,0},{3,1},{4,6},{5,7},{6,4},{7,5},{8,10},{9,11},{10,... | collective-permute-start | bytes 294920 | tf_op jit(solution)/shard_map/ppermute | solution.py:118
  23.2 2.0 %collective-permute-done.4 = bf16[48,8,128]{2,1,0:T(8,128)(2,1)S(1)} collective-permute-done((bf16[48,8,128]{2,1,0:T(8,128)(2,1)S(1)}, bf16[48,8,128]{2,1,0:T(8,128)(2,1)S(1)}, u32[]{:S(2)}, u32[]{:S(2)}) %collective-permute-start.4) | collective-permute-done | bytes 98336 | tf_op jit(solution)/shard_map/ppermute | solution.py:118
  25.3 0.3 fusion.40
  25.8 5.7 %collective-permute-done.7 = bf16[48,8,128]{2,1,0:T(8,128)(2,1)S(1)} collective-permute-done((bf16[48,8,128]{2,1,0:T(8,128)(2,1)S(1)}, bf16[48,8,128]{2,1,0:T(8,128)(2,1)S(1)}, u32[]{:S(2)}, u32[]{:S(2)}) %collective-permute-start.7) | collective-permute-done | bytes 98336 | tf_op jit(solution)/shard_map/ppermute | solution.py:118
  31.5 0.6 %multiply_reduce_fusion = (f32[48,32]{1,0:T(8,128)S(1)}, bf16[48,32,128]{2,1,0:T(8,128)(2,1)S(1)}) fusion(f32[48,32]{1,0:T(8,128)S(1)} %fusion.3, bf16[48,8,128]{2,1,0:T(8,128)(2,1)S(1)} %collective-permute-done.8, bf16[48,8,128]{2,1,0:T(8,128)(2,1)S(1)} %collective-permute-done.7, bf16[48,8,128]{2,1,0:T(8,128)(2,1)S(1)} %collective-permute-done.6, ...), kind=kOutput, calls=%fused_computation.7 | convolution fusion | flops 15235584 | bytes 1001472 | tf_op jit(solution)/shard_map/iqk,ikd->iqd/dot_general | solution.py:24
  32.5 0.6 %gather_fusion = f32[4,8,64]{2,1,0:T(8,128)S(1)} fusion(f32[4,8,64]{2,1,0:T(8,128)S(1)} %fusion.33, s32[1024]{0:T(1024)S(1)} %pad_clamp_fusion), kind=kCustom, calls=%fused_computation | custom fusion | bytes 16400 | tf_op jit(solution)/shard_map/jit(_take)/gather | solution.py:35
  33.1 0.7 %reshape.1249 = f32[16,1,512]{2,1,0:T(1,128)} reshape(f32[16,1,8,64]{3,2,1,0:T(8,128)S(1)} %bitcast.95) | data formatting | bytes 65536
  33.8 4.9 %all-to-all-start = ((f32[16,1,512]{2,1,0:T(1,128)}), f32[16,1,512]{2,1,0:T(1,128)S(1)}, u32[]{:S(2)}, u32[]{:S(2)}) async-start(f32[16,1,512]{2,1,0:T(1,128)} %reshape.1249), calls=%async_computation | async-start | bytes 65536 | tf_op jit(solution)/shard_map/all_to_all | solution.py:41
  38.9 6.4 %all-to-all-done = f32[16,1,512]{2,1,0:T(1,128)S(1)} async-done(((f32[16,1,512]{2,1,0:T(1,128)}), f32[16,1,512]{2,1,0:T(1,128)S(1)}, u32[]{:S(2)}, u32[]{:S(2)}) %all-to-all-start) | async-done | bytes 32800 | tf_op jit(solution)/shard_map/all_to_all | solution.py:41
  45.3 0.5 %broadcast.1266 = f32[]{:T(128)} broadcast(f32[]{:T(128)} %constant.188), dimensions={} | broadcast | bytes 8 | tf_op jit(solution)/shard_map/all_to_all | solution.py:41
  45.8 0.7 %reduce.6 = f32[16,512]{1,0:T(8,128)S(1)} reduce(f32[16,1,512]{2,1,0:T(1,128)S(1)} %all-to-all-done, f32[]{:T(128)} %broadcast.1266), dimensions={1}, to_apply=%all_to_all.3.reduce_sub_computation | reduce | bytes 65540 | tf_op jit(solution)/shard_map/all_to_all | solution.py:41
  46.7 0.6 %copy-done.3 = f32[64,8]{0,1:T(8,128)S(1)} copy-done((f32[64,8]{0,1:T(8,128)S(1)}, f32[64,8]{0,1:T(8,128)}, u32[]{:S(2)}) %copy-start.3) | copy-done | bytes 2072
  47.3 0.6 %fusion.34 = f32[4,64,8]{1,2,0:T(8,128)} fusion(f32[1,8,64]{2,1,0:T(8,128)S(1)} %add_bitcast_fusion, f32[1,8,64]{2,1,0:T(8,128)S(1)} %add_bitcast_fusion.1, f32[1,8,64]{2,1,0:T(8,128)S(1)} %add_bitcast_fusion.2, f32[1,8,64]{2,1,0:T(8,128)S(1)} %add_bitcast_fusion.3, f32[8,64]{1,0:T(8,128)S(1)} %bitcast.97), kind=kLoop, calls=%fused_computation.57 | loop fusion | flops 8192 | bytes 18432 | tf_op jit(solution)/shard_map/transpose | solution.py:54
  (40 shorter events, 1.5 us)
Async XLA Ops:
  0.0 32.2 %copy-start = (bf16[64,3072]{1,0:T(8,128)(2,1)S(1)}, bf16[64,3072]{1,0:T(8,128)(2,1)}, u32[]{:S(2)}) copy-start(bf16[64,3072]{1,0:T(8,128)(2,1)} %param.13) | copy-start | bytes 1179652
  0.0 6.8 %copy-start.1 = (bf16[4,2,24,8,128]{4,3,2,1,0:T(8,128)(2,1)S(1)}, bf16[4,2,24,8,128]{4,3,2,1,0:T(8,128)(2,1)}, u32[]{:S(2)}) copy-start(bf16[4,2,24,8,128]{4,3,2,1,0:T(8,128)(2,1)} %param.10) | copy-start | bytes 1179652
  1.1 15.0 %collective-permute-start = (bf16[48,8,128]{2,1,0:T(8,128)(2,1)S(1)}, bf16[48,8,128]{2,1,0:T(8,128)(2,1)S(1)}, u32[]{:S(2)}, u32[]{:S(2)}) collective-permute-start(bf16[48,8,128]{2,1,0:T(8,128)(2,1)S(1)} %get-tuple-element.16), channel_id=1, source_target_pairs={{0,1},{1,0},{2,3},{3,2},{4,5},{5,4},{6,7},{7,6},{8,9},{9,8},{10,11... | collective-permute-start | bytes 294920 | tf_op jit(solution)/shard_map/ppermute | solution.py:118
  4.2 12.3 %collective-permute-start.1 = (bf16[48,8,128]{2,1,0:T(8,128)(2,1)S(1)}, bf16[48,8,128]{2,1,0:T(8,128)(2,1)S(1)}, u32[]{:S(2)}, u32[]{:S(2)}) collective-permute-start(bf16[48,8,128]{2,1,0:T(8,128)(2,1)S(1)} %get-tuple-element.15), channel_id=1, source_target_pairs={{0,2},{1,3},{2,0},{3,1},{4,6},{5,7},{6,4},{7,5},{8,10},{9,11},{10,... | collective-permute-start | bytes 294920 | tf_op jit(solution)/shard_map/ppermute | solution.py:118
  6.8 10.0 %collective-permute-start.2 = (bf16[48,8,128]{2,1,0:T(8,128)(2,1)S(1)}, bf16[48,8,128]{2,1,0:T(8,128)(2,1)S(1)}, u32[]{:S(2)}, u32[]{:S(2)}) collective-permute-start(bf16[48,8,128]{2,1,0:T(8,128)(2,1)S(1)} %get-tuple-element.14), channel_id=1, source_target_pairs={{0,3},{1,2},{2,1},{3,0},{4,7},{5,6},{6,5},{7,4},{8,11},{9,10},{10,... | collective-permute-start | bytes 294920 | tf_op jit(solution)/shard_map/ppermute | solution.py:118
  6.8 4.5 %copy-start.2 = (bf16[4,2,24,8,128]{4,3,2,1,0:T(8,128)(2,1)S(1)}, bf16[4,2,24,8,128]{4,3,2,1,0:T(8,128)(2,1)}, u32[]{:S(2)}) copy-start(bf16[4,2,24,8,128]{4,3,2,1,0:T(8,128)(2,1)} %param.11) | copy-start | bytes 1179652
  6.9 16.4 %collective-permute-start.3 = (bf16[48,8,128]{2,1,0:T(8,128)(2,1)S(1)}, bf16[48,8,128]{2,1,0:T(8,128)(2,1)S(1)}, u32[]{:S(2)}, u32[]{:S(2)}) collective-permute-start(bf16[48,8,128]{2,1,0:T(8,128)(2,1)S(1)} %get-tuple-element.12), channel_id=1, source_target_pairs={{0,1},{1,0},{2,3},{3,2},{4,5},{5,4},{6,7},{7,6},{8,9},{9,8},{10,11... | collective-permute-start | bytes 294920 | tf_op jit(solution)/shard_map/ppermute | solution.py:118
  7.8 17.5 %collective-permute-start.4 = (bf16[48,8,128]{2,1,0:T(8,128)(2,1)S(1)}, bf16[48,8,128]{2,1,0:T(8,128)(2,1)S(1)}, u32[]{:S(2)}, u32[]{:S(2)}) collective-permute-start(bf16[48,8,128]{2,1,0:T(8,128)(2,1)S(1)} %get-tuple-element.11), channel_id=1, source_target_pairs={{0,2},{1,3},{2,0},{3,1},{4,6},{5,7},{6,4},{7,5},{8,10},{9,11},{10,... | collective-permute-start | bytes 294920 | tf_op jit(solution)/shard_map/ppermute | solution.py:118
  11.3 0.7 %copy-start.4 = (f32[1000]{0:T(1024)S(1)}, f32[1000]{0:T(1024)}, u32[]{:S(2)}) copy-start(f32[1000]{0:T(1024)} %param.16) | copy-start | bytes 12004
  11.3 0.7 %copy-start.5 = (s32[4]{0:T(128)S(1)}, s32[4]{0:T(128)}, u32[]{:S(2)}) copy-start(s32[4]{0:T(128)} %param.17) | copy-start | bytes 52
  13.4 0.7 %copy-start.6 = (f32[8]{0:T(128)S(1)}, f32[8]{0:T(128)}, u32[]{:S(2)}) copy-start(f32[8]{0:T(128)} %param.14) | copy-start | bytes 100
  16.1 9.2 %collective-permute-start.5 = (bf16[48,8,128]{2,1,0:T(8,128)(2,1)S(1)}, bf16[48,8,128]{2,1,0:T(8,128)(2,1)S(1)}, u32[]{:S(2)}, u32[]{:S(2)}) collective-permute-start(bf16[48,8,128]{2,1,0:T(8,128)(2,1)S(1)} %get-tuple-element.10), channel_id=1, source_target_pairs={{0,3},{1,2},{2,1},{3,0},{4,7},{5,6},{6,5},{7,4},{8,11},{9,10},{10,... | collective-permute-start | bytes 294920 | tf_op jit(solution)/shard_map/ppermute | solution.py:118
  16.5 9.3 %collective-permute-start.6 = (bf16[48,8,128]{2,1,0:T(8,128)(2,1)S(1)}, bf16[48,8,128]{2,1,0:T(8,128)(2,1)S(1)}, u32[]{:S(2)}, u32[]{:S(2)}) collective-permute-start(bf16[48,8,128]{2,1,0:T(8,128)(2,1)S(1)} %get-tuple-element.8), channel_id=1, source_target_pairs={{0,1},{1,0},{2,3},{3,2},{4,5},{5,4},{6,7},{7,6},{8,9},{9,8},{10,11... | collective-permute-start | bytes 294920 | tf_op jit(solution)/shard_map/ppermute | solution.py:118
  16.8 14.7 %collective-permute-start.7 = (bf16[48,8,128]{2,1,0:T(8,128)(2,1)S(1)}, bf16[48,8,128]{2,1,0:T(8,128)(2,1)S(1)}, u32[]{:S(2)}, u32[]{:S(2)}) collective-permute-start(bf16[48,8,128]{2,1,0:T(8,128)(2,1)S(1)} %get-tuple-element.7), channel_id=1, source_target_pairs={{0,2},{1,3},{2,0},{3,1},{4,6},{5,7},{6,4},{7,5},{8,10},{9,11},{10,... | collective-permute-start | bytes 294920 | tf_op jit(solution)/shard_map/ppermute | solution.py:118
  23.2 8.3 %collective-permute-start.8 = (bf16[48,8,128]{2,1,0:T(8,128)(2,1)S(1)}, bf16[48,8,128]{2,1,0:T(8,128)(2,1)S(1)}, u32[]{:S(2)}, u32[]{:S(2)}) collective-permute-start(bf16[48,8,128]{2,1,0:T(8,128)(2,1)S(1)} %get-tuple-element.6), channel_id=1, source_target_pairs={{0,3},{1,2},{2,1},{3,0},{4,7},{5,6},{6,5},{7,4},{8,11},{9,10},{10,... | collective-permute-start | bytes 294920 | tf_op jit(solution)/shard_map/ppermute | solution.py:118
  33.8 11.4 %all-to-all-start = ((f32[16,1,512]{2,1,0:T(1,128)}), f32[16,1,512]{2,1,0:T(1,128)S(1)}, u32[]{:S(2)}, u32[]{:S(2)}) async-start(f32[16,1,512]{2,1,0:T(1,128)} %reshape.1249), calls=%async_computation | async-start | bytes 65536 | tf_op jit(solution)/shard_map/all_to_all | solution.py:41
  46.6 0.7 %copy-start.3 = (f32[64,8]{0,1:T(8,128)S(1)}, f32[64,8]{0,1:T(8,128)}, u32[]{:S(2)}) copy-start(f32[64,8]{0,1:T(8,128)} %param.12) | copy-start | bytes 6148

commit v13 on v11

--- a/solution.py
+++ b/solution.py
@@ -101,6 +101,12 @@
         gathered = lax.all_to_all(stacked, "seq", split_axis=0, concat_axis=3, tiled=True)
         gathered = gathered.reshape(3, per_dev, length, head_size)
         partner_order = False
+    if partner_order:
+        far_q, cfg_table, cfg_index, step_table, time_index = lax.optimization_barrier(
+            (arrived[groups - 1][0], cfg_table, cfg_index, step_table, time_index)
+        )
+        arrived[groups - 1][0] = far_q
+        gathered[0] = jnp.concatenate([arrived[k][0] for k in range(groups)], axis=1)
     heads_out = attend(gathered[0], gathered[1], gathered[2])
 
     weight_heads = out_weight.reshape(channels, heads, head_size)

time: 46.1 us -> 49.2 us (1.067)
  waiting for transfers between devices: 12.3 us -> 19.5 us
  starting transfers between devices: 25.3 us -> 20.6 us
  local copies, waits for them, and re-layouts: 3.94 us -> 4.55 us
    ppermute x9, waiting for transfers between devices: 6.19 us -> 13.3 us  [on_device(): pieces = [lax.ppermute(p, 'seq', xor_pairs(groups, k)) for p in pieces]]
    ppermute x9, starting transfers between devices: 19.3 us -> 14.1 us  [on_device(): pieces = [lax.ppermute(p, 'seq', xor_pairs(groups, k)) for p in pieces]]
    unnamed x14, local copies, waits for them, and re-layouts: 1.35 us -> 1.98 us
    ppermute x3, starting transfers between devices: 4.04 us -> 4.55 us  [gather_prefix(): pieces.append(lax.ppermute(ordered[:, k], 'seq', xor_pairs(groups, k)))]
  transfers between devices with their start and end apart: 15 -> 15, of which waited for: 6 -> 8; matrix products, arithmetic and copies ran while one was open for 8% -> 1% of each run, Pallas kernels for 0% -> 0%
where the time goes in v13:
time: 49.2 us; the launch traced here: 49 us
  starting transfers between devices  20.6 us (42%)
  waiting for transfers between devices  19.5 us (40%)
  local copies, waits for them, and re-layouts  4.55 us (9%)
  other arithmetic  2.39 us (5%)
  matrix products  1.24 us (3%)
  between operations  0.8 us (2%)
    ppermute x9, starting transfers between devices, on_device(): pieces = [lax.ppermute(p, 'seq', xor_pairs(groups, k)) for p in pieces]  14.1 us
    ppermute x9, waiting for transfers between devices, on_device(): pieces = [lax.ppermute(p, 'seq', xor_pairs(groups, k)) for p in pieces]  13.3 us
    ppermute x3, starting transfers between devices, gather_prefix(): pieces.append(lax.ppermute(ordered[:, k], 'seq', xor_pairs(groups, k)))  4.55 us
    ppermute x3, waiting for transfers between devices, gather_prefix(): pieces.append(lax.ppermute(ordered[:, k], 'seq', xor_pairs(groups, k)))  4.14 us
    ppermute x3, waiting for transfers between devices, gather_prefix(): other = lax.ppermute(total, 'step', xor_pairs(steps_axis, k))  2.01 us
    unnamed x14, local copies, waits for them, and re-layouts  1.98 us
    ppermute x3, starting transfers between devices, gather_prefix(): other = lax.ppermute(total, 'step', xor_pairs(steps_axis, k))  1.93 us
    another operation x2, local copies, waits for them, and re-layouts, on_device(): jnp.stack([jnp.broadcast_to(guide_scale, shape), jnp.broadcast_to(len_ful...  1.38 us
  transfers between devices with their start and end apart: 15, of which 8 were waited for; matrix products, arithmetic and copies ran while one was open for 1% of the time, Pallas kernels for 0%

profile of v13, /device:TPU:0, one launch (start us, length us, event | category | flops | bytes accessed | tf_op | source)
XLA Modules:
  0.0 49.0 jit_solution(842273600794143428)
XLA Ops:
  0.0 1.1 %dynamic-slice_bitcast_fusion.10 = (bf16[48,8,128]{2,1,0:T(8,128)(2,1)S(1)}, bf16[48,8,128]{2,1,0:T(8,128)(2,1)S(1)}, bf16[48,8,128]{2,1,0:T(8,128)(2,1)S(1)}, bf16[48,8,128]{2,1,0:T(8,128)(2,1)S(1)}) fusion(bf16[4,48,8,128]{3,2,1,0:T(8,128)(2,1)} %bitcast.119, s32[]{:T(128)S(6)} %select_n.239, s32[]{:T(128)S(6)} %select_n.241, s32[]{:T(128)S(6)} %select_n.240, ...), kind=kLoop, calls=%fused_computation.44 | loop fusion | bytes 786448 | tf_op jit(solution)/shard_map/jit(dynamic_index_in_dim)/squeeze | solution.py:91
  1.1 5.1 %collective-permute-start = (bf16[48,8,128]{2,1,0:T(8,128)(2,1)S(1)}, bf16[48,8,128]{2,1,0:T(8,128)(2,1)S(1)}, u32[]{:S(2)}, u32[]{:S(2)}) collective-permute-start(bf16[48,8,128]{2,1,0:T(8,128)(2,1)S(1)} %get-tuple-element.26), channel_id=1, source_target_pairs={{0,3},{1,2},{2,1},{3,0},{4,7},{5,6},{6,5},{7,4},{8,11},{9,10},{10,... | collective-permute-start | bytes 294920 | tf_op jit(solution)/shard_map/ppermute | solution.py:93
  7.0 3.8 %collective-permute-start.5 = (bf16[48,8,128]{2,1,0:T(8,128)(2,1)S(1)}, bf16[48,8,128]{2,1,0:T(8,128)(2,1)S(1)}, u32[]{:S(2)}, u32[]{:S(2)}) collective-permute-start(bf16[48,8,128]{2,1,0:T(8,128)(2,1)S(1)} %get-tuple-element.20), channel_id=1, source_target_pairs={{0,3},{1,2},{2,1},{3,0},{4,7},{5,6},{6,5},{7,4},{8,11},{9,10},{10,... | collective-permute-start | bytes 294920 | tf_op jit(solution)/shard_map/ppermute | solution.py:93
  11.4 0.7 %collective-permute-start.2 = (bf16[48,8,128]{2,1,0:T(8,128)(2,1)S(1)}, bf16[48,8,128]{2,1,0:T(8,128)(2,1)S(1)}, u32[]{:S(2)}, u32[]{:S(2)}) collective-permute-start(bf16[48,8,128]{2,1,0:T(8,128)(2,1)S(1)} %get-tuple-element.24), channel_id=1, source_target_pairs={{0,2},{1,3},{2,0},{3,1},{4,6},{5,7},{6,4},{7,5},{8,10},{9,11},{10,... | collective-permute-start | bytes 294920 | tf_op jit(solution)/shard_map/ppermute | solution.py:93
  12.1 0.6 %collective-permute-done.3 = bf16[48,8,128]{2,1,0:T(8,128)(2,1)S(1)} collective-permute-done((bf16[48,8,128]{2,1,0:T(8,128)(2,1)S(1)}, bf16[48,8,128]{2,1,0:T(8,128)(2,1)S(1)}, u32[]{:S(2)}, u32[]{:S(2)}) %collective-permute-start.3) | collective-permute-done | bytes 98336 | tf_op jit(solution)/shard_map/ppermute | solution.py:93
  12.8 1.7 %collective-permute-start.6 = (bf16[48,8,128]{2,1,0:T(8,128)(2,1)S(1)}, bf16[48,8,128]{2,1,0:T(8,128)(2,1)S(1)}, u32[]{:S(2)}, u32[]{:S(2)}) collective-permute-start(bf16[48,8,128]{2,1,0:T(8,128)(2,1)S(1)} %get-tuple-element.18), channel_id=1, source_target_pairs={{0,1},{1,0},{2,3},{3,2},{4,5},{5,4},{6,7},{7,6},{8,9},{9,8},{10,11... | collective-permute-start | bytes 294920 | tf_op jit(solution)/shard_map/ppermute | solution.py:93
  14.4 3.5 %collective-permute-done.4 = bf16[48,8,128]{2,1,0:T(8,128)(2,1)S(1)} collective-permute-done((bf16[48,8,128]{2,1,0:T(8,128)(2,1)S(1)}, bf16[48,8,128]{2,1,0:T(8,128)(2,1)S(1)}, u32[]{:S(2)}, u32[]{:S(2)}) %collective-permute-start.4) | collective-permute-done | bytes 98336 | tf_op jit(solution)/shard_map/ppermute | solution.py:93
  17.9 2.2 %collective-permute-start.8 = (bf16[48,8,128]{2,1,0:T(8,128)(2,1)S(1)}, bf16[48,8,128]{2,1,0:T(8,128)(2,1)S(1)}, u32[]{:S(2)}, u32[]{:S(2)}) collective-permute-start(bf16[48,8,128]{2,1,0:T(8,128)(2,1)S(1)} %get-tuple-element.16), channel_id=1, source_target_pairs={{0,3},{1,2},{2,1},{3,0},{4,7},{5,6},{6,5},{7,4},{8,11},{9,10},{10,... | collective-permute-start | bytes 294920 | tf_op jit(solution)/shard_map/ppermute | solution.py:93
  20.1 7.6 %collective-permute-done.2 = bf16[48,8,128]{2,1,0:T(8,128)(2,1)S(1)} collective-permute-done((bf16[48,8,128]{2,1,0:T(8,128)(2,1)S(1)}, bf16[48,8,128]{2,1,0:T(8,128)(2,1)S(1)}, u32[]{:S(2)}, u32[]{:S(2)}) %collective-permute-start.2) | collective-permute-done | bytes 98336 | tf_op jit(solution)/shard_map/ppermute | solution.py:93
  28.3 1.6 %collective-permute-done.7 = bf16[48,8,128]{2,1,0:T(8,128)(2,1)S(1)} collective-permute-done((bf16[48,8,128]{2,1,0:T(8,128)(2,1)S(1)}, bf16[48,8,128]{2,1,0:T(8,128)(2,1)S(1)}, u32[]{:S(2)}, u32[]{:S(2)}) %collective-permute-start.7) | collective-permute-done | bytes 98336 | tf_op jit(solution)/shard_map/ppermute | solution.py:93
  29.8 0.7 %multiply_reduce_fusion = (f32[48,32]{1,0:T(8,128)S(1)}, bf16[48,32,128]{2,1,0:T(8,128)(2,1)S(1)}) fusion(f32[48,32]{1,0:T(8,128)S(1)} %fusion.3, bf16[48,8,128]{2,1,0:T(8,128)(2,1)S(1)} %collective-permute-done.8, bf16[48,8,128]{2,1,0:T(8,128)(2,1)S(1)} %collective-permute-done.7, bf16[48,8,128]{2,1,0:T(8,128)(2,1)S(1)} %collective-permute-done.6, ...), kind=kOutput, calls=%fused_computation.6 | convolution fusion | flops 15235584 | bytes 1001472 | tf_op jit(solution)/shard_map/iqk,ikd->iqd/dot_general | solution.py:24
  30.5 0.6 %copy-done.5 = s32[4]{0:T(128)S(1)} copy-done((s32[4]{0:T(128)S(1)}, s32[4]{0:T(128)}, u32[]{:S(2)}) %copy-start.5) | copy-done | bytes 40
  31.3 0.7 %fusion.42 = f32[]{:T(128)} fusion(f32[4]{0:T(128)S(1)} %select_reduce_fusion, s32[]{:T(128)S(6)} %axis_index.22), kind=kLoop, calls=%fused_computation.81 | loop fusion | flops 11 | bytes 24 | tf_op jit(solution)/shard_map/reduce_sum | solution.py:129
  32.0 0.7 %copy-done.6 = f32[8]{0:T(128)S(1)} copy-done((f32[8]{0:T(128)S(1)}, f32[8]{0:T(128)}, u32[]{:S(2)}) %copy-start.6) | copy-done | bytes 56
  32.6 0.7 %fusion.41 = f32[]{:T(128)} fusion(f32[8]{0:T(128)S(1)} %copy-done.6, s32[]{:T(128)} %bitcast.118), kind=kLoop, calls=%fused_computation.80 | loop fusion | flops 23 | bytes 40 | tf_op jit(solution)/shard_map/reduce_sum | solution.py:13
  33.3 1.3 %stack.12 = f32[2]{0:T(128)S(1)} pad(f32[1]{0:T(128)} %bitcast.3, f32[]{:T(128)} %fusion.42), padding=0_1 | pad | bytes 16 | tf_op jit(solution)/shard_map/stack | solution.py:134
  35.0 3.3 %collective-permute-start.10 = (f32[1,8,64]{2,1,0:T(8,128)S(1)}, f32[1,8,64]{2,1,0:T(8,128)S(1)}, u32[]{:S(2)}, u32[]{:S(2)}) collective-permute-start(f32[1,8,64]{2,1,0:T(8,128)S(1)} %get-tuple-element.32), channel_id=1, source_target_pairs={{0,2},{1,3},{2,0},{3,1},{4,6},{5,7},{6,4},{7,5},{8,10},{9,11},{10,... | collective-permute-start | bytes 6152 | tf_op jit(solution)/shard_map/ppermute | solution.py:42
  38.3 1.3 %collective-permute-start.11 = (f32[1,8,64]{2,1,0:T(8,128)S(1)}, f32[1,8,64]{2,1,0:T(8,128)S(1)}, u32[]{:S(2)}, u32[]{:S(2)}) collective-permute-start(f32[1,8,64]{2,1,0:T(8,128)S(1)} %get-tuple-element.31), channel_id=1, source_target_pairs={{0,3},{1,2},{2,1},{3,0},{4,7},{5,6},{6,5},{7,4},{8,11},{9,10},{10,... | collective-permute-start | bytes 6152 | tf_op jit(solution)/shard_map/ppermute | solution.py:42
  39.9 3.8 %collective-permute-done.11 = f32[1,8,64]{2,1,0:T(8,128)S(1)} collective-permute-done((f32[1,8,64]{2,1,0:T(8,128)S(1)}, f32[1,8,64]{2,1,0:T(8,128)S(1)}, u32[]{:S(2)}, u32[]{:S(2)}) %collective-permute-start.11) | collective-permute-done | bytes 2080 | tf_op jit(solution)/shard_map/ppermute | solution.py:42
  43.8 1.6 %collective-permute-start.13 = (f32[8,64]{1,0:T(8,128)S(1)}, f32[8,64]{1,0:T(8,128)S(1)}, u32[]{:S(2)}, u32[]{:S(2)}) collective-permute-start(f32[8,64]{1,0:T(8,128)S(1)} %bitcast_add_fusion), channel_id=1, source_target_pairs={{0,8},{4,12},{8,0},{12,4},{1,9},{5,13},{9,1},{13,5},{2,10},{6,14},... | collective-permute-start | bytes 6152 | tf_op jit(solution)/shard_map/ppermute | solution.py:58
  45.7 0.7 %copy-done.3 = f32[64,8]{0,1:T(8,128)S(1)} copy-done((f32[64,8]{0,1:T(8,128)S(1)}, f32[64,8]{0,1:T(8,128)}, u32[]{:S(2)}) %copy-start.3) | copy-done | bytes 2072
  46.4 1.1 %collective-permute-done.13 = f32[8,64]{1,0:T(8,128)S(1)} collective-permute-done((f32[8,64]{1,0:T(8,128)S(1)}, f32[8,64]{1,0:T(8,128)S(1)}, u32[]{:S(2)}, u32[]{:S(2)}) %collective-permute-start.13) | collective-permute-done | bytes 2080 | tf_op jit(solution)/shard_map/ppermute | solution.py:58
  47.5 0.9 %collective-permute-done.14 = f32[8,64]{1,0:T(8,128)S(1)} collective-permute-done((f32[8,64]{1,0:T(8,128)S(1)}, f32[8,64]{1,0:T(8,128)S(1)}, u32[]{:S(2)}, u32[]{:S(2)}) %collective-permute-start.14) | collective-permute-done | bytes 2080 | tf_op jit(solution)/shard_map/ppermute | solution.py:58
  48.4 0.6 %add_bitcast_fusion = f32[4,64,8]{1,2,0:T(8,128)} fusion(f32[4,8,64]{2,1,0:T(8,128)S(1)} %maximum_add_fusion, f32[8,64]{1,0:T(8,128)S(1)} %select_add_fusion), kind=kLoop, calls=%fused_computation.55 | loop fusion | flops 2048 | bytes 18432 | tf_op jit(solution)/shard_map/transpose | solution.py:60
  (42 shorter events, 2.6 us)
Async XLA Ops:
  0.0 34.7 %copy-start = (bf16[64,3072]{1,0:T(8,128)(2,1)S(1)}, bf16[64,3072]{1,0:T(8,128)(2,1)}, u32[]{:S(2)}) copy-start(bf16[64,3072]{1,0:T(8,128)(2,1)} %param.13) | copy-start | bytes 1179652
  0.0 6.3 %copy-start.1 = (bf16[4,2,24,8,128]{4,3,2,1,0:T(8,128)(2,1)S(1)}, bf16[4,2,24,8,128]{4,3,2,1,0:T(8,128)(2,1)}, u32[]{:S(2)}) copy-start(bf16[4,2,24,8,128]{4,3,2,1,0:T(8,128)(2,1)} %param.10) | copy-start | bytes 1179652
  1.1 10.3 %collective-permute-start = (bf16[48,8,128]{2,1,0:T(8,128)(2,1)S(1)}, bf16[48,8,128]{2,1,0:T(8,128)(2,1)S(1)}, u32[]{:S(2)}, u32[]{:S(2)}) collective-permute-start(bf16[48,8,128]{2,1,0:T(8,128)(2,1)S(1)} %get-tuple-element.26), channel_id=1, source_target_pairs={{0,3},{1,2},{2,1},{3,0},{4,7},{5,6},{6,5},{7,4},{8,11},{9,10},{10,... | collective-permute-start | bytes 294920 | tf_op jit(solution)/shard_map/ppermute | solution.py:93
  6.3 5.8 %copy-start.2 = (bf16[4,2,24,8,128]{4,3,2,1,0:T(8,128)(2,1)S(1)}, bf16[4,2,24,8,128]{4,3,2,1,0:T(8,128)(2,1)}, u32[]{:S(2)}) copy-start(bf16[4,2,24,8,128]{4,3,2,1,0:T(8,128)(2,1)} %param.11) | copy-start | bytes 1179652
  6.3 6.5 %collective-permute-start.3 = (bf16[48,8,128]{2,1,0:T(8,128)(2,1)S(1)}, bf16[48,8,128]{2,1,0:T(8,128)(2,1)S(1)}, u32[]{:S(2)}, u32[]{:S(2)}) collective-permute-start(bf16[48,8,128]{2,1,0:T(8,128)(2,1)S(1)} %get-tuple-element.22), channel_id=1, source_target_pairs={{0,1},{1,0},{2,3},{3,2},{4,5},{5,4},{6,7},{7,6},{8,9},{9,8},{10,11... | collective-permute-start | bytes 294920 | tf_op jit(solution)/shard_map/ppermute | solution.py:93
  6.4 11.5 %collective-permute-start.4 = (bf16[48,8,128]{2,1,0:T(8,128)(2,1)S(1)}, bf16[48,8,128]{2,1,0:T(8,128)(2,1)S(1)}, u32[]{:S(2)}, u32[]{:S(2)}) collective-permute-start(bf16[48,8,128]{2,1,0:T(8,128)(2,1)S(1)} %get-tuple-element.21), channel_id=1, source_target_pairs={{0,2},{1,3},{2,0},{3,1},{4,6},{5,7},{6,4},{7,5},{8,10},{9,11},{10,... | collective-permute-start | bytes 294920 | tf_op jit(solution)/shard_map/ppermute | solution.py:93
  7.0 10.9 %collective-permute-start.5 = (bf16[48,8,128]{2,1,0:T(8,128)(2,1)S(1)}, bf16[48,8,128]{2,1,0:T(8,128)(2,1)S(1)}, u32[]{:S(2)}, u32[]{:S(2)}) collective-permute-start(bf16[48,8,128]{2,1,0:T(8,128)(2,1)S(1)} %get-tuple-element.20), channel_id=1, source_target_pairs={{0,3},{1,2},{2,1},{3,0},{4,7},{5,6},{6,5},{7,4},{8,11},{9,10},{10,... | collective-permute-start | bytes 294920 | tf_op jit(solution)/shard_map/ppermute | solution.py:93
  10.7 9.3 %collective-permute-start.1 = (bf16[48,8,128]{2,1,0:T(8,128)(2,1)S(1)}, bf16[48,8,128]{2,1,0:T(8,128)(2,1)S(1)}, u32[]{:S(2)}, u32[]{:S(2)}) collective-permute-start(bf16[48,8,128]{2,1,0:T(8,128)(2,1)S(1)} %get-tuple-element.25), channel_id=1, source_target_pairs={{0,1},{1,0},{2,3},{3,2},{4,5},{5,4},{6,7},{7,6},{8,9},{9,8},{10,11... | collective-permute-start | bytes 294920 | tf_op jit(solution)/shard_map/ppermute | solution.py:93
  11.4 16.3 %collective-permute-start.2 = (bf16[48,8,128]{2,1,0:T(8,128)(2,1)S(1)}, bf16[48,8,128]{2,1,0:T(8,128)(2,1)S(1)}, u32[]{:S(2)}, u32[]{:S(2)}) collective-permute-start(bf16[48,8,128]{2,1,0:T(8,128)(2,1)S(1)} %get-tuple-element.24), channel_id=1, source_target_pairs={{0,2},{1,3},{2,0},{3,1},{4,6},{5,7},{6,4},{7,5},{8,10},{9,11},{10,... | collective-permute-start | bytes 294920 | tf_op jit(solution)/shard_map/ppermute | solution.py:93
  12.8 15.5 %collective-permute-start.6 = (bf16[48,8,128]{2,1,0:T(8,128)(2,1)S(1)}, bf16[48,8,128]{2,1,0:T(8,128)(2,1)S(1)}, u32[]{:S(2)}, u32[]{:S(2)}) collective-permute-start(bf16[48,8,128]{2,1,0:T(8,128)(2,1)S(1)} %get-tuple-element.18), channel_id=1, source_target_pairs={{0,1},{1,0},{2,3},{3,2},{4,5},{5,4},{6,7},{7,6},{8,9},{9,8},{10,11... | collective-permute-start | bytes 294920 | tf_op jit(solution)/shard_map/ppermute | solution.py:93
  17.9 11.9 %collective-permute-start.7 = (bf16[48,8,128]{2,1,0:T(8,128)(2,1)S(1)}, bf16[48,8,128]{2,1,0:T(8,128)(2,1)S(1)}, u32[]{:S(2)}, u32[]{:S(2)}) collective-permute-start(bf16[48,8,128]{2,1,0:T(8,128)(2,1)S(1)} %get-tuple-element.17), channel_id=1, source_target_pairs={{0,2},{1,3},{2,0},{3,1},{4,6},{5,7},{6,4},{7,5},{8,10},{9,11},{10,... | collective-permute-start | bytes 294920 | tf_op jit(solution)/shard_map/ppermute | solution.py:93
  17.9 11.9 %collective-permute-start.8 = (bf16[48,8,128]{2,1,0:T(8,128)(2,1)S(1)}, bf16[48,8,128]{2,1,0:T(8,128)(2,1)S(1)}, u32[]{:S(2)}, u32[]{:S(2)}) collective-permute-start(bf16[48,8,128]{2,1,0:T(8,128)(2,1)S(1)} %get-tuple-element.16), channel_id=1, source_target_pairs={{0,3},{1,2},{2,1},{3,0},{4,7},{5,6},{6,5},{7,4},{8,11},{9,10},{10,... | collective-permute-start | bytes 294920 | tf_op jit(solution)/shard_map/ppermute | solution.py:93
  29.8 0.7 %copy-start.4 = (f32[1000]{0:T(1024)S(1)}, f32[1000]{0:T(1024)}, u32[]{:S(2)}) copy-start(f32[1000]{0:T(1024)} %param.16) | copy-start | bytes 12004
  30.5 0.7 %copy-start.5 = (s32[4]{0:T(128)S(1)}, s32[4]{0:T(128)}, u32[]{:S(2)}) copy-start(s32[4]{0:T(128)} %param.17) | copy-start | bytes 52
  32.0 0.7 %copy-start.6 = (f32[8]{0:T(128)S(1)}, f32[8]{0:T(128)}, u32[]{:S(2)}) copy-start(f32[8]{0:T(128)} %param.14) | copy-start | bytes 100
  35.0 4.9 %collective-permute-start.10 = (f32[1,8,64]{2,1,0:T(8,128)S(1)}, f32[1,8,64]{2,1,0:T(8,128)S(1)}, u32[]{:S(2)}, u32[]{:S(2)}) collective-permute-start(f32[1,8,64]{2,1,0:T(8,128)S(1)} %get-tuple-element.32), channel_id=1, source_target_pairs={{0,2},{1,3},{2,0},{3,1},{4,6},{5,7},{6,4},{7,5},{8,10},{9,11},{10,... | collective-permute-start | bytes 6152 | tf_op jit(solution)/shard_map/ppermute | solution.py:42
  38.3 5.4 %collective-permute-start.11 = (f32[1,8,64]{2,1,0:T(8,128)S(1)}, f32[1,8,64]{2,1,0:T(8,128)S(1)}, u32[]{:S(2)}, u32[]{:S(2)}) collective-permute-start(f32[1,8,64]{2,1,0:T(8,128)S(1)} %get-tuple-element.31), channel_id=1, source_target_pairs={{0,3},{1,2},{2,1},{3,0},{4,7},{5,6},{6,5},{7,4},{8,11},{9,10},{10,... | collective-permute-start | bytes 6152 | tf_op jit(solution)/shard_map/ppermute | solution.py:42
  39.5 4.1 %collective-permute-start.9 = (f32[1,8,64]{2,1,0:T(8,128)S(1)}, f32[1,8,64]{2,1,0:T(8,128)S(1)}, u32[]{:S(2)}, u32[]{:S(2)}) collective-permute-start(f32[1,8,64]{2,1,0:T(8,128)S(1)} %get-tuple-element.30), channel_id=1, source_target_pairs={{0,1},{1,0},{2,3},{3,2},{4,5},{5,4},{6,7},{7,6},{8,9},{9,8},{10,11... | collective-permute-start | bytes 6152 | tf_op jit(solution)/shard_map/ppermute | solution.py:42
  43.7 2.7 %collective-permute-start.12 = (f32[8,64]{1,0:T(8,128)S(1)}, f32[8,64]{1,0:T(8,128)S(1)}, u32[]{:S(2)}, u32[]{:S(2)}) collective-permute-start(f32[8,64]{1,0:T(8,128)S(1)} %bitcast_add_fusion), channel_id=1, source_target_pairs={{0,4},{4,0},{8,12},{12,8},{1,5},{5,1},{9,13},{13,9},{2,6},{6,2},{1... | collective-permute-start | bytes 6152 | tf_op jit(solution)/shard_map/ppermute | solution.py:58
  43.8 3.7 %collective-permute-start.13 = (f32[8,64]{1,0:T(8,128)S(1)}, f32[8,64]{1,0:T(8,128)S(1)}, u32[]{:S(2)}, u32[]{:S(2)}) collective-permute-start(f32[8,64]{1,0:T(8,128)S(1)} %bitcast_add_fusion), channel_id=1, source_target_pairs={{0,8},{4,12},{8,0},{12,4},{1,9},{5,13},{9,1},{13,5},{2,10},{6,14},... | collective-permute-start | bytes 6152 | tf_op jit(solution)/shard_map/ppermute | solution.py:58
  45.3 3.0 %collective-permute-start.14 = (f32[8,64]{1,0:T(8,128)S(1)}, f32[8,64]{1,0:T(8,128)S(1)}, u32[]{:S(2)}, u32[]{:S(2)}) collective-permute-start(f32[8,64]{1,0:T(8,128)S(1)} %bitcast_add_fusion), channel_id=1, source_target_pairs={{0,12},{4,8},{8,4},{12,0},{1,13},{5,9},{9,5},{13,1},{2,14},{6,10},... | collective-permute-start | bytes 6152 | tf_op jit(solution)/shard_map/ppermute | solution.py:58
  45.7 0.7 %copy-start.3 = (f32[64,8]{0,1:T(8,128)S(1)}, f32[64,8]{0,1:T(8,128)}, u32[]{:S(2)}) copy-start(f32[64,8]{0,1:T(8,128)} %param.12) | copy-start | bytes 6148

commit v14 on v13

--- a/solution.py
+++ b/solution.py
@@ -102,12 +102,11 @@
         gathered = gathered.reshape(3, per_dev, length, head_size)
         partner_order = False
     if partner_order:
-        far_q, cfg_table, cfg_index, step_table, time_index = lax.optimization_barrier(
-            (arrived[groups - 1][0], cfg_table, cfg_index, step_table, time_index)
+        near_q, cfg_table, cfg_index, step_table, time_index = lax.optimization_barrier(
+            (arrived[1][0], cfg_table, cfg_index, step_table, time_index)
         )
-        arrived[groups - 1][0] = far_q
+        arrived[1][0] = near_q
         gathered[0] = jnp.concatenate([arrived[k][0] for k in range(groups)], axis=1)
-    heads_out = attend(gathered[0], gathered[1], gathered[2])
 
     weight_heads = out_weight.reshape(channels, heads, head_size)
     guide_scale = lookup(cfg_table, cfg_index)[0]
@@ -115,6 +114,18 @@
 
     if whole_steps:
         local_steps = per_dev // (branches * heads)
+        owner = jnp.arange(step_dev, dtype=jnp.int32) // local_steps == me
+        slot = jnp.arange(step_dev, dtype=jnp.int32) % local_steps
+        mine = (owner[:, None] & (slot[:, None] == jnp.arange(local_steps)))[:, :, None, None]
+        len_full = jnp.sum(
+            jnp.where(mine, step_len[:, None, None, None], jnp.zeros((), jnp.float32)), axis=0
+        )
+        shape = (local_steps, length, channels)
+        coef = jnp.stack([jnp.broadcast_to(guide_scale, shape), jnp.broadcast_to(len_full, shape)])
+        gathered[0], coef = lax.optimization_barrier((gathered[0], coef))
+    heads_out = attend(gathered[0], gathered[1], gathered[2])
+
+    if whole_steps:
         ho = heads_out.reshape(local_steps, branches, heads, length, head_size)
         wide = ho.astype(jnp.float32)
         square_sum = jnp.sum(wide * wide, axis=(2, 4))
@@ -122,16 +133,6 @@
         drift = (
             jnp.einsum("chd,sbhld->sblc", weight_heads, ho, preferred_element_type=jnp.float32)
             / root_mean[:, :, :, None]
-        )
-        owner = jnp.arange(step_dev, dtype=jnp.int32) // local_steps == me
-        slot = jnp.arange(step_dev, dtype=jnp.int32) % local_steps
-        mine = (owner[:, None] & (slot[:, None] == jnp.arange(local_steps)))[:, :, None, None]
-        len_full = jnp.sum(
-            jnp.where(mine, step_len[:, None, None, None], jnp.zeros((), jnp.float32)), axis=0
-        )
-        shape = (local_steps, length, channels)
-        coef = lax.optimization_barrier(
-            jnp.stack([jnp.broadcast_to(guide_scale, shape), jnp.broadcast_to(len_full, shape)])
         )
         scale_full, len_full = coef[0], coef[1]
         start_t = start_latent.T

time: 49.2 us -> 46.1 us (0.937)
  waiting for transfers between devices: 19.5 us -> 11.8 us
  starting transfers between devices: 20.6 us -> 25 us
    ppermute x9, waiting for transfers between devices: 13.3 us -> 5.76 us  [on_device(): pieces = [lax.ppermute(p, 'seq', xor_pairs(groups, k)) for p in pieces]]
    ppermute x9, starting transfers between devices: 14.1 us -> 19.1 us  [on_device(): pieces = [lax.ppermute(p, 'seq', xor_pairs(groups, k)) for p in pieces]]
    ppermute x3, starting transfers between devices: 4.55 us -> 4.04 us  [gather_prefix(): pieces.append(lax.ppermute(ordered[:, k], 'seq', xor_pairs(groups, k)))]
  transfers between devices with their start and end apart: 15 -> 15, of which waited for: 8 -> 6; matrix products, arithmetic and copies ran while one was open for 1% -> 8% of each run, Pallas kernels for 0% -> 0%
where the time goes in v14:
time: 46.1 us; the launch traced here: 45.9 us
  starting transfers between devices  25 us (54%)
  waiting for transfers between devices  11.8 us (26%)
  local copies, waits for them, and re-layouts  4.5 us (10%)
  other arithmetic  2.46 us (5%)
  matrix products  1.25 us (3%)
  between operations  0.83 us (2%)
    ppermute x9, starting transfers between devices, on_device(): pieces = [lax.ppermute(p, 'seq', xor_pairs(groups, k)) for p in pieces]  19.1 us
    ppermute x9, waiting for transfers between devices, on_device(): pieces = [lax.ppermute(p, 'seq', xor_pairs(groups, k)) for p in pieces]  5.76 us
    ppermute x3, waiting for transfers between devices, gather_prefix(): pieces.append(lax.ppermute(ordered[:, k], 'seq', xor_pairs(groups, k)))  4.06 us
    ppermute x3, starting transfers between devices, gather_prefix(): pieces.append(lax.ppermute(ordered[:, k], 'seq', xor_pairs(groups, k)))  4.04 us
    ppermute x3, waiting for transfers between devices, gather_prefix(): other = lax.ppermute(total, 'step', xor_pairs(steps_axis, k))  2 us
    ppermute x3, starting transfers between devices, gather_prefix(): other = lax.ppermute(total, 'step', xor_pairs(steps_axis, k))  1.93 us
    unnamed x14, local copies, waits for them, and re-layouts  1.91 us
    another operation x2, local copies, waits for them, and re-layouts, on_device(): jnp.stack([jnp.broadcast_to(guide_scale, shape), jnp.broadcast_to(len_ful...  1.38 us
  transfers between devices with their start and end apart: 15, of which 6 were waited for; matrix products, arithmetic and copies ran while one was open for 8% of the time, Pallas kernels for 0%

profile of v14, /device:TPU:0, one launch (start us, length us, event | category | flops | bytes accessed | tf_op | source)
XLA Modules:
  0.0 45.9 jit_solution(229550276778820051)
XLA Ops:
  0.0 1.1 %dynamic-slice_bitcast_fusion.11 = (bf16[48,8,128]{2,1,0:T(8,128)(2,1)S(1)}, bf16[48,8,128]{2,1,0:T(8,128)(2,1)S(1)}, bf16[48,8,128]{2,1,0:T(8,128)(2,1)S(1)}, bf16[48,8,128]{2,1,0:T(8,128)(2,1)S(1)}) fusion(bf16[4,48,8,128]{3,2,1,0:T(8,128)(2,1)} %bitcast.116, s32[]{:T(128)S(6)} %select_n.235, s32[]{:T(128)S(6)} %select_n.238, s32[]{:T(128)S(6)} %select_n.237, ...), kind=kLoop, calls=%fused_computation.39 | loop fusion | bytes 786448 | tf_op jit(solution)/shard_map/jit(dynamic_index_in_dim)/squeeze | solution.py:91
  1.1 3.1 %collective-permute-start = (bf16[48,8,128]{2,1,0:T(8,128)(2,1)S(1)}, bf16[48,8,128]{2,1,0:T(8,128)(2,1)S(1)}, u32[]{:S(2)}, u32[]{:S(2)}) collective-permute-start(bf16[48,8,128]{2,1,0:T(8,128)(2,1)S(1)} %get-tuple-element.30), channel_id=1, source_target_pairs={{0,1},{1,0},{2,3},{3,2},{4,5},{5,4},{6,7},{7,6},{8,9},{9,8},{10,11... | collective-permute-start | bytes 294920 | tf_op jit(solution)/shard_map/ppermute | solution.py:93
  4.2 2.6 %collective-permute-start.1 = (bf16[48,8,128]{2,1,0:T(8,128)(2,1)S(1)}, bf16[48,8,128]{2,1,0:T(8,128)(2,1)S(1)}, u32[]{:S(2)}, u32[]{:S(2)}) collective-permute-start(bf16[48,8,128]{2,1,0:T(8,128)(2,1)S(1)} %get-tuple-element.29), channel_id=1, source_target_pairs={{0,2},{1,3},{2,0},{3,1},{4,6},{5,7},{6,4},{7,5},{8,10},{9,11},{10,... | collective-permute-start | bytes 294920 | tf_op jit(solution)/shard_map/ppermute | solution.py:93
  6.9 1.0 %collective-permute-start.3 = (bf16[48,8,128]{2,1,0:T(8,128)(2,1)S(1)}, bf16[48,8,128]{2,1,0:T(8,128)(2,1)S(1)}, u32[]{:S(2)}, u32[]{:S(2)}) collective-permute-start(bf16[48,8,128]{2,1,0:T(8,128)(2,1)S(1)} %get-tuple-element.26), channel_id=1, source_target_pairs={{0,1},{1,0},{2,3},{3,2},{4,5},{5,4},{6,7},{7,6},{8,9},{9,8},{10,11... | collective-permute-start | bytes 294920 | tf_op jit(solution)/shard_map/ppermute | solution.py:93
  7.8 3.5 %collective-permute-start.4 = (bf16[48,8,128]{2,1,0:T(8,128)(2,1)S(1)}, bf16[48,8,128]{2,1,0:T(8,128)(2,1)S(1)}, u32[]{:S(2)}, u32[]{:S(2)}) collective-permute-start(bf16[48,8,128]{2,1,0:T(8,128)(2,1)S(1)} %get-tuple-element.25), channel_id=1, source_target_pairs={{0,2},{1,3},{2,0},{3,1},{4,6},{5,7},{6,4},{7,5},{8,10},{9,11},{10,... | collective-permute-start | bytes 294920 | tf_op jit(solution)/shard_map/ppermute | solution.py:93
  12.1 0.5 %copy-done.4 = f32[1000]{0:T(1024)S(1)} copy-done((f32[1000]{0:T(1024)S(1)}, f32[1000]{0:T(1024)}, u32[]{:S(2)}) %copy-start.4) | copy-done | bytes 4024
  12.9 0.7 %fusion.35 = f32[]{:T(128)} fusion(f32[4]{0:T(128)S(1)} %select_reduce_fusion, s32[]{:T(128)S(6)} %axis_index.22), kind=kLoop, calls=%fused_computation.73 | loop fusion | flops 11 | bytes 24 | tf_op jit(solution)/shard_map/reduce_sum | solution.py:120
  13.5 0.7 %copy-done.6 = f32[8]{0:T(128)S(1)} copy-done((f32[8]{0:T(128)S(1)}, f32[8]{0:T(128)}, u32[]{:S(2)}) %copy-start.6) | copy-done | bytes 56
  14.2 0.7 %fusion.34 = f32[]{:T(128)} fusion(f32[8]{0:T(128)S(1)} %copy-done.6, s32[]{:T(128)} %bitcast.115), kind=kLoop, calls=%fused_computation.72 | loop fusion | flops 23 | bytes 40 | tf_op jit(solution)/shard_map/reduce_sum | solution.py:13
  14.9 1.3 %stack.12 = f32[2]{0:T(128)S(1)} pad(f32[1]{0:T(128)} %bitcast.6, f32[]{:T(128)} %fusion.35), padding=0_1 | pad | bytes 16 | tf_op jit(solution)/shard_map/stack | solution.py:124
  16.3 8.4 %collective-permute-start.7 = (bf16[48,8,128]{2,1,0:T(8,128)(2,1)S(1)}, bf16[48,8,128]{2,1,0:T(8,128)(2,1)S(1)}, u32[]{:S(2)}, u32[]{:S(2)}) collective-permute-start(bf16[48,8,128]{2,1,0:T(8,128)(2,1)S(1)} %get-tuple-element.21), channel_id=1, source_target_pairs={{0,2},{1,3},{2,0},{3,1},{4,6},{5,7},{6,4},{7,5},{8,10},{9,11},{10,... | collective-permute-start | bytes 294920 | tf_op jit(solution)/shard_map/ppermute | solution.py:93
  25.3 0.3 fusion.38
  25.8 5.7 %collective-permute-done.7 = bf16[48,8,128]{2,1,0:T(8,128)(2,1)S(1)} collective-permute-done((bf16[48,8,128]{2,1,0:T(8,128)(2,1)S(1)}, bf16[48,8,128]{2,1,0:T(8,128)(2,1)S(1)}, u32[]{:S(2)}, u32[]{:S(2)}) %collective-permute-start.7) | collective-permute-done | bytes 98336 | tf_op jit(solution)/shard_map/ppermute | solution.py:93
  31.5 0.7 %multiply_reduce_fusion = (f32[48,32]{1,0:T(8,128)S(1)}, bf16[48,32,128]{2,1,0:T(8,128)(2,1)S(1)}) fusion(f32[48,32]{1,0:T(8,128)S(1)} %fusion.3, bf16[48,8,128]{2,1,0:T(8,128)(2,1)S(1)} %collective-permute-done.8, bf16[48,8,128]{2,1,0:T(8,128)(2,1)S(1)} %collective-permute-done.7, bf16[48,8,128]{2,1,0:T(8,128)(2,1)S(1)} %collective-permute-done.6, ...), kind=kOutput, calls=%fused_computation.6 | convolution fusion | flops 15235584 | bytes 1001472 | tf_op jit(solution)/shard_map/iqk,ikd->iqd/dot_general | solution.py:24
  32.5 2.7 %collective-permute-start.10 = (f32[1,8,64]{2,1,0:T(8,128)S(1)}, f32[1,8,64]{2,1,0:T(8,128)S(1)}, u32[]{:S(2)}, u32[]{:S(2)}) collective-permute-start(f32[1,8,64]{2,1,0:T(8,128)S(1)} %get-tuple-element.36), channel_id=1, source_target_pairs={{0,2},{1,3},{2,0},{3,1},{4,6},{5,7},{6,4},{7,5},{8,10},{9,11},{10,... | collective-permute-start | bytes 6152 | tf_op jit(solution)/shard_map/ppermute | solution.py:42
  35.2 1.3 %collective-permute-start.11 = (f32[1,8,64]{2,1,0:T(8,128)S(1)}, f32[1,8,64]{2,1,0:T(8,128)S(1)}, u32[]{:S(2)}, u32[]{:S(2)}) collective-permute-start(f32[1,8,64]{2,1,0:T(8,128)S(1)} %get-tuple-element.35), channel_id=1, source_target_pairs={{0,3},{1,2},{2,1},{3,0},{4,7},{5,6},{6,5},{7,4},{8,11},{9,10},{10,... | collective-permute-start | bytes 6152 | tf_op jit(solution)/shard_map/ppermute | solution.py:42
  36.5 0.5 %collective-permute-done.10 = f32[1,8,64]{2,1,0:T(8,128)S(1)} collective-permute-done((f32[1,8,64]{2,1,0:T(8,128)S(1)}, f32[1,8,64]{2,1,0:T(8,128)S(1)}, u32[]{:S(2)}, u32[]{:S(2)}) %collective-permute-start.10) | collective-permute-done | bytes 2080 | tf_op jit(solution)/shard_map/ppermute | solution.py:42
  37.1 3.5 %collective-permute-done.11 = f32[1,8,64]{2,1,0:T(8,128)S(1)} collective-permute-done((f32[1,8,64]{2,1,0:T(8,128)S(1)}, f32[1,8,64]{2,1,0:T(8,128)S(1)}, u32[]{:S(2)}, u32[]{:S(2)}) %collective-permute-start.11) | collective-permute-done | bytes 2080 | tf_op jit(solution)/shard_map/ppermute | solution.py:42
  40.7 1.6 %collective-permute-start.13 = (f32[8,64]{1,0:T(8,128)S(1)}, f32[8,64]{1,0:T(8,128)S(1)}, u32[]{:S(2)}, u32[]{:S(2)}) collective-permute-start(f32[8,64]{1,0:T(8,128)S(1)} %bitcast_add_fusion), channel_id=1, source_target_pairs={{0,8},{4,12},{8,0},{12,4},{1,9},{5,13},{9,1},{13,5},{2,10},{6,14},... | collective-permute-start | bytes 6152 | tf_op jit(solution)/shard_map/ppermute | solution.py:58
  42.3 0.3 collective-permute-start.14
  42.6 0.7 %copy-done.3 = f32[64,8]{0,1:T(8,128)S(1)} copy-done((f32[64,8]{0,1:T(8,128)S(1)}, f32[64,8]{0,1:T(8,128)}, u32[]{:S(2)}) %copy-start.3) | copy-done | bytes 2072
  43.3 1.1 %collective-permute-done.13 = f32[8,64]{1,0:T(8,128)S(1)} collective-permute-done((f32[8,64]{1,0:T(8,128)S(1)}, f32[8,64]{1,0:T(8,128)S(1)}, u32[]{:S(2)}, u32[]{:S(2)}) %collective-permute-start.13) | collective-permute-done | bytes 2080 | tf_op jit(solution)/shard_map/ppermute | solution.py:58
  44.4 0.9 %collective-permute-done.14 = f32[8,64]{1,0:T(8,128)S(1)} collective-permute-done((f32[8,64]{1,0:T(8,128)S(1)}, f32[8,64]{1,0:T(8,128)S(1)}, u32[]{:S(2)}, u32[]{:S(2)}) %collective-permute-start.14) | collective-permute-done | bytes 2080 | tf_op jit(solution)/shard_map/ppermute | solution.py:58
  45.3 0.6 %add_bitcast_fusion = f32[4,64,8]{1,2,0:T(8,128)} fusion(f32[4,8,64]{2,1,0:T(8,128)S(1)} %maximum_add_fusion, f32[8,64]{1,0:T(8,128)S(1)} %select_add_fusion), kind=kLoop, calls=%fused_computation.47 | loop fusion | flops 2048 | bytes 18432 | tf_op jit(solution)/shard_map/transpose | solution.py:60
  (43 shorter events, 1.7 us)
Async XLA Ops:
  0.0 32.2 %copy-start = (bf16[64,3072]{1,0:T(8,128)(2,1)S(1)}, bf16[64,3072]{1,0:T(8,128)(2,1)}, u32[]{:S(2)}) copy-start(bf16[64,3072]{1,0:T(8,128)(2,1)} %param.13) | copy-start | bytes 1179652
  0.0 6.8 %copy-start.1 = (bf16[4,2,24,8,128]{4,3,2,1,0:T(8,128)(2,1)S(1)}, bf16[4,2,24,8,128]{4,3,2,1,0:T(8,128)(2,1)}, u32[]{:S(2)}) copy-start(bf16[4,2,24,8,128]{4,3,2,1,0:T(8,128)(2,1)} %param.10) | copy-start | bytes 1179652
  1.1 10.9 %collective-permute-start = (bf16[48,8,128]{2,1,0:T(8,128)(2,1)S(1)}, bf16[48,8,128]{2,1,0:T(8,128)(2,1)S(1)}, u32[]{:S(2)}, u32[]{:S(2)}) collective-permute-start(bf16[48,8,128]{2,1,0:T(8,128)(2,1)S(1)} %get-tuple-element.30), channel_id=1, source_target_pairs={{0,1},{1,0},{2,3},{3,2},{4,5},{5,4},{6,7},{7,6},{8,9},{9,8},{10,11... | collective-permute-start | bytes 294920 | tf_op jit(solution)/shard_map/ppermute | solution.py:93
  4.2 11.9 %collective-permute-start.1 = (bf16[48,8,128]{2,1,0:T(8,128)(2,1)S(1)}, bf16[48,8,128]{2,1,0:T(8,128)(2,1)S(1)}, u32[]{:S(2)}, u32[]{:S(2)}) collective-permute-start(bf16[48,8,128]{2,1,0:T(8,128)(2,1)S(1)} %get-tuple-element.29), channel_id=1, source_target_pairs={{0,2},{1,3},{2,0},{3,1},{4,6},{5,7},{6,4},{7,5},{8,10},{9,11},{10,... | collective-permute-start | bytes 294920 | tf_op jit(solution)/shard_map/ppermute | solution.py:93
  6.8 9.5 %collective-permute-start.2 = (bf16[48,8,128]{2,1,0:T(8,128)(2,1)S(1)}, bf16[48,8,128]{2,1,0:T(8,128)(2,1)S(1)}, u32[]{:S(2)}, u32[]{:S(2)}) collective-permute-start(bf16[48,8,128]{2,1,0:T(8,128)(2,1)S(1)} %get-tuple-element.28), channel_id=1, source_target_pairs={{0,3},{1,2},{2,1},{3,0},{4,7},{5,6},{6,5},{7,4},{8,11},{9,10},{10,... | collective-permute-start | bytes 294920 | tf_op jit(solution)/shard_map/ppermute | solution.py:93
  6.8 5.1 %copy-start.2 = (bf16[4,2,24,8,128]{4,3,2,1,0:T(8,128)(2,1)S(1)}, bf16[4,2,24,8,128]{4,3,2,1,0:T(8,128)(2,1)}, u32[]{:S(2)}) copy-start(bf16[4,2,24,8,128]{4,3,2,1,0:T(8,128)(2,1)} %param.11) | copy-start | bytes 1179652
  6.9 18.0 %collective-permute-start.3 = (bf16[48,8,128]{2,1,0:T(8,128)(2,1)S(1)}, bf16[48,8,128]{2,1,0:T(8,128)(2,1)S(1)}, u32[]{:S(2)}, u32[]{:S(2)}) collective-permute-start(bf16[48,8,128]{2,1,0:T(8,128)(2,1)S(1)} %get-tuple-element.26), channel_id=1, source_target_pairs={{0,1},{1,0},{2,3},{3,2},{4,5},{5,4},{6,7},{7,6},{8,9},{9,8},{10,11... | collective-permute-start | bytes 294920 | tf_op jit(solution)/shard_map/ppermute | solution.py:93
  7.8 17.5 %collective-permute-start.4 = (bf16[48,8,128]{2,1,0:T(8,128)(2,1)S(1)}, bf16[48,8,128]{2,1,0:T(8,128)(2,1)S(1)}, u32[]{:S(2)}, u32[]{:S(2)}) collective-permute-start(bf16[48,8,128]{2,1,0:T(8,128)(2,1)S(1)} %get-tuple-element.25), channel_id=1, source_target_pairs={{0,2},{1,3},{2,0},{3,1},{4,6},{5,7},{6,4},{7,5},{8,10},{9,11},{10,... | collective-permute-start | bytes 294920 | tf_op jit(solution)/shard_map/ppermute | solution.py:93
  12.0 0.7 %copy-start.4 = (f32[1000]{0:T(1024)S(1)}, f32[1000]{0:T(1024)}, u32[]{:S(2)}) copy-start(f32[1000]{0:T(1024)} %param.16) | copy-start | bytes 12004
  12.0 0.7 %copy-start.5 = (s32[4]{0:T(128)S(1)}, s32[4]{0:T(128)}, u32[]{:S(2)}) copy-start(s32[4]{0:T(128)} %param.17) | copy-start | bytes 52
  12.1 13.2 %collective-permute-start.5 = (bf16[48,8,128]{2,1,0:T(8,128)(2,1)S(1)}, bf16[48,8,128]{2,1,0:T(8,128)(2,1)S(1)}, u32[]{:S(2)}, u32[]{:S(2)}) collective-permute-start(bf16[48,8,128]{2,1,0:T(8,128)(2,1)S(1)} %get-tuple-element.24), channel_id=1, source_target_pairs={{0,3},{1,2},{2,1},{3,0},{4,7},{5,6},{6,5},{7,4},{8,11},{9,10},{10,... | collective-permute-start | bytes 294920 | tf_op jit(solution)/shard_map/ppermute | solution.py:93
  13.5 0.7 %copy-start.6 = (f32[8]{0:T(128)S(1)}, f32[8]{0:T(128)}, u32[]{:S(2)}) copy-start(f32[8]{0:T(128)} %param.14) | copy-start | bytes 100
  16.2 9.6 %collective-permute-start.6 = (bf16[48,8,128]{2,1,0:T(8,128)(2,1)S(1)}, bf16[48,8,128]{2,1,0:T(8,128)(2,1)S(1)}, u32[]{:S(2)}, u32[]{:S(2)}) collective-permute-start(bf16[48,8,128]{2,1,0:T(8,128)(2,1)S(1)} %get-tuple-element.22), channel_id=1, source_target_pairs={{0,1},{1,0},{2,3},{3,2},{4,5},{5,4},{6,7},{7,6},{8,9},{9,8},{10,11... | collective-permute-start | bytes 294920 | tf_op jit(solution)/shard_map/ppermute | solution.py:93
  16.3 15.2 %collective-permute-start.7 = (bf16[48,8,128]{2,1,0:T(8,128)(2,1)S(1)}, bf16[48,8,128]{2,1,0:T(8,128)(2,1)S(1)}, u32[]{:S(2)}, u32[]{:S(2)}) collective-permute-start(bf16[48,8,128]{2,1,0:T(8,128)(2,1)S(1)} %get-tuple-element.21), channel_id=1, source_target_pairs={{0,2},{1,3},{2,0},{3,1},{4,6},{5,7},{6,4},{7,5},{8,10},{9,11},{10,... | collective-permute-start | bytes 294920 | tf_op jit(solution)/shard_map/ppermute | solution.py:93
  24.9 6.6 %collective-permute-start.8 = (bf16[48,8,128]{2,1,0:T(8,128)(2,1)S(1)}, bf16[48,8,128]{2,1,0:T(8,128)(2,1)S(1)}, u32[]{:S(2)}, u32[]{:S(2)}) collective-permute-start(bf16[48,8,128]{2,1,0:T(8,128)(2,1)S(1)} %get-tuple-element.20), channel_id=1, source_target_pairs={{0,3},{1,2},{2,1},{3,0},{4,7},{5,6},{6,5},{7,4},{8,11},{9,10},{10,... | collective-permute-start | bytes 294920 | tf_op jit(solution)/shard_map/ppermute | solution.py:93
  32.5 4.6 %collective-permute-start.10 = (f32[1,8,64]{2,1,0:T(8,128)S(1)}, f32[1,8,64]{2,1,0:T(8,128)S(1)}, u32[]{:S(2)}, u32[]{:S(2)}) collective-permute-start(f32[1,8,64]{2,1,0:T(8,128)S(1)} %get-tuple-element.36), channel_id=1, source_target_pairs={{0,2},{1,3},{2,0},{3,1},{4,6},{5,7},{6,4},{7,5},{8,10},{9,11},{10,... | collective-permute-start | bytes 6152 | tf_op jit(solution)/shard_map/ppermute | solution.py:42
  35.2 5.4 %collective-permute-start.11 = (f32[1,8,64]{2,1,0:T(8,128)S(1)}, f32[1,8,64]{2,1,0:T(8,128)S(1)}, u32[]{:S(2)}, u32[]{:S(2)}) collective-permute-start(f32[1,8,64]{2,1,0:T(8,128)S(1)} %get-tuple-element.35), channel_id=1, source_target_pairs={{0,3},{1,2},{2,1},{3,0},{4,7},{5,6},{6,5},{7,4},{8,11},{9,10},{10,... | collective-permute-start | bytes 6152 | tf_op jit(solution)/shard_map/ppermute | solution.py:42
  36.5 4.1 %collective-permute-start.9 = (f32[1,8,64]{2,1,0:T(8,128)S(1)}, f32[1,8,64]{2,1,0:T(8,128)S(1)}, u32[]{:S(2)}, u32[]{:S(2)}) collective-permute-start(f32[1,8,64]{2,1,0:T(8,128)S(1)} %get-tuple-element.34), channel_id=1, source_target_pairs={{0,1},{1,0},{2,3},{3,2},{4,5},{5,4},{6,7},{7,6},{8,9},{9,8},{10,11... | collective-permute-start | bytes 6152 | tf_op jit(solution)/shard_map/ppermute | solution.py:42
  40.6 2.7 %collective-permute-start.12 = (f32[8,64]{1,0:T(8,128)S(1)}, f32[8,64]{1,0:T(8,128)S(1)}, u32[]{:S(2)}, u32[]{:S(2)}) collective-permute-start(f32[8,64]{1,0:T(8,128)S(1)} %bitcast_add_fusion), channel_id=1, source_target_pairs={{0,4},{4,0},{8,12},{12,8},{1,5},{5,1},{9,13},{13,9},{2,6},{6,2},{1... | collective-permute-start | bytes 6152 | tf_op jit(solution)/shard_map/ppermute | solution.py:58
  40.7 3.7 %collective-permute-start.13 = (f32[8,64]{1,0:T(8,128)S(1)}, f32[8,64]{1,0:T(8,128)S(1)}, u32[]{:S(2)}, u32[]{:S(2)}) collective-permute-start(f32[8,64]{1,0:T(8,128)S(1)} %bitcast_add_fusion), channel_id=1, source_target_pairs={{0,8},{4,12},{8,0},{12,4},{1,9},{5,13},{9,1},{13,5},{2,10},{6,14},... | collective-permute-start | bytes 6152 | tf_op jit(solution)/shard_map/ppermute | solution.py:58
  42.3 3.0 %collective-permute-start.14 = (f32[8,64]{1,0:T(8,128)S(1)}, f32[8,64]{1,0:T(8,128)S(1)}, u32[]{:S(2)}, u32[]{:S(2)}) collective-permute-start(f32[8,64]{1,0:T(8,128)S(1)} %bitcast_add_fusion), channel_id=1, source_target_pairs={{0,12},{4,8},{8,4},{12,0},{1,13},{5,9},{9,5},{13,1},{2,14},{6,10},... | collective-permute-start | bytes 6152 | tf_op jit(solution)/shard_map/ppermute | solution.py:58
  42.6 0.7 %copy-start.3 = (f32[64,8]{0,1:T(8,128)S(1)}, f32[64,8]{0,1:T(8,128)}, u32[]{:S(2)}) copy-start(f32[64,8]{0,1:T(8,128)} %param.12) | copy-start | bytes 6148

commit v15 on v11

--- a/solution.py
+++ b/solution.py
@@ -21,7 +21,21 @@
     expo = jnp.exp(scores - jnp.max(scores, axis=-1, keepdims=True))
     total = jnp.sum(expo, axis=-1, keepdims=True)
     weights = expo.astype(jnp.bfloat16)
-    out = jnp.einsum("iqk,ikd->iqd", weights, value_rows, preferred_element_type=jnp.float32)
+    if isinstance(value_rows, list):
+        out = None
+        first = 0
+        for block in value_rows:
+            size = block.shape[1]
+            part = jnp.einsum(
+                "iqk,ikd->iqd",
+                weights[:, :, first : first + size],
+                block,
+                preferred_element_type=jnp.float32,
+            )
+            out = part if out is None else out + part
+            first += size
+    else:
+        out = jnp.einsum("iqk,ikd->iqd", weights, value_rows, preferred_element_type=jnp.float32)
     return (out / total).astype(jnp.bfloat16)
 
 
@@ -93,8 +107,9 @@
                 pieces = [lax.ppermute(p, "seq", xor_pairs(groups, k)) for p in pieces]
             arrived[k] = pieces
         gathered = [
-            jnp.concatenate([arrived[k][i] for k in range(groups)], axis=1) for i in range(3)
+            jnp.concatenate([arrived[k][i] for k in range(groups)], axis=1) for i in range(2)
         ]
+        gathered.append([arrived[k][2] for k in range(groups)])
         partner_order = True
     else:
         stacked = jnp.stack(chunks, axis=1)

time: 46.1 us -> 45.4 us (0.985)
  waiting for transfers between devices: 12.3 us -> 11.1 us
  matrix products: 1.25 us -> 2.3 us
  starting transfers between devices: 25.3 us -> 24.8 us
    ppermute x3, waiting for transfers between devices: 4.05 us -> 2.77 us  [gather_prefix(): pieces.append(lax.ppermute(ordered[:, k], 'seq', xor_pairs(groups, k)))]
    dot_general x2 -> x4, matrix products: 0.99 us -> 1.59 us  [attend(): jnp.einsum('iqk,ikd->iqd', weights[:, :, first:first + size], block, pref...]
    ppermute x3, starting transfers between devices: 4.04 us -> 3.55 us  [gather_prefix(): pieces.append(lax.ppermute(ordered[:, k], 'seq', xor_pairs(groups, k)))]
    sub x0 -> x1, matrix products: none -> 0.46 us  [attend(): expo = jnp.exp(scores - jnp.max(scores, axis=-1, keepdims=True))]
  transfers between devices with their start and end apart: 15 -> 15, of which waited for: 6 -> 6; matrix products, arithmetic and copies ran while one was open for 8% -> 10% of each run, Pallas kernels for 0% -> 0%
where the time goes in v15:
time: 45.4 us; the launch traced here: 45.2 us
  starting transfers between devices  24.8 us (55%)
  waiting for transfers between devices  11.1 us (24%)
  local copies, waits for them, and re-layouts  3.93 us (9%)
  matrix products  2.3 us (5%)
  other arithmetic  2.2 us (5%)
  between operations  0.83 us (2%)
    ppermute x9, starting transfers between devices, on_device(): pieces = [lax.ppermute(p, 'seq', xor_pairs(groups, k)) for p in pieces]  19.3 us
    ppermute x9, waiting for transfers between devices, on_device(): pieces = [lax.ppermute(p, 'seq', xor_pairs(groups, k)) for p in pieces]  6.34 us
    ppermute x3, starting transfers between devices, gather_prefix(): pieces.append(lax.ppermute(ordered[:, k], 'seq', xor_pairs(groups, k)))  3.55 us
    ppermute x3, waiting for transfers between devices, gather_prefix(): pieces.append(lax.ppermute(ordered[:, k], 'seq', xor_pairs(groups, k)))  2.77 us
    ppermute x3, waiting for transfers between devices, gather_prefix(): other = lax.ppermute(total, 'step', xor_pairs(steps_axis, k))  2 us
    ppermute x3, starting transfers between devices, gather_prefix(): other = lax.ppermute(total, 'step', xor_pairs(steps_axis, k))  1.93 us
    dot_general x4, matrix products, attend(): jnp.einsum('iqk,ikd->iqd', weights[:, :, first:first + size], block, pref...  1.59 us
    another operation x2, local copies, waits for them, and re-layouts, on_device(): jnp.stack([jnp.broadcast_to(guide_scale, shape), jnp.broadcast_to(len_ful...  1.38 us
  transfers between devices with their start and end apart: 15, of which 6 were waited for; matrix products, arithmetic and copies ran while one was open for 10% of the time, Pallas kernels for 0%

profile of v15, /device:TPU:0, one launch (start us, length us, event | category | flops | bytes accessed | tf_op | source)
XLA Modules:
  0.0 45.2 jit_solution(3497184279434400303)
XLA Ops:
  0.0 1.1 %dynamic-slice_bitcast_fusion.6 = (bf16[48,8,128]{2,1,0:T(8,128)(2,1)S(1)}, bf16[48,8,128]{2,1,0:T(8,128)(2,1)S(1)}, bf16[48,8,128]{2,1,0:T(8,128)(2,1)S(1)}, bf16[48,8,128]{2,1,0:T(8,128)(2,1)S(1)}) fusion(bf16[4,48,8,128]{3,2,1,0:T(8,128)(2,1)} %bitcast.123, s32[]{:T(128)S(6)} %select_n.238, s32[]{:T(128)S(6)} %select_n.241, s32[]{:T(128)S(6)} %select_n.240, ...), kind=kLoop, calls=%fused_computation.43 | loop fusion | bytes 786448 | tf_op jit(solution)/shard_map/jit(dynamic_index_in_dim)/squeeze | solution.py:105
  1.1 3.1 %collective-permute-start.3 = (bf16[48,8,128]{2,1,0:T(8,128)(2,1)S(1)}, bf16[48,8,128]{2,1,0:T(8,128)(2,1)S(1)}, u32[]{:S(2)}, u32[]{:S(2)}) collective-permute-start(bf16[48,8,128]{2,1,0:T(8,128)(2,1)S(1)} %get-tuple-element.13), channel_id=1, source_target_pairs={{0,1},{1,0},{2,3},{3,2},{4,5},{5,4},{6,7},{7,6},{8,9},{9,8},{10,11... | collective-permute-start | bytes 294920 | tf_op jit(solution)/shard_map/ppermute | solution.py:107
  4.2 2.6 %collective-permute-start.4 = (bf16[48,8,128]{2,1,0:T(8,128)(2,1)S(1)}, bf16[48,8,128]{2,1,0:T(8,128)(2,1)S(1)}, u32[]{:S(2)}, u32[]{:S(2)}) collective-permute-start(bf16[48,8,128]{2,1,0:T(8,128)(2,1)S(1)} %get-tuple-element.12), channel_id=1, source_target_pairs={{0,2},{1,3},{2,0},{3,1},{4,6},{5,7},{6,4},{7,5},{8,10},{9,11},{10,... | collective-permute-start | bytes 294920 | tf_op jit(solution)/shard_map/ppermute | solution.py:107
  6.9 0.9 %collective-permute-start = (bf16[48,8,128]{2,1,0:T(8,128)(2,1)S(1)}, bf16[48,8,128]{2,1,0:T(8,128)(2,1)S(1)}, u32[]{:S(2)}, u32[]{:S(2)}) collective-permute-start(bf16[48,8,128]{2,1,0:T(8,128)(2,1)S(1)} %get-tuple-element.17), channel_id=1, source_target_pairs={{0,1},{1,0},{2,3},{3,2},{4,5},{5,4},{6,7},{7,6},{8,9},{9,8},{10,11... | collective-permute-start | bytes 294920 | tf_op jit(solution)/shard_map/ppermute | solution.py:107
  7.8 3.5 %collective-permute-start.1 = (bf16[48,8,128]{2,1,0:T(8,128)(2,1)S(1)}, bf16[48,8,128]{2,1,0:T(8,128)(2,1)S(1)}, u32[]{:S(2)}, u32[]{:S(2)}) collective-permute-start(bf16[48,8,128]{2,1,0:T(8,128)(2,1)S(1)} %get-tuple-element.16), channel_id=1, source_target_pairs={{0,2},{1,3},{2,0},{3,1},{4,6},{5,7},{6,4},{7,5},{8,10},{9,11},{10,... | collective-permute-start | bytes 294920 | tf_op jit(solution)/shard_map/ppermute | solution.py:107
  11.5 0.7 %fusion.49 = f32[]{:T(128)} fusion(f32[4]{0:T(128)S(1)} %select_reduce_fusion, s32[]{:T(128)S(6)} %axis_index.22), kind=kLoop, calls=%fused_computation.84 | loop fusion | flops 11 | bytes 24 | tf_op jit(solution)/shard_map/reduce_sum | solution.py:138
  12.8 0.6 %copy-done.6 = f32[8]{0:T(128)S(1)} copy-done((f32[8]{0:T(128)S(1)}, f32[8]{0:T(128)}, u32[]{:S(2)}) %copy-start.6) | copy-done | bytes 56
  13.5 0.7 %fusion.48 = f32[]{:T(128)} fusion(f32[8]{0:T(128)S(1)} %copy-done.6, s32[]{:T(128)} %bitcast.122), kind=kLoop, calls=%fused_computation.83 | loop fusion | flops 23 | bytes 40 | tf_op jit(solution)/shard_map/reduce_sum | solution.py:13
  14.2 1.3 %stack.12 = f32[2]{0:T(128)S(1)} pad(f32[1]{0:T(128)} %bitcast.1, f32[]{:T(128)} %fusion.49), padding=0_1 | pad | bytes 16 | tf_op jit(solution)/shard_map/stack | solution.py:143
  16.2 4.2 %collective-permute-start.8 = (bf16[48,8,128]{2,1,0:T(8,128)(2,1)S(1)}, bf16[48,8,128]{2,1,0:T(8,128)(2,1)S(1)}, u32[]{:S(2)}, u32[]{:S(2)}) collective-permute-start(bf16[48,8,128]{2,1,0:T(8,128)(2,1)S(1)} %get-tuple-element.8), channel_id=1, source_target_pairs={{0,3},{1,2},{2,1},{3,0},{4,7},{5,6},{6,5},{7,4},{8,11},{9,10},{10,... | collective-permute-start | bytes 294920 | tf_op jit(solution)/shard_map/ppermute | solution.py:107
  20.4 4.3 %collective-permute-start.7 = (bf16[48,8,128]{2,1,0:T(8,128)(2,1)S(1)}, bf16[48,8,128]{2,1,0:T(8,128)(2,1)S(1)}, u32[]{:S(2)}, u32[]{:S(2)}) collective-permute-start(bf16[48,8,128]{2,1,0:T(8,128)(2,1)S(1)} %get-tuple-element.7), channel_id=1, source_target_pairs={{0,2},{1,3},{2,0},{3,1},{4,6},{5,7},{6,4},{7,5},{8,10},{9,11},{10,... | collective-permute-start | bytes 294920 | tf_op jit(solution)/shard_map/ppermute | solution.py:107
  24.8 1.6 %collective-permute-done.1 = bf16[48,8,128]{2,1,0:T(8,128)(2,1)S(1)} collective-permute-done((bf16[48,8,128]{2,1,0:T(8,128)(2,1)S(1)}, bf16[48,8,128]{2,1,0:T(8,128)(2,1)S(1)}, u32[]{:S(2)}, u32[]{:S(2)}) %collective-permute-start.1) | collective-permute-done | bytes 98336 | tf_op jit(solution)/shard_map/ppermute | solution.py:107
  27.8 4.8 %collective-permute-done.7 = bf16[48,8,128]{2,1,0:T(8,128)(2,1)S(1)} collective-permute-done((bf16[48,8,128]{2,1,0:T(8,128)(2,1)S(1)}, bf16[48,8,128]{2,1,0:T(8,128)(2,1)S(1)}, u32[]{:S(2)}, u32[]{:S(2)}) %collective-permute-start.7) | collective-permute-done | bytes 98336 | tf_op jit(solution)/shard_map/ppermute | solution.py:107
  32.6 0.6 %multiply_reduce_fusion = (f32[48,32]{1,0:T(8,128)S(1)}, bf16[48,32,128]{2,1,0:T(8,128)(2,1)S(1)}) fusion(f32[48,32]{1,0:T(8,128)S(1)} %get-tuple-element.5, f32[48,32,128]{2,1,0:T(8,128)S(1)} %fusion.27, f32[48,32,128]{2,1,0:T(8,128)S(1)} %convolution_add_fusion.1, bf16[48,8,128]{2,1,0:T(8,128)(2,1)S(1)} %collective-permute-done.7, ...), kind=kOutput, calls=%fused_computation.12 | convolution fusion | flops 4520448 | bytes 2193408 | tf_op jit(solution)/shard_map/iqk,ikd->iqd/dot_general | solution.py:29
  33.5 0.9 %collective-permute-start.10 = (f32[1,8,64]{2,1,0:T(8,128)S(1)}, f32[1,8,64]{2,1,0:T(8,128)S(1)}, u32[]{:S(2)}, u32[]{:S(2)}) collective-permute-start(f32[1,8,64]{2,1,0:T(8,128)S(1)} %get-tuple-element.23), channel_id=1, source_target_pairs={{0,2},{1,3},{2,0},{3,1},{4,6},{5,7},{6,4},{7,5},{8,10},{9,11},{10,... | collective-permute-start | bytes 6152 | tf_op jit(solution)/shard_map/ppermute | solution.py:56
  34.5 1.7 %collective-permute-start.11 = (f32[1,8,64]{2,1,0:T(8,128)S(1)}, f32[1,8,64]{2,1,0:T(8,128)S(1)}, u32[]{:S(2)}, u32[]{:S(2)}) collective-permute-start(f32[1,8,64]{2,1,0:T(8,128)S(1)} %get-tuple-element.22), channel_id=1, source_target_pairs={{0,3},{1,2},{2,1},{3,0},{4,7},{5,6},{6,5},{7,4},{8,11},{9,10},{10,... | collective-permute-start | bytes 6152 | tf_op jit(solution)/shard_map/ppermute | solution.py:56
  36.2 0.9 %collective-permute-start.9 = (f32[1,8,64]{2,1,0:T(8,128)S(1)}, f32[1,8,64]{2,1,0:T(8,128)S(1)}, u32[]{:S(2)}, u32[]{:S(2)}) collective-permute-start(f32[1,8,64]{2,1,0:T(8,128)S(1)} %get-tuple-element.21), channel_id=1, source_target_pairs={{0,1},{1,0},{2,3},{3,2},{4,5},{5,4},{6,7},{7,6},{8,9},{9,8},{10,11... | collective-permute-start | bytes 6152 | tf_op jit(solution)/shard_map/ppermute | solution.py:56
  37.1 1.0 %collective-permute-done.10 = f32[1,8,64]{2,1,0:T(8,128)S(1)} collective-permute-done((f32[1,8,64]{2,1,0:T(8,128)S(1)}, f32[1,8,64]{2,1,0:T(8,128)S(1)}, u32[]{:S(2)}, u32[]{:S(2)}) %collective-permute-start.10) | collective-permute-done | bytes 2080 | tf_op jit(solution)/shard_map/ppermute | solution.py:56
  38.1 1.8 %collective-permute-done.11 = f32[1,8,64]{2,1,0:T(8,128)S(1)} collective-permute-done((f32[1,8,64]{2,1,0:T(8,128)S(1)}, f32[1,8,64]{2,1,0:T(8,128)S(1)}, u32[]{:S(2)}, u32[]{:S(2)}) %collective-permute-start.11) | collective-permute-done | bytes 2080 | tf_op jit(solution)/shard_map/ppermute | solution.py:56
  40.0 1.6 %collective-permute-start.13 = (f32[8,64]{1,0:T(8,128)S(1)}, f32[8,64]{1,0:T(8,128)S(1)}, u32[]{:S(2)}, u32[]{:S(2)}) collective-permute-start(f32[8,64]{1,0:T(8,128)S(1)} %bitcast_add_fusion), channel_id=1, source_target_pairs={{0,8},{4,12},{8,0},{12,4},{1,9},{5,13},{9,1},{13,5},{2,10},{6,14},... | collective-permute-start | bytes 6152 | tf_op jit(solution)/shard_map/ppermute | solution.py:72
  41.9 0.7 %copy-done.3 = f32[64,8]{0,1:T(8,128)S(1)} copy-done((f32[64,8]{0,1:T(8,128)S(1)}, f32[64,8]{0,1:T(8,128)}, u32[]{:S(2)}) %copy-start.3) | copy-done | bytes 2072
  42.5 1.1 %collective-permute-done.13 = f32[8,64]{1,0:T(8,128)S(1)} collective-permute-done((f32[8,64]{1,0:T(8,128)S(1)}, f32[8,64]{1,0:T(8,128)S(1)}, u32[]{:S(2)}, u32[]{:S(2)}) %collective-permute-start.13) | collective-permute-done | bytes 2080 | tf_op jit(solution)/shard_map/ppermute | solution.py:72
  43.6 0.9 %collective-permute-done.14 = f32[8,64]{1,0:T(8,128)S(1)} collective-permute-done((f32[8,64]{1,0:T(8,128)S(1)}, f32[8,64]{1,0:T(8,128)S(1)}, u32[]{:S(2)}, u32[]{:S(2)}) %collective-permute-start.14) | collective-permute-done | bytes 2080 | tf_op jit(solution)/shard_map/ppermute | solution.py:72
  44.6 0.6 %add_bitcast_fusion = f32[4,64,8]{1,2,0:T(8,128)} fusion(f32[4,8,64]{2,1,0:T(8,128)S(1)} %maximum_add_fusion, f32[8,64]{1,0:T(8,128)S(1)} %select_add_fusion), kind=kLoop, calls=%fused_computation.57 | loop fusion | flops 2048 | bytes 18432 | tf_op jit(solution)/shard_map/transpose | solution.py:74
  (44 shorter events, 3.1 us)
Async XLA Ops:
  0.0 33.2 %copy-start = (bf16[64,3072]{1,0:T(8,128)(2,1)S(1)}, bf16[64,3072]{1,0:T(8,128)(2,1)}, u32[]{:S(2)}) copy-start(bf16[64,3072]{1,0:T(8,128)(2,1)} %param.13) | copy-start | bytes 1179652
  0.0 6.8 %copy-start.1 = (bf16[4,2,24,8,128]{4,3,2,1,0:T(8,128)(2,1)S(1)}, bf16[4,2,24,8,128]{4,3,2,1,0:T(8,128)(2,1)}, u32[]{:S(2)}) copy-start(bf16[4,2,24,8,128]{4,3,2,1,0:T(8,128)(2,1)} %param.9) | copy-start | bytes 1179652
  1.1 14.4 %collective-permute-start.3 = (bf16[48,8,128]{2,1,0:T(8,128)(2,1)S(1)}, bf16[48,8,128]{2,1,0:T(8,128)(2,1)S(1)}, u32[]{:S(2)}, u32[]{:S(2)}) collective-permute-start(bf16[48,8,128]{2,1,0:T(8,128)(2,1)S(1)} %get-tuple-element.13), channel_id=1, source_target_pairs={{0,1},{1,0},{2,3},{3,2},{4,5},{5,4},{6,7},{7,6},{8,9},{9,8},{10,11... | collective-permute-start | bytes 294920 | tf_op jit(solution)/shard_map/ppermute | solution.py:107
  4.2 11.4 %collective-permute-start.4 = (bf16[48,8,128]{2,1,0:T(8,128)(2,1)S(1)}, bf16[48,8,128]{2,1,0:T(8,128)(2,1)S(1)}, u32[]{:S(2)}, u32[]{:S(2)}) collective-permute-start(bf16[48,8,128]{2,1,0:T(8,128)(2,1)S(1)} %get-tuple-element.12), channel_id=1, source_target_pairs={{0,2},{1,3},{2,0},{3,1},{4,6},{5,7},{6,4},{7,5},{8,10},{9,11},{10,... | collective-permute-start | bytes 294920 | tf_op jit(solution)/shard_map/ppermute | solution.py:107
  6.8 9.4 %collective-permute-start.5 = (bf16[48,8,128]{2,1,0:T(8,128)(2,1)S(1)}, bf16[48,8,128]{2,1,0:T(8,128)(2,1)S(1)}, u32[]{:S(2)}, u32[]{:S(2)}) collective-permute-start(bf16[48,8,128]{2,1,0:T(8,128)(2,1)S(1)} %get-tuple-element.11), channel_id=1, source_target_pairs={{0,3},{1,2},{2,1},{3,0},{4,7},{5,6},{6,5},{7,4},{8,11},{9,10},{10,... | collective-permute-start | bytes 294920 | tf_op jit(solution)/shard_map/ppermute | solution.py:107
  6.8 4.5 %copy-start.4 = (f32[1000]{0:T(1024)S(1)}, f32[1000]{0:T(1024)}, u32[]{:S(2)}) copy-start(f32[1000]{0:T(1024)} %param.16) | copy-start | bytes 12004
  6.8 8.8 %copy-start.2 = (bf16[4,2,24,8,128]{4,3,2,1,0:T(8,128)(2,1)S(1)}, bf16[4,2,24,8,128]{4,3,2,1,0:T(8,128)(2,1)}, u32[]{:S(2)}) copy-start(bf16[4,2,24,8,128]{4,3,2,1,0:T(8,128)(2,1)} %param.11) | copy-start | bytes 1179652
  6.9 4.4 %copy-start.5 = (s32[4]{0:T(128)S(1)}, s32[4]{0:T(128)}, u32[]{:S(2)}) copy-start(s32[4]{0:T(128)} %param.17) | copy-start | bytes 52
  6.9 13.5 %collective-permute-start = (bf16[48,8,128]{2,1,0:T(8,128)(2,1)S(1)}, bf16[48,8,128]{2,1,0:T(8,128)(2,1)S(1)}, u32[]{:S(2)}, u32[]{:S(2)}) collective-permute-start(bf16[48,8,128]{2,1,0:T(8,128)(2,1)S(1)} %get-tuple-element.17), channel_id=1, source_target_pairs={{0,1},{1,0},{2,3},{3,2},{4,5},{5,4},{6,7},{7,6},{8,9},{9,8},{10,11... | collective-permute-start | bytes 294920 | tf_op jit(solution)/shard_map/ppermute | solution.py:107
  7.8 18.5 %collective-permute-start.1 = (bf16[48,8,128]{2,1,0:T(8,128)(2,1)S(1)}, bf16[48,8,128]{2,1,0:T(8,128)(2,1)S(1)}, u32[]{:S(2)}, u32[]{:S(2)}) collective-permute-start(bf16[48,8,128]{2,1,0:T(8,128)(2,1)S(1)} %get-tuple-element.16), channel_id=1, source_target_pairs={{0,2},{1,3},{2,0},{3,1},{4,6},{5,7},{6,4},{7,5},{8,10},{9,11},{10,... | collective-permute-start | bytes 294920 | tf_op jit(solution)/shard_map/ppermute | solution.py:107
  12.8 0.7 %copy-start.6 = (f32[8]{0:T(128)S(1)}, f32[8]{0:T(128)}, u32[]{:S(2)}) copy-start(f32[8]{0:T(128)} %param.14) | copy-start | bytes 100
  15.5 10.8 %collective-permute-start.2 = (bf16[48,8,128]{2,1,0:T(8,128)(2,1)S(1)}, bf16[48,8,128]{2,1,0:T(8,128)(2,1)S(1)}, u32[]{:S(2)}, u32[]{:S(2)}) collective-permute-start(bf16[48,8,128]{2,1,0:T(8,128)(2,1)S(1)} %get-tuple-element.15), channel_id=1, source_target_pairs={{0,3},{1,2},{2,1},{3,0},{4,7},{5,6},{6,5},{7,4},{8,11},{9,10},{10,... | collective-permute-start | bytes 294920 | tf_op jit(solution)/shard_map/ppermute | solution.py:107
  15.7 11.5 %collective-permute-start.6 = (bf16[48,8,128]{2,1,0:T(8,128)(2,1)S(1)}, bf16[48,8,128]{2,1,0:T(8,128)(2,1)S(1)}, u32[]{:S(2)}, u32[]{:S(2)}) collective-permute-start(bf16[48,8,128]{2,1,0:T(8,128)(2,1)S(1)} %get-tuple-element.9), channel_id=1, source_target_pairs={{0,1},{1,0},{2,3},{3,2},{4,5},{5,4},{6,7},{7,6},{8,9},{9,8},{10,11... | collective-permute-start | bytes 294920 | tf_op jit(solution)/shard_map/ppermute | solution.py:107
  16.2 11.2 %collective-permute-start.8 = (bf16[48,8,128]{2,1,0:T(8,128)(2,1)S(1)}, bf16[48,8,128]{2,1,0:T(8,128)(2,1)S(1)}, u32[]{:S(2)}, u32[]{:S(2)}) collective-permute-start(bf16[48,8,128]{2,1,0:T(8,128)(2,1)S(1)} %get-tuple-element.8), channel_id=1, source_target_pairs={{0,3},{1,2},{2,1},{3,0},{4,7},{5,6},{6,5},{7,4},{8,11},{9,10},{10,... | collective-permute-start | bytes 294920 | tf_op jit(solution)/shard_map/ppermute | solution.py:107
  20.4 12.1 %collective-permute-start.7 = (bf16[48,8,128]{2,1,0:T(8,128)(2,1)S(1)}, bf16[48,8,128]{2,1,0:T(8,128)(2,1)S(1)}, u32[]{:S(2)}, u32[]{:S(2)}) collective-permute-start(bf16[48,8,128]{2,1,0:T(8,128)(2,1)S(1)} %get-tuple-element.7), channel_id=1, source_target_pairs={{0,2},{1,3},{2,0},{3,1},{4,6},{5,7},{6,4},{7,5},{8,10},{9,11},{10,... | collective-permute-start | bytes 294920 | tf_op jit(solution)/shard_map/ppermute | solution.py:107
  33.5 4.6 %collective-permute-start.10 = (f32[1,8,64]{2,1,0:T(8,128)S(1)}, f32[1,8,64]{2,1,0:T(8,128)S(1)}, u32[]{:S(2)}, u32[]{:S(2)}) collective-permute-start(f32[1,8,64]{2,1,0:T(8,128)S(1)} %get-tuple-element.23), channel_id=1, source_target_pairs={{0,2},{1,3},{2,0},{3,1},{4,6},{5,7},{6,4},{7,5},{8,10},{9,11},{10,... | collective-permute-start | bytes 6152 | tf_op jit(solution)/shard_map/ppermute | solution.py:56
  34.5 5.4 %collective-permute-start.11 = (f32[1,8,64]{2,1,0:T(8,128)S(1)}, f32[1,8,64]{2,1,0:T(8,128)S(1)}, u32[]{:S(2)}, u32[]{:S(2)}) collective-permute-start(f32[1,8,64]{2,1,0:T(8,128)S(1)} %get-tuple-element.22), channel_id=1, source_target_pairs={{0,3},{1,2},{2,1},{3,0},{4,7},{5,6},{6,5},{7,4},{8,11},{9,10},{10,... | collective-permute-start | bytes 6152 | tf_op jit(solution)/shard_map/ppermute | solution.py:56
  36.2 3.7 %collective-permute-start.9 = (f32[1,8,64]{2,1,0:T(8,128)S(1)}, f32[1,8,64]{2,1,0:T(8,128)S(1)}, u32[]{:S(2)}, u32[]{:S(2)}) collective-permute-start(f32[1,8,64]{2,1,0:T(8,128)S(1)} %get-tuple-element.21), channel_id=1, source_target_pairs={{0,1},{1,0},{2,3},{3,2},{4,5},{5,4},{6,7},{7,6},{8,9},{9,8},{10,11... | collective-permute-start | bytes 6152 | tf_op jit(solution)/shard_map/ppermute | solution.py:56
  39.9 2.7 %collective-permute-start.12 = (f32[8,64]{1,0:T(8,128)S(1)}, f32[8,64]{1,0:T(8,128)S(1)}, u32[]{:S(2)}, u32[]{:S(2)}) collective-permute-start(f32[8,64]{1,0:T(8,128)S(1)} %bitcast_add_fusion), channel_id=1, source_target_pairs={{0,4},{4,0},{8,12},{12,8},{1,5},{5,1},{9,13},{13,9},{2,6},{6,2},{1... | collective-permute-start | bytes 6152 | tf_op jit(solution)/shard_map/ppermute | solution.py:72
  40.0 3.7 %collective-permute-start.13 = (f32[8,64]{1,0:T(8,128)S(1)}, f32[8,64]{1,0:T(8,128)S(1)}, u32[]{:S(2)}, u32[]{:S(2)}) collective-permute-start(f32[8,64]{1,0:T(8,128)S(1)} %bitcast_add_fusion), channel_id=1, source_target_pairs={{0,8},{4,12},{8,0},{12,4},{1,9},{5,13},{9,1},{13,5},{2,10},{6,14},... | collective-permute-start | bytes 6152 | tf_op jit(solution)/shard_map/ppermute | solution.py:72
  41.5 3.0 %collective-permute-start.14 = (f32[8,64]{1,0:T(8,128)S(1)}, f32[8,64]{1,0:T(8,128)S(1)}, u32[]{:S(2)}, u32[]{:S(2)}) collective-permute-start(f32[8,64]{1,0:T(8,128)S(1)} %bitcast_add_fusion), channel_id=1, source_target_pairs={{0,12},{4,8},{8,4},{12,0},{1,13},{5,9},{9,5},{13,1},{2,14},{6,10},... | collective-permute-start | bytes 6152 | tf_op jit(solution)/shard_map/ppermute | solution.py:72
  41.8 0.7 %copy-start.3 = (f32[64,8]{0,1:T(8,128)S(1)}, f32[64,8]{0,1:T(8,128)}, u32[]{:S(2)}) copy-start(f32[64,8]{0,1:T(8,128)} %param.12) | copy-start | bytes 6148

commit v16 on v15

--- a/solution.py
+++ b/solution.py
@@ -41,6 +41,27 @@
 
 def xor_pairs(size, k):
     return [(i, i ^ k) for i in range(size)]
+
+
+def prefix_from_pieces(pieces, sources, start, step_dev, steps_axis):
+    local_steps = pieces[0].shape[0]
+    zero = jnp.zeros((), jnp.float32)
+    outs = []
+    for s in range(step_dev):
+        acc = None
+        for piece, source in zip(pieces, sources):
+            for t in range(local_steps):
+                term = jnp.where(source * local_steps + t <= s, piece[t], zero)
+                acc = term if acc is None else acc + term
+        outs.append(acc)
+    total = outs[-1]
+    local_cum = lax.optimization_barrier(jnp.stack(outs) + start[None])
+    position = lax.axis_index("step")
+    earlier = jnp.zeros_like(total)
+    for k in range(1, steps_axis):
+        other = lax.ppermute(total, "step", xor_pairs(steps_axis, k))
+        earlier = earlier + jnp.where((position ^ k) < position, other, zero)
+    return jnp.transpose(local_cum + earlier[None], (0, 2, 1))
 
 
 def gather_prefix(update, start, me, groups, step_dev, steps_axis, partner_order):
@@ -99,24 +120,18 @@
 
     chunks = [a.reshape(groups, per_dev, tok_dev, head_size) for a in (queries, keys, values)]
     whole_steps = per_dev % (branches * heads) == 0
-    if whole_steps and groups & (groups - 1) == 0:
+    partner_order = whole_steps and groups & (groups - 1) == 0
+    if partner_order:
         arrived = {}
         for k in reversed(range(groups)):
-            pieces = [lax.dynamic_index_in_dim(c, me ^ k, 0, keepdims=False) for c in chunks]
+            sent = [lax.dynamic_index_in_dim(c, me ^ k, 0, keepdims=False) for c in chunks[::-1]]
             if k:
-                pieces = [lax.ppermute(p, "seq", xor_pairs(groups, k)) for p in pieces]
-            arrived[k] = pieces
-        gathered = [
-            jnp.concatenate([arrived[k][i] for k in range(groups)], axis=1) for i in range(2)
-        ]
-        gathered.append([arrived[k][2] for k in range(groups)])
-        partner_order = True
+                sent = [lax.ppermute(p, "seq", xor_pairs(groups, k)) for p in sent]
+            arrived[k] = sent[::-1]
     else:
         stacked = jnp.stack(chunks, axis=1)
         gathered = lax.all_to_all(stacked, "seq", split_axis=0, concat_axis=3, tiled=True)
         gathered = gathered.reshape(3, per_dev, length, head_size)
-        partner_order = False
-    heads_out = attend(gathered[0], gathered[1], gathered[2])
 
     weight_heads = out_weight.reshape(channels, heads, head_size)
     guide_scale = lookup(cfg_table, cfg_index)[0]
@@ -124,32 +139,48 @@
 
     if whole_steps:
         local_steps = per_dev // (branches * heads)
-        ho = heads_out.reshape(local_steps, branches, heads, length, head_size)
-        wide = ho.astype(jnp.float32)
-        square_sum = jnp.sum(wide * wide, axis=(2, 4))
-        root_mean = jnp.sqrt(square_sum / (H * HD) + 1e-06)
-        drift = (
-            jnp.einsum("chd,sbhld->sblc", weight_heads, ho, preferred_element_type=jnp.float32)
-            / root_mean[:, :, :, None]
-        )
+        rows = tok_dev if partner_order else length
         owner = jnp.arange(step_dev, dtype=jnp.int32) // local_steps == me
         slot = jnp.arange(step_dev, dtype=jnp.int32) % local_steps
         mine = (owner[:, None] & (slot[:, None] == jnp.arange(local_steps)))[:, :, None, None]
         len_full = jnp.sum(
             jnp.where(mine, step_len[:, None, None, None], jnp.zeros((), jnp.float32)), axis=0
         )
-        shape = (local_steps, length, channels)
+        shape = (local_steps, rows, channels)
         coef = lax.optimization_barrier(
             jnp.stack([jnp.broadcast_to(guide_scale, shape), jnp.broadcast_to(len_full, shape)])
         )
         scale_full, len_full = coef[0], coef[1]
         start_t = start_latent.T
-        guided = drift[:, 1] + scale_full * (drift[:, 0] - drift[:, 1])
-        update = len_full * guided
+
+        def finish(heads_out):
+            ho = heads_out.reshape(local_steps, branches, heads, rows, head_size)
+            wide = ho.astype(jnp.float32)
+            square_sum = jnp.sum(wide * wide, axis=(2, 4))
+            root_mean = jnp.sqrt(square_sum / (H * HD) + 1e-06)
+            drift = (
+                jnp.einsum("chd,sbhld->sblc", weight_heads, ho, preferred_element_type=jnp.float32)
+                / root_mean[:, :, :, None]
+            )
+            guided = drift[:, 1] + scale_full * (drift[:, 0] - drift[:, 1])
+            return len_full * guided
+
+        if partner_order:
+            keys_all = jnp.concatenate([arrived[k][1] for k in range(groups)], axis=1)
+            values_list = [arrived[k][2] for k in range(groups)]
+            pieces = []
+            for k in range(groups):
+                piece = finish(attend(arrived[k][0], keys_all, values_list))
+                if k:
+                    piece = lax.ppermute(piece, "seq", xor_pairs(groups, k))
+                pieces.append(piece)
+            sources = [me ^ k for k in range(groups)]
+            return prefix_from_pieces(pieces, sources, start_t, step_dev, steps_axis)
+        update = finish(attend(gathered[0], gathered[1], gathered[2]))
         update = update.reshape(local_steps, groups, tok_dev, channels)
-        return gather_prefix(
-            update, start_t, me, groups, step_dev, steps_axis, partner_order
-        )
+        return gather_prefix(update, start_t, me, groups, step_dev, steps_axis, False)
+
+    heads_out = attend(gathered[0], gathered[1], gathered[2])
 
     assert heads % per_dev == 0
     share = heads // per_dev

time: 45.4 us -> 51.8 us (1.14)
  matrix products: 2.3 us -> 7.76 us
  waiting for transfers between devices: 11.1 us -> 12.5 us
    dot_general x4 -> x16, matrix products: 1.59 us -> 4.1 us  [attend(): jnp.einsum('iqk,ikd->iqd', weights[:, :, first:first + size], block, pref...]
    sub x1 -> x4, matrix products: 0.46 us -> 2.8 us  [attend(): expo = jnp.exp(scores - jnp.max(scores, axis=-1, keepdims=True))]
    ppermute x15, waiting for transfers between devices: 11.1 us -> 12.5 us  [the longest x9 7.13 us: on_device(): sent = [lax.ppermute(p, 'seq', xor_pairs(groups, k)) for p in sent]]
    dot_general x1 -> x4, matrix products: 0.25 us -> 0.86 us  [finish(): jnp.einsum('chd,sbhld->sblc', weight_heads, ho, preferred_element_type=jn...]
  transfers between devices with their start and end apart: 15 -> 15, of which waited for: 6 -> 6; matrix products, arithmetic and copies ran while one was open for 10% -> 17% of each run, Pallas kernels for 0% -> 0%
where the time goes in v16:
time: 51.8 us; the launch traced here: 51.5 us
  starting transfers between devices  24.3 us (47%)
  waiting for transfers between devices  12.5 us (24%)
  matrix products  7.76 us (15%)
  local copies, waits for them, and re-layouts  3.8 us (7%)
  other arithmetic  2.27 us (4%)
  between operations  0.89 us (2%)
    ppermute x9, starting transfers between devices, on_device(): sent = [lax.ppermute(p, 'seq', xor_pairs(groups, k)) for p in sent]  18.9 us
    ppermute x9, waiting for transfers between devices, on_device(): sent = [lax.ppermute(p, 'seq', xor_pairs(groups, k)) for p in sent]  7.13 us
    ppermute x3, waiting for transfers between devices, on_device(): piece = lax.ppermute(piece, 'seq', xor_pairs(groups, k))  4.25 us
    dot_general x16, matrix products, attend(): jnp.einsum('iqk,ikd->iqd', weights[:, :, first:first + size], block, pref...  4.1 us
    ppermute x3, starting transfers between devices, on_device(): piece = lax.ppermute(piece, 'seq', xor_pairs(groups, k))  3.55 us
    sub x4, matrix products, attend(): expo = jnp.exp(scores - jnp.max(scores, axis=-1, keepdims=True))  2.8 us
    ppermute x3, starting transfers between devices, prefix_from_pieces(): other = lax.ppermute(total, 'step', xor_pairs(steps_axis, k))  1.92 us
    unnamed x14, local copies, waits for them, and re-layouts  1.36 us
  transfers between devices with their start and end apart: 15, of which 6 were waited for; matrix products, arithmetic and copies ran while one was open for 17% of the time, Pallas kernels for 0%

profile of v16, /device:TPU:0, one launch (start us, length us, event | category | flops | bytes accessed | tf_op | source)
XLA Modules:
  0.0 51.5 jit_solution(3840939945356512939)
XLA Ops:
  0.0 1.1 %dynamic-slice_bitcast_fusion.2 = (bf16[48,8,128]{2,1,0:T(8,128)(2,1)S(1)}, bf16[48,8,128]{2,1,0:T(8,128)(2,1)S(1)}, bf16[48,8,128]{2,1,0:T(8,128)(2,1)S(1)}) fusion(bf16[4,48,8,128]{3,2,1,0:T(8,128)(2,1)} %bitcast.236, s32[]{:T(128)S(6)} %select_n.228, s32[]{:T(128)S(6)} %select_n.230, s32[]{:T(128)S(6)} %select_n.229), kind=kLoop, calls=%fused_computation.89 | loop fusion | bytes 589836 | tf_op jit(solution)/shard_map/jit(dynamic_index_in_dim)/squeeze | solution.py:127
  1.1 3.1 %collective-permute-start.6 = (bf16[48,8,128]{2,1,0:T(8,128)(2,1)S(1)}, bf16[48,8,128]{2,1,0:T(8,128)(2,1)S(1)}, u32[]{:S(2)}, u32[]{:S(2)}) collective-permute-start(bf16[48,8,128]{2,1,0:T(8,128)(2,1)S(1)} %get-tuple-element.7), channel_id=1, source_target_pairs={{0,1},{1,0},{2,3},{3,2},{4,5},{5,4},{6,7},{7,6},{8,9},{9,8},{10,11... | collective-permute-start | bytes 294920 | tf_op jit(solution)/shard_map/ppermute | solution.py:129
  4.2 2.5 %collective-permute-start.10 = (bf16[48,8,128]{2,1,0:T(8,128)(2,1)S(1)}, bf16[48,8,128]{2,1,0:T(8,128)(2,1)S(1)}, u32[]{:S(2)}, u32[]{:S(2)}) collective-permute-start(bf16[48,8,128]{2,1,0:T(8,128)(2,1)S(1)} %get-tuple-element.8), channel_id=1, source_target_pairs={{0,3},{1,2},{2,1},{3,0},{4,7},{5,6},{6,5},{7,4},{8,11},{9,10},{10,... | collective-permute-start | bytes 294920 | tf_op jit(solution)/shard_map/ppermute | solution.py:129
  6.7 1.4 %collective-permute-start.2 = (bf16[48,8,128]{2,1,0:T(8,128)(2,1)S(1)}, bf16[48,8,128]{2,1,0:T(8,128)(2,1)S(1)}, u32[]{:S(2)}, u32[]{:S(2)}) collective-permute-start(bf16[48,8,128]{2,1,0:T(8,128)(2,1)S(1)} %get-tuple-element.14), channel_id=1, source_target_pairs={{0,3},{1,2},{2,1},{3,0},{4,7},{5,6},{6,5},{7,4},{8,11},{9,10},{10,... | collective-permute-start | bytes 294920 | tf_op jit(solution)/shard_map/ppermute | solution.py:129
  8.1 0.8 %collective-permute-start.1 = (bf16[48,8,128]{2,1,0:T(8,128)(2,1)S(1)}, bf16[48,8,128]{2,1,0:T(8,128)(2,1)S(1)}, u32[]{:S(2)}, u32[]{:S(2)}) collective-permute-start(bf16[48,8,128]{2,1,0:T(8,128)(2,1)S(1)} %get-tuple-element.15), channel_id=1, source_target_pairs={{0,2},{1,3},{2,0},{3,1},{4,6},{5,7},{6,4},{7,5},{8,10},{9,11},{10,... | collective-permute-start | bytes 294920 | tf_op jit(solution)/shard_map/ppermute | solution.py:129
  8.9 2.2 %collective-permute-start = (bf16[48,8,128]{2,1,0:T(8,128)(2,1)S(1)}, bf16[48,8,128]{2,1,0:T(8,128)(2,1)S(1)}, u32[]{:S(2)}, u32[]{:S(2)}) collective-permute-start(bf16[48,8,128]{2,1,0:T(8,128)(2,1)S(1)} %get-tuple-element.16), channel_id=1, source_target_pairs={{0,1},{1,0},{2,3},{3,2},{4,5},{5,4},{6,7},{7,6},{8,9},{9,8},{10,11... | collective-permute-start | bytes 294920 | tf_op jit(solution)/shard_map/ppermute | solution.py:129
  12.0 0.6 %fusion.95 = f32[]{:T(128)} fusion(f32[4]{0:T(128)S(1)} %select_reduce_fusion, s32[]{:T(128)S(6)} %axis_index.22), kind=kLoop, calls=%fused_computation.153 | loop fusion | flops 11 | bytes 24 | tf_op jit(solution)/shard_map/reduce_sum | solution.py:146
  12.6 0.7 %copy-done.6 = f32[8]{0:T(128)S(1)} copy-done((f32[8]{0:T(128)S(1)}, f32[8]{0:T(128)}, u32[]{:S(2)}) %copy-start.6) | copy-done | bytes 56
  13.3 0.7 %fusion.94 = f32[]{:T(128)} fusion(f32[8]{0:T(128)S(1)} %copy-done.6, s32[]{:T(128)} %bitcast.229), kind=kLoop, calls=%fused_computation.152 | loop fusion | flops 23 | bytes 40 | tf_op jit(solution)/shard_map/reduce_sum | solution.py:13
  14.0 1.2 %stack.12 = f32[2]{0:T(128)S(1)} pad(f32[1]{0:T(128)} %bitcast.1, f32[]{:T(128)} %fusion.95), padding=0_1 | pad | bytes 16 | tf_op jit(solution)/shard_map/stack | solution.py:151
  15.3 2.9 %collective-permute-start.8 = (bf16[48,8,128]{2,1,0:T(8,128)(2,1)S(1)}, bf16[48,8,128]{2,1,0:T(8,128)(2,1)S(1)}, u32[]{:S(2)}, u32[]{:S(2)}) collective-permute-start(bf16[48,8,128]{2,1,0:T(8,128)(2,1)S(1)} %get-tuple-element.9), channel_id=1, source_target_pairs={{0,2},{1,3},{2,0},{3,1},{4,6},{5,7},{6,4},{7,5},{8,10},{9,11},{10,... | collective-permute-start | bytes 294920 | tf_op jit(solution)/shard_map/ppermute | solution.py:129
  18.3 3.2 %collective-permute-start.4 = (bf16[48,8,128]{2,1,0:T(8,128)(2,1)S(1)}, bf16[48,8,128]{2,1,0:T(8,128)(2,1)S(1)}, u32[]{:S(2)}, u32[]{:S(2)}) collective-permute-start(bf16[48,8,128]{2,1,0:T(8,128)(2,1)S(1)} %get-tuple-element.10), channel_id=1, source_target_pairs={{0,2},{1,3},{2,0},{3,1},{4,6},{5,7},{6,4},{7,5},{8,10},{9,11},{10,... | collective-permute-start | bytes 294920 | tf_op jit(solution)/shard_map/ppermute | solution.py:129
  21.4 2.4 %collective-permute-done.1 = bf16[48,8,128]{2,1,0:T(8,128)(2,1)S(1)} collective-permute-done((bf16[48,8,128]{2,1,0:T(8,128)(2,1)S(1)}, bf16[48,8,128]{2,1,0:T(8,128)(2,1)S(1)}, u32[]{:S(2)}, u32[]{:S(2)}) %collective-permute-start.1) | collective-permute-done | bytes 98336 | tf_op jit(solution)/shard_map/ppermute | solution.py:129
  23.8 2.7 %collective-permute-start.5 = (bf16[48,8,128]{2,1,0:T(8,128)(2,1)S(1)}, bf16[48,8,128]{2,1,0:T(8,128)(2,1)S(1)}, u32[]{:S(2)}, u32[]{:S(2)}) collective-permute-start(bf16[48,8,128]{2,1,0:T(8,128)(2,1)S(1)} %get-tuple-element.11), channel_id=1, source_target_pairs={{0,3},{1,2},{2,1},{3,0},{4,7},{5,6},{6,5},{7,4},{8,11},{9,10},{10,... | collective-permute-start | bytes 294920 | tf_op jit(solution)/shard_map/ppermute | solution.py:129
  27.2 4.7 %collective-permute-done.3 = bf16[48,8,128]{2,1,0:T(8,128)(2,1)S(1)} collective-permute-done((bf16[48,8,128]{2,1,0:T(8,128)(2,1)S(1)}, bf16[48,8,128]{2,1,0:T(8,128)(2,1)S(1)}, u32[]{:S(2)}, u32[]{:S(2)}) %collective-permute-start.3) | collective-permute-done | bytes 98336 | tf_op jit(solution)/shard_map/ppermute | solution.py:129
  32.9 1.4 %fusion.99 = (f32[48,8]{1,0:T(8,128)S(1)}, bf16[48,8,32]{2,1,0:T(8,128)(2,1)S(1)}) fusion(bf16[4,48,8,128]{3,2,1,0:T(8,128)(2,1)} %bitcast.237, s32[]{:T(128)S(6)} %select_n.227, bf16[48,8,128]{2,1,0:T(8,128)(2,1)S(1)} %collective-permute-done.2, bf16[48,8,128]{2,1,0:T(8,128)(2,1)S(1)} %collective-permute-done.1, ...), kind=kOutput, calls=%fused_computation.154 | convolution fusion | flops 4767775 | bytes 517636 | tf_op jit(solution)/shard_map/sub | solution.py:21
  39.1 0.9 %collective-permute-start.7 = (f32[1,8,64]{2,1,0:T(8,128)S(1)}, f32[1,8,64]{2,1,0:T(8,128)S(1)}, u32[]{:S(2)}, u32[]{:S(2)}) collective-permute-start(f32[1,8,64]{2,1,0:T(8,128)S(1)} %get-tuple-element.28), channel_id=1, source_target_pairs={{0,1},{1,0},{2,3},{3,2},{4,5},{5,4},{6,7},{7,6},{8,9},{9,8},{10,11... | collective-permute-start | bytes 6152 | tf_op jit(solution)/shard_map/ppermute | solution.py:175
  40.0 2.6 %collective-permute-start.11 = (f32[1,8,64]{2,1,0:T(8,128)S(1)}, f32[1,8,64]{2,1,0:T(8,128)S(1)}, u32[]{:S(2)}, u32[]{:S(2)}) collective-permute-start(f32[1,8,64]{2,1,0:T(8,128)S(1)} %get-tuple-element.29), channel_id=1, source_target_pairs={{0,3},{1,2},{2,1},{3,0},{4,7},{5,6},{6,5},{7,4},{8,11},{9,10},{10,... | collective-permute-start | bytes 6152 | tf_op jit(solution)/shard_map/ppermute | solution.py:175
  42.9 2.6 %collective-permute-done.11 = f32[1,8,64]{2,1,0:T(8,128)S(1)} collective-permute-done((f32[1,8,64]{2,1,0:T(8,128)S(1)}, f32[1,8,64]{2,1,0:T(8,128)S(1)}, u32[]{:S(2)}, u32[]{:S(2)}) %collective-permute-start.11) | collective-permute-done | bytes 2080 | tf_op jit(solution)/shard_map/ppermute | solution.py:175
  45.4 1.7 %collective-permute-done.9 = f32[1,8,64]{2,1,0:T(8,128)S(1)} collective-permute-done((f32[1,8,64]{2,1,0:T(8,128)S(1)}, f32[1,8,64]{2,1,0:T(8,128)S(1)}, u32[]{:S(2)}, u32[]{:S(2)}) %collective-permute-start.9) | collective-permute-done | bytes 2080 | tf_op jit(solution)/shard_map/ppermute | solution.py:175
  47.2 1.6 %collective-permute-start.13 = (f32[8,64]{1,0:T(8,128)S(1)}, f32[8,64]{1,0:T(8,128)S(1)}, u32[]{:S(2)}, u32[]{:S(2)}) collective-permute-start(f32[8,64]{1,0:T(8,128)S(1)} %bitcast_add_fusion), channel_id=1, source_target_pairs={{0,8},{4,12},{8,0},{12,4},{1,9},{5,13},{9,1},{13,5},{2,10},{6,14},... | collective-permute-start | bytes 6152 | tf_op jit(solution)/shard_map/ppermute | solution.py:62
  49.1 0.7 %copy-done.3 = f32[64,8]{0,1:T(8,128)S(1)} copy-done((f32[64,8]{0,1:T(8,128)S(1)}, f32[64,8]{0,1:T(8,128)}, u32[]{:S(2)}) %copy-start.3) | copy-done | bytes 2072
  50.2 0.7 %collective-permute-done.13 = f32[8,64]{1,0:T(8,128)S(1)} collective-permute-done((f32[8,64]{1,0:T(8,128)S(1)}, f32[8,64]{1,0:T(8,128)S(1)}, u32[]{:S(2)}, u32[]{:S(2)}) %collective-permute-start.13) | collective-permute-done | bytes 2080 | tf_op jit(solution)/shard_map/ppermute | solution.py:62
  50.9 0.6 %add_bitcast_fusion = f32[4,64,8]{1,2,0:T(8,128)} fusion(f32[4,8,64]{2,1,0:T(8,128)S(1)} %maximum_add_fusion, f32[8,64]{1,0:T(8,128)S(1)} %select_add_fusion), kind=kLoop, calls=%fused_computation.103 | loop fusion | flops 2048 | bytes 18432 | tf_op jit(solution)/shard_map/transpose | solution.py:64
  (67 shorter events, 7.8 us)
Async XLA Ops:
  0.0 38.4 %copy-start = (bf16[64,3072]{1,0:T(8,128)(2,1)S(1)}, bf16[64,3072]{1,0:T(8,128)(2,1)}, u32[]{:S(2)}) copy-start(bf16[64,3072]{1,0:T(8,128)(2,1)} %param.13) | copy-start | bytes 1179652
  0.0 6.7 %copy-start.2 = (bf16[4,2,24,8,128]{4,3,2,1,0:T(8,128)(2,1)S(1)}, bf16[4,2,24,8,128]{4,3,2,1,0:T(8,128)(2,1)}, u32[]{:S(2)}) copy-start(bf16[4,2,24,8,128]{4,3,2,1,0:T(8,128)(2,1)} %param.10) | copy-start | bytes 1179652
  1.1 35.8 %collective-permute-start.6 = (bf16[48,8,128]{2,1,0:T(8,128)(2,1)S(1)}, bf16[48,8,128]{2,1,0:T(8,128)(2,1)S(1)}, u32[]{:S(2)}, u32[]{:S(2)}) collective-permute-start(bf16[48,8,128]{2,1,0:T(8,128)(2,1)S(1)} %get-tuple-element.7), channel_id=1, source_target_pairs={{0,1},{1,0},{2,3},{3,2},{4,5},{5,4},{6,7},{7,6},{8,9},{9,8},{10,11... | collective-permute-start | bytes 294920 | tf_op jit(solution)/shard_map/ppermute | solution.py:129
  4.2 11.2 %collective-permute-start.10 = (bf16[48,8,128]{2,1,0:T(8,128)(2,1)S(1)}, bf16[48,8,128]{2,1,0:T(8,128)(2,1)S(1)}, u32[]{:S(2)}, u32[]{:S(2)}) collective-permute-start(bf16[48,8,128]{2,1,0:T(8,128)(2,1)S(1)} %get-tuple-element.8), channel_id=1, source_target_pairs={{0,3},{1,2},{2,1},{3,0},{4,7},{5,6},{6,5},{7,4},{8,11},{9,10},{10,... | collective-permute-start | bytes 294920 | tf_op jit(solution)/shard_map/ppermute | solution.py:129
  6.7 8.6 %copy-start.1 = (bf16[4,2,24,8,128]{4,3,2,1,0:T(8,128)(2,1)S(1)}, bf16[4,2,24,8,128]{4,3,2,1,0:T(8,128)(2,1)}, u32[]{:S(2)}) copy-start(bf16[4,2,24,8,128]{4,3,2,1,0:T(8,128)(2,1)} %param.11) | copy-start | bytes 1179652
  6.7 11.6 %collective-permute-start.2 = (bf16[48,8,128]{2,1,0:T(8,128)(2,1)S(1)}, bf16[48,8,128]{2,1,0:T(8,128)(2,1)S(1)}, u32[]{:S(2)}, u32[]{:S(2)}) collective-permute-start(bf16[48,8,128]{2,1,0:T(8,128)(2,1)S(1)} %get-tuple-element.14), channel_id=1, source_target_pairs={{0,3},{1,2},{2,1},{3,0},{4,7},{5,6},{6,5},{7,4},{8,11},{9,10},{10,... | collective-permute-start | bytes 294920 | tf_op jit(solution)/shard_map/ppermute | solution.py:129
  8.1 15.7 %collective-permute-start.1 = (bf16[48,8,128]{2,1,0:T(8,128)(2,1)S(1)}, bf16[48,8,128]{2,1,0:T(8,128)(2,1)S(1)}, u32[]{:S(2)}, u32[]{:S(2)}) collective-permute-start(bf16[48,8,128]{2,1,0:T(8,128)(2,1)S(1)} %get-tuple-element.15), channel_id=1, source_target_pairs={{0,2},{1,3},{2,0},{3,1},{4,6},{5,7},{6,4},{7,5},{8,10},{9,11},{10,... | collective-permute-start | bytes 294920 | tf_op jit(solution)/shard_map/ppermute | solution.py:129
  8.9 17.7 %collective-permute-start = (bf16[48,8,128]{2,1,0:T(8,128)(2,1)S(1)}, bf16[48,8,128]{2,1,0:T(8,128)(2,1)S(1)}, u32[]{:S(2)}, u32[]{:S(2)}) collective-permute-start(bf16[48,8,128]{2,1,0:T(8,128)(2,1)S(1)} %get-tuple-element.16), channel_id=1, source_target_pairs={{0,1},{1,0},{2,3},{3,2},{4,5},{5,4},{6,7},{7,6},{8,9},{9,8},{10,11... | collective-permute-start | bytes 294920 | tf_op jit(solution)/shard_map/ppermute | solution.py:129
  11.1 0.7 %copy-start.4 = (f32[1000]{0:T(1024)S(1)}, f32[1000]{0:T(1024)}, u32[]{:S(2)}) copy-start(f32[1000]{0:T(1024)} %param.16) | copy-start | bytes 12004
  11.1 0.7 %copy-start.5 = (s32[4]{0:T(128)S(1)}, s32[4]{0:T(128)}, u32[]{:S(2)}) copy-start(s32[4]{0:T(128)} %param.17) | copy-start | bytes 52
  12.6 0.7 %copy-start.6 = (f32[8]{0:T(128)S(1)}, f32[8]{0:T(128)}, u32[]{:S(2)}) copy-start(f32[8]{0:T(128)} %param.14) | copy-start | bytes 100
  15.3 20.0 %collective-permute-start.8 = (bf16[48,8,128]{2,1,0:T(8,128)(2,1)S(1)}, bf16[48,8,128]{2,1,0:T(8,128)(2,1)S(1)}, u32[]{:S(2)}, u32[]{:S(2)}) collective-permute-start(bf16[48,8,128]{2,1,0:T(8,128)(2,1)S(1)} %get-tuple-element.9), channel_id=1, source_target_pairs={{0,2},{1,3},{2,0},{3,1},{4,6},{5,7},{6,4},{7,5},{8,10},{9,11},{10,... | collective-permute-start | bytes 294920 | tf_op jit(solution)/shard_map/ppermute | solution.py:129
  18.3 14.2 %collective-permute-start.4 = (bf16[48,8,128]{2,1,0:T(8,128)(2,1)S(1)}, bf16[48,8,128]{2,1,0:T(8,128)(2,1)S(1)}, u32[]{:S(2)}, u32[]{:S(2)}) collective-permute-start(bf16[48,8,128]{2,1,0:T(8,128)(2,1)S(1)} %get-tuple-element.10), channel_id=1, source_target_pairs={{0,2},{1,3},{2,0},{3,1},{4,6},{5,7},{6,4},{7,5},{8,10},{9,11},{10,... | collective-permute-start | bytes 294920 | tf_op jit(solution)/shard_map/ppermute | solution.py:129
  23.8 8.4 %collective-permute-start.5 = (bf16[48,8,128]{2,1,0:T(8,128)(2,1)S(1)}, bf16[48,8,128]{2,1,0:T(8,128)(2,1)S(1)}, u32[]{:S(2)}, u32[]{:S(2)}) collective-permute-start(bf16[48,8,128]{2,1,0:T(8,128)(2,1)S(1)} %get-tuple-element.11), channel_id=1, source_target_pairs={{0,3},{1,2},{2,1},{3,0},{4,7},{5,6},{6,5},{7,4},{8,11},{9,10},{10,... | collective-permute-start | bytes 294920 | tf_op jit(solution)/shard_map/ppermute | solution.py:129
  26.6 5.4 %collective-permute-start.3 = (bf16[48,8,128]{2,1,0:T(8,128)(2,1)S(1)}, bf16[48,8,128]{2,1,0:T(8,128)(2,1)S(1)}, u32[]{:S(2)}, u32[]{:S(2)}) collective-permute-start(bf16[48,8,128]{2,1,0:T(8,128)(2,1)S(1)} %get-tuple-element.12), channel_id=1, source_target_pairs={{0,1},{1,0},{2,3},{3,2},{4,5},{5,4},{6,7},{7,6},{8,9},{9,8},{10,11... | collective-permute-start | bytes 294920 | tf_op jit(solution)/shard_map/ppermute | solution.py:129
  39.1 3.8 %collective-permute-start.7 = (f32[1,8,64]{2,1,0:T(8,128)S(1)}, f32[1,8,64]{2,1,0:T(8,128)S(1)}, u32[]{:S(2)}, u32[]{:S(2)}) collective-permute-start(f32[1,8,64]{2,1,0:T(8,128)S(1)} %get-tuple-element.28), channel_id=1, source_target_pairs={{0,1},{1,0},{2,3},{3,2},{4,5},{5,4},{6,7},{7,6},{8,9},{9,8},{10,11... | collective-permute-start | bytes 6152 | tf_op jit(solution)/shard_map/ppermute | solution.py:175
  40.0 5.4 %collective-permute-start.11 = (f32[1,8,64]{2,1,0:T(8,128)S(1)}, f32[1,8,64]{2,1,0:T(8,128)S(1)}, u32[]{:S(2)}, u32[]{:S(2)}) collective-permute-start(f32[1,8,64]{2,1,0:T(8,128)S(1)} %get-tuple-element.29), channel_id=1, source_target_pairs={{0,3},{1,2},{2,1},{3,0},{4,7},{5,6},{6,5},{7,4},{8,11},{9,10},{10,... | collective-permute-start | bytes 6152 | tf_op jit(solution)/shard_map/ppermute | solution.py:175
  42.6 4.5 %collective-permute-start.9 = (f32[1,8,64]{2,1,0:T(8,128)S(1)}, f32[1,8,64]{2,1,0:T(8,128)S(1)}, u32[]{:S(2)}, u32[]{:S(2)}) collective-permute-start(f32[1,8,64]{2,1,0:T(8,128)S(1)} %get-tuple-element.30), channel_id=1, source_target_pairs={{0,2},{1,3},{2,0},{3,1},{4,6},{5,7},{6,4},{7,5},{8,10},{9,11},{10,... | collective-permute-start | bytes 6152 | tf_op jit(solution)/shard_map/ppermute | solution.py:175
  47.2 3.1 %collective-permute-start.14 = (f32[8,64]{1,0:T(8,128)S(1)}, f32[8,64]{1,0:T(8,128)S(1)}, u32[]{:S(2)}, u32[]{:S(2)}) collective-permute-start(f32[8,64]{1,0:T(8,128)S(1)} %bitcast_add_fusion), channel_id=1, source_target_pairs={{0,12},{4,8},{8,4},{12,0},{1,13},{5,9},{9,5},{13,1},{2,14},{6,10},... | collective-permute-start | bytes 6152 | tf_op jit(solution)/shard_map/ppermute | solution.py:62
  47.2 3.7 %collective-permute-start.13 = (f32[8,64]{1,0:T(8,128)S(1)}, f32[8,64]{1,0:T(8,128)S(1)}, u32[]{:S(2)}, u32[]{:S(2)}) collective-permute-start(f32[8,64]{1,0:T(8,128)S(1)} %bitcast_add_fusion), channel_id=1, source_target_pairs={{0,8},{4,12},{8,0},{12,4},{1,9},{5,13},{9,1},{13,5},{2,10},{6,14},... | collective-permute-start | bytes 6152 | tf_op jit(solution)/shard_map/ppermute | solution.py:62
  48.8 2.1 %collective-permute-start.12 = (f32[8,64]{1,0:T(8,128)S(1)}, f32[8,64]{1,0:T(8,128)S(1)}, u32[]{:S(2)}, u32[]{:S(2)}) collective-permute-start(f32[8,64]{1,0:T(8,128)S(1)} %bitcast_add_fusion), channel_id=1, source_target_pairs={{0,4},{4,0},{8,12},{12,8},{1,5},{5,1},{9,13},{13,9},{2,6},{6,2},{1... | collective-permute-start | bytes 6152 | tf_op jit(solution)/shard_map/ppermute | solution.py:62
  49.1 0.7 %copy-start.3 = (f32[64,8]{0,1:T(8,128)S(1)}, f32[64,8]{0,1:T(8,128)}, u32[]{:S(2)}) copy-start(f32[64,8]{0,1:T(8,128)} %param.12) | copy-start | bytes 6148

commit v17 on v15

--- a/solution.py
+++ b/solution.py
@@ -50,11 +50,12 @@
     else:
         partners = me ^ jnp.arange(groups, dtype=jnp.int32)
         ordered = jnp.take(update, partners, axis=1)
-    pieces = [ordered[:, 0]]
-    sources = [me]
-    for k in range(1, groups):
-        pieces.append(lax.ppermute(ordered[:, k], "seq", xor_pairs(groups, k)))
-        sources.append(me ^ k)
+    every = lax.all_gather(ordered, "seq", axis=0, tiled=False)
+    pieces = []
+    sources = []
+    for j in range(groups):
+        pieces.append(lax.dynamic_index_in_dim(every[j], j ^ me, 1, keepdims=False))
+        sources.append(j)
     zero = jnp.zeros((), jnp.float32)
     outs = []
     for s in range(step_dev):

time: 45.4 us -> 52.3 us (1.15)
  blocking collectives: 0 us -> 13.3 us
  starting transfers between devices: 24.8 us -> 19.6 us
  waiting for transfers between devices: 11.1 us -> 9.31 us
  local copies, waits for them, and re-layouts: 3.93 us -> 4.56 us
    all_gather x0 -> x1, blocking collectives: none -> 13.3 us  [gather_prefix(): every = lax.all_gather(ordered, 'seq', axis=0, tiled=False)]
    ppermute x3 -> x0, starting transfers between devices: 3.55 us -> none  [gather_prefix(): pieces.append(lax.ppermute(ordered[:, k], 'seq', xor_pairs(groups, k)))]
    ppermute x3 -> x0, waiting for transfers between devices: 2.77 us -> none  [gather_prefix(): pieces.append(lax.ppermute(ordered[:, k], 'seq', xor_pairs(groups, k)))]
    ppermute x9, starting transfers between devices: 19.3 us -> 17.4 us  [on_device(): pieces = [lax.ppermute(p, 'seq', xor_pairs(groups, k)) for p in pieces]]
    ppermute x9, waiting for transfers between devices: 6.34 us -> 7.63 us  [on_device(): pieces = [lax.ppermute(p, 'seq', xor_pairs(groups, k)) for p in pieces]]
    unnamed x14, local copies, waits for them, and re-layouts: 1.35 us -> 2.04 us
  transfers between devices with their start and end apart: 15 -> 12, of which waited for: 6 -> 5; matrix products, arithmetic and copies ran while one was open for 10% -> 8% of each run, Pallas kernels for 0% -> 0%
where the time goes in v17:
time: 52.3 us; the launch traced here: 52.1 us
  starting transfers between devices  19.6 us (37%)
  blocking collectives  13.3 us (25%)
  waiting for transfers between devices  9.31 us (18%)
  local copies, waits for them, and re-layouts  4.56 us (9%)
  matrix products  2.3 us (4%)
  other arithmetic  2.14 us (4%)
  between operations  0.8 us (2%)
    ppermute x9, starting transfers between devices, on_device(): pieces = [lax.ppermute(p, 'seq', xor_pairs(groups, k)) for p in pieces]  17.4 us
    all_gather x1, blocking collectives, gather_prefix(): every = lax.all_gather(ordered, 'seq', axis=0, tiled=False)  13.3 us
    ppermute x9, waiting for transfers between devices, on_device(): pieces = [lax.ppermute(p, 'seq', xor_pairs(groups, k)) for p in pieces]  7.63 us
    ppermute x3, starting transfers between devices, gather_prefix(): other = lax.ppermute(total, 'step', xor_pairs(steps_axis, k))  2.21 us
    unnamed x14, local copies, waits for them, and re-layouts  2.04 us
    ppermute x3, waiting for transfers between devices, gather_prefix(): other = lax.ppermute(total, 'step', xor_pairs(steps_axis, k))  1.68 us
    dot_general x4, matrix products, attend(): jnp.einsum('iqk,ikd->iqd', weights[:, :, first:first + size], block, pref...  1.59 us
    another operation x2, local copies, waits for them, and re-layouts, on_device(): jnp.stack([jnp.broadcast_to(guide_scale, shape), jnp.broadcast_to(len_ful...  1.32 us
  transfers between devices with their start and end apart: 12, of which 5 were waited for; matrix products, arithmetic and copies ran while one was open for 8% of the time, Pallas kernels for 0%

profile of v17, /device:TPU:0, one launch (start us, length us, event | category | flops | bytes accessed | tf_op | source)
XLA Modules:
  0.0 52.1 jit_solution(10395034169218056892)
XLA Ops:
  0.0 1.1 %dynamic-slice_bitcast_fusion.6 = (bf16[48,8,128]{2,1,0:T(8,128)(2,1)S(1)}, bf16[48,8,128]{2,1,0:T(8,128)(2,1)S(1)}, bf16[48,8,128]{2,1,0:T(8,128)(2,1)S(1)}, bf16[48,8,128]{2,1,0:T(8,128)(2,1)S(1)}) fusion(bf16[4,48,8,128]{3,2,1,0:T(8,128)(2,1)} %bitcast.94, s32[]{:T(128)S(6)} %select_n.116, s32[]{:T(128)S(6)} %select_n.119, s32[]{:T(128)S(6)} %select_n.118, ...), kind=kLoop, calls=%fused_computation.43 | loop fusion | bytes 786448 | tf_op jit(solution)/shard_map/jit(dynamic_index_in_dim)/squeeze | solution.py:106
  1.1 3.1 %collective-permute-start.3 = (bf16[48,8,128]{2,1,0:T(8,128)(2,1)S(1)}, bf16[48,8,128]{2,1,0:T(8,128)(2,1)S(1)}, u32[]{:S(2)}, u32[]{:S(2)}) collective-permute-start(bf16[48,8,128]{2,1,0:T(8,128)(2,1)S(1)} %get-tuple-element.17), channel_id=1, source_target_pairs={{0,1},{1,0},{2,3},{3,2},{4,5},{5,4},{6,7},{7,6},{8,9},{9,8},{10,11... | collective-permute-start | bytes 294920 | tf_op jit(solution)/shard_map/ppermute | solution.py:108
  4.2 2.6 %collective-permute-start.4 = (bf16[48,8,128]{2,1,0:T(8,128)(2,1)S(1)}, bf16[48,8,128]{2,1,0:T(8,128)(2,1)S(1)}, u32[]{:S(2)}, u32[]{:S(2)}) collective-permute-start(bf16[48,8,128]{2,1,0:T(8,128)(2,1)S(1)} %get-tuple-element.16), channel_id=1, source_target_pairs={{0,2},{1,3},{2,0},{3,1},{4,6},{5,7},{6,4},{7,5},{8,10},{9,11},{10,... | collective-permute-start | bytes 294920 | tf_op jit(solution)/shard_map/ppermute | solution.py:108
  6.9 1.0 %collective-permute-start = (bf16[48,8,128]{2,1,0:T(8,128)(2,1)S(1)}, bf16[48,8,128]{2,1,0:T(8,128)(2,1)S(1)}, u32[]{:S(2)}, u32[]{:S(2)}) collective-permute-start(bf16[48,8,128]{2,1,0:T(8,128)(2,1)S(1)} %get-tuple-element.21), channel_id=1, source_target_pairs={{0,1},{1,0},{2,3},{3,2},{4,5},{5,4},{6,7},{7,6},{8,9},{9,8},{10,11... | collective-permute-start | bytes 294920 | tf_op jit(solution)/shard_map/ppermute | solution.py:108
  7.8 3.5 %collective-permute-start.1 = (bf16[48,8,128]{2,1,0:T(8,128)(2,1)S(1)}, bf16[48,8,128]{2,1,0:T(8,128)(2,1)S(1)}, u32[]{:S(2)}, u32[]{:S(2)}) collective-permute-start(bf16[48,8,128]{2,1,0:T(8,128)(2,1)S(1)} %get-tuple-element.20), channel_id=1, source_target_pairs={{0,2},{1,3},{2,0},{3,1},{4,6},{5,7},{6,4},{7,5},{8,10},{9,11},{10,... | collective-permute-start | bytes 294920 | tf_op jit(solution)/shard_map/ppermute | solution.py:108
  11.3 0.7 %copy-done.4 = f32[1000]{0:T(1024)S(1)} copy-done((f32[1000]{0:T(1024)S(1)}, f32[1000]{0:T(1024)}, u32[]{:S(2)}) %copy-start.4) | copy-done | bytes 4024
  12.2 0.7 %fusion.42 = f32[]{:T(128)} fusion(f32[4]{0:T(128)S(1)} %select_reduce_fusion, s32[]{:T(128)S(6)} %axis_index.22), kind=kLoop, calls=%fused_computation.75 | loop fusion | flops 11 | bytes 24 | tf_op jit(solution)/shard_map/reduce_sum | solution.py:139
  13.5 0.6 %copy-done.6 = f32[8]{0:T(128)S(1)} copy-done((f32[8]{0:T(128)S(1)}, f32[8]{0:T(128)}, u32[]{:S(2)}) %copy-start.6) | copy-done | bytes 56
  14.2 0.6 %fusion.41 = f32[]{:T(128)} fusion(f32[8]{0:T(128)S(1)} %copy-done.6, s32[]{:T(128)} %bitcast.93), kind=kLoop, calls=%fused_computation.74 | loop fusion | flops 23 | bytes 40 | tf_op jit(solution)/shard_map/reduce_sum | solution.py:13
  14.8 1.2 %stack.14 = f32[2]{0:T(128)S(1)} pad(f32[1]{0:T(128)} %bitcast.1, f32[]{:T(128)} %fusion.42), padding=0_1 | pad | bytes 16 | tf_op jit(solution)/shard_map/stack | solution.py:144
  16.2 0.6 %collective-permute-start.6 = (bf16[48,8,128]{2,1,0:T(8,128)(2,1)S(1)}, bf16[48,8,128]{2,1,0:T(8,128)(2,1)S(1)}, u32[]{:S(2)}, u32[]{:S(2)}) collective-permute-start(bf16[48,8,128]{2,1,0:T(8,128)(2,1)S(1)} %get-tuple-element.13), channel_id=1, source_target_pairs={{0,1},{1,0},{2,3},{3,2},{4,5},{5,4},{6,7},{7,6},{8,9},{9,8},{10,11... | collective-permute-start | bytes 294920 | tf_op jit(solution)/shard_map/ppermute | solution.py:108
  16.8 3.6 %collective-permute-start.8 = (bf16[48,8,128]{2,1,0:T(8,128)(2,1)S(1)}, bf16[48,8,128]{2,1,0:T(8,128)(2,1)S(1)}, u32[]{:S(2)}, u32[]{:S(2)}) collective-permute-start(bf16[48,8,128]{2,1,0:T(8,128)(2,1)S(1)} %get-tuple-element.12), channel_id=1, source_target_pairs={{0,3},{1,2},{2,1},{3,0},{4,7},{5,6},{6,5},{7,4},{8,11},{9,10},{10,... | collective-permute-start | bytes 294920 | tf_op jit(solution)/shard_map/ppermute | solution.py:108
  20.4 3.1 %collective-permute-start.7 = (bf16[48,8,128]{2,1,0:T(8,128)(2,1)S(1)}, bf16[48,8,128]{2,1,0:T(8,128)(2,1)S(1)}, u32[]{:S(2)}, u32[]{:S(2)}) collective-permute-start(bf16[48,8,128]{2,1,0:T(8,128)(2,1)S(1)} %get-tuple-element.11), channel_id=1, source_target_pairs={{0,2},{1,3},{2,0},{3,1},{4,6},{5,7},{6,4},{7,5},{8,10},{9,11},{10,... | collective-permute-start | bytes 294920 | tf_op jit(solution)/shard_map/ppermute | solution.py:108
  23.5 1.8 %collective-permute-done.1 = bf16[48,8,128]{2,1,0:T(8,128)(2,1)S(1)} collective-permute-done((bf16[48,8,128]{2,1,0:T(8,128)(2,1)S(1)}, bf16[48,8,128]{2,1,0:T(8,128)(2,1)S(1)}, u32[]{:S(2)}, u32[]{:S(2)}) %collective-permute-start.1) | collective-permute-done | bytes 98336 | tf_op jit(solution)/shard_map/ppermute | solution.py:108
  25.3 0.5 fusion.53
  26.8 5.7 %collective-permute-done.7 = bf16[48,8,128]{2,1,0:T(8,128)(2,1)S(1)} collective-permute-done((bf16[48,8,128]{2,1,0:T(8,128)(2,1)S(1)}, bf16[48,8,128]{2,1,0:T(8,128)(2,1)S(1)}, u32[]{:S(2)}, u32[]{:S(2)}) %collective-permute-start.7) | collective-permute-done | bytes 98336 | tf_op jit(solution)/shard_map/ppermute | solution.py:108
  32.6 0.7 %multiply_reduce_fusion = (f32[48,32]{1,0:T(8,128)S(1)}, bf16[48,32,128]{2,1,0:T(8,128)(2,1)S(1)}) fusion(f32[48,32]{1,0:T(8,128)S(1)} %get-tuple-element.9, f32[48,32,128]{2,1,0:T(8,128)S(1)} %fusion.27, f32[48,32,128]{2,1,0:T(8,128)S(1)} %convolution_add_fusion.1, bf16[48,8,128]{2,1,0:T(8,128)(2,1)S(1)} %collective-permute-done.7, ...), kind=kOutput, calls=%fused_computation.12 | convolution fusion | flops 4520448 | bytes 2193408 | tf_op jit(solution)/shard_map/iqk,ikd->iqd/dot_general | solution.py:29
  33.5 13.3 %all_gather.3 = f32[4,1,4,8,64]{4,3,2,1,0:T(8,128)S(1)} all-gather(f32[1,1,4,8,64]{4,3,2,1,0:T(8,128)S(1)} %fusion.38), channel_id=1, replica_groups=mesh['scene'=2,'step'=4,'seq'=4] {'seq'}, dimensions={0}, use_global_device_ids=true | all-gather | bytes 40960 | tf_op jit(solution)/shard_map/all_gather | solution.py:53
  46.8 1.6 %collective-permute-start.10 = (f32[8,64]{1,0:T(8,128)S(1)}, f32[8,64]{1,0:T(8,128)S(1)}, u32[]{:S(2)}, u32[]{:S(2)}) collective-permute-start(f32[8,64]{1,0:T(8,128)S(1)} %add_bitcast_fusion.1), channel_id=1, source_target_pairs={{0,8},{4,12},{8,0},{12,4},{1,9},{5,13},{9,1},{13,5},{2,10},{6,14},... | collective-permute-start | bytes 6152 | tf_op jit(solution)/shard_map/ppermute | solution.py:73
  48.4 0.6 %collective-permute-start.9 = (f32[8,64]{1,0:T(8,128)S(1)}, f32[8,64]{1,0:T(8,128)S(1)}, u32[]{:S(2)}, u32[]{:S(2)}) collective-permute-start(f32[8,64]{1,0:T(8,128)S(1)} %add_bitcast_fusion.1), channel_id=1, source_target_pairs={{0,4},{4,0},{8,12},{12,8},{1,5},{5,1},{9,13},{13,9},{2,6},{6,2},{1... | collective-permute-start | bytes 6152 | tf_op jit(solution)/shard_map/ppermute | solution.py:73
  49.1 0.7 %copy-done.3 = f32[64,8]{0,1:T(8,128)S(1)} copy-done((f32[64,8]{0,1:T(8,128)S(1)}, f32[64,8]{0,1:T(8,128)}, u32[]{:S(2)}) %copy-start.3) | copy-done | bytes 2072
  49.8 0.8 %collective-permute-done.10 = f32[8,64]{1,0:T(8,128)S(1)} collective-permute-done((f32[8,64]{1,0:T(8,128)S(1)}, f32[8,64]{1,0:T(8,128)S(1)}, u32[]{:S(2)}, u32[]{:S(2)}) %collective-permute-start.10) | collective-permute-done | bytes 2080 | tf_op jit(solution)/shard_map/ppermute | solution.py:73
  50.5 0.9 %collective-permute-done.11 = f32[8,64]{1,0:T(8,128)S(1)} collective-permute-done((f32[8,64]{1,0:T(8,128)S(1)}, f32[8,64]{1,0:T(8,128)S(1)}, u32[]{:S(2)}, u32[]{:S(2)}) %collective-permute-start.11) | collective-permute-done | bytes 2080 | tf_op jit(solution)/shard_map/ppermute | solution.py:73
  51.4 0.6 %add_bitcast_fusion = f32[4,64,8]{1,2,0:T(8,128)} fusion(f32[4,8,64]{2,1,0:T(8,128)S(1)} %maximum_add_fusion, f32[8,64]{1,0:T(8,128)S(1)} %select_add_fusion), kind=kLoop, calls=%fused_computation.57 | loop fusion | flops 2048 | bytes 18432 | tf_op jit(solution)/shard_map/transpose | solution.py:75
  (38 shorter events, 1.8 us)
Async XLA Ops:
  0.0 33.3 %copy-start = (bf16[64,3072]{1,0:T(8,128)(2,1)S(1)}, bf16[64,3072]{1,0:T(8,128)(2,1)}, u32[]{:S(2)}) copy-start(bf16[64,3072]{1,0:T(8,128)(2,1)} %param.13) | copy-start | bytes 1179652
  0.0 6.8 %copy-start.1 = (bf16[4,2,24,8,128]{4,3,2,1,0:T(8,128)(2,1)S(1)}, bf16[4,2,24,8,128]{4,3,2,1,0:T(8,128)(2,1)}, u32[]{:S(2)}) copy-start(bf16[4,2,24,8,128]{4,3,2,1,0:T(8,128)(2,1)} %param.9) | copy-start | bytes 1179652
  1.1 15.0 %collective-permute-start.3 = (bf16[48,8,128]{2,1,0:T(8,128)(2,1)S(1)}, bf16[48,8,128]{2,1,0:T(8,128)(2,1)S(1)}, u32[]{:S(2)}, u32[]{:S(2)}) collective-permute-start(bf16[48,8,128]{2,1,0:T(8,128)(2,1)S(1)} %get-tuple-element.17), channel_id=1, source_target_pairs={{0,1},{1,0},{2,3},{3,2},{4,5},{5,4},{6,7},{7,6},{8,9},{9,8},{10,11... | collective-permute-start | bytes 294920 | tf_op jit(solution)/shard_map/ppermute | solution.py:108
  4.2 12.0 %collective-permute-start.4 = (bf16[48,8,128]{2,1,0:T(8,128)(2,1)S(1)}, bf16[48,8,128]{2,1,0:T(8,128)(2,1)S(1)}, u32[]{:S(2)}, u32[]{:S(2)}) collective-permute-start(bf16[48,8,128]{2,1,0:T(8,128)(2,1)S(1)} %get-tuple-element.16), channel_id=1, source_target_pairs={{0,2},{1,3},{2,0},{3,1},{4,6},{5,7},{6,4},{7,5},{8,10},{9,11},{10,... | collective-permute-start | bytes 294920 | tf_op jit(solution)/shard_map/ppermute | solution.py:108
  6.8 10.0 %collective-permute-start.5 = (bf16[48,8,128]{2,1,0:T(8,128)(2,1)S(1)}, bf16[48,8,128]{2,1,0:T(8,128)(2,1)S(1)}, u32[]{:S(2)}, u32[]{:S(2)}) collective-permute-start(bf16[48,8,128]{2,1,0:T(8,128)(2,1)S(1)} %get-tuple-element.15), channel_id=1, source_target_pairs={{0,3},{1,2},{2,1},{3,0},{4,7},{5,6},{6,5},{7,4},{8,11},{9,10},{10,... | collective-permute-start | bytes 294920 | tf_op jit(solution)/shard_map/ppermute | solution.py:108
  6.8 9.3 %copy-start.2 = (bf16[4,2,24,8,128]{4,3,2,1,0:T(8,128)(2,1)S(1)}, bf16[4,2,24,8,128]{4,3,2,1,0:T(8,128)(2,1)}, u32[]{:S(2)}) copy-start(bf16[4,2,24,8,128]{4,3,2,1,0:T(8,128)(2,1)} %param.11) | copy-start | bytes 1179652
  6.9 13.5 %collective-permute-start = (bf16[48,8,128]{2,1,0:T(8,128)(2,1)S(1)}, bf16[48,8,128]{2,1,0:T(8,128)(2,1)S(1)}, u32[]{:S(2)}, u32[]{:S(2)}) collective-permute-start(bf16[48,8,128]{2,1,0:T(8,128)(2,1)S(1)} %get-tuple-element.21), channel_id=1, source_target_pairs={{0,1},{1,0},{2,3},{3,2},{4,5},{5,4},{6,7},{7,6},{8,9},{9,8},{10,11... | collective-permute-start | bytes 294920 | tf_op jit(solution)/shard_map/ppermute | solution.py:108
  7.8 17.5 %collective-permute-start.1 = (bf16[48,8,128]{2,1,0:T(8,128)(2,1)S(1)}, bf16[48,8,128]{2,1,0:T(8,128)(2,1)S(1)}, u32[]{:S(2)}, u32[]{:S(2)}) collective-permute-start(bf16[48,8,128]{2,1,0:T(8,128)(2,1)S(1)} %get-tuple-element.20), channel_id=1, source_target_pairs={{0,2},{1,3},{2,0},{3,1},{4,6},{5,7},{6,4},{7,5},{8,10},{9,11},{10,... | collective-permute-start | bytes 294920 | tf_op jit(solution)/shard_map/ppermute | solution.py:108
  11.3 0.7 %copy-start.4 = (f32[1000]{0:T(1024)S(1)}, f32[1000]{0:T(1024)}, u32[]{:S(2)}) copy-start(f32[1000]{0:T(1024)} %param.16) | copy-start | bytes 12004
  11.3 0.7 %copy-start.5 = (s32[4]{0:T(128)S(1)}, s32[4]{0:T(128)}, u32[]{:S(2)}) copy-start(s32[4]{0:T(128)} %param.17) | copy-start | bytes 52
  13.5 0.7 %copy-start.6 = (f32[8]{0:T(128)S(1)}, f32[8]{0:T(128)}, u32[]{:S(2)}) copy-start(f32[8]{0:T(128)} %param.14) | copy-start | bytes 100
  16.1 9.2 %collective-permute-start.2 = (bf16[48,8,128]{2,1,0:T(8,128)(2,1)S(1)}, bf16[48,8,128]{2,1,0:T(8,128)(2,1)S(1)}, u32[]{:S(2)}, u32[]{:S(2)}) collective-permute-start(bf16[48,8,128]{2,1,0:T(8,128)(2,1)S(1)} %get-tuple-element.19), channel_id=1, source_target_pairs={{0,3},{1,2},{2,1},{3,0},{4,7},{5,6},{6,5},{7,4},{8,11},{9,10},{10,... | collective-permute-start | bytes 294920 | tf_op jit(solution)/shard_map/ppermute | solution.py:108
  16.2 9.9 %collective-permute-start.6 = (bf16[48,8,128]{2,1,0:T(8,128)(2,1)S(1)}, bf16[48,8,128]{2,1,0:T(8,128)(2,1)S(1)}, u32[]{:S(2)}, u32[]{:S(2)}) collective-permute-start(bf16[48,8,128]{2,1,0:T(8,128)(2,1)S(1)} %get-tuple-element.13), channel_id=1, source_target_pairs={{0,1},{1,0},{2,3},{3,2},{4,5},{5,4},{6,7},{7,6},{8,9},{9,8},{10,11... | collective-permute-start | bytes 294920 | tf_op jit(solution)/shard_map/ppermute | solution.py:108
  16.8 9.7 %collective-permute-start.8 = (bf16[48,8,128]{2,1,0:T(8,128)(2,1)S(1)}, bf16[48,8,128]{2,1,0:T(8,128)(2,1)S(1)}, u32[]{:S(2)}, u32[]{:S(2)}) collective-permute-start(bf16[48,8,128]{2,1,0:T(8,128)(2,1)S(1)} %get-tuple-element.12), channel_id=1, source_target_pairs={{0,3},{1,2},{2,1},{3,0},{4,7},{5,6},{6,5},{7,4},{8,11},{9,10},{10,... | collective-permute-start | bytes 294920 | tf_op jit(solution)/shard_map/ppermute | solution.py:108
  20.4 12.2 %collective-permute-start.7 = (bf16[48,8,128]{2,1,0:T(8,128)(2,1)S(1)}, bf16[48,8,128]{2,1,0:T(8,128)(2,1)S(1)}, u32[]{:S(2)}, u32[]{:S(2)}) collective-permute-start(bf16[48,8,128]{2,1,0:T(8,128)(2,1)S(1)} %get-tuple-element.11), channel_id=1, source_target_pairs={{0,2},{1,3},{2,0},{3,1},{4,6},{5,7},{6,4},{7,5},{8,10},{9,11},{10,... | collective-permute-start | bytes 294920 | tf_op jit(solution)/shard_map/ppermute | solution.py:108
  46.8 3.7 %collective-permute-start.10 = (f32[8,64]{1,0:T(8,128)S(1)}, f32[8,64]{1,0:T(8,128)S(1)}, u32[]{:S(2)}, u32[]{:S(2)}) collective-permute-start(f32[8,64]{1,0:T(8,128)S(1)} %add_bitcast_fusion.1), channel_id=1, source_target_pairs={{0,8},{4,12},{8,0},{12,4},{1,9},{5,13},{9,1},{13,5},{2,10},{6,14},... | collective-permute-start | bytes 6152 | tf_op jit(solution)/shard_map/ppermute | solution.py:73
  48.4 3.0 %collective-permute-start.11 = (f32[8,64]{1,0:T(8,128)S(1)}, f32[8,64]{1,0:T(8,128)S(1)}, u32[]{:S(2)}, u32[]{:S(2)}) collective-permute-start(f32[8,64]{1,0:T(8,128)S(1)} %add_bitcast_fusion.1), channel_id=1, source_target_pairs={{0,12},{4,8},{8,4},{12,0},{1,13},{5,9},{9,5},{13,1},{2,14},{6,10},... | collective-permute-start | bytes 6152 | tf_op jit(solution)/shard_map/ppermute | solution.py:73
  48.4 3.0 %collective-permute-start.9 = (f32[8,64]{1,0:T(8,128)S(1)}, f32[8,64]{1,0:T(8,128)S(1)}, u32[]{:S(2)}, u32[]{:S(2)}) collective-permute-start(f32[8,64]{1,0:T(8,128)S(1)} %add_bitcast_fusion.1), channel_id=1, source_target_pairs={{0,4},{4,0},{8,12},{12,8},{1,5},{5,1},{9,13},{13,9},{2,6},{6,2},{1... | collective-permute-start | bytes 6152 | tf_op jit(solution)/shard_map/ppermute | solution.py:73
  49.1 0.7 %copy-start.3 = (f32[64,8]{0,1:T(8,128)S(1)}, f32[64,8]{0,1:T(8,128)}, u32[]{:S(2)}) copy-start(f32[64,8]{0,1:T(8,128)} %param.12) | copy-start | bytes 6148

commit v18 on v15

--- a/solution.py
+++ b/solution.py
@@ -68,9 +68,18 @@
     local_cum = lax.optimization_barrier(jnp.stack(outs) + start[None])
     position = lax.axis_index("step")
     earlier = jnp.zeros_like(total)
-    for k in range(1, steps_axis):
-        other = lax.ppermute(total, "step", xor_pairs(steps_axis, k))
-        earlier = earlier + jnp.where((position ^ k) < position, other, zero)
+    if steps_axis & (steps_axis - 1) == 0:
+        block = total
+        k = 1
+        while k < steps_axis:
+            other = lax.ppermute(block, "step", xor_pairs(steps_axis, k))
+            earlier = earlier + jnp.where(position & k != 0, other, zero)
+            block = block + other
+            k *= 2
+    else:
+        every_total = lax.all_gather(total[None], "step", axis=0, tiled=True)
+        order = jnp.arange(steps_axis, dtype=jnp.int32)
+        earlier = jnp.sum(jnp.where((order < position)[:, None, None], every_total, zero), axis=0)
     return jnp.transpose(local_cum + earlier[None], (0, 2, 1))
 
 

time: 45.4 us -> 45.5 us (level)
  waiting for transfers between devices: 11.1 us -> 12.3 us
  local copies, waits for them, and re-layouts: 3.93 us -> 3.18 us
    ppermute x3 -> x2, waiting for transfers between devices: 2 us -> 3.22 us  [gather_prefix(): other = lax.ppermute(block, 'step', xor_pairs(steps_axis, k))]
    unnamed x14, local copies, waits for them, and re-layouts: 1.35 us -> 0.68 us
    ppermute x3 -> x2, starting transfers between devices: 1.93 us -> 1.56 us  [gather_prefix(): other = lax.ppermute(block, 'step', xor_pairs(steps_axis, k))]
  transfers between devices with their start and end apart: 15 -> 14, of which waited for: 6 -> 6; matrix products, arithmetic and copies ran while one was open for 10% -> 9% of each run, Pallas kernels for 0% -> 0%
where the time goes in v18:
time: 45.5 us; the launch traced here: 45.3 us
  starting transfers between devices  24.5 us (54%)
  waiting for transfers between devices  12.3 us (27%)
  local copies, waits for them, and re-layouts  3.18 us (7%)
  matrix products  2.3 us (5%)
  other arithmetic  2.16 us (5%)
  between operations  0.83 us (2%)
    ppermute x9, starting transfers between devices, on_device(): pieces = [lax.ppermute(p, 'seq', xor_pairs(groups, k)) for p in pieces]  19.4 us
    ppermute x9, waiting for transfers between devices, on_device(): pieces = [lax.ppermute(p, 'seq', xor_pairs(groups, k)) for p in pieces]  6.34 us
    ppermute x3, starting transfers between devices, gather_prefix(): pieces.append(lax.ppermute(ordered[:, k], 'seq', xor_pairs(groups, k)))  3.55 us
    ppermute x2, waiting for transfers between devices, gather_prefix(): other = lax.ppermute(block, 'step', xor_pairs(steps_axis, k))  3.22 us
    ppermute x3, waiting for transfers between devices, gather_prefix(): pieces.append(lax.ppermute(ordered[:, k], 'seq', xor_pairs(groups, k)))  2.77 us
    dot_general x4, matrix products, attend(): jnp.einsum('iqk,ikd->iqd', weights[:, :, first:first + size], block, pref...  1.59 us
    ppermute x2, starting transfers between devices, gather_prefix(): other = lax.ppermute(block, 'step', xor_pairs(steps_axis, k))  1.56 us
    another operation x2, local copies, waits for them, and re-layouts, on_device(): jnp.stack([jnp.broadcast_to(guide_scale, shape), jnp.broadcast_to(len_ful...  1.31 us
  transfers between devices with their start and end apart: 14, of which 6 were waited for; matrix products, arithmetic and copies ran while one was open for 9% of the time, Pallas kernels for 0%

profile of v18, /device:TPU:0, one launch (start us, length us, event | category | flops | bytes accessed | tf_op | source)
XLA Modules:
  0.0 45.3 jit_solution(15001264804784042265)
XLA Ops:
  0.0 1.1 %dynamic-slice_bitcast_fusion.6 = (bf16[48,8,128]{2,1,0:T(8,128)(2,1)S(1)}, bf16[48,8,128]{2,1,0:T(8,128)(2,1)S(1)}, bf16[48,8,128]{2,1,0:T(8,128)(2,1)S(1)}, bf16[48,8,128]{2,1,0:T(8,128)(2,1)S(1)}) fusion(bf16[4,48,8,128]{3,2,1,0:T(8,128)(2,1)} %bitcast.123, s32[]{:T(128)S(6)} %select_n.232, s32[]{:T(128)S(6)} %select_n.235, s32[]{:T(128)S(6)} %select_n.234, ...), kind=kLoop, calls=%fused_computation.43 | loop fusion | bytes 786448 | tf_op jit(solution)/shard_map/jit(dynamic_index_in_dim)/squeeze | solution.py:114
  1.1 3.1 %collective-permute-start.3 = (bf16[48,8,128]{2,1,0:T(8,128)(2,1)S(1)}, bf16[48,8,128]{2,1,0:T(8,128)(2,1)S(1)}, u32[]{:S(2)}, u32[]{:S(2)}) collective-permute-start(bf16[48,8,128]{2,1,0:T(8,128)(2,1)S(1)} %get-tuple-element.13), channel_id=1, source_target_pairs={{0,1},{1,0},{2,3},{3,2},{4,5},{5,4},{6,7},{7,6},{8,9},{9,8},{10,11... | collective-permute-start | bytes 294920 | tf_op jit(solution)/shard_map/ppermute | solution.py:116
  4.2 2.6 %collective-permute-start.4 = (bf16[48,8,128]{2,1,0:T(8,128)(2,1)S(1)}, bf16[48,8,128]{2,1,0:T(8,128)(2,1)S(1)}, u32[]{:S(2)}, u32[]{:S(2)}) collective-permute-start(bf16[48,8,128]{2,1,0:T(8,128)(2,1)S(1)} %get-tuple-element.12), channel_id=1, source_target_pairs={{0,2},{1,3},{2,0},{3,1},{4,6},{5,7},{6,4},{7,5},{8,10},{9,11},{10,... | collective-permute-start | bytes 294920 | tf_op jit(solution)/shard_map/ppermute | solution.py:116
  6.9 0.9 %collective-permute-start = (bf16[48,8,128]{2,1,0:T(8,128)(2,1)S(1)}, bf16[48,8,128]{2,1,0:T(8,128)(2,1)S(1)}, u32[]{:S(2)}, u32[]{:S(2)}) collective-permute-start(bf16[48,8,128]{2,1,0:T(8,128)(2,1)S(1)} %get-tuple-element.17), channel_id=1, source_target_pairs={{0,1},{1,0},{2,3},{3,2},{4,5},{5,4},{6,7},{7,6},{8,9},{9,8},{10,11... | collective-permute-start | bytes 294920 | tf_op jit(solution)/shard_map/ppermute | solution.py:116
  7.8 3.5 %collective-permute-start.1 = (bf16[48,8,128]{2,1,0:T(8,128)(2,1)S(1)}, bf16[48,8,128]{2,1,0:T(8,128)(2,1)S(1)}, u32[]{:S(2)}, u32[]{:S(2)}) collective-permute-start(bf16[48,8,128]{2,1,0:T(8,128)(2,1)S(1)} %get-tuple-element.16), channel_id=1, source_target_pairs={{0,2},{1,3},{2,0},{3,1},{4,6},{5,7},{6,4},{7,5},{8,10},{9,11},{10,... | collective-permute-start | bytes 294920 | tf_op jit(solution)/shard_map/ppermute | solution.py:116
  11.5 0.7 %fusion.49 = f32[]{:T(128)} fusion(f32[4]{0:T(128)S(1)} %select_reduce_fusion, s32[]{:T(128)S(6)} %axis_index.22), kind=kLoop, calls=%fused_computation.84 | loop fusion | flops 11 | bytes 24 | tf_op jit(solution)/shard_map/reduce_sum | solution.py:147
  12.9 0.6 %copy-done.6 = f32[8]{0:T(128)S(1)} copy-done((f32[8]{0:T(128)S(1)}, f32[8]{0:T(128)}, u32[]{:S(2)}) %copy-start.6) | copy-done | bytes 56
  13.5 0.6 %fusion.48 = f32[]{:T(128)} fusion(f32[8]{0:T(128)S(1)} %copy-done.6, s32[]{:T(128)} %bitcast.122), kind=kLoop, calls=%fused_computation.83 | loop fusion | flops 23 | bytes 40 | tf_op jit(solution)/shard_map/reduce_sum | solution.py:13
  14.1 1.2 %stack.12 = f32[2]{0:T(128)S(1)} pad(f32[1]{0:T(128)} %bitcast.1, f32[]{:T(128)} %fusion.49), padding=0_1 | pad | bytes 16 | tf_op jit(solution)/shard_map/stack | solution.py:152
  15.5 0.6 %collective-permute-start.6 = (bf16[48,8,128]{2,1,0:T(8,128)(2,1)S(1)}, bf16[48,8,128]{2,1,0:T(8,128)(2,1)S(1)}, u32[]{:S(2)}, u32[]{:S(2)}) collective-permute-start(bf16[48,8,128]{2,1,0:T(8,128)(2,1)S(1)} %get-tuple-element.9), channel_id=1, source_target_pairs={{0,1},{1,0},{2,3},{3,2},{4,5},{5,4},{6,7},{7,6},{8,9},{9,8},{10,11... | collective-permute-start | bytes 294920 | tf_op jit(solution)/shard_map/ppermute | solution.py:116
  16.1 4.3 %collective-permute-start.8 = (bf16[48,8,128]{2,1,0:T(8,128)(2,1)S(1)}, bf16[48,8,128]{2,1,0:T(8,128)(2,1)S(1)}, u32[]{:S(2)}, u32[]{:S(2)}) collective-permute-start(bf16[48,8,128]{2,1,0:T(8,128)(2,1)S(1)} %get-tuple-element.8), channel_id=1, source_target_pairs={{0,3},{1,2},{2,1},{3,0},{4,7},{5,6},{6,5},{7,4},{8,11},{9,10},{10,... | collective-permute-start | bytes 294920 | tf_op jit(solution)/shard_map/ppermute | solution.py:116
  20.4 4.3 %collective-permute-start.7 = (bf16[48,8,128]{2,1,0:T(8,128)(2,1)S(1)}, bf16[48,8,128]{2,1,0:T(8,128)(2,1)S(1)}, u32[]{:S(2)}, u32[]{:S(2)}) collective-permute-start(bf16[48,8,128]{2,1,0:T(8,128)(2,1)S(1)} %get-tuple-element.7), channel_id=1, source_target_pairs={{0,2},{1,3},{2,0},{3,1},{4,6},{5,7},{6,4},{7,5},{8,10},{9,11},{10,... | collective-permute-start | bytes 294920 | tf_op jit(solution)/shard_map/ppermute | solution.py:116
  24.8 1.6 %collective-permute-done.1 = bf16[48,8,128]{2,1,0:T(8,128)(2,1)S(1)} collective-permute-done((bf16[48,8,128]{2,1,0:T(8,128)(2,1)S(1)}, bf16[48,8,128]{2,1,0:T(8,128)(2,1)S(1)}, u32[]{:S(2)}, u32[]{:S(2)}) %collective-permute-start.1) | collective-permute-done | bytes 98336 | tf_op jit(solution)/shard_map/ppermute | solution.py:116
  27.8 4.8 %collective-permute-done.7 = bf16[48,8,128]{2,1,0:T(8,128)(2,1)S(1)} collective-permute-done((bf16[48,8,128]{2,1,0:T(8,128)(2,1)S(1)}, bf16[48,8,128]{2,1,0:T(8,128)(2,1)S(1)}, u32[]{:S(2)}, u32[]{:S(2)}) %collective-permute-start.7) | collective-permute-done | bytes 98336 | tf_op jit(solution)/shard_map/ppermute | solution.py:116
  32.6 0.6 %multiply_reduce_fusion = (f32[48,32]{1,0:T(8,128)S(1)}, bf16[48,32,128]{2,1,0:T(8,128)(2,1)S(1)}) fusion(f32[48,32]{1,0:T(8,128)S(1)} %get-tuple-element.5, f32[48,32,128]{2,1,0:T(8,128)S(1)} %fusion.27, f32[48,32,128]{2,1,0:T(8,128)S(1)} %convolution_add_fusion.1, bf16[48,8,128]{2,1,0:T(8,128)(2,1)S(1)} %collective-permute-done.7, ...), kind=kOutput, calls=%fused_computation.12 | convolution fusion | flops 4520448 | bytes 2193408 | tf_op jit(solution)/shard_map/iqk,ikd->iqd/dot_general | solution.py:29
  33.5 0.9 %collective-permute-start.10 = (f32[1,8,64]{2,1,0:T(8,128)S(1)}, f32[1,8,64]{2,1,0:T(8,128)S(1)}, u32[]{:S(2)}, u32[]{:S(2)}) collective-permute-start(f32[1,8,64]{2,1,0:T(8,128)S(1)} %get-tuple-element.23), channel_id=1, source_target_pairs={{0,2},{1,3},{2,0},{3,1},{4,6},{5,7},{6,4},{7,5},{8,10},{9,11},{10,... | collective-permute-start | bytes 6152 | tf_op jit(solution)/shard_map/ppermute | solution.py:56
  34.5 1.7 %collective-permute-start.11 = (f32[1,8,64]{2,1,0:T(8,128)S(1)}, f32[1,8,64]{2,1,0:T(8,128)S(1)}, u32[]{:S(2)}, u32[]{:S(2)}) collective-permute-start(f32[1,8,64]{2,1,0:T(8,128)S(1)} %get-tuple-element.22), channel_id=1, source_target_pairs={{0,3},{1,2},{2,1},{3,0},{4,7},{5,6},{6,5},{7,4},{8,11},{9,10},{10,... | collective-permute-start | bytes 6152 | tf_op jit(solution)/shard_map/ppermute | solution.py:56
  36.2 0.9 %collective-permute-start.9 = (f32[1,8,64]{2,1,0:T(8,128)S(1)}, f32[1,8,64]{2,1,0:T(8,128)S(1)}, u32[]{:S(2)}, u32[]{:S(2)}) collective-permute-start(f32[1,8,64]{2,1,0:T(8,128)S(1)} %get-tuple-element.21), channel_id=1, source_target_pairs={{0,1},{1,0},{2,3},{3,2},{4,5},{5,4},{6,7},{7,6},{8,9},{9,8},{10,11... | collective-permute-start | bytes 6152 | tf_op jit(solution)/shard_map/ppermute | solution.py:56
  37.1 1.0 %collective-permute-done.10 = f32[1,8,64]{2,1,0:T(8,128)S(1)} collective-permute-done((f32[1,8,64]{2,1,0:T(8,128)S(1)}, f32[1,8,64]{2,1,0:T(8,128)S(1)}, u32[]{:S(2)}, u32[]{:S(2)}) %collective-permute-start.10) | collective-permute-done | bytes 2080 | tf_op jit(solution)/shard_map/ppermute | solution.py:56
  38.1 1.8 %collective-permute-done.11 = f32[1,8,64]{2,1,0:T(8,128)S(1)} collective-permute-done((f32[1,8,64]{2,1,0:T(8,128)S(1)}, f32[1,8,64]{2,1,0:T(8,128)S(1)}, u32[]{:S(2)}, u32[]{:S(2)}) %collective-permute-start.11) | collective-permute-done | bytes 2080 | tf_op jit(solution)/shard_map/ppermute | solution.py:56
  40.0 1.1 %collective-permute-done.12 = f32[8,64]{1,0:T(8,128)S(1)} collective-permute-done((f32[8,64]{1,0:T(8,128)S(1)}, f32[8,64]{1,0:T(8,128)S(1)}, u32[]{:S(2)}, u32[]{:S(2)}) %collective-permute-start.12) | collective-permute-done | bytes 2080 | tf_op jit(solution)/shard_map/ppermute | solution.py:75
  41.1 1.5 %collective-permute-start.13 = (f32[8,64]{1,0:T(8,128)S(1)}, f32[8,64]{1,0:T(8,128)S(1)}, u32[]{:S(2)}, u32[]{:S(2)}) collective-permute-start(f32[8,64]{1,0:T(8,128)S(1)} %add.168), channel_id=1, source_target_pairs={{0,8},{4,12},{8,0},{12,4},{1,9},{5,13},{9,1},{13,5},{2,10},{6,14},... | collective-permute-start | bytes 6152 | tf_op jit(solution)/shard_map/ppermute | solution.py:75
  42.6 2.1 %collective-permute-done.13 = f32[8,64]{1,0:T(8,128)S(1)} collective-permute-done((f32[8,64]{1,0:T(8,128)S(1)}, f32[8,64]{1,0:T(8,128)S(1)}, u32[]{:S(2)}, u32[]{:S(2)}) %collective-permute-start.13) | collective-permute-done | bytes 2080 | tf_op jit(solution)/shard_map/ppermute | solution.py:75
  44.7 0.6 %add_bitcast_fusion = f32[4,64,8]{1,2,0:T(8,128)} fusion(f32[4,8,64]{2,1,0:T(8,128)S(1)} %maximum_add_fusion, f32[8,64]{1,0:T(8,128)S(1)} %select_add_fusion), kind=kLoop, calls=%fused_computation.57 | loop fusion | flops 2048 | bytes 18432 | tf_op jit(solution)/shard_map/transpose | solution.py:83
  (43 shorter events, 2.3 us)
Async XLA Ops:
  0.0 33.2 %copy-start = (bf16[64,3072]{1,0:T(8,128)(2,1)S(1)}, bf16[64,3072]{1,0:T(8,128)(2,1)}, u32[]{:S(2)}) copy-start(bf16[64,3072]{1,0:T(8,128)(2,1)} %param.13) | copy-start | bytes 1179652
  0.0 6.8 %copy-start.1 = (bf16[4,2,24,8,128]{4,3,2,1,0:T(8,128)(2,1)S(1)}, bf16[4,2,24,8,128]{4,3,2,1,0:T(8,128)(2,1)}, u32[]{:S(2)}) copy-start(bf16[4,2,24,8,128]{4,3,2,1,0:T(8,128)(2,1)} %param.9) | copy-start | bytes 1179652
  1.1 14.3 %collective-permute-start.3 = (bf16[48,8,128]{2,1,0:T(8,128)(2,1)S(1)}, bf16[48,8,128]{2,1,0:T(8,128)(2,1)S(1)}, u32[]{:S(2)}, u32[]{:S(2)}) collective-permute-start(bf16[48,8,128]{2,1,0:T(8,128)(2,1)S(1)} %get-tuple-element.13), channel_id=1, source_target_pairs={{0,1},{1,0},{2,3},{3,2},{4,5},{5,4},{6,7},{7,6},{8,9},{9,8},{10,11... | collective-permute-start | bytes 294920 | tf_op jit(solution)/shard_map/ppermute | solution.py:116
  4.2 11.3 %collective-permute-start.4 = (bf16[48,8,128]{2,1,0:T(8,128)(2,1)S(1)}, bf16[48,8,128]{2,1,0:T(8,128)(2,1)S(1)}, u32[]{:S(2)}, u32[]{:S(2)}) collective-permute-start(bf16[48,8,128]{2,1,0:T(8,128)(2,1)S(1)} %get-tuple-element.12), channel_id=1, source_target_pairs={{0,2},{1,3},{2,0},{3,1},{4,6},{5,7},{6,4},{7,5},{8,10},{9,11},{10,... | collective-permute-start | bytes 294920 | tf_op jit(solution)/shard_map/ppermute | solution.py:116
  6.8 9.3 %collective-permute-start.5 = (bf16[48,8,128]{2,1,0:T(8,128)(2,1)S(1)}, bf16[48,8,128]{2,1,0:T(8,128)(2,1)S(1)}, u32[]{:S(2)}, u32[]{:S(2)}) collective-permute-start(bf16[48,8,128]{2,1,0:T(8,128)(2,1)S(1)} %get-tuple-element.11), channel_id=1, source_target_pairs={{0,3},{1,2},{2,1},{3,0},{4,7},{5,6},{6,5},{7,4},{8,11},{9,10},{10,... | collective-permute-start | bytes 294920 | tf_op jit(solution)/shard_map/ppermute | solution.py:116
  6.8 4.5 %copy-start.4 = (f32[1000]{0:T(1024)S(1)}, f32[1000]{0:T(1024)}, u32[]{:S(2)}) copy-start(f32[1000]{0:T(1024)} %param.16) | copy-start | bytes 12004
  6.8 8.7 %copy-start.2 = (bf16[4,2,24,8,128]{4,3,2,1,0:T(8,128)(2,1)S(1)}, bf16[4,2,24,8,128]{4,3,2,1,0:T(8,128)(2,1)}, u32[]{:S(2)}) copy-start(bf16[4,2,24,8,128]{4,3,2,1,0:T(8,128)(2,1)} %param.11) | copy-start | bytes 1179652
  6.9 4.4 %copy-start.5 = (s32[4]{0:T(128)S(1)}, s32[4]{0:T(128)}, u32[]{:S(2)}) copy-start(s32[4]{0:T(128)} %param.17) | copy-start | bytes 52
  6.9 13.5 %collective-permute-start = (bf16[48,8,128]{2,1,0:T(8,128)(2,1)S(1)}, bf16[48,8,128]{2,1,0:T(8,128)(2,1)S(1)}, u32[]{:S(2)}, u32[]{:S(2)}) collective-permute-start(bf16[48,8,128]{2,1,0:T(8,128)(2,1)S(1)} %get-tuple-element.17), channel_id=1, source_target_pairs={{0,1},{1,0},{2,3},{3,2},{4,5},{5,4},{6,7},{7,6},{8,9},{9,8},{10,11... | collective-permute-start | bytes 294920 | tf_op jit(solution)/shard_map/ppermute | solution.py:116
  7.8 18.5 %collective-permute-start.1 = (bf16[48,8,128]{2,1,0:T(8,128)(2,1)S(1)}, bf16[48,8,128]{2,1,0:T(8,128)(2,1)S(1)}, u32[]{:S(2)}, u32[]{:S(2)}) collective-permute-start(bf16[48,8,128]{2,1,0:T(8,128)(2,1)S(1)} %get-tuple-element.16), channel_id=1, source_target_pairs={{0,2},{1,3},{2,0},{3,1},{4,6},{5,7},{6,4},{7,5},{8,10},{9,11},{10,... | collective-permute-start | bytes 294920 | tf_op jit(solution)/shard_map/ppermute | solution.py:116
  12.8 0.7 %copy-start.6 = (f32[8]{0:T(128)S(1)}, f32[8]{0:T(128)}, u32[]{:S(2)}) copy-start(f32[8]{0:T(128)} %param.14) | copy-start | bytes 100
  15.4 10.9 %collective-permute-start.2 = (bf16[48,8,128]{2,1,0:T(8,128)(2,1)S(1)}, bf16[48,8,128]{2,1,0:T(8,128)(2,1)S(1)}, u32[]{:S(2)}, u32[]{:S(2)}) collective-permute-start(bf16[48,8,128]{2,1,0:T(8,128)(2,1)S(1)} %get-tuple-element.15), channel_id=1, source_target_pairs={{0,3},{1,2},{2,1},{3,0},{4,7},{5,6},{6,5},{7,4},{8,11},{9,10},{10,... | collective-permute-start | bytes 294920 | tf_op jit(solution)/shard_map/ppermute | solution.py:116
  15.5 11.6 %collective-permute-start.6 = (bf16[48,8,128]{2,1,0:T(8,128)(2,1)S(1)}, bf16[48,8,128]{2,1,0:T(8,128)(2,1)S(1)}, u32[]{:S(2)}, u32[]{:S(2)}) collective-permute-start(bf16[48,8,128]{2,1,0:T(8,128)(2,1)S(1)} %get-tuple-element.9), channel_id=1, source_target_pairs={{0,1},{1,0},{2,3},{3,2},{4,5},{5,4},{6,7},{7,6},{8,9},{9,8},{10,11... | collective-permute-start | bytes 294920 | tf_op jit(solution)/shard_map/ppermute | solution.py:116
  16.1 11.4 %collective-permute-start.8 = (bf16[48,8,128]{2,1,0:T(8,128)(2,1)S(1)}, bf16[48,8,128]{2,1,0:T(8,128)(2,1)S(1)}, u32[]{:S(2)}, u32[]{:S(2)}) collective-permute-start(bf16[48,8,128]{2,1,0:T(8,128)(2,1)S(1)} %get-tuple-element.8), channel_id=1, source_target_pairs={{0,3},{1,2},{2,1},{3,0},{4,7},{5,6},{6,5},{7,4},{8,11},{9,10},{10,... | collective-permute-start | bytes 294920 | tf_op jit(solution)/shard_map/ppermute | solution.py:116
  20.4 12.1 %collective-permute-start.7 = (bf16[48,8,128]{2,1,0:T(8,128)(2,1)S(1)}, bf16[48,8,128]{2,1,0:T(8,128)(2,1)S(1)}, u32[]{:S(2)}, u32[]{:S(2)}) collective-permute-start(bf16[48,8,128]{2,1,0:T(8,128)(2,1)S(1)} %get-tuple-element.7), channel_id=1, source_target_pairs={{0,2},{1,3},{2,0},{3,1},{4,6},{5,7},{6,4},{7,5},{8,10},{9,11},{10,... | collective-permute-start | bytes 294920 | tf_op jit(solution)/shard_map/ppermute | solution.py:116
  33.5 4.6 %collective-permute-start.10 = (f32[1,8,64]{2,1,0:T(8,128)S(1)}, f32[1,8,64]{2,1,0:T(8,128)S(1)}, u32[]{:S(2)}, u32[]{:S(2)}) collective-permute-start(f32[1,8,64]{2,1,0:T(8,128)S(1)} %get-tuple-element.23), channel_id=1, source_target_pairs={{0,2},{1,3},{2,0},{3,1},{4,6},{5,7},{6,4},{7,5},{8,10},{9,11},{10,... | collective-permute-start | bytes 6152 | tf_op jit(solution)/shard_map/ppermute | solution.py:56
  34.5 5.4 %collective-permute-start.11 = (f32[1,8,64]{2,1,0:T(8,128)S(1)}, f32[1,8,64]{2,1,0:T(8,128)S(1)}, u32[]{:S(2)}, u32[]{:S(2)}) collective-permute-start(f32[1,8,64]{2,1,0:T(8,128)S(1)} %get-tuple-element.22), channel_id=1, source_target_pairs={{0,3},{1,2},{2,1},{3,0},{4,7},{5,6},{6,5},{7,4},{8,11},{9,10},{10,... | collective-permute-start | bytes 6152 | tf_op jit(solution)/shard_map/ppermute | solution.py:56
  36.2 3.7 %collective-permute-start.9 = (f32[1,8,64]{2,1,0:T(8,128)S(1)}, f32[1,8,64]{2,1,0:T(8,128)S(1)}, u32[]{:S(2)}, u32[]{:S(2)}) collective-permute-start(f32[1,8,64]{2,1,0:T(8,128)S(1)} %get-tuple-element.21), channel_id=1, source_target_pairs={{0,1},{1,0},{2,3},{3,2},{4,5},{5,4},{6,7},{7,6},{8,9},{9,8},{10,11... | collective-permute-start | bytes 6152 | tf_op jit(solution)/shard_map/ppermute | solution.py:56
  39.9 1.2 %collective-permute-start.12 = (f32[8,64]{1,0:T(8,128)S(1)}, f32[8,64]{1,0:T(8,128)S(1)}, u32[]{:S(2)}, u32[]{:S(2)}) collective-permute-start(f32[8,64]{1,0:T(8,128)S(1)} %bitcast_add_fusion), channel_id=1, source_target_pairs={{0,4},{4,0},{8,12},{12,8},{1,5},{5,1},{9,13},{13,9},{2,6},{6,2},{1... | collective-permute-start | bytes 6152 | tf_op jit(solution)/shard_map/ppermute | solution.py:75
  41.1 1.5 %copy-start.3 = (f32[64,8]{0,1:T(8,128)S(1)}, f32[64,8]{0,1:T(8,128)}, u32[]{:S(2)}) copy-start(f32[64,8]{0,1:T(8,128)} %param.12) | copy-start | bytes 6148
  41.1 3.6 %collective-permute-start.13 = (f32[8,64]{1,0:T(8,128)S(1)}, f32[8,64]{1,0:T(8,128)S(1)}, u32[]{:S(2)}, u32[]{:S(2)}) collective-permute-start(f32[8,64]{1,0:T(8,128)S(1)} %add.168), channel_id=1, source_target_pairs={{0,8},{4,12},{8,0},{12,4},{1,9},{5,13},{9,1},{13,5},{2,10},{6,14},... | collective-permute-start | bytes 6152 | tf_op jit(solution)/shard_map/ppermute | solution.py:75

commit v19 on v15

--- a/solution.py
+++ b/solution.py
@@ -41,6 +41,27 @@
 
 def xor_pairs(size, k):
     return [(i, i ^ k) for i in range(size)]
+
+
+def prefix_from_pieces(pieces, sources, start, step_dev, steps_axis):
+    local_steps = pieces[0].shape[0]
+    zero = jnp.zeros((), jnp.float32)
+    outs = []
+    for s in range(step_dev):
+        acc = None
+        for piece, source in zip(pieces, sources):
+            for t in range(local_steps):
+                term = jnp.where(source * local_steps + t <= s, piece[t], zero)
+                acc = term if acc is None else acc + term
+        outs.append(acc)
+    total = outs[-1]
+    local_cum = lax.optimization_barrier(jnp.stack(outs) + start[None])
+    position = lax.axis_index("step")
+    earlier = jnp.zeros_like(total)
+    for k in range(1, steps_axis):
+        other = lax.ppermute(total, "step", xor_pairs(steps_axis, k))
+        earlier = earlier + jnp.where((position ^ k) < position, other, zero)
+    return jnp.transpose(local_cum + earlier[None], (0, 2, 1))
 
 
 def gather_prefix(update, start, me, groups, step_dev, steps_axis, partner_order):
@@ -116,6 +137,12 @@
         gathered = lax.all_to_all(stacked, "seq", split_axis=0, concat_axis=3, tiled=True)
         gathered = gathered.reshape(3, per_dev, length, head_size)
         partner_order = False
+    if partner_order:
+        far_q, cfg_table, cfg_index, step_table, time_index = lax.optimization_barrier(
+            (arrived[groups - 1][0], cfg_table, cfg_index, step_table, time_index)
+        )
+        arrived[groups - 1][0] = far_q
+        gathered[0] = jnp.concatenate([arrived[k][0] for k in range(groups)], axis=1)
     heads_out = attend(gathered[0], gathered[1], gathered[2])
 
     weight_heads = out_weight.reshape(channels, heads, head_size)
@@ -132,6 +159,29 @@
             jnp.einsum("chd,sbhld->sblc", weight_heads, ho, preferred_element_type=jnp.float32)
             / root_mean[:, :, :, None]
         )
+        start_t = start_latent.T
+        if partner_order:
+            pieces = drift.reshape(local_steps, branches, groups, tok_dev, channels)
+            sent = [pieces[:, :, 0]]
+            for k in range(1, groups):
+                sent.append(lax.ppermute(pieces[:, :, k], "seq", xor_pairs(groups, k)))
+            index = (me ^ jnp.arange(groups, dtype=jnp.int32))[:, None] * local_steps + jnp.arange(
+                local_steps, dtype=jnp.int32
+            )
+            picks = index[:, :, None] == jnp.arange(step_dev, dtype=jnp.int32)
+            lens = jnp.sum(jnp.where(picks, step_len, jnp.zeros((), jnp.float32)), axis=-1)
+            shape = (groups, local_steps, tok_dev, channels)
+            coef = lax.optimization_barrier(
+                jnp.stack(
+                    [jnp.broadcast_to(guide_scale, shape), jnp.broadcast_to(lens[:, :, None, None], shape)]
+                )
+            )
+            updates = []
+            for k in range(groups):
+                guided = sent[k][:, 1] + coef[0, k] * (sent[k][:, 0] - sent[k][:, 1])
+                updates.append(coef[1, k] * guided)
+            sources = [me ^ k for k in range(groups)]
+            return prefix_from_pieces(updates, sources, start_t, step_dev, steps_axis)
         owner = jnp.arange(step_dev, dtype=jnp.int32) // local_steps == me
         slot = jnp.arange(step_dev, dtype=jnp.int32) % local_steps
         mine = (owner[:, None] & (slot[:, None] == jnp.arange(local_steps)))[:, :, None, None]
@@ -143,7 +193,6 @@
             jnp.stack([jnp.broadcast_to(guide_scale, shape), jnp.broadcast_to(len_full, shape)])
         )
         scale_full, len_full = coef[0], coef[1]
-        start_t = start_latent.T
         guided = drift[:, 1] + scale_full * (drift[:, 0] - drift[:, 1])
         update = len_full * guided
         update = update.reshape(local_steps, groups, tok_dev, channels)

time: 45.4 us -> 44.2 us (0.974)
  starting transfers between devices: 24.8 us -> 21.3 us
  waiting for transfers between devices: 11.1 us -> 14.6 us
  local copies, waits for them, and re-layouts: 3.93 us -> 3.25 us
  other arithmetic: 2.2 us -> 1.72 us
    ppermute x9, waiting for transfers between devices: 6.34 us -> 12.2 us  [on_device(): pieces = [lax.ppermute(p, 'seq', xor_pairs(groups, k)) for p in pieces]]
    ppermute x9, starting transfers between devices: 19.3 us -> 15.8 us  [on_device(): pieces = [lax.ppermute(p, 'seq', xor_pairs(groups, k)) for p in pieces]]
    ppermute x6, waiting for transfers between devices: 4.78 us -> 2.39 us  [the longest x3 1.97 us: prefix_from_pieces(): other = lax.ppermute(total, 'step', xor_pairs(steps_axis, k))]
    another operation x2, local copies, waits for them, and re-layouts: 1.38 us -> 0.7 us  [on_device(): jnp.stack([jnp.broadcast_to(guide_scale, shape), jnp.broadcast_to(lens[:,...]
    reduce_sum x1, other arithmetic: 0.66 us -> 0.18 us  [on_device(): jnp.sum(jnp.where(picks, step_len, jnp.zeros((), jnp.float32)), axis=-1)]
  transfers between devices with their start and end apart: 15 -> 15, of which waited for: 6 -> 7; matrix products, arithmetic and copies ran while one was open for 10% -> 7% of each run, Pallas kernels for 0% -> 0%
where the time goes in v19:
time: 44.2 us; the launch traced here: 44 us
  starting transfers between devices  21.3 us (48%)
  waiting for transfers between devices  14.6 us (33%)
  local copies, waits for them, and re-layouts  3.25 us (7%)
  matrix products  2.3 us (5%)
  other arithmetic  1.72 us (4%)
  between operations  0.86 us (2%)
    ppermute x9, starting transfers between devices, on_device(): pieces = [lax.ppermute(p, 'seq', xor_pairs(groups, k)) for p in pieces]  15.8 us
    ppermute x9, waiting for transfers between devices, on_device(): pieces = [lax.ppermute(p, 'seq', xor_pairs(groups, k)) for p in pieces]  12.2 us
    ppermute x3, starting transfers between devices, on_device(): sent.append(lax.ppermute(pieces[:, :, k], 'seq', xor_pairs(groups, k)))  3.55 us
    ppermute x3, waiting for transfers between devices, prefix_from_pieces(): other = lax.ppermute(total, 'step', xor_pairs(steps_axis, k))  1.97 us
    ppermute x3, starting transfers between devices, prefix_from_pieces(): other = lax.ppermute(total, 'step', xor_pairs(steps_axis, k))  1.93 us
    dot_general x4, matrix products, attend(): jnp.einsum('iqk,ikd->iqd', weights[:, :, first:first + size], block, pref...  1.59 us
    unnamed x14, local copies, waits for them, and re-layouts  1.36 us
    squeeze x3, local copies, waits for them, and re-layouts, on_device(): lax.dynamic_index_in_dim(c, me ^ k, 0, keepdims=False)  1.19 us
  transfers between devices with their start and end apart: 15, of which 7 were waited for; matrix products, arithmetic and copies ran while one was open for 7% of the time, Pallas kernels for 0%

profile of v19, /device:TPU:0, one launch (start us, length us, event | category | flops | bytes accessed | tf_op | source)
XLA Modules:
  0.0 44.0 jit_solution(15203850368583218862)
XLA Ops:
  0.0 1.1 %dynamic-slice_bitcast_fusion.9 = (bf16[48,8,128]{2,1,0:T(8,128)(2,1)S(1)}, bf16[48,8,128]{2,1,0:T(8,128)(2,1)S(1)}, bf16[48,8,128]{2,1,0:T(8,128)(2,1)S(1)}, bf16[48,8,128]{2,1,0:T(8,128)(2,1)S(1)}) fusion(bf16[4,48,8,128]{3,2,1,0:T(8,128)(2,1)} %bitcast.222, s32[]{:T(128)S(6)} %select_n.291, s32[]{:T(128)S(6)} %select_n.293, s32[]{:T(128)S(6)} %select_n.292, ...), kind=kLoop, calls=%fused_computation.46 | loop fusion | bytes 786448 | tf_op jit(solution)/shard_map/jit(dynamic_index_in_dim)/squeeze | solution.py:126
  1.1 5.1 %collective-permute-start = (bf16[48,8,128]{2,1,0:T(8,128)(2,1)S(1)}, bf16[48,8,128]{2,1,0:T(8,128)(2,1)S(1)}, u32[]{:S(2)}, u32[]{:S(2)}) collective-permute-start(bf16[48,8,128]{2,1,0:T(8,128)(2,1)S(1)} %get-tuple-element.32), channel_id=1, source_target_pairs={{0,3},{1,2},{2,1},{3,0},{4,7},{5,6},{6,5},{7,4},{8,11},{9,10},{10,... | collective-permute-start | bytes 294920 | tf_op jit(solution)/shard_map/ppermute | solution.py:128
  6.4 0.6 %collective-permute-start.4 = (bf16[48,8,128]{2,1,0:T(8,128)(2,1)S(1)}, bf16[48,8,128]{2,1,0:T(8,128)(2,1)S(1)}, u32[]{:S(2)}, u32[]{:S(2)}) collective-permute-start(bf16[48,8,128]{2,1,0:T(8,128)(2,1)S(1)} %get-tuple-element.27), channel_id=1, source_target_pairs={{0,2},{1,3},{2,0},{3,1},{4,6},{5,7},{6,4},{7,5},{8,10},{9,11},{10,... | collective-permute-start | bytes 294920 | tf_op jit(solution)/shard_map/ppermute | solution.py:128
  7.0 3.8 %collective-permute-start.5 = (bf16[48,8,128]{2,1,0:T(8,128)(2,1)S(1)}, bf16[48,8,128]{2,1,0:T(8,128)(2,1)S(1)}, u32[]{:S(2)}, u32[]{:S(2)}) collective-permute-start(bf16[48,8,128]{2,1,0:T(8,128)(2,1)S(1)} %get-tuple-element.26), channel_id=1, source_target_pairs={{0,3},{1,2},{2,1},{3,0},{4,7},{5,6},{6,5},{7,4},{8,11},{9,10},{10,... | collective-permute-start | bytes 294920 | tf_op jit(solution)/shard_map/ppermute | solution.py:128
  11.5 0.7 %collective-permute-start.2 = (bf16[48,8,128]{2,1,0:T(8,128)(2,1)S(1)}, bf16[48,8,128]{2,1,0:T(8,128)(2,1)S(1)}, u32[]{:S(2)}, u32[]{:S(2)}) collective-permute-start(bf16[48,8,128]{2,1,0:T(8,128)(2,1)S(1)} %get-tuple-element.30), channel_id=1, source_target_pairs={{0,2},{1,3},{2,0},{3,1},{4,6},{5,7},{6,4},{7,5},{8,10},{9,11},{10,... | collective-permute-start | bytes 294920 | tf_op jit(solution)/shard_map/ppermute | solution.py:128
  12.1 0.6 %collective-permute-done.3 = bf16[48,8,128]{2,1,0:T(8,128)(2,1)S(1)} collective-permute-done((bf16[48,8,128]{2,1,0:T(8,128)(2,1)S(1)}, bf16[48,8,128]{2,1,0:T(8,128)(2,1)S(1)}, u32[]{:S(2)}, u32[]{:S(2)}) %collective-permute-start.3) | collective-permute-done | bytes 98336 | tf_op jit(solution)/shard_map/ppermute | solution.py:128
  12.8 1.6 %collective-permute-start.6 = (bf16[48,8,128]{2,1,0:T(8,128)(2,1)S(1)}, bf16[48,8,128]{2,1,0:T(8,128)(2,1)S(1)}, u32[]{:S(2)}, u32[]{:S(2)}) collective-permute-start(bf16[48,8,128]{2,1,0:T(8,128)(2,1)S(1)} %get-tuple-element.24), channel_id=1, source_target_pairs={{0,1},{1,0},{2,3},{3,2},{4,5},{5,4},{6,7},{7,6},{8,9},{9,8},{10,11... | collective-permute-start | bytes 294920 | tf_op jit(solution)/shard_map/ppermute | solution.py:128
  14.3 3.6 %collective-permute-done.4 = bf16[48,8,128]{2,1,0:T(8,128)(2,1)S(1)} collective-permute-done((bf16[48,8,128]{2,1,0:T(8,128)(2,1)S(1)}, bf16[48,8,128]{2,1,0:T(8,128)(2,1)S(1)}, u32[]{:S(2)}, u32[]{:S(2)}) %collective-permute-start.4) | collective-permute-done | bytes 98336 | tf_op jit(solution)/shard_map/ppermute | solution.py:128
  17.9 0.7 %collective-permute-start.8 = (bf16[48,8,128]{2,1,0:T(8,128)(2,1)S(1)}, bf16[48,8,128]{2,1,0:T(8,128)(2,1)S(1)}, u32[]{:S(2)}, u32[]{:S(2)}) collective-permute-start(bf16[48,8,128]{2,1,0:T(8,128)(2,1)S(1)} %get-tuple-element.23), channel_id=1, source_target_pairs={{0,3},{1,2},{2,1},{3,0},{4,7},{5,6},{6,5},{7,4},{8,11},{9,10},{10,... | collective-permute-start | bytes 294920 | tf_op jit(solution)/shard_map/ppermute | solution.py:128
  18.6 3.3 %collective-permute-start.7 = (bf16[48,8,128]{2,1,0:T(8,128)(2,1)S(1)}, bf16[48,8,128]{2,1,0:T(8,128)(2,1)S(1)}, u32[]{:S(2)}, u32[]{:S(2)}) collective-permute-start(bf16[48,8,128]{2,1,0:T(8,128)(2,1)S(1)} %get-tuple-element.22), channel_id=1, source_target_pairs={{0,2},{1,3},{2,0},{3,1},{4,6},{5,7},{6,4},{7,5},{8,10},{9,11},{10,... | collective-permute-start | bytes 294920 | tf_op jit(solution)/shard_map/ppermute | solution.py:128
  21.9 4.7 %collective-permute-done.2 = bf16[48,8,128]{2,1,0:T(8,128)(2,1)S(1)} collective-permute-done((bf16[48,8,128]{2,1,0:T(8,128)(2,1)S(1)}, bf16[48,8,128]{2,1,0:T(8,128)(2,1)S(1)}, u32[]{:S(2)}, u32[]{:S(2)}) %collective-permute-start.2) | collective-permute-done | bytes 98336 | tf_op jit(solution)/shard_map/ppermute | solution.py:128
  26.7 0.5 %fusion.81 = (f32[48,32]{1,0:T(8,128)S(1)}, bf16[48,32,32]{1,2,0:T(8,128)(2,1)S(1)}) fusion(bf16[48,8,128]{2,1,0:T(8,128)(2,1)S(1)} %collective-permute-done, bf16[48,8,128]{2,1,0:T(8,128)(2,1)S(1)} %collective-permute-done.2, bf16[48,8,128]{2,1,0:T(8,128)(2,1)S(1)} %collective-permute-done.1, bf16[48,8,128]{2,1,0:T(8,128)(2,1)S(1)} %get-tuple-element.29, ...), kind=kOutput, calls=%fused_computation.111 | convolution fusion | flops 15925279 | bytes 890880 | tf_op jit(solution)/shard_map/sub | solution.py:21
  28.1 3.3 %collective-permute-done.7 = bf16[48,8,128]{2,1,0:T(8,128)(2,1)S(1)} collective-permute-done((bf16[48,8,128]{2,1,0:T(8,128)(2,1)S(1)}, bf16[48,8,128]{2,1,0:T(8,128)(2,1)S(1)}, u32[]{:S(2)}, u32[]{:S(2)}) %collective-permute-start.7) | collective-permute-done | bytes 98336 | tf_op jit(solution)/shard_map/ppermute | solution.py:128
  31.4 0.7 %multiply_reduce_fusion = (f32[48,32]{1,0:T(8,128)S(1)}, bf16[48,32,128]{2,1,0:T(8,128)(2,1)S(1)}) fusion(f32[48,32]{1,0:T(8,128)S(1)} %get-tuple-element.20, f32[48,32,128]{2,1,0:T(8,128)S(1)} %fusion.27, f32[48,32,128]{2,1,0:T(8,128)S(1)} %convolution_add_fusion.1, bf16[48,8,128]{2,1,0:T(8,128)(2,1)S(1)} %collective-permute-done.7, ...), kind=kOutput, calls=%fused_computation.12 | convolution fusion | flops 4520448 | bytes 2193408 | tf_op jit(solution)/shard_map/iqk,ikd->iqd/dot_general | solution.py:29
  32.5 2.6 %collective-permute-start.11 = (f32[1,2,8,64]{3,2,1,0:T(8,128)S(1)}, f32[1,2,8,64]{3,2,1,0:T(8,128)S(1)}, u32[]{:S(2)}, u32[]{:S(2)}) collective-permute-start(f32[1,2,8,64]{3,2,1,0:T(8,128)S(1)} %get-tuple-element.33), channel_id=1, source_target_pairs={{0,3},{1,2},{2,1},{3,0},{4,7},{5,6},{6,5},{7,4},{8,11},{9,10},{10,... | collective-permute-start | bytes 12296 | tf_op jit(solution)/shard_map/ppermute | solution.py:167
  35.1 0.8 %collective-permute-start.9 = (f32[1,2,8,64]{3,2,1,0:T(8,128)S(1)}, f32[1,2,8,64]{3,2,1,0:T(8,128)S(1)}, u32[]{:S(2)}, u32[]{:S(2)}) collective-permute-start(f32[1,2,8,64]{3,2,1,0:T(8,128)S(1)} %get-tuple-element.35), channel_id=1, source_target_pairs={{0,1},{1,0},{2,3},{3,2},{4,5},{5,4},{6,7},{7,6},{8,9},{9,8},{10,11... | collective-permute-start | bytes 12296 | tf_op jit(solution)/shard_map/ppermute | solution.py:167
  36.3 0.7 %copy-done.6 = f32[8]{0:T(128)S(1)} copy-done((f32[8]{0:T(128)S(1)}, f32[8]{0:T(128)}, u32[]{:S(2)}) %copy-start.6) | copy-done | bytes 56
  37.0 0.6 %fusion.67 = f32[]{:T(128)} fusion(f32[8]{0:T(128)S(1)} %copy-done.6, s32[]{:T(128)} %bitcast.221), kind=kLoop, calls=%fused_computation.105 | loop fusion | flops 23 | bytes 40 | tf_op jit(solution)/shard_map/reduce_sum | solution.py:13
  37.7 0.6 %stack.4 = f32[2,4,1,8,64]{4,3,2,1,0:T(8,128)S(1)} pad(f32[1,4,1,8,64]{4,3,2,1,0:T(8,128)S(1)} %stack_broadcast_in_dim.2, f32[]{:T(128)} %fusion.67), padding=1_0x0_0x0_0x0_0x0_0 | pad | bytes 24580 | tf_op jit(solution)/shard_map/stack | solution.py:175
  38.8 1.5 %collective-permute-start.13 = (f32[8,64]{1,0:T(8,128)S(1)}, f32[8,64]{1,0:T(8,128)S(1)}, u32[]{:S(2)}, u32[]{:S(2)}) collective-permute-start(f32[8,64]{1,0:T(8,128)S(1)} %fusion.39), channel_id=1, source_target_pairs={{0,8},{4,12},{8,0},{12,4},{1,9},{5,13},{9,1},{13,5},{2,10},{6,14},... | collective-permute-start | bytes 6152 | tf_op jit(solution)/shard_map/ppermute | solution.py:62
  40.7 0.7 %copy-done.3 = f32[64,8]{0,1:T(8,128)S(1)} copy-done((f32[64,8]{0,1:T(8,128)S(1)}, f32[64,8]{0,1:T(8,128)}, u32[]{:S(2)}) %copy-start.3) | copy-done | bytes 2072
  41.4 1.1 %collective-permute-done.13 = f32[8,64]{1,0:T(8,128)S(1)} collective-permute-done((f32[8,64]{1,0:T(8,128)S(1)}, f32[8,64]{1,0:T(8,128)S(1)}, u32[]{:S(2)}, u32[]{:S(2)}) %collective-permute-start.13) | collective-permute-done | bytes 2080 | tf_op jit(solution)/shard_map/ppermute | solution.py:62
  42.5 0.9 %collective-permute-done.14 = f32[8,64]{1,0:T(8,128)S(1)} collective-permute-done((f32[8,64]{1,0:T(8,128)S(1)}, f32[8,64]{1,0:T(8,128)S(1)}, u32[]{:S(2)}, u32[]{:S(2)}) %collective-permute-start.14) | collective-permute-done | bytes 2080 | tf_op jit(solution)/shard_map/ppermute | solution.py:62
  43.4 0.6 %add_bitcast_fusion = f32[4,64,8]{1,2,0:T(8,128)} fusion(f32[4,8,64]{2,1,0:T(8,128)S(1)} %maximum_add_fusion, f32[8,64]{1,0:T(8,128)S(1)} %select_add_fusion), kind=kLoop, calls=%fused_computation.49 | loop fusion | flops 2048 | bytes 18432 | tf_op jit(solution)/shard_map/transpose | solution.py:64
  (44 shorter events, 2.8 us)
Async XLA Ops:
  0.0 32.1 %copy-start = (bf16[64,3072]{1,0:T(8,128)(2,1)S(1)}, bf16[64,3072]{1,0:T(8,128)(2,1)}, u32[]{:S(2)}) copy-start(bf16[64,3072]{1,0:T(8,128)(2,1)} %param.13) | copy-start | bytes 1179652
  0.0 6.3 %copy-start.1 = (bf16[4,2,24,8,128]{4,3,2,1,0:T(8,128)(2,1)S(1)}, bf16[4,2,24,8,128]{4,3,2,1,0:T(8,128)(2,1)}, u32[]{:S(2)}) copy-start(bf16[4,2,24,8,128]{4,3,2,1,0:T(8,128)(2,1)} %param.10) | copy-start | bytes 1179652
  1.1 10.3 %collective-permute-start = (bf16[48,8,128]{2,1,0:T(8,128)(2,1)S(1)}, bf16[48,8,128]{2,1,0:T(8,128)(2,1)S(1)}, u32[]{:S(2)}, u32[]{:S(2)}) collective-permute-start(bf16[48,8,128]{2,1,0:T(8,128)(2,1)S(1)} %get-tuple-element.32), channel_id=1, source_target_pairs={{0,3},{1,2},{2,1},{3,0},{4,7},{5,6},{6,5},{7,4},{8,11},{9,10},{10,... | collective-permute-start | bytes 294920 | tf_op jit(solution)/shard_map/ppermute | solution.py:128
  6.3 5.2 %copy-start.2 = (bf16[4,2,24,8,128]{4,3,2,1,0:T(8,128)(2,1)S(1)}, bf16[4,2,24,8,128]{4,3,2,1,0:T(8,128)(2,1)}, u32[]{:S(2)}) copy-start(bf16[4,2,24,8,128]{4,3,2,1,0:T(8,128)(2,1)} %param.11) | copy-start | bytes 1179652
  6.3 6.5 %collective-permute-start.3 = (bf16[48,8,128]{2,1,0:T(8,128)(2,1)S(1)}, bf16[48,8,128]{2,1,0:T(8,128)(2,1)S(1)}, u32[]{:S(2)}, u32[]{:S(2)}) collective-permute-start(bf16[48,8,128]{2,1,0:T(8,128)(2,1)S(1)} %get-tuple-element.28), channel_id=1, source_target_pairs={{0,1},{1,0},{2,3},{3,2},{4,5},{5,4},{6,7},{7,6},{8,9},{9,8},{10,11... | collective-permute-start | bytes 294920 | tf_op jit(solution)/shard_map/ppermute | solution.py:128
  6.4 11.5 %collective-permute-start.4 = (bf16[48,8,128]{2,1,0:T(8,128)(2,1)S(1)}, bf16[48,8,128]{2,1,0:T(8,128)(2,1)S(1)}, u32[]{:S(2)}, u32[]{:S(2)}) collective-permute-start(bf16[48,8,128]{2,1,0:T(8,128)(2,1)S(1)} %get-tuple-element.27), channel_id=1, source_target_pairs={{0,2},{1,3},{2,0},{3,1},{4,6},{5,7},{6,4},{7,5},{8,10},{9,11},{10,... | collective-permute-start | bytes 294920 | tf_op jit(solution)/shard_map/ppermute | solution.py:128
  7.0 11.7 %collective-permute-start.5 = (bf16[48,8,128]{2,1,0:T(8,128)(2,1)S(1)}, bf16[48,8,128]{2,1,0:T(8,128)(2,1)S(1)}, u32[]{:S(2)}, u32[]{:S(2)}) collective-permute-start(bf16[48,8,128]{2,1,0:T(8,128)(2,1)S(1)} %get-tuple-element.26), channel_id=1, source_target_pairs={{0,3},{1,2},{2,1},{3,0},{4,7},{5,6},{6,5},{7,4},{8,11},{9,10},{10,... | collective-permute-start | bytes 294920 | tf_op jit(solution)/shard_map/ppermute | solution.py:128
  10.7 11.2 %collective-permute-start.1 = (bf16[48,8,128]{2,1,0:T(8,128)(2,1)S(1)}, bf16[48,8,128]{2,1,0:T(8,128)(2,1)S(1)}, u32[]{:S(2)}, u32[]{:S(2)}) collective-permute-start(bf16[48,8,128]{2,1,0:T(8,128)(2,1)S(1)} %get-tuple-element.31), channel_id=1, source_target_pairs={{0,1},{1,0},{2,3},{3,2},{4,5},{5,4},{6,7},{7,6},{8,9},{9,8},{10,11... | collective-permute-start | bytes 294920 | tf_op jit(solution)/shard_map/ppermute | solution.py:128
  11.5 15.2 %collective-permute-start.2 = (bf16[48,8,128]{2,1,0:T(8,128)(2,1)S(1)}, bf16[48,8,128]{2,1,0:T(8,128)(2,1)S(1)}, u32[]{:S(2)}, u32[]{:S(2)}) collective-permute-start(bf16[48,8,128]{2,1,0:T(8,128)(2,1)S(1)} %get-tuple-element.30), channel_id=1, source_target_pairs={{0,2},{1,3},{2,0},{3,1},{4,6},{5,7},{6,4},{7,5},{8,10},{9,11},{10,... | collective-permute-start | bytes 294920 | tf_op jit(solution)/shard_map/ppermute | solution.py:128
  12.8 14.7 %collective-permute-start.6 = (bf16[48,8,128]{2,1,0:T(8,128)(2,1)S(1)}, bf16[48,8,128]{2,1,0:T(8,128)(2,1)S(1)}, u32[]{:S(2)}, u32[]{:S(2)}) collective-permute-start(bf16[48,8,128]{2,1,0:T(8,128)(2,1)S(1)} %get-tuple-element.24), channel_id=1, source_target_pairs={{0,1},{1,0},{2,3},{3,2},{4,5},{5,4},{6,7},{7,6},{8,9},{9,8},{10,11... | collective-permute-start | bytes 294920 | tf_op jit(solution)/shard_map/ppermute | solution.py:128
  17.9 9.9 %collective-permute-start.8 = (bf16[48,8,128]{2,1,0:T(8,128)(2,1)S(1)}, bf16[48,8,128]{2,1,0:T(8,128)(2,1)S(1)}, u32[]{:S(2)}, u32[]{:S(2)}) collective-permute-start(bf16[48,8,128]{2,1,0:T(8,128)(2,1)S(1)} %get-tuple-element.23), channel_id=1, source_target_pairs={{0,3},{1,2},{2,1},{3,0},{4,7},{5,6},{6,5},{7,4},{8,11},{9,10},{10,... | collective-permute-start | bytes 294920 | tf_op jit(solution)/shard_map/ppermute | solution.py:128
  18.6 12.8 %collective-permute-start.7 = (bf16[48,8,128]{2,1,0:T(8,128)(2,1)S(1)}, bf16[48,8,128]{2,1,0:T(8,128)(2,1)S(1)}, u32[]{:S(2)}, u32[]{:S(2)}) collective-permute-start(bf16[48,8,128]{2,1,0:T(8,128)(2,1)S(1)} %get-tuple-element.22), channel_id=1, source_target_pairs={{0,2},{1,3},{2,0},{3,1},{4,6},{5,7},{6,4},{7,5},{8,10},{9,11},{10,... | collective-permute-start | bytes 294920 | tf_op jit(solution)/shard_map/ppermute | solution.py:128
  32.3 3.6 %copy-start.4 = (f32[1000]{0:T(1024)S(1)}, f32[1000]{0:T(1024)}, u32[]{:S(2)}) copy-start(f32[1000]{0:T(1024)} %param.16) | copy-start | bytes 12004
  32.4 6.0 %collective-permute-start.10 = (f32[1,2,8,64]{3,2,1,0:T(8,128)S(1)}, f32[1,2,8,64]{3,2,1,0:T(8,128)S(1)}, u32[]{:S(2)}, u32[]{:S(2)}) collective-permute-start(f32[1,2,8,64]{3,2,1,0:T(8,128)S(1)} %get-tuple-element.34), channel_id=1, source_target_pairs={{0,2},{1,3},{2,0},{3,1},{4,6},{5,7},{6,4},{7,5},{8,10},{9,11},{10,... | collective-permute-start | bytes 12296 | tf_op jit(solution)/shard_map/ppermute | solution.py:167
  32.5 3.5 %copy-start.5 = (s32[4]{0:T(128)S(1)}, s32[4]{0:T(128)}, u32[]{:S(2)}) copy-start(s32[4]{0:T(128)} %param.17) | copy-start | bytes 52
  32.5 5.9 %collective-permute-start.11 = (f32[1,2,8,64]{3,2,1,0:T(8,128)S(1)}, f32[1,2,8,64]{3,2,1,0:T(8,128)S(1)}, u32[]{:S(2)}, u32[]{:S(2)}) collective-permute-start(f32[1,2,8,64]{3,2,1,0:T(8,128)S(1)} %get-tuple-element.33), channel_id=1, source_target_pairs={{0,3},{1,2},{2,1},{3,0},{4,7},{5,6},{6,5},{7,4},{8,11},{9,10},{10,... | collective-permute-start | bytes 12296 | tf_op jit(solution)/shard_map/ppermute | solution.py:167
  35.1 3.7 %collective-permute-start.9 = (f32[1,2,8,64]{3,2,1,0:T(8,128)S(1)}, f32[1,2,8,64]{3,2,1,0:T(8,128)S(1)}, u32[]{:S(2)}, u32[]{:S(2)}) collective-permute-start(f32[1,2,8,64]{3,2,1,0:T(8,128)S(1)} %get-tuple-element.35), channel_id=1, source_target_pairs={{0,1},{1,0},{2,3},{3,2},{4,5},{5,4},{6,7},{7,6},{8,9},{9,8},{10,11... | collective-permute-start | bytes 12296 | tf_op jit(solution)/shard_map/ppermute | solution.py:167
  36.3 0.7 %copy-start.6 = (f32[8]{0:T(128)S(1)}, f32[8]{0:T(128)}, u32[]{:S(2)}) copy-start(f32[8]{0:T(128)} %param.14) | copy-start | bytes 100
  38.8 2.7 %collective-permute-start.12 = (f32[8,64]{1,0:T(8,128)S(1)}, f32[8,64]{1,0:T(8,128)S(1)}, u32[]{:S(2)}, u32[]{:S(2)}) collective-permute-start(f32[8,64]{1,0:T(8,128)S(1)} %fusion.39), channel_id=1, source_target_pairs={{0,4},{4,0},{8,12},{12,8},{1,5},{5,1},{9,13},{13,9},{2,6},{6,2},{1... | collective-permute-start | bytes 6152 | tf_op jit(solution)/shard_map/ppermute | solution.py:62
  38.8 3.7 %collective-permute-start.13 = (f32[8,64]{1,0:T(8,128)S(1)}, f32[8,64]{1,0:T(8,128)S(1)}, u32[]{:S(2)}, u32[]{:S(2)}) collective-permute-start(f32[8,64]{1,0:T(8,128)S(1)} %fusion.39), channel_id=1, source_target_pairs={{0,8},{4,12},{8,0},{12,4},{1,9},{5,13},{9,1},{13,5},{2,10},{6,14},... | collective-permute-start | bytes 6152 | tf_op jit(solution)/shard_map/ppermute | solution.py:62
  40.4 3.0 %collective-permute-start.14 = (f32[8,64]{1,0:T(8,128)S(1)}, f32[8,64]{1,0:T(8,128)S(1)}, u32[]{:S(2)}, u32[]{:S(2)}) collective-permute-start(f32[8,64]{1,0:T(8,128)S(1)} %fusion.39), channel_id=1, source_target_pairs={{0,12},{4,8},{8,4},{12,0},{1,13},{5,9},{9,5},{13,1},{2,14},{6,10},... | collective-permute-start | bytes 6152 | tf_op jit(solution)/shard_map/ppermute | solution.py:62
  40.7 0.7 %copy-start.3 = (f32[64,8]{0,1:T(8,128)S(1)}, f32[64,8]{0,1:T(8,128)}, u32[]{:S(2)}) copy-start(f32[64,8]{0,1:T(8,128)} %param.12) | copy-start | bytes 6148

commit v20 on v19

--- a/solution.py
+++ b/solution.py
@@ -138,8 +138,8 @@
         gathered = gathered.reshape(3, per_dev, length, head_size)
         partner_order = False
     if partner_order:
-        far_q, cfg_table, cfg_index, step_table, time_index = lax.optimization_barrier(
-            (arrived[groups - 1][0], cfg_table, cfg_index, step_table, time_index)
+        far_q, step_table, time_index = lax.optimization_barrier(
+            (arrived[groups - 1][0], step_table, time_index)
         )
         arrived[groups - 1][0] = far_q
         gathered[0] = jnp.concatenate([arrived[k][0] for k in range(groups)], axis=1)

time: 44.2 us -> 46.3 us (1.048)
  starting transfers between devices: 21.3 us -> 23.5 us
    ppermute x9, starting transfers between devices: 15.8 us -> 18.1 us  [on_device(): pieces = [lax.ppermute(p, 'seq', xor_pairs(groups, k)) for p in pieces]]
    ppermute x9, waiting for transfers between devices: 12.2 us -> 11.3 us  [on_device(): pieces = [lax.ppermute(p, 'seq', xor_pairs(groups, k)) for p in pieces]]
    ppermute x3, waiting for transfers between devices: 0.41 us -> 1.17 us  [on_device(): sent.append(lax.ppermute(pieces[:, :, k], 'seq', xor_pairs(groups, k)))]
  transfers between devices with their start and end apart: 15 -> 15, of which waited for: 7 -> 8; matrix products, arithmetic and copies ran while one was open for 7% -> 7% of each run, Pallas kernels for 0% -> 0%
where the time goes in v20:
time: 46.3 us; the launch traced here: 46.1 us
  starting transfers between devices  23.5 us (51%)
  waiting for transfers between devices  14.4 us (31%)
  local copies, waits for them, and re-layouts  3.26 us (7%)
  matrix products  2.3 us (5%)
  other arithmetic  1.72 us (4%)
  between operations  0.85 us (2%)
    ppermute x9, starting transfers between devices, on_device(): pieces = [lax.ppermute(p, 'seq', xor_pairs(groups, k)) for p in pieces]  18.1 us
    ppermute x9, waiting for transfers between devices, on_device(): pieces = [lax.ppermute(p, 'seq', xor_pairs(groups, k)) for p in pieces]  11.3 us
    ppermute x3, starting transfers between devices, on_device(): sent.append(lax.ppermute(pieces[:, :, k], 'seq', xor_pairs(groups, k)))  3.54 us
    ppermute x3, waiting for transfers between devices, prefix_from_pieces(): other = lax.ppermute(total, 'step', xor_pairs(steps_axis, k))  1.99 us
    ppermute x3, starting transfers between devices, prefix_from_pieces(): other = lax.ppermute(total, 'step', xor_pairs(steps_axis, k))  1.93 us
    dot_general x4, matrix products, attend(): jnp.einsum('iqk,ikd->iqd', weights[:, :, first:first + size], block, pref...  1.59 us
    unnamed x14, local copies, waits for them, and re-layouts  1.36 us
    squeeze x3, local copies, waits for them, and re-layouts, on_device(): lax.dynamic_index_in_dim(c, me ^ k, 0, keepdims=False)  1.19 us
  transfers between devices with their start and end apart: 15, of which 8 were waited for; matrix products, arithmetic and copies ran while one was open for 7% of the time, Pallas kernels for 0%

profile of v20, /device:TPU:0, one launch (start us, length us, event | category | flops | bytes accessed | tf_op | source)
XLA Modules:
  0.0 46.1 jit_solution(12011363023472296477)
XLA Ops:
  0.0 1.1 %dynamic-slice_bitcast_fusion.6 = (bf16[48,8,128]{2,1,0:T(8,128)(2,1)S(1)}, bf16[48,8,128]{2,1,0:T(8,128)(2,1)S(1)}, bf16[48,8,128]{2,1,0:T(8,128)(2,1)S(1)}, bf16[48,8,128]{2,1,0:T(8,128)(2,1)S(1)}) fusion(bf16[4,48,8,128]{3,2,1,0:T(8,128)(2,1)} %bitcast.222, s32[]{:T(128)S(6)} %select_n.291, s32[]{:T(128)S(6)} %select_n.287, s32[]{:T(128)S(6)} %select_n.293, ...), kind=kLoop, calls=%fused_computation.43 | loop fusion | bytes 786448 | tf_op jit(solution)/shard_map/jit(dynamic_index_in_dim)/squeeze | solution.py:126
  1.1 3.1 %collective-permute-start.3 = (bf16[48,8,128]{2,1,0:T(8,128)(2,1)S(1)}, bf16[48,8,128]{2,1,0:T(8,128)(2,1)S(1)}, u32[]{:S(2)}, u32[]{:S(2)}) collective-permute-start(bf16[48,8,128]{2,1,0:T(8,128)(2,1)S(1)} %get-tuple-element.24), channel_id=1, source_target_pairs={{0,1},{1,0},{2,3},{3,2},{4,5},{5,4},{6,7},{7,6},{8,9},{9,8},{10,11... | collective-permute-start | bytes 294920 | tf_op jit(solution)/shard_map/ppermute | solution.py:128
  4.2 2.6 %collective-permute-start.4 = (bf16[48,8,128]{2,1,0:T(8,128)(2,1)S(1)}, bf16[48,8,128]{2,1,0:T(8,128)(2,1)S(1)}, u32[]{:S(2)}, u32[]{:S(2)}) collective-permute-start(bf16[48,8,128]{2,1,0:T(8,128)(2,1)S(1)} %get-tuple-element.23), channel_id=1, source_target_pairs={{0,2},{1,3},{2,0},{3,1},{4,6},{5,7},{6,4},{7,5},{8,10},{9,11},{10,... | collective-permute-start | bytes 294920 | tf_op jit(solution)/shard_map/ppermute | solution.py:128
  6.9 3.9 %collective-permute-start = (bf16[48,8,128]{2,1,0:T(8,128)(2,1)S(1)}, bf16[48,8,128]{2,1,0:T(8,128)(2,1)S(1)}, u32[]{:S(2)}, u32[]{:S(2)}) collective-permute-start(bf16[48,8,128]{2,1,0:T(8,128)(2,1)S(1)} %get-tuple-element.28), channel_id=1, source_target_pairs={{0,3},{1,2},{2,1},{3,0},{4,7},{5,6},{6,5},{7,4},{8,11},{9,10},{10,... | collective-permute-start | bytes 294920 | tf_op jit(solution)/shard_map/ppermute | solution.py:128
  11.5 0.6 %copy-done.6 = f32[8]{0:T(128)S(1)} copy-done((f32[8]{0:T(128)S(1)}, f32[8]{0:T(128)}, u32[]{:S(2)}) %copy-start.6) | copy-done | bytes 56
  12.1 0.6 %fusion.67 = f32[]{:T(128)} fusion(f32[8]{0:T(128)S(1)} %copy-done.6, s32[]{:T(128)} %bitcast.221), kind=kLoop, calls=%fused_computation.105 | loop fusion | flops 23 | bytes 40 | tf_op jit(solution)/shard_map/reduce_sum | solution.py:13
  12.7 3.7 %collective-permute-done = bf16[48,8,128]{2,1,0:T(8,128)(2,1)S(1)} collective-permute-done((bf16[48,8,128]{2,1,0:T(8,128)(2,1)S(1)}, bf16[48,8,128]{2,1,0:T(8,128)(2,1)S(1)}, u32[]{:S(2)}, u32[]{:S(2)}) %collective-permute-start) | collective-permute-done | bytes 98336 | tf_op jit(solution)/shard_map/ppermute | solution.py:128
  16.5 5.0 %collective-permute-start.2 = (bf16[48,8,128]{2,1,0:T(8,128)(2,1)S(1)}, bf16[48,8,128]{2,1,0:T(8,128)(2,1)S(1)}, u32[]{:S(2)}, u32[]{:S(2)}) collective-permute-start(bf16[48,8,128]{2,1,0:T(8,128)(2,1)S(1)} %get-tuple-element.26), channel_id=1, source_target_pairs={{0,2},{1,3},{2,0},{3,1},{4,6},{5,7},{6,4},{7,5},{8,10},{9,11},{10,... | collective-permute-start | bytes 294920 | tf_op jit(solution)/shard_map/ppermute | solution.py:128
  21.5 1.5 %collective-permute-start.8 = (bf16[48,8,128]{2,1,0:T(8,128)(2,1)S(1)}, bf16[48,8,128]{2,1,0:T(8,128)(2,1)S(1)}, u32[]{:S(2)}, u32[]{:S(2)}) collective-permute-start(bf16[48,8,128]{2,1,0:T(8,128)(2,1)S(1)} %get-tuple-element.19), channel_id=1, source_target_pairs={{0,3},{1,2},{2,1},{3,0},{4,7},{5,6},{6,5},{7,4},{8,11},{9,10},{10,... | collective-permute-start | bytes 294920 | tf_op jit(solution)/shard_map/ppermute | solution.py:128
  23.0 2.0 %collective-permute-start.7 = (bf16[48,8,128]{2,1,0:T(8,128)(2,1)S(1)}, bf16[48,8,128]{2,1,0:T(8,128)(2,1)S(1)}, u32[]{:S(2)}, u32[]{:S(2)}) collective-permute-start(bf16[48,8,128]{2,1,0:T(8,128)(2,1)S(1)} %get-tuple-element.18), channel_id=1, source_target_pairs={{0,2},{1,3},{2,0},{3,1},{4,6},{5,7},{6,4},{7,5},{8,10},{9,11},{10,... | collective-permute-start | bytes 294920 | tf_op jit(solution)/shard_map/ppermute | solution.py:128
  25.0 2.6 %collective-permute-done.2 = bf16[48,8,128]{2,1,0:T(8,128)(2,1)S(1)} collective-permute-done((bf16[48,8,128]{2,1,0:T(8,128)(2,1)S(1)}, bf16[48,8,128]{2,1,0:T(8,128)(2,1)S(1)}, u32[]{:S(2)}, u32[]{:S(2)}) %collective-permute-start.2) | collective-permute-done | bytes 98336 | tf_op jit(solution)/shard_map/ppermute | solution.py:128
  27.6 0.5 %fusion.81 = (f32[48,32]{1,0:T(8,128)S(1)}, bf16[48,32,32]{1,2,0:T(8,128)(2,1)S(1)}) fusion(bf16[48,8,128]{2,1,0:T(8,128)(2,1)S(1)} %collective-permute-done, bf16[48,8,128]{2,1,0:T(8,128)(2,1)S(1)} %collective-permute-done.2, bf16[48,8,128]{2,1,0:T(8,128)(2,1)S(1)} %collective-permute-done.1, bf16[48,8,128]{2,1,0:T(8,128)(2,1)S(1)} %get-tuple-element.25, ...), kind=kOutput, calls=%fused_computation.111 | convolution fusion | flops 15925279 | bytes 890880 | tf_op jit(solution)/shard_map/sub | solution.py:21
  28.8 1.1 %collective-permute-done.8 = bf16[48,8,128]{2,1,0:T(8,128)(2,1)S(1)} collective-permute-done((bf16[48,8,128]{2,1,0:T(8,128)(2,1)S(1)}, bf16[48,8,128]{2,1,0:T(8,128)(2,1)S(1)}, u32[]{:S(2)}, u32[]{:S(2)}) %collective-permute-start.8) | collective-permute-done | bytes 98336 | tf_op jit(solution)/shard_map/ppermute | solution.py:128
  30.2 3.8 %collective-permute-done.7 = bf16[48,8,128]{2,1,0:T(8,128)(2,1)S(1)} collective-permute-done((bf16[48,8,128]{2,1,0:T(8,128)(2,1)S(1)}, bf16[48,8,128]{2,1,0:T(8,128)(2,1)S(1)}, u32[]{:S(2)}, u32[]{:S(2)}) %collective-permute-start.7) | collective-permute-done | bytes 98336 | tf_op jit(solution)/shard_map/ppermute | solution.py:128
  34.0 0.7 %multiply_reduce_fusion = (f32[48,32]{1,0:T(8,128)S(1)}, bf16[48,32,128]{2,1,0:T(8,128)(2,1)S(1)}) fusion(f32[48,32]{1,0:T(8,128)S(1)} %get-tuple-element.16, f32[48,32,128]{2,1,0:T(8,128)S(1)} %fusion.27, f32[48,32,128]{2,1,0:T(8,128)S(1)} %convolution_add_fusion.1, bf16[48,8,128]{2,1,0:T(8,128)(2,1)S(1)} %collective-permute-done.7, ...), kind=kOutput, calls=%fused_computation.12 | convolution fusion | flops 4520448 | bytes 2193408 | tf_op jit(solution)/shard_map/iqk,ikd->iqd/dot_general | solution.py:29
  35.1 2.1 %collective-permute-start.11 = (f32[1,2,8,64]{3,2,1,0:T(8,128)S(1)}, f32[1,2,8,64]{3,2,1,0:T(8,128)S(1)}, u32[]{:S(2)}, u32[]{:S(2)}) collective-permute-start(f32[1,2,8,64]{3,2,1,0:T(8,128)S(1)} %get-tuple-element.29), channel_id=1, source_target_pairs={{0,3},{1,2},{2,1},{3,0},{4,7},{5,6},{6,5},{7,4},{8,11},{9,10},{10,... | collective-permute-start | bytes 12296 | tf_op jit(solution)/shard_map/ppermute | solution.py:167
  37.2 1.4 %collective-permute-start.9 = (f32[1,2,8,64]{3,2,1,0:T(8,128)S(1)}, f32[1,2,8,64]{3,2,1,0:T(8,128)S(1)}, u32[]{:S(2)}, u32[]{:S(2)}) collective-permute-start(f32[1,2,8,64]{3,2,1,0:T(8,128)S(1)} %get-tuple-element.31), channel_id=1, source_target_pairs={{0,1},{1,0},{2,3},{3,2},{4,5},{5,4},{6,7},{7,6},{8,9},{9,8},{10,11... | collective-permute-start | bytes 12296 | tf_op jit(solution)/shard_map/ppermute | solution.py:167
  39.0 0.6 %stack.4 = f32[2,4,1,8,64]{4,3,2,1,0:T(8,128)S(1)} pad(f32[1,4,1,8,64]{4,3,2,1,0:T(8,128)S(1)} %stack_broadcast_in_dim.2, f32[]{:T(128)} %fusion.67), padding=1_0x0_0x0_0x0_0x0_0 | pad | bytes 24580 | tf_op jit(solution)/shard_map/stack | solution.py:175
  39.6 0.9 %collective-permute-done.11 = f32[1,2,8,64]{3,2,1,0:T(8,128)S(1)} collective-permute-done((f32[1,2,8,64]{3,2,1,0:T(8,128)S(1)}, f32[1,2,8,64]{3,2,1,0:T(8,128)S(1)}, u32[]{:S(2)}, u32[]{:S(2)}) %collective-permute-start.11) | collective-permute-done | bytes 4128 | tf_op jit(solution)/shard_map/ppermute | solution.py:167
  40.9 1.6 %collective-permute-start.13 = (f32[8,64]{1,0:T(8,128)S(1)}, f32[8,64]{1,0:T(8,128)S(1)}, u32[]{:S(2)}, u32[]{:S(2)}) collective-permute-start(f32[8,64]{1,0:T(8,128)S(1)} %fusion.39), channel_id=1, source_target_pairs={{0,8},{4,12},{8,0},{12,4},{1,9},{5,13},{9,1},{13,5},{2,10},{6,14},... | collective-permute-start | bytes 6152 | tf_op jit(solution)/shard_map/ppermute | solution.py:62
  42.8 0.7 %copy-done.3 = f32[64,8]{0,1:T(8,128)S(1)} copy-done((f32[64,8]{0,1:T(8,128)S(1)}, f32[64,8]{0,1:T(8,128)}, u32[]{:S(2)}) %copy-start.3) | copy-done | bytes 2072
  43.5 1.1 %collective-permute-done.13 = f32[8,64]{1,0:T(8,128)S(1)} collective-permute-done((f32[8,64]{1,0:T(8,128)S(1)}, f32[8,64]{1,0:T(8,128)S(1)}, u32[]{:S(2)}, u32[]{:S(2)}) %collective-permute-start.13) | collective-permute-done | bytes 2080 | tf_op jit(solution)/shard_map/ppermute | solution.py:62
  44.6 0.9 %collective-permute-done.14 = f32[8,64]{1,0:T(8,128)S(1)} collective-permute-done((f32[8,64]{1,0:T(8,128)S(1)}, f32[8,64]{1,0:T(8,128)S(1)}, u32[]{:S(2)}, u32[]{:S(2)}) %collective-permute-start.14) | collective-permute-done | bytes 2080 | tf_op jit(solution)/shard_map/ppermute | solution.py:62
  45.5 0.6 %add_bitcast_fusion = f32[4,64,8]{1,2,0:T(8,128)} fusion(f32[4,8,64]{2,1,0:T(8,128)S(1)} %maximum_add_fusion, f32[8,64]{1,0:T(8,128)S(1)} %select_add_fusion), kind=kLoop, calls=%fused_computation.49 | loop fusion | flops 2048 | bytes 18432 | tf_op jit(solution)/shard_map/transpose | solution.py:64
  (44 shorter events, 2.5 us)
Async XLA Ops:
  0.0 34.7 %copy-start = (bf16[64,3072]{1,0:T(8,128)(2,1)S(1)}, bf16[64,3072]{1,0:T(8,128)(2,1)}, u32[]{:S(2)}) copy-start(bf16[64,3072]{1,0:T(8,128)(2,1)} %param.13) | copy-start | bytes 1179652
  0.0 6.8 %copy-start.1 = (bf16[4,2,24,8,128]{4,3,2,1,0:T(8,128)(2,1)S(1)}, bf16[4,2,24,8,128]{4,3,2,1,0:T(8,128)(2,1)}, u32[]{:S(2)}) copy-start(bf16[4,2,24,8,128]{4,3,2,1,0:T(8,128)(2,1)} %param.9) | copy-start | bytes 1179652
  1.1 20.4 %collective-permute-start.3 = (bf16[48,8,128]{2,1,0:T(8,128)(2,1)S(1)}, bf16[48,8,128]{2,1,0:T(8,128)(2,1)S(1)}, u32[]{:S(2)}, u32[]{:S(2)}) collective-permute-start(bf16[48,8,128]{2,1,0:T(8,128)(2,1)S(1)} %get-tuple-element.24), channel_id=1, source_target_pairs={{0,1},{1,0},{2,3},{3,2},{4,5},{5,4},{6,7},{7,6},{8,9},{9,8},{10,11... | collective-permute-start | bytes 294920 | tf_op jit(solution)/shard_map/ppermute | solution.py:128
  4.2 17.3 %collective-permute-start.4 = (bf16[48,8,128]{2,1,0:T(8,128)(2,1)S(1)}, bf16[48,8,128]{2,1,0:T(8,128)(2,1)S(1)}, u32[]{:S(2)}, u32[]{:S(2)}) collective-permute-start(bf16[48,8,128]{2,1,0:T(8,128)(2,1)S(1)} %get-tuple-element.23), channel_id=1, source_target_pairs={{0,2},{1,3},{2,0},{3,1},{4,6},{5,7},{6,4},{7,5},{8,10},{9,11},{10,... | collective-permute-start | bytes 294920 | tf_op jit(solution)/shard_map/ppermute | solution.py:128
  6.8 16.2 %collective-permute-start.5 = (bf16[48,8,128]{2,1,0:T(8,128)(2,1)S(1)}, bf16[48,8,128]{2,1,0:T(8,128)(2,1)S(1)}, u32[]{:S(2)}, u32[]{:S(2)}) collective-permute-start(bf16[48,8,128]{2,1,0:T(8,128)(2,1)S(1)} %get-tuple-element.22), channel_id=1, source_target_pairs={{0,3},{1,2},{2,1},{3,0},{4,7},{5,6},{6,5},{7,4},{8,11},{9,10},{10,... | collective-permute-start | bytes 294920 | tf_op jit(solution)/shard_map/ppermute | solution.py:128
  6.8 3.9 %copy-start.2 = (bf16[4,2,24,8,128]{4,3,2,1,0:T(8,128)(2,1)S(1)}, bf16[4,2,24,8,128]{4,3,2,1,0:T(8,128)(2,1)}, u32[]{:S(2)}) copy-start(bf16[4,2,24,8,128]{4,3,2,1,0:T(8,128)(2,1)} %param.11) | copy-start | bytes 1179652
  6.9 9.6 %collective-permute-start = (bf16[48,8,128]{2,1,0:T(8,128)(2,1)S(1)}, bf16[48,8,128]{2,1,0:T(8,128)(2,1)S(1)}, u32[]{:S(2)}, u32[]{:S(2)}) collective-permute-start(bf16[48,8,128]{2,1,0:T(8,128)(2,1)S(1)} %get-tuple-element.28), channel_id=1, source_target_pairs={{0,3},{1,2},{2,1},{3,0},{4,7},{5,6},{6,5},{7,4},{8,11},{9,10},{10,... | collective-permute-start | bytes 294920 | tf_op jit(solution)/shard_map/ppermute | solution.py:128
  10.7 14.3 %collective-permute-start.1 = (bf16[48,8,128]{2,1,0:T(8,128)(2,1)S(1)}, bf16[48,8,128]{2,1,0:T(8,128)(2,1)S(1)}, u32[]{:S(2)}, u32[]{:S(2)}) collective-permute-start(bf16[48,8,128]{2,1,0:T(8,128)(2,1)S(1)} %get-tuple-element.27), channel_id=1, source_target_pairs={{0,1},{1,0},{2,3},{3,2},{4,5},{5,4},{6,7},{7,6},{8,9},{9,8},{10,11... | collective-permute-start | bytes 294920 | tf_op jit(solution)/shard_map/ppermute | solution.py:128
  11.4 0.7 %copy-start.6 = (f32[8]{0:T(128)S(1)}, f32[8]{0:T(128)}, u32[]{:S(2)}) copy-start(f32[8]{0:T(128)} %param.14) | copy-start | bytes 100
  16.5 11.2 %collective-permute-start.2 = (bf16[48,8,128]{2,1,0:T(8,128)(2,1)S(1)}, bf16[48,8,128]{2,1,0:T(8,128)(2,1)S(1)}, u32[]{:S(2)}, u32[]{:S(2)}) collective-permute-start(bf16[48,8,128]{2,1,0:T(8,128)(2,1)S(1)} %get-tuple-element.26), channel_id=1, source_target_pairs={{0,2},{1,3},{2,0},{3,1},{4,6},{5,7},{6,4},{7,5},{8,10},{9,11},{10,... | collective-permute-start | bytes 294920 | tf_op jit(solution)/shard_map/ppermute | solution.py:128
  21.5 6.9 %collective-permute-start.6 = (bf16[48,8,128]{2,1,0:T(8,128)(2,1)S(1)}, bf16[48,8,128]{2,1,0:T(8,128)(2,1)S(1)}, u32[]{:S(2)}, u32[]{:S(2)}) collective-permute-start(bf16[48,8,128]{2,1,0:T(8,128)(2,1)S(1)} %get-tuple-element.20), channel_id=1, source_target_pairs={{0,1},{1,0},{2,3},{3,2},{4,5},{5,4},{6,7},{7,6},{8,9},{9,8},{10,11... | collective-permute-start | bytes 294920 | tf_op jit(solution)/shard_map/ppermute | solution.py:128
  21.5 8.4 %collective-permute-start.8 = (bf16[48,8,128]{2,1,0:T(8,128)(2,1)S(1)}, bf16[48,8,128]{2,1,0:T(8,128)(2,1)S(1)}, u32[]{:S(2)}, u32[]{:S(2)}) collective-permute-start(bf16[48,8,128]{2,1,0:T(8,128)(2,1)S(1)} %get-tuple-element.19), channel_id=1, source_target_pairs={{0,3},{1,2},{2,1},{3,0},{4,7},{5,6},{6,5},{7,4},{8,11},{9,10},{10,... | collective-permute-start | bytes 294920 | tf_op jit(solution)/shard_map/ppermute | solution.py:128
  23.0 11.0 %collective-permute-start.7 = (bf16[48,8,128]{2,1,0:T(8,128)(2,1)S(1)}, bf16[48,8,128]{2,1,0:T(8,128)(2,1)S(1)}, u32[]{:S(2)}, u32[]{:S(2)}) collective-permute-start(bf16[48,8,128]{2,1,0:T(8,128)(2,1)S(1)} %get-tuple-element.18), channel_id=1, source_target_pairs={{0,2},{1,3},{2,0},{3,1},{4,6},{5,7},{6,4},{7,5},{8,10},{9,11},{10,... | collective-permute-start | bytes 294920 | tf_op jit(solution)/shard_map/ppermute | solution.py:128
  35.0 3.6 %copy-start.4 = (f32[1000]{0:T(1024)S(1)}, f32[1000]{0:T(1024)}, u32[]{:S(2)}) copy-start(f32[1000]{0:T(1024)} %param.16) | copy-start | bytes 12004
  35.0 4.7 %collective-permute-start.10 = (f32[1,2,8,64]{3,2,1,0:T(8,128)S(1)}, f32[1,2,8,64]{3,2,1,0:T(8,128)S(1)}, u32[]{:S(2)}, u32[]{:S(2)}) collective-permute-start(f32[1,2,8,64]{3,2,1,0:T(8,128)S(1)} %get-tuple-element.30), channel_id=1, source_target_pairs={{0,2},{1,3},{2,0},{3,1},{4,6},{5,7},{6,4},{7,5},{8,10},{9,11},{10,... | collective-permute-start | bytes 12296 | tf_op jit(solution)/shard_map/ppermute | solution.py:167
  35.1 3.5 %copy-start.5 = (s32[4]{0:T(128)S(1)}, s32[4]{0:T(128)}, u32[]{:S(2)}) copy-start(s32[4]{0:T(128)} %param.17) | copy-start | bytes 52
  35.1 5.5 %collective-permute-start.11 = (f32[1,2,8,64]{3,2,1,0:T(8,128)S(1)}, f32[1,2,8,64]{3,2,1,0:T(8,128)S(1)}, u32[]{:S(2)}, u32[]{:S(2)}) collective-permute-start(f32[1,2,8,64]{3,2,1,0:T(8,128)S(1)} %get-tuple-element.29), channel_id=1, source_target_pairs={{0,3},{1,2},{2,1},{3,0},{4,7},{5,6},{6,5},{7,4},{8,11},{9,10},{10,... | collective-permute-start | bytes 12296 | tf_op jit(solution)/shard_map/ppermute | solution.py:167
  37.2 3.7 %collective-permute-start.9 = (f32[1,2,8,64]{3,2,1,0:T(8,128)S(1)}, f32[1,2,8,64]{3,2,1,0:T(8,128)S(1)}, u32[]{:S(2)}, u32[]{:S(2)}) collective-permute-start(f32[1,2,8,64]{3,2,1,0:T(8,128)S(1)} %get-tuple-element.31), channel_id=1, source_target_pairs={{0,1},{1,0},{2,3},{3,2},{4,5},{5,4},{6,7},{7,6},{8,9},{9,8},{10,11... | collective-permute-start | bytes 12296 | tf_op jit(solution)/shard_map/ppermute | solution.py:167
  40.8 2.7 %collective-permute-start.12 = (f32[8,64]{1,0:T(8,128)S(1)}, f32[8,64]{1,0:T(8,128)S(1)}, u32[]{:S(2)}, u32[]{:S(2)}) collective-permute-start(f32[8,64]{1,0:T(8,128)S(1)} %fusion.39), channel_id=1, source_target_pairs={{0,4},{4,0},{8,12},{12,8},{1,5},{5,1},{9,13},{13,9},{2,6},{6,2},{1... | collective-permute-start | bytes 6152 | tf_op jit(solution)/shard_map/ppermute | solution.py:62
  40.9 3.7 %collective-permute-start.13 = (f32[8,64]{1,0:T(8,128)S(1)}, f32[8,64]{1,0:T(8,128)S(1)}, u32[]{:S(2)}, u32[]{:S(2)}) collective-permute-start(f32[8,64]{1,0:T(8,128)S(1)} %fusion.39), channel_id=1, source_target_pairs={{0,8},{4,12},{8,0},{12,4},{1,9},{5,13},{9,1},{13,5},{2,10},{6,14},... | collective-permute-start | bytes 6152 | tf_op jit(solution)/shard_map/ppermute | solution.py:62
  42.5 3.0 %collective-permute-start.14 = (f32[8,64]{1,0:T(8,128)S(1)}, f32[8,64]{1,0:T(8,128)S(1)}, u32[]{:S(2)}, u32[]{:S(2)}) collective-permute-start(f32[8,64]{1,0:T(8,128)S(1)} %fusion.39), channel_id=1, source_target_pairs={{0,12},{4,8},{8,4},{12,0},{1,13},{5,9},{9,5},{13,1},{2,14},{6,10},... | collective-permute-start | bytes 6152 | tf_op jit(solution)/shard_map/ppermute | solution.py:62
  42.8 0.7 %copy-start.3 = (f32[64,8]{0,1:T(8,128)S(1)}, f32[64,8]{0,1:T(8,128)}, u32[]{:S(2)}) copy-start(f32[64,8]{0,1:T(8,128)} %param.12) | copy-start | bytes 6148

commit v21 on v19

--- a/solution.py
+++ b/solution.py
@@ -121,9 +121,16 @@
     chunks = [a.reshape(groups, per_dev, tok_dev, head_size) for a in (queries, keys, values)]
     whole_steps = per_dev % (branches * heads) == 0
     if whole_steps and groups & (groups - 1) == 0:
+        sliced = {
+            k: [lax.dynamic_index_in_dim(c, me ^ k, 0, keepdims=False) for c in chunks]
+            for k in range(groups)
+        }
+        if groups > 2:
+            near, far = lax.optimization_barrier((sliced[1], sliced[groups - 1]))
+            sliced[1] = near
         arrived = {}
         for k in reversed(range(groups)):
-            pieces = [lax.dynamic_index_in_dim(c, me ^ k, 0, keepdims=False) for c in chunks]
+            pieces = sliced[k]
             if k:
                 pieces = [lax.ppermute(p, "seq", xor_pairs(groups, k)) for p in pieces]
             arrived[k] = pieces

time: 44.2 us -> 44.3 us (level)
  local copies, waits for them, and re-layouts: 3.25 us -> 4.09 us
  starting transfers between devices: 21.3 us -> 20.5 us
    unnamed x14, local copies, waits for them, and re-layouts: 1.36 us -> 2.21 us
    ppermute x9, starting transfers between devices: 15.8 us -> 15 us  [on_device(): pieces = [lax.ppermute(p, 'seq', xor_pairs(groups, k)) for p in pieces]]
where the time goes in v21:
time: 44.3 us; the launch traced here: 44.1 us
  starting transfers between devices  20.5 us (46%)
  waiting for transfers between devices  14.6 us (33%)
  local copies, waits for them, and re-layouts  4.09 us (9%)
  matrix products  2.3 us (5%)
  other arithmetic  1.72 us (4%)
  between operations  0.84 us (2%)
    ppermute x9, starting transfers between devices, on_device(): pieces = [lax.ppermute(p, 'seq', xor_pairs(groups, k)) for p in pieces]  15 us
    ppermute x9, waiting for transfers between devices, on_device(): pieces = [lax.ppermute(p, 'seq', xor_pairs(groups, k)) for p in pieces]  12.2 us
    ppermute x3, starting transfers between devices, on_device(): sent.append(lax.ppermute(pieces[:, :, k], 'seq', xor_pairs(groups, k)))  3.55 us
    unnamed x14, local copies, waits for them, and re-layouts  2.21 us
    ppermute x3, waiting for transfers between devices, prefix_from_pieces(): other = lax.ppermute(total, 'step', xor_pairs(steps_axis, k))  2 us
    ppermute x3, starting transfers between devices, prefix_from_pieces(): other = lax.ppermute(total, 'step', xor_pairs(steps_axis, k))  1.93 us
    dot_general x4, matrix products, attend(): jnp.einsum('iqk,ikd->iqd', weights[:, :, first:first + size], block, pref...  1.59 us
    squeeze x3, local copies, waits for them, and re-layouts, on_device(): lax.dynamic_index_in_dim(c, me ^ k, 0, keepdims=False)  1.18 us
  transfers between devices with their start and end apart: 15, of which 7 were waited for; matrix products, arithmetic and copies ran while one was open for 7% of the time, Pallas kernels for 0%

profile of v21, /device:TPU:0, one launch (start us, length us, event | category | flops | bytes accessed | tf_op | source)
XLA Modules:
  0.0 44.1 jit_solution(12308218149933168612)
XLA Ops:
  0.0 1.1 %dynamic-slice_bitcast_fusion.9 = (bf16[48,8,128]{2,1,0:T(8,128)(2,1)S(1)}, bf16[48,8,128]{2,1,0:T(8,128)(2,1)S(1)}, bf16[48,8,128]{2,1,0:T(8,128)(2,1)S(1)}, bf16[48,8,128]{2,1,0:T(8,128)(2,1)S(1)}) fusion(bf16[4,48,8,128]{3,2,1,0:T(8,128)(2,1)} %bitcast.222, s32[]{:T(128)S(6)} %select_n.291, s32[]{:T(128)S(6)} %select_n.293, s32[]{:T(128)S(6)} %select_n.292, ...), kind=kLoop, calls=%fused_computation.46 | loop fusion | bytes 786448 | tf_op jit(solution)/shard_map/jit(dynamic_index_in_dim)/squeeze | solution.py:125
  1.1 5.1 %collective-permute-start = (bf16[48,8,128]{2,1,0:T(8,128)(2,1)S(1)}, bf16[48,8,128]{2,1,0:T(8,128)(2,1)S(1)}, u32[]{:S(2)}, u32[]{:S(2)}) collective-permute-start(bf16[48,8,128]{2,1,0:T(8,128)(2,1)S(1)} %get-tuple-element.38), channel_id=1, source_target_pairs={{0,3},{1,2},{2,1},{3,0},{4,7},{5,6},{6,5},{7,4},{8,11},{9,10},{10,... | collective-permute-start | bytes 294920 | tf_op jit(solution)/shard_map/ppermute | solution.py:135
  6.4 0.9 %copy-done.2 = bf16[4,2,24,8,128]{4,3,2,1,0:T(8,128)(2,1)S(1)} copy-done((bf16[4,2,24,8,128]{4,3,2,1,0:T(8,128)(2,1)S(1)}, bf16[4,2,24,8,128]{4,3,2,1,0:T(8,128)(2,1)}, u32[]{:S(2)}) %copy-start.2) | copy-done | bytes 393240
  7.4 2.0 %collective-permute-start.3 = (bf16[48,8,128]{2,1,0:T(8,128)(2,1)S(1)}, bf16[48,8,128]{2,1,0:T(8,128)(2,1)S(1)}, u32[]{:S(2)}, u32[]{:S(2)}) collective-permute-start(bf16[48,8,128]{2,1,0:T(8,128)(2,1)S(1)} %get-tuple-element.19), channel_id=1, source_target_pairs={{0,1},{1,0},{2,3},{3,2},{4,5},{5,4},{6,7},{7,6},{8,9},{9,8},{10,11... | collective-permute-start | bytes 294920 | tf_op jit(solution)/shard_map/ppermute | solution.py:135
  9.4 1.5 %collective-permute-start.4 = (bf16[48,8,128]{2,1,0:T(8,128)(2,1)S(1)}, bf16[48,8,128]{2,1,0:T(8,128)(2,1)S(1)}, u32[]{:S(2)}, u32[]{:S(2)}) collective-permute-start(bf16[48,8,128]{2,1,0:T(8,128)(2,1)S(1)} %get-tuple-element.32), channel_id=1, source_target_pairs={{0,2},{1,3},{2,0},{3,1},{4,6},{5,7},{6,4},{7,5},{8,10},{9,11},{10,... | collective-permute-start | bytes 294920 | tf_op jit(solution)/shard_map/ppermute | solution.py:135
  11.6 3.6 %collective-permute-start.2 = (bf16[48,8,128]{2,1,0:T(8,128)(2,1)S(1)}, bf16[48,8,128]{2,1,0:T(8,128)(2,1)S(1)}, u32[]{:S(2)}, u32[]{:S(2)}) collective-permute-start(bf16[48,8,128]{2,1,0:T(8,128)(2,1)S(1)} %get-tuple-element.36), channel_id=1, source_target_pairs={{0,2},{1,3},{2,0},{3,1},{4,6},{5,7},{6,4},{7,5},{8,10},{9,11},{10,... | collective-permute-start | bytes 294920 | tf_op jit(solution)/shard_map/ppermute | solution.py:135
  15.1 0.5 %collective-permute-done.1 = bf16[48,8,128]{2,1,0:T(8,128)(2,1)S(1)} collective-permute-done((bf16[48,8,128]{2,1,0:T(8,128)(2,1)S(1)}, bf16[48,8,128]{2,1,0:T(8,128)(2,1)S(1)}, u32[]{:S(2)}, u32[]{:S(2)}) %collective-permute-start.1) | collective-permute-done | bytes 98336 | tf_op jit(solution)/shard_map/ppermute | solution.py:135
  15.7 2.4 %collective-permute-start.8 = (bf16[48,8,128]{2,1,0:T(8,128)(2,1)S(1)}, bf16[48,8,128]{2,1,0:T(8,128)(2,1)S(1)}, u32[]{:S(2)}, u32[]{:S(2)}) collective-permute-start(bf16[48,8,128]{2,1,0:T(8,128)(2,1)S(1)} %get-tuple-element.29), channel_id=1, source_target_pairs={{0,3},{1,2},{2,1},{3,0},{4,7},{5,6},{6,5},{7,4},{8,11},{9,10},{10,... | collective-permute-start | bytes 294920 | tf_op jit(solution)/shard_map/ppermute | solution.py:135
  18.3 5.6 %collective-permute-done.4 = bf16[48,8,128]{2,1,0:T(8,128)(2,1)S(1)} collective-permute-done((bf16[48,8,128]{2,1,0:T(8,128)(2,1)S(1)}, bf16[48,8,128]{2,1,0:T(8,128)(2,1)S(1)}, u32[]{:S(2)}, u32[]{:S(2)}) %collective-permute-start.4) | collective-permute-done | bytes 98336 | tf_op jit(solution)/shard_map/ppermute | solution.py:135
  23.9 3.2 %collective-permute-done.2 = bf16[48,8,128]{2,1,0:T(8,128)(2,1)S(1)} collective-permute-done((bf16[48,8,128]{2,1,0:T(8,128)(2,1)S(1)}, bf16[48,8,128]{2,1,0:T(8,128)(2,1)S(1)}, u32[]{:S(2)}, u32[]{:S(2)}) %collective-permute-start.2) | collective-permute-done | bytes 98336 | tf_op jit(solution)/shard_map/ppermute | solution.py:135
  27.1 0.5 %fusion.81 = (f32[48,32]{1,0:T(8,128)S(1)}, bf16[48,32,32]{1,2,0:T(8,128)(2,1)S(1)}) fusion(bf16[48,8,128]{2,1,0:T(8,128)(2,1)S(1)} %collective-permute-done, bf16[48,8,128]{2,1,0:T(8,128)(2,1)S(1)} %collective-permute-done.2, bf16[48,8,128]{2,1,0:T(8,128)(2,1)S(1)} %collective-permute-done.1, bf16[48,8,128]{2,1,0:T(8,128)(2,1)S(1)} %get-tuple-element.35, ...), kind=kOutput, calls=%fused_computation.111 | convolution fusion | flops 15925279 | bytes 890880 | tf_op jit(solution)/shard_map/sub | solution.py:21
  28.6 2.9 %collective-permute-done.7 = bf16[48,8,128]{2,1,0:T(8,128)(2,1)S(1)} collective-permute-done((bf16[48,8,128]{2,1,0:T(8,128)(2,1)S(1)}, bf16[48,8,128]{2,1,0:T(8,128)(2,1)S(1)}, u32[]{:S(2)}, u32[]{:S(2)}) %collective-permute-start.7) | collective-permute-done | bytes 98336 | tf_op jit(solution)/shard_map/ppermute | solution.py:135
  31.4 0.7 %multiply_reduce_fusion = (f32[48,32]{1,0:T(8,128)S(1)}, bf16[48,32,128]{2,1,0:T(8,128)(2,1)S(1)}) fusion(f32[48,32]{1,0:T(8,128)S(1)} %get-tuple-element.26, f32[48,32,128]{2,1,0:T(8,128)S(1)} %fusion.27, f32[48,32,128]{2,1,0:T(8,128)S(1)} %convolution_add_fusion.1, bf16[48,8,128]{2,1,0:T(8,128)(2,1)S(1)} %collective-permute-done.7, ...), kind=kOutput, calls=%fused_computation.12 | convolution fusion | flops 4520448 | bytes 2193408 | tf_op jit(solution)/shard_map/iqk,ikd->iqd/dot_general | solution.py:29
  32.4 0.9 %collective-permute-start.10 = (f32[1,2,8,64]{3,2,1,0:T(8,128)S(1)}, f32[1,2,8,64]{3,2,1,0:T(8,128)S(1)}, u32[]{:S(2)}, u32[]{:S(2)}) collective-permute-start(f32[1,2,8,64]{3,2,1,0:T(8,128)S(1)} %get-tuple-element.40), channel_id=1, source_target_pairs={{0,2},{1,3},{2,0},{3,1},{4,6},{5,7},{6,4},{7,5},{8,10},{9,11},{10,... | collective-permute-start | bytes 12296 | tf_op jit(solution)/shard_map/ppermute | solution.py:174
  33.3 1.7 %collective-permute-start.11 = (f32[1,2,8,64]{3,2,1,0:T(8,128)S(1)}, f32[1,2,8,64]{3,2,1,0:T(8,128)S(1)}, u32[]{:S(2)}, u32[]{:S(2)}) collective-permute-start(f32[1,2,8,64]{3,2,1,0:T(8,128)S(1)} %get-tuple-element.39), channel_id=1, source_target_pairs={{0,3},{1,2},{2,1},{3,0},{4,7},{5,6},{6,5},{7,4},{8,11},{9,10},{10,... | collective-permute-start | bytes 12296 | tf_op jit(solution)/shard_map/ppermute | solution.py:174
  35.0 0.9 %collective-permute-start.9 = (f32[1,2,8,64]{3,2,1,0:T(8,128)S(1)}, f32[1,2,8,64]{3,2,1,0:T(8,128)S(1)}, u32[]{:S(2)}, u32[]{:S(2)}) collective-permute-start(f32[1,2,8,64]{3,2,1,0:T(8,128)S(1)} %get-tuple-element.41), channel_id=1, source_target_pairs={{0,1},{1,0},{2,3},{3,2},{4,5},{5,4},{6,7},{7,6},{8,9},{9,8},{10,11... | collective-permute-start | bytes 12296 | tf_op jit(solution)/shard_map/ppermute | solution.py:174
  36.3 0.7 %copy-done.6 = f32[8]{0:T(128)S(1)} copy-done((f32[8]{0:T(128)S(1)}, f32[8]{0:T(128)}, u32[]{:S(2)}) %copy-start.6) | copy-done | bytes 56
  37.0 0.6 %fusion.67 = f32[]{:T(128)} fusion(f32[8]{0:T(128)S(1)} %copy-done.6, s32[]{:T(128)} %bitcast.221), kind=kLoop, calls=%fused_computation.105 | loop fusion | flops 23 | bytes 40 | tf_op jit(solution)/shard_map/reduce_sum | solution.py:13
  37.7 0.6 %stack.4 = f32[2,4,1,8,64]{4,3,2,1,0:T(8,128)S(1)} pad(f32[1,4,1,8,64]{4,3,2,1,0:T(8,128)S(1)} %stack_broadcast_in_dim.2, f32[]{:T(128)} %fusion.67), padding=1_0x0_0x0_0x0_0x0_0 | pad | bytes 24580 | tf_op jit(solution)/shard_map/stack | solution.py:182
  38.9 1.6 %collective-permute-start.13 = (f32[8,64]{1,0:T(8,128)S(1)}, f32[8,64]{1,0:T(8,128)S(1)}, u32[]{:S(2)}, u32[]{:S(2)}) collective-permute-start(f32[8,64]{1,0:T(8,128)S(1)} %fusion.39), channel_id=1, source_target_pairs={{0,8},{4,12},{8,0},{12,4},{1,9},{5,13},{9,1},{13,5},{2,10},{6,14},... | collective-permute-start | bytes 6152 | tf_op jit(solution)/shard_map/ppermute | solution.py:62
  40.8 0.7 %copy-done.3 = f32[64,8]{0,1:T(8,128)S(1)} copy-done((f32[64,8]{0,1:T(8,128)S(1)}, f32[64,8]{0,1:T(8,128)}, u32[]{:S(2)}) %copy-start.3) | copy-done | bytes 2072
  41.5 1.1 %collective-permute-done.13 = f32[8,64]{1,0:T(8,128)S(1)} collective-permute-done((f32[8,64]{1,0:T(8,128)S(1)}, f32[8,64]{1,0:T(8,128)S(1)}, u32[]{:S(2)}, u32[]{:S(2)}) %collective-permute-start.13) | collective-permute-done | bytes 2080 | tf_op jit(solution)/shard_map/ppermute | solution.py:62
  42.5 0.9 %collective-permute-done.14 = f32[8,64]{1,0:T(8,128)S(1)} collective-permute-done((f32[8,64]{1,0:T(8,128)S(1)}, f32[8,64]{1,0:T(8,128)S(1)}, u32[]{:S(2)}, u32[]{:S(2)}) %collective-permute-start.14) | collective-permute-done | bytes 2080 | tf_op jit(solution)/shard_map/ppermute | solution.py:62
  43.5 0.6 %add_bitcast_fusion = f32[4,64,8]{1,2,0:T(8,128)} fusion(f32[4,8,64]{2,1,0:T(8,128)S(1)} %maximum_add_fusion, f32[8,64]{1,0:T(8,128)S(1)} %select_add_fusion), kind=kLoop, calls=%fused_computation.49 | loop fusion | flops 2048 | bytes 18432 | tf_op jit(solution)/shard_map/transpose | solution.py:64
  (44 shorter events, 3.0 us)
Async XLA Ops:
  0.0 32.1 %copy-start = (bf16[64,3072]{1,0:T(8,128)(2,1)S(1)}, bf16[64,3072]{1,0:T(8,128)(2,1)}, u32[]{:S(2)}) copy-start(bf16[64,3072]{1,0:T(8,128)(2,1)} %param.13) | copy-start | bytes 1179652
  0.0 6.3 %copy-start.1 = (bf16[4,2,24,8,128]{4,3,2,1,0:T(8,128)(2,1)S(1)}, bf16[4,2,24,8,128]{4,3,2,1,0:T(8,128)(2,1)}, u32[]{:S(2)}) copy-start(bf16[4,2,24,8,128]{4,3,2,1,0:T(8,128)(2,1)} %param.10) | copy-start | bytes 1179652
  1.1 10.4 %collective-permute-start = (bf16[48,8,128]{2,1,0:T(8,128)(2,1)S(1)}, bf16[48,8,128]{2,1,0:T(8,128)(2,1)S(1)}, u32[]{:S(2)}, u32[]{:S(2)}) collective-permute-start(bf16[48,8,128]{2,1,0:T(8,128)(2,1)S(1)} %get-tuple-element.38), channel_id=1, source_target_pairs={{0,3},{1,2},{2,1},{3,0},{4,7},{5,6},{6,5},{7,4},{8,11},{9,10},{10,... | collective-permute-start | bytes 294920 | tf_op jit(solution)/shard_map/ppermute | solution.py:135
  6.3 1.0 %copy-start.2 = (bf16[4,2,24,8,128]{4,3,2,1,0:T(8,128)(2,1)S(1)}, bf16[4,2,24,8,128]{4,3,2,1,0:T(8,128)(2,1)}, u32[]{:S(2)}) copy-start(bf16[4,2,24,8,128]{4,3,2,1,0:T(8,128)(2,1)} %param.11) | copy-start | bytes 1179652
  6.3 17.6 %collective-permute-start.5 = (bf16[48,8,128]{2,1,0:T(8,128)(2,1)S(1)}, bf16[48,8,128]{2,1,0:T(8,128)(2,1)S(1)}, u32[]{:S(2)}, u32[]{:S(2)}) collective-permute-start(bf16[48,8,128]{2,1,0:T(8,128)(2,1)S(1)} %get-tuple-element.33), channel_id=1, source_target_pairs={{0,3},{1,2},{2,1},{3,0},{4,7},{5,6},{6,5},{7,4},{8,11},{9,10},{10,... | collective-permute-start | bytes 294920 | tf_op jit(solution)/shard_map/ppermute | solution.py:135
  7.3 8.4 %collective-permute-start.1 = (bf16[48,8,128]{2,1,0:T(8,128)(2,1)S(1)}, bf16[48,8,128]{2,1,0:T(8,128)(2,1)S(1)}, u32[]{:S(2)}, u32[]{:S(2)}) collective-permute-start(bf16[48,8,128]{2,1,0:T(8,128)(2,1)S(1)} %get-tuple-element.17), channel_id=1, source_target_pairs={{0,1},{1,0},{2,3},{3,2},{4,5},{5,4},{6,7},{7,6},{8,9},{9,8},{10,11... | collective-permute-start | bytes 294920 | tf_op jit(solution)/shard_map/ppermute | solution.py:135
  7.4 10.7 %collective-permute-start.3 = (bf16[48,8,128]{2,1,0:T(8,128)(2,1)S(1)}, bf16[48,8,128]{2,1,0:T(8,128)(2,1)S(1)}, u32[]{:S(2)}, u32[]{:S(2)}) collective-permute-start(bf16[48,8,128]{2,1,0:T(8,128)(2,1)S(1)} %get-tuple-element.19), channel_id=1, source_target_pairs={{0,1},{1,0},{2,3},{3,2},{4,5},{5,4},{6,7},{7,6},{8,9},{9,8},{10,11... | collective-permute-start | bytes 294920 | tf_op jit(solution)/shard_map/ppermute | solution.py:135
  9.4 14.5 %collective-permute-start.4 = (bf16[48,8,128]{2,1,0:T(8,128)(2,1)S(1)}, bf16[48,8,128]{2,1,0:T(8,128)(2,1)S(1)}, u32[]{:S(2)}, u32[]{:S(2)}) collective-permute-start(bf16[48,8,128]{2,1,0:T(8,128)(2,1)S(1)} %get-tuple-element.32), channel_id=1, source_target_pairs={{0,2},{1,3},{2,0},{3,1},{4,6},{5,7},{6,4},{7,5},{8,10},{9,11},{10,... | collective-permute-start | bytes 294920 | tf_op jit(solution)/shard_map/ppermute | solution.py:135
  11.6 15.5 %collective-permute-start.2 = (bf16[48,8,128]{2,1,0:T(8,128)(2,1)S(1)}, bf16[48,8,128]{2,1,0:T(8,128)(2,1)S(1)}, u32[]{:S(2)}, u32[]{:S(2)}) collective-permute-start(bf16[48,8,128]{2,1,0:T(8,128)(2,1)S(1)} %get-tuple-element.36), channel_id=1, source_target_pairs={{0,2},{1,3},{2,0},{3,1},{4,6},{5,7},{6,4},{7,5},{8,10},{9,11},{10,... | collective-permute-start | bytes 294920 | tf_op jit(solution)/shard_map/ppermute | solution.py:135
  15.7 12.6 %collective-permute-start.8 = (bf16[48,8,128]{2,1,0:T(8,128)(2,1)S(1)}, bf16[48,8,128]{2,1,0:T(8,128)(2,1)S(1)}, u32[]{:S(2)}, u32[]{:S(2)}) collective-permute-start(bf16[48,8,128]{2,1,0:T(8,128)(2,1)S(1)} %get-tuple-element.29), channel_id=1, source_target_pairs={{0,3},{1,2},{2,1},{3,0},{4,7},{5,6},{6,5},{7,4},{8,11},{9,10},{10,... | collective-permute-start | bytes 294920 | tf_op jit(solution)/shard_map/ppermute | solution.py:135
  18.1 9.9 %collective-permute-start.6 = (bf16[48,8,128]{2,1,0:T(8,128)(2,1)S(1)}, bf16[48,8,128]{2,1,0:T(8,128)(2,1)S(1)}, u32[]{:S(2)}, u32[]{:S(2)}) collective-permute-start(bf16[48,8,128]{2,1,0:T(8,128)(2,1)S(1)} %get-tuple-element.20), channel_id=1, source_target_pairs={{0,1},{1,0},{2,3},{3,2},{4,5},{5,4},{6,7},{7,6},{8,9},{9,8},{10,11... | collective-permute-start | bytes 294920 | tf_op jit(solution)/shard_map/ppermute | solution.py:135
  23.9 7.5 %collective-permute-start.7 = (bf16[48,8,128]{2,1,0:T(8,128)(2,1)S(1)}, bf16[48,8,128]{2,1,0:T(8,128)(2,1)S(1)}, u32[]{:S(2)}, u32[]{:S(2)}) collective-permute-start(bf16[48,8,128]{2,1,0:T(8,128)(2,1)S(1)} %get-tuple-element.28), channel_id=1, source_target_pairs={{0,2},{1,3},{2,0},{3,1},{4,6},{5,7},{6,4},{7,5},{8,10},{9,11},{10,... | collective-permute-start | bytes 294920 | tf_op jit(solution)/shard_map/ppermute | solution.py:135
  32.4 3.6 %copy-start.4 = (f32[1000]{0:T(1024)S(1)}, f32[1000]{0:T(1024)}, u32[]{:S(2)}) copy-start(f32[1000]{0:T(1024)} %param.16) | copy-start | bytes 12004
  32.4 6.0 %collective-permute-start.10 = (f32[1,2,8,64]{3,2,1,0:T(8,128)S(1)}, f32[1,2,8,64]{3,2,1,0:T(8,128)S(1)}, u32[]{:S(2)}, u32[]{:S(2)}) collective-permute-start(f32[1,2,8,64]{3,2,1,0:T(8,128)S(1)} %get-tuple-element.40), channel_id=1, source_target_pairs={{0,2},{1,3},{2,0},{3,1},{4,6},{5,7},{6,4},{7,5},{8,10},{9,11},{10,... | collective-permute-start | bytes 12296 | tf_op jit(solution)/shard_map/ppermute | solution.py:174
  33.3 2.6 %copy-start.5 = (s32[4]{0:T(128)S(1)}, s32[4]{0:T(128)}, u32[]{:S(2)}) copy-start(s32[4]{0:T(128)} %param.17) | copy-start | bytes 52
  33.3 5.4 %collective-permute-start.11 = (f32[1,2,8,64]{3,2,1,0:T(8,128)S(1)}, f32[1,2,8,64]{3,2,1,0:T(8,128)S(1)}, u32[]{:S(2)}, u32[]{:S(2)}) collective-permute-start(f32[1,2,8,64]{3,2,1,0:T(8,128)S(1)} %get-tuple-element.39), channel_id=1, source_target_pairs={{0,3},{1,2},{2,1},{3,0},{4,7},{5,6},{6,5},{7,4},{8,11},{9,10},{10,... | collective-permute-start | bytes 12296 | tf_op jit(solution)/shard_map/ppermute | solution.py:174
  35.0 3.7 %collective-permute-start.9 = (f32[1,2,8,64]{3,2,1,0:T(8,128)S(1)}, f32[1,2,8,64]{3,2,1,0:T(8,128)S(1)}, u32[]{:S(2)}, u32[]{:S(2)}) collective-permute-start(f32[1,2,8,64]{3,2,1,0:T(8,128)S(1)} %get-tuple-element.41), channel_id=1, source_target_pairs={{0,1},{1,0},{2,3},{3,2},{4,5},{5,4},{6,7},{7,6},{8,9},{9,8},{10,11... | collective-permute-start | bytes 12296 | tf_op jit(solution)/shard_map/ppermute | solution.py:174
  36.3 0.7 %copy-start.6 = (f32[8]{0:T(128)S(1)}, f32[8]{0:T(128)}, u32[]{:S(2)}) copy-start(f32[8]{0:T(128)} %param.14) | copy-start | bytes 100
  38.8 2.7 %collective-permute-start.12 = (f32[8,64]{1,0:T(8,128)S(1)}, f32[8,64]{1,0:T(8,128)S(1)}, u32[]{:S(2)}, u32[]{:S(2)}) collective-permute-start(f32[8,64]{1,0:T(8,128)S(1)} %fusion.39), channel_id=1, source_target_pairs={{0,4},{4,0},{8,12},{12,8},{1,5},{5,1},{9,13},{13,9},{2,6},{6,2},{1... | collective-permute-start | bytes 6152 | tf_op jit(solution)/shard_map/ppermute | solution.py:62
  38.9 3.7 %collective-permute-start.13 = (f32[8,64]{1,0:T(8,128)S(1)}, f32[8,64]{1,0:T(8,128)S(1)}, u32[]{:S(2)}, u32[]{:S(2)}) collective-permute-start(f32[8,64]{1,0:T(8,128)S(1)} %fusion.39), channel_id=1, source_target_pairs={{0,8},{4,12},{8,0},{12,4},{1,9},{5,13},{9,1},{13,5},{2,10},{6,14},... | collective-permute-start | bytes 6152 | tf_op jit(solution)/shard_map/ppermute | solution.py:62
  40.4 3.0 %collective-permute-start.14 = (f32[8,64]{1,0:T(8,128)S(1)}, f32[8,64]{1,0:T(8,128)S(1)}, u32[]{:S(2)}, u32[]{:S(2)}) collective-permute-start(f32[8,64]{1,0:T(8,128)S(1)} %fusion.39), channel_id=1, source_target_pairs={{0,12},{4,8},{8,4},{12,0},{1,13},{5,9},{9,5},{13,1},{2,14},{6,10},... | collective-permute-start | bytes 6152 | tf_op jit(solution)/shard_map/ppermute | solution.py:62
  40.8 0.7 %copy-start.3 = (f32[64,8]{0,1:T(8,128)S(1)}, f32[64,8]{0,1:T(8,128)}, u32[]{:S(2)}) copy-start(f32[64,8]{0,1:T(8,128)} %param.12) | copy-start | bytes 6148
